TPU v7x, 32 devices: a whole 2x2x4 slice. The times are simulated.
32 devices in a mesh: img: 8 (over z, core), slab: 4 (over y, x).
Axes of the slice: x: 2, y: 2, z: 4, core: 2. Of those that a mesh axis runs over, the one named last changes fastest.
Arguments:
- image_masses: float32 [8, 3072, 3072], P('img', 'slab'), may hold values from 0.1 to 10
- dual_multipliers: float32 [8, 3072, 3072], P('img', 'slab'), may hold values from 0.1 to 10
- fraction_tops: int32 [8], P('img'), may hold values from 1 to 8
- banded_submatrices: bfloat16 [24, 3, 128, 128], replicated, as said below
- band_starts: int32 [24, 3], replicated, may hold values from -2 to 2, as said below
Outputs:
- barycenter: float32 [3072, 3072], P('slab')
- new_scalings: float32 [8, 3072, 3072], P('img', 'slab')
Inputs may be any that keep to these rules, and one draw needn't show every extreme that they name: `band_starts`: each row of offsets holds three consecutive numbers in increasing order; the first row is 0, 1, 2 and the last row is -2, -1, 0. `banded_submatrices`: all entries are positive.
All inputs are finite; a program needn't handle non-finite values.
Results may differ from a plain program's by a relative error of at most 0.0032.
Values may be sent and summed in bfloat16 or wider, within the bound.
No kernel may reach another device: no remote copies, remote signals or barrier semaphores. Data moves between devices by JAX's collectives and lax.ppermute only.
A program may use at most 192 MiB of HBM per device.

v0:
```python
import jax
import jax.numpy as jnp
from jax import lax
from jax.sharding import PartitionSpec as P

ITERS = 2


def offset_terms(banded_submatrices, band_starts):
    offsets = jnp.arange(-2, 3, dtype=jnp.int32)
    matches = band_starts[:, None, :] == offsets[None, :, None]
    picked = jnp.where(
        matches[:, :, :, None, None], banded_submatrices[:, None], jnp.zeros((), jnp.bfloat16)
    )
    return jnp.sum(picked, axis=2)


def column_sweep(field, terms):
    block_stack = terms.shape[0]
    width = terms.shape[2]
    count = field.shape[0]
    height = field.shape[1]
    leading = field.reshape((count * height, block_stack, width)).transpose(1, 0, 2)
    padded = jnp.pad(leading, ((2, 2), (0, 0), (0, 0)))
    total = jnp.zeros((block_stack, count * height, width), jnp.float32)
    for offset in range(5):
        total = total + lax.dot_general(
            padded[offset : offset + block_stack],
            terms[:, offset],
            (((2,), (2,)), ((0,), (0,))),
            preferred_element_type=jnp.float32,
        )
    return total.transpose(1, 0, 2).reshape((count, height, block_stack * width))


def rows_pass(padded, terms):
    block_stack = terms.shape[0]
    width = terms.shape[2]
    columns = padded.shape[2]
    split = padded[0].reshape((block_stack + 4, width, columns))
    total = jnp.zeros((block_stack, width, columns), jnp.float32)
    for offset in range(5):
        total = total + lax.dot_general(
            terms[:, offset],
            split[offset : offset + block_stack],
            (((2,), (1,)), ((0,), (0,))),
            preferred_element_type=jnp.float32,
        )
    outputs = [total.reshape((block_stack * width, columns))]
    return jnp.stack(outputs, axis=0)


def per_device(image_masses, dual_multipliers, fraction_tops, banded_submatrices, band_starts):
    width = banded_submatrices.shape[2]
    terms = offset_terms(banded_submatrices, band_starts)
    total_weight = lax.psum(jnp.sum(fraction_tops).astype(jnp.float32), "img")
    weights = fraction_tops.astype(jnp.float32)

    def apply_kernel(field):
        inner = column_sweep(field, terms).astype(jnp.bfloat16)
        columns = lax.all_to_all(inner, "slab", split_axis=2, concat_axis=1, tiled=True)
        padded = jnp.pad(columns, ((0, 0), (2 * width, 2 * width), (0, 0)))
        result = rows_pass(padded, terms).astype(jnp.bfloat16)
        return lax.all_to_all(result, "slab", split_axis=1, concat_axis=2, tiled=True)

    latest_multiplier = dual_multipliers
    barycenter = jnp.zeros(image_masses.shape[1:], jnp.float32)
    for iteration in range(ITERS):
        kernel_v = apply_kernel(latest_multiplier.astype(jnp.bfloat16))
        scaled_u = (image_masses / kernel_v.astype(jnp.float32)).astype(jnp.bfloat16)
        kernel_u = apply_kernel(scaled_u)
        value_portion = jnp.einsum("i,irc->rc", weights, jnp.log(kernel_u.astype(jnp.float32)))
        barycenter = jnp.exp(lax.psum(value_portion, "img") / total_weight)
        latest_multiplier = barycenter[None] / kernel_u.astype(jnp.float32)
    return (barycenter, latest_multiplier)


def solution(mesh):
    placed = (P("img", "slab", None), P("img", "slab", None), P("img"), P(), P())
    return jax.shard_map(
        per_device,
        mesh=mesh,
        in_specs=placed,
        out_specs=(P("slab", None), P("img", "slab", None)),
        check_vma=False,
    )
```

profile of v0, /device:TPU:0, one launch (start us, length us, event | category | flops | bytes accessed | tf_op | source)
XLA Modules:
  0.0 2068.6 jit_solution(6369687439953317268)
XLA Ops:
  50.3 16.8 fusion.3
  77.7 49.0 %reduce.1 = bf16[3072,768]{1,0:T(8,128)(2,1)} reduce(bf16[3072,1,768]{2,1,0:T(2,128)(2,1)} %bitcast.287, bf16[]{:T(256)} %broadcast.49), dimensions={1}, to_apply=%bitcast.273.reduce_sub_computation | reduce | bytes 9437186
  132.1 61.0 %all_to_all.108 = bf16[4,2,294912]{2,1,0:T(2,128)(2,1)} all-to-all(bf16[4,2,294912]{2,1,0:T(2,128)(2,1)} %reshape.244), channel_id=1, replica_groups=mesh['img'=8,'slab'=4] {'slab'}, dimensions={0} | all-to-all | bytes 9437184 | tf_op jit(solution)/shard_map/all_to_all | solution.py:61
  241.3 18.2 add_convert_fusion.6
  269.0 49.2 %reduce.2 = bf16[3072,768]{1,0:T(8,128)(2,1)} reduce(bf16[3072,1,768]{2,1,0:T(2,128)(2,1)} %bitcast.290, bf16[]{:T(256)} %broadcast.49), dimensions={1}, to_apply=%bitcast.272.reduce_sub_computation | reduce | bytes 9437186
  338.2 42.8 %all-to-all-done.1 = bf16[4,2,294912]{2,1,0:T(2,128)(2,1)} async-done(((bf16[4,2,294912]{2,1,0:T(2,128)(2,1)}), bf16[4,2,294912]{2,1,0:T(2,128)(2,1)}, u32[]{:S(2)}, u32[]{:S(2)}) %all-to-all-start.1) | async-done | bytes 4718624 | tf_op jit(solution)/shard_map/all_to_all | solution.py:64
  389.0 23.5 %copy.138 = f32[1,4,768,768]{2,3,1,0:T(8,128)} copy(bf16[1,4,768,768]{3,0,2,1:T(2,128)(2,1)} %bitcast.291) | data formatting | bytes 14155776 | tf_op jit(solution)/shard_map/convert_element_type | solution.py:70
  452.1 16.8 add_convert_fusion.5
  478.4 49.4 %reduce.3 = bf16[3072,768]{1,0:T(8,128)(2,1)} reduce(bf16[3072,1,768]{2,1,0:T(2,128)(2,1)} %bitcast.292, bf16[]{:T(256)} %broadcast.49), dimensions={1}, to_apply=%bitcast.271.reduce_sub_computation | reduce | bytes 9437186
  533.1 58.9 %all_to_all.109 = bf16[4,2,294912]{2,1,0:T(2,128)(2,1)} all-to-all(bf16[4,2,294912]{2,1,0:T(2,128)(2,1)} %reshape.248), channel_id=1, replica_groups=mesh['img'=8,'slab'=4] {'slab'}, dimensions={0} | all-to-all | bytes 9437184 | tf_op jit(solution)/shard_map/all_to_all | solution.py:61
  640.1 18.1 add_convert_fusion.4
  667.7 49.1 %reduce.4 = bf16[3072,768]{1,0:T(8,128)(2,1)} reduce(bf16[3072,1,768]{2,1,0:T(2,128)(2,1)} %bitcast.294, bf16[]{:T(256)} %broadcast.49), dimensions={1}, to_apply=%bitcast.270.reduce_sub_computation | reduce | bytes 9437186
  727.9 50.3 %all-to-all-done.3 = bf16[4,2,294912]{2,1,0:T(2,128)(2,1)} async-done(((bf16[4,2,294912]{2,1,0:T(2,128)(2,1)}), bf16[4,2,294912]{2,1,0:T(2,128)(2,1)}, u32[]{:S(2)}, u32[]{:S(2)}) %all-to-all-start.3) | async-done | bytes 4718624 | tf_op jit(solution)/shard_map/all_to_all | solution.py:64
  801.7 23.3 %copy.145 = f32[1,4,768,768]{2,3,1,0:T(8,128)} copy(f32[1,4,768,768]{3,0,2,1:T(1,128)} %bitcast.302) | data formatting | bytes 18874368 | tf_op jit(solution)/shard_map/i,irc->rc/dot_general | solution.py:72
  825.0 16.9 psum.22
  841.9 23.6 %copy.146 = f32[1,4,768,768]{2,3,1,0:T(8,128)} copy(bf16[1,4,768,768]{3,0,2,1:T(2,128)(2,1)} %bitcast.274) | data formatting | bytes 14155776 | tf_op jit(solution)/shard_map/convert_element_type | solution.py:72
  865.5 155.0 %all-reduce.11.cloned.1.call-done = f32[768,3072]{0,1:T(8,128)} async-done(((f32[768,3072]{0,1:T(8,128)}), f32[768,3072]{0,1:T(8,128)}) %all-reduce.11.cloned.1.call-update) | async-done | bytes 9437200 | tf_op jit(solution)/shard_map/psum | solution.py:73
  1086.8 49.4 %reduce.5 = bf16[3072,768]{1,0:T(8,128)(2,1)} reduce(bf16[3072,1,768]{2,1,0:T(2,128)(2,1)} %bitcast.295, bf16[]{:T(256)} %broadcast.49), dimensions={1}, to_apply=%bitcast.269.reduce_sub_computation | reduce | bytes 9437186
  1141.6 59.5 %all_to_all.110 = bf16[4,2,294912]{2,1,0:T(2,128)(2,1)} all-to-all(bf16[4,2,294912]{2,1,0:T(2,128)(2,1)} %reshape.252), channel_id=1, replica_groups=mesh['img'=8,'slab'=4] {'slab'}, dimensions={0} | all-to-all | bytes 9437184 | tf_op jit(solution)/shard_map/all_to_all | solution.py:61
  1249.2 18.1 add_convert_fusion.2
  1276.9 49.1 %reduce.6 = bf16[3072,768]{1,0:T(8,128)(2,1)} reduce(bf16[3072,1,768]{2,1,0:T(2,128)(2,1)} %bitcast.297, bf16[]{:T(256)} %broadcast.49), dimensions={1}, to_apply=%bitcast.268.reduce_sub_computation | reduce | bytes 9437186
  1331.4 58.2 %all_to_all.111 = bf16[4,2,294912]{2,1,0:T(2,128)(2,1)} all-to-all(bf16[4,2,294912]{2,1,0:T(2,128)(2,1)} %reshape.254), channel_id=1, replica_groups=mesh['img'=8,'slab'=4] {'slab'}, dimensions={0} | all-to-all | bytes 9437184 | tf_op jit(solution)/shard_map/all_to_all | solution.py:64
  1397.6 23.5 %copy.152 = f32[1,4,768,768]{2,3,1,0:T(8,128)} copy(bf16[1,4,768,768]{3,0,2,1:T(2,128)(2,1)} %bitcast.298) | data formatting | bytes 14155776 | tf_op jit(solution)/shard_map/convert_element_type | solution.py:70
  1460.6 16.8 add_convert_fusion.1
  1486.9 49.4 %reduce.7 = bf16[3072,768]{1,0:T(8,128)(2,1)} reduce(bf16[3072,1,768]{2,1,0:T(2,128)(2,1)} %bitcast.299, bf16[]{:T(256)} %broadcast.49), dimensions={1}, to_apply=%bitcast.267.reduce_sub_computation | reduce | bytes 9437186
  1541.8 56.8 %all_to_all.112 = bf16[4,2,294912]{2,1,0:T(2,128)(2,1)} all-to-all(bf16[4,2,294912]{2,1,0:T(2,128)(2,1)} %reshape.256), channel_id=1, replica_groups=mesh['img'=8,'slab'=4] {'slab'}, dimensions={0} | all-to-all | bytes 9437184 | tf_op jit(solution)/shard_map/all_to_all | solution.py:61
  1646.7 18.2 add_convert_fusion
  1674.4 49.2 %reduce.8 = bf16[3072,768]{1,0:T(8,128)(2,1)} reduce(bf16[3072,1,768]{2,1,0:T(2,128)(2,1)} %bitcast.288, bf16[]{:T(256)} %broadcast.49), dimensions={1}, to_apply=%bitcast.266.reduce_sub_computation | reduce | bytes 9437186
  1729.0 55.4 %all_to_all.113 = bf16[4,2,294912]{2,1,0:T(2,128)(2,1)} all-to-all(bf16[4,2,294912]{2,1,0:T(2,128)(2,1)} %reshape.258), channel_id=1, replica_groups=mesh['img'=8,'slab'=4] {'slab'}, dimensions={0} | all-to-all | bytes 9437184 | tf_op jit(solution)/shard_map/all_to_all | solution.py:64
  1807.7 23.3 %copy.159 = f32[1,4,768,768]{2,3,1,0:T(8,128)} copy(f32[1,4,768,768]{3,0,2,1:T(1,128)} %bitcast.301) | data formatting | bytes 18874368 | tf_op jit(solution)/shard_map/i,irc->rc/dot_general | solution.py:72
  1831.0 23.5 %copy.160 = f32[1,4,768,768]{2,3,1,0:T(8,128)} copy(bf16[1,4,768,768]{3,0,2,1:T(2,128)(2,1)} %bitcast.275) | data formatting | bytes 14155776 | tf_op jit(solution)/shard_map/convert_element_type | solution.py:72
  1854.5 172.9 %all-reduce.13.cloned.1.call-done = f32[768,3072]{0,1:T(8,128)} async-done(((f32[768,3072]{0,1:T(8,128)}), f32[768,3072]{0,1:T(8,128)}) %all-reduce.13.cloned.1.call-update) | async-done | bytes 9437200 | tf_op jit(solution)/shard_map/psum | solution.py:73
  (128 shorter events, 608.5 us)
Async XLA Ops:
  15.6 6.9 copy-start.16
  26.3 18.9 copy-start
  26.3 8.9 copy-start.12
  214.4 7.8 copy-start.8
  222.3 3.8 copy-start.1
  323.6 57.3 %all-to-all-start.1 = ((bf16[4,2,294912]{2,1,0:T(2,128)(2,1)}), bf16[4,2,294912]{2,1,0:T(2,128)(2,1)}, u32[]{:S(2)}, u32[]{:S(2)}) async-start(bf16[4,2,294912]{2,1,0:T(2,128)(2,1)} %reshape.246), calls=%async_computation.1 | async-start | bytes 9437184 | tf_op jit(solution)/shard_map/all_to_all | solution.py:64
  429.2 7.7 copy-start.2
  429.2 7.7 copy-start.13
  613.3 7.7 copy-start.9
  621.0 3.8 copy-start.3
  722.3 56.0 %all-to-all-start.3 = ((bf16[4,2,294912]{2,1,0:T(2,128)(2,1)}), bf16[4,2,294912]{2,1,0:T(2,128)(2,1)}, u32[]{:S(2)}, u32[]{:S(2)}) async-start(bf16[4,2,294912]{2,1,0:T(2,128)(2,1)} %reshape.250), calls=%async_computation.3 | async-start | bytes 9437184 | tf_op jit(solution)/shard_map/all_to_all | solution.py:64
  727.2 293.3 %all-reduce.11.cloned.1.call-start = ((), (), s32[]{:S(2)}) async-start(), calls=%async_computation.8 | async-start | bytes 18874368 | tf_op jit(solution)/shard_map/psum | solution.py:73
  824.9 1202.4 %all-reduce.13.cloned.1.call-start = ((), (), s32[]{:S(2)}) async-start(), calls=%async_computation.9 | async-start | bytes 18874368 | tf_op jit(solution)/shard_map/psum | solution.py:73
  1037.6 7.7 copy-start.4
  1037.6 7.7 copy-start.14
  1222.4 7.7 copy-start.10
  1230.1 3.8 copy-start.5
  1437.7 7.8 copy-start.6
  1437.7 7.8 copy-start.15
  1619.9 7.8 copy-start.11
  1627.7 3.8 copy-start.7
Sparse Core Ops, SparseCore 0:
  825.1 195.3 all-reduce.10
  1831.1 196.2 all-reduce.12
where the time goes:
time: 2080 us; the launch traced here: 2070 us
  other arithmetic  474 us (23%)
  local copies, waits for them, and re-layouts  458 us (22%)
  waiting for transfers between devices  421 us (20%)
  blocking collectives  367 us (18%)
  matrix products  324 us (16%)
    unnamed x8, other arithmetic  394 us
    psum x2, waiting for transfers between devices, per_device(): barycenter = jnp.exp(lax.psum(value_portion, 'img') / total_weight)  328 us
    all_to_all x4, blocking collectives, apply_kernel(): lax.all_to_all(inner, 'slab', split_axis=2, concat_axis=1, tiled=True)  236 us
    unnamed x60, local copies, waits for them, and re-layouts  174 us
    dot_general x20, matrix products, rows_pass(): lax.dot_general(terms[:, offset], split[offset:offset + block_stack], (((...  165 us
    dot_general x20, matrix products, column_sweep(): lax.dot_general(padded[offset:offset + block_stack], terms[:, offset], ((...  160 us
    all_to_all x2, blocking collectives, apply_kernel(): lax.all_to_all(result, 'slab', split_axis=1, concat_axis=2, tiled=True)  114 us
    all_to_all x2, waiting for transfers between devices, apply_kernel(): lax.all_to_all(result, 'slab', split_axis=1, concat_axis=2, tiled=True)  93.1 us
  transfers between devices with their start and end apart: 4, of which 4 were waited for; matrix products, arithmetic and copies ran while one was open for 3% of the time, Pallas kernels for 0%

commit v1 on v0

v1 whole, which is shorter than its diff:
```python
import jax
import jax.numpy as jnp
from jax import lax
from jax.sharding import PartitionSpec as P

ITERS = 2
HALO_BLOCKS = 2


def dense_blocks(banded_submatrices, band_starts, first_row, rows, first_col, cols):
    width = banded_submatrices.shape[2]
    block_rows = lax.dynamic_slice_in_dim(banded_submatrices, first_row, rows, axis=0)
    starts = lax.dynamic_slice_in_dim(band_starts, first_row, rows, axis=0)
    total_blocks = banded_submatrices.shape[0]
    global_col = first_row + jnp.arange(rows, dtype=jnp.int32)[:, None] + starts
    in_range = (global_col >= 0) & (global_col < total_blocks)
    local_col = global_col - first_col
    matches = (local_col[:, :, None] == jnp.arange(cols, dtype=jnp.int32)[None, None, :]) & in_range[:, :, None]
    picked = jnp.where(matches[:, :, :, None, None], block_rows[:, :, None], jnp.zeros((), jnp.bfloat16))
    blocks = jnp.sum(picked, axis=1)
    return blocks.transpose(0, 2, 1, 3).reshape((rows * width, cols * width))


def per_device(image_masses, dual_multipliers, fraction_tops, banded_submatrices, band_starts, nslab):
    width = banded_submatrices.shape[2]
    total_blocks = banded_submatrices.shape[0]
    rows = image_masses.shape[1]
    local_blocks = rows // width
    halo = HALO_BLOCKS * width
    slab = lax.axis_index("slab")
    first = slab * local_blocks

    a_full = dense_blocks(banded_submatrices, band_starts, 0, total_blocks, 0, total_blocks)
    a_local = dense_blocks(
        banded_submatrices, band_starts, first, local_blocks, first - HALO_BLOCKS, local_blocks + 2 * HALO_BLOCKS
    )
    a_prev = a_local[:, :halo]
    a_mid = a_local[:, halo : halo + rows]
    a_next = a_local[:, halo + rows :]

    total_weight = lax.psum(jnp.sum(fraction_tops).astype(jnp.float32), "img")
    weight = fraction_tops.astype(jnp.float32)[0]

    up = [(i, i + 1) for i in range(nslab - 1)]
    down = [(i + 1, i) for i in range(nslab - 1)]

    def column_pass(field):
        return lax.dot_general(
            field, a_full, (((1,), (1,)), ((), ())), preferred_element_type=jnp.float32
        ).astype(jnp.bfloat16)

    def row_pass(inner):
        from_prev = lax.ppermute(inner[rows - halo :], "slab", up)
        from_next = lax.ppermute(inner[:halo], "slab", down)
        total = jnp.dot(a_mid, inner, preferred_element_type=jnp.float32)
        total = total + jnp.dot(a_prev, from_prev, preferred_element_type=jnp.float32)
        total = total + jnp.dot(a_next, from_next, preferred_element_type=jnp.float32)
        return total.astype(jnp.bfloat16)

    def apply_kernel(field):
        return row_pass(column_pass(field))

    masses = image_masses[0]
    scaling = dual_multipliers[0]
    barycenter = None
    for iteration in range(ITERS):
        kernel_v = apply_kernel(scaling.astype(jnp.bfloat16))
        scaled_u = (masses / kernel_v.astype(jnp.float32)).astype(jnp.bfloat16)
        kernel_u = apply_kernel(scaled_u).astype(jnp.float32)
        value_portion = weight * jnp.log(kernel_u)
        barycenter = jnp.exp(lax.psum(value_portion, "img") / total_weight)
        scaling = barycenter / kernel_u
    return (barycenter, scaling[None])


def solution(mesh):
    nslab = mesh.shape["slab"]
    placed = (P("img", "slab", None), P("img", "slab", None), P("img"), P(), P())

    def body(*args):
        return per_device(*args, nslab=nslab)

    return jax.shard_map(
        body,
        mesh=mesh,
        in_specs=placed,
        out_specs=(P("slab", None), P("img", "slab", None)),
        check_vma=False,
    )
```

time: 2080 us -> 908 us (0.44)
  other arithmetic: 474 us -> 45.8 us
  local copies, waits for them, and re-layouts: 458 us -> 39.6 us
  blocking collectives: 367 us -> 16.7 us
  waiting for transfers between devices: 421 us -> 591 us
  matrix products: 324 us -> 172 us
    unnamed x8 -> x0, other arithmetic: 394 us -> none
    all_to_all x6 -> x0, blocking collectives: 350 us -> none  [the longest x4 236 us: apply_kernel(): lax.all_to_all(inner, 'slab', split_axis=2, concat_axis=1, tiled=True)]
    ppermute x0 -> x8, waiting for transfers between devices: none -> 219 us  [the longest x4 126 us: row_pass(): from_next = lax.ppermute(inner[:halo], 'slab', down)]
    convert_element_type x12 -> x0, local copies, waits for them, and re-layouts: 171 us -> none  [the longest x2 47.1 us: per_device(): kernel_u.astype(jnp.float32)]
    unnamed x60 -> x11, local copies, waits for them, and re-layouts: 174 us -> 4.36 us
    dot_general x40 -> x14, matrix products: 324 us -> 172 us  [the longest x4 118 us: column_pass(): lax.dot_general(field, a_full, (((1,), (1,)), ((), ())), preferred_elemen...]
    all_to_all x2 -> x0, waiting for transfers between devices: 93.1 us -> none  [apply_kernel(): lax.all_to_all(result, 'slab', split_axis=1, concat_axis=2, tiled=True)]
    dot_general x2 -> x0, local copies, waits for them, and re-layouts: 46.5 us -> none  [per_device(): jnp.einsum('i,irc->rc', weights, jnp.log(kernel_u.astype(jnp.float32)))]
  transfers between devices with their start and end apart: 4 -> 10, of which waited for: 4 -> 10; matrix products, arithmetic and copies ran while one was open for 3% -> 5% of each run, Pallas kernels for 0% -> 0%
where the time goes in v1:
time: 908 us; the launch traced here: 903 us
  waiting for transfers between devices  591 us (65%)
  matrix products  172 us (19%)
  other arithmetic  45.8 us (5%)
  local copies, waits for them, and re-layouts  39.6 us (4%)
  starting transfers between devices  23.3 us (3%)
  blocking collectives  16.7 us (2%)
  between operations  15.1 us (2%)
    psum x2, waiting for transfers between devices, per_device(): barycenter = jnp.exp(lax.psum(value_portion, 'img') / total_weight)  373 us
    ppermute x4, waiting for transfers between devices, row_pass(): from_next = lax.ppermute(inner[:halo], 'slab', down)  126 us
    dot_general x4, matrix products, column_pass(): lax.dot_general(field, a_full, (((1,), (1,)), ((), ())), preferred_elemen...  118 us
    ppermute x4, waiting for transfers between devices, row_pass(): from_prev = lax.ppermute(inner[rows - halo:], 'slab', up)  92.8 us
    reduce_sum x2, other arithmetic, dense_blocks(): blocks = jnp.sum(picked, axis=1)  30.7 us
    transpose x2, local copies, waits for them, and re-layouts, dense_blocks(): return blocks.transpose(0, 2, 1, 3).reshape((rows * width, cols * width))  25.2 us
    dot_general x4, matrix products, row_pass(): total = jnp.dot(a_mid, inner, preferred_element_type=jnp.float32)  23.1 us
  transfers between devices with their start and end apart: 10, of which 10 were waited for; matrix products, arithmetic and copies ran while one was open for 5% of the time, Pallas kernels for 0%

profile of v1, /device:TPU:0, one launch (start us, length us, event | category | flops | bytes accessed | tf_op | source)
XLA Modules:
  0.0 903.4 jit_solution(9013752518304244725)
XLA Ops:
  8.9 29.3 %select_reduce_fusion = bf16[24,24,128,128]{3,2,1,0:T(8,128)(2,1)} fusion(pred[24,3,24]{2,1,0:T(4,128)(4,1)S(1)} %fusion.58, bf16[24,3,128,128]{3,2,1,0:T(8,128)(2,1)} %param.8), kind=kLoop, calls=%fused_computation | loop fusion | flops 47185920 | bytes 21235392 | tf_op jit(solution)/shard_map/reduce_sum | solution.py:20
  38.2 22.0 %copy.20 = bf16[24,128,24,128]{3,2,1,0:T(8,128)(2,1)} copy(bf16[24,128,24,128]{3,1,2,0:T(8,128)(2,1)} %bitcast.56) | data formatting | bytes 37748736 | tf_op jit(solution)/shard_map/transpose | solution.py:21
  60.2 24.9 %fusion.18 = bf16[3072,768]{1,0:T(8,128)(2,1)S(1)} fusion(bf16[384,8,24,128]{3,2,1,0:T(8,128)(2,1)} %bitcast.69, f32[1,768,3072]{2,1,0:T(8,128)} %param.6), kind=kOutput, calls=%fused_computation.31 | convolution fusion | flops 14500233216 | bytes 33030144 | tf_op jit(solution)/shard_map/dot_general | solution.py:48
  89.1 6.0 collective-permute-start
  99.7 3.2 copy.17
  105.1 8.7 fusion.42
  113.8 14.1 %collective-permute-done = bf16[256,3072]{0,1:T(8,128)(2,1)} collective-permute-done((bf16[256,3072]{0,1:T(8,128)(2,1)}, bf16[256,3072]{0,1:T(8,128)(2,1)}, u32[]{:S(2)}, u32[]{:S(2)}) %collective-permute-start) | collective-permute-done | bytes 1572896 | tf_op jit(solution)/shard_map/ppermute | solution.py:53
  127.9 6.6 fusion.56
  134.5 29.1 %collective-permute-done.1 = bf16[256,3072]{0,1:T(8,128)(2,1)} collective-permute-done((bf16[256,3072]{0,1:T(8,128)(2,1)}, bf16[256,3072]{0,1:T(8,128)(2,1)}, u32[]{:S(2)}, u32[]{:S(2)}) %collective-permute-start.1) | collective-permute-done | bytes 1572896 | tf_op jit(solution)/shard_map/ppermute | solution.py:54
  163.6 31.7 %fusion.21 = bf16[768,3072]{1,0:T(8,128)(2,1)} fusion(bf16[384,8,24,128]{3,2,1,0:T(8,128)(2,1)} %bitcast.70, f32[1,768,3072]{2,1,0:T(8,128)} %param.5, f32[768,3072]{1,0:T(8,128)} %fusion.42, f32[768,3072]{1,0:T(8,128)} %fusion.56, bf16[256,3072]{0,1:T(8,128)(2,1)} %collective-permute-done.1, bf16[768,1280]{0,1:T(8,128)(2,1)S(1)} %bitcast.59), kind=kOutput, calls=%fused_computation.32 | convolution fusion | flops 15719989248 | bytes 53870592 | tf_op jit(solution)/shard_map/dot_general | solution.py:48
  195.3 2.2 fusion.63
  197.5 3.6 collective-permute-start.2
  203.6 4.0 fusion.40
  207.6 26.2 %collective-permute-done.2 = bf16[256,3072]{1,0:T(8,128)(2,1)S(1)} collective-permute-done((bf16[256,3072]{1,0:T(8,128)(2,1)S(1)}, bf16[256,3072]{1,0:T(8,128)(2,1)S(1)}, u32[]{:S(2)}, u32[]{:S(2)}) %collective-permute-start.2) | collective-permute-done | bytes 1572896 | tf_op jit(solution)/shard_map/ppermute | solution.py:53
  235.3 33.1 %collective-permute-done.3 = bf16[256,3072]{1,0:T(8,128)(2,1)} collective-permute-done((bf16[256,3072]{1,0:T(8,128)(2,1)S(1)}, bf16[256,3072]{1,0:T(8,128)(2,1)}, u32[]{:S(2)}, u32[]{:S(2)}) %collective-permute-start.3) | collective-permute-done | bytes 1572896 | tf_op jit(solution)/shard_map/ppermute | solution.py:54
  268.4 8.0 fusion.12
  276.5 16.7 %psum.22 = f32[]{:T(128)} all-reduce(f32[]{:T(128)} %bitcast), channel_id=1, replica_groups=mesh['img'=8,'slab'=4] {'img'}, use_global_device_ids=true, to_apply=%region_3.4 | all-reduce | flops 1 | bytes 8 | tf_op jit(solution)/shard_map/psum | solution.py:41
  293.2 178.1 %all-reduce.3.cloned.1.call-done = f32[768,3072]{1,0:T(8,128)} async-done(((f32[768,3072]{1,0:T(8,128)}), f32[768,3072]{1,0:T(8,128)}) %all-reduce.3.cloned.1.call-update) | async-done | bytes 9437200 | tf_op jit(solution)/shard_map/psum | solution.py:71
  471.3 24.1 %fusion.24 = bf16[768,3072]{1,0:T(8,128)(2,1)} fusion(bf16[384,8,24,128]{3,2,1,0:T(8,128)(2,1)} %bitcast.71, bf16[768,3072]{1,0:T(8,128)(2,1)} %get-tuple-element.13, f32[768,3072]{1,0:T(8,128)} %all-reduce.3.cloned.1.call-done, f32[]{:T(128)} %psum.22), kind=kOutput, calls=%fused_computation.33 | convolution fusion | flops 14507311104 | bytes 37748740 | tf_op jit(solution)/shard_map/dot_general | solution.py:48
  497.7 3.6 collective-permute-start.4
  502.8 6.3 fusion.38
  509.1 25.5 %collective-permute-done.4 = bf16[256,3072]{1,0:T(8,128)(2,1)S(1)} collective-permute-done((bf16[256,3072]{1,0:T(8,128)(2,1)S(1)}, bf16[256,3072]{1,0:T(8,128)(2,1)S(1)}, u32[]{:S(2)}, u32[]{:S(2)}) %collective-permute-start.4) | collective-permute-done | bytes 1572896 | tf_op jit(solution)/shard_map/ppermute | solution.py:53
  534.6 5.2 fusion.52
  539.8 30.6 %collective-permute-done.5 = bf16[256,3072]{1,0:T(8,128)(2,1)} collective-permute-done((bf16[256,3072]{1,0:T(8,128)(2,1)S(1)}, bf16[256,3072]{1,0:T(8,128)(2,1)}, u32[]{:S(2)}, u32[]{:S(2)}) %collective-permute-start.5) | collective-permute-done | bytes 1572896 | tf_op jit(solution)/shard_map/ppermute | solution.py:54
  570.4 37.2 %fusion.27 = bf16[768,3072]{1,0:T(8,128)(2,1)} fusion(bf16[384,8,24,128]{3,2,1,0:T(8,128)(2,1)} %bitcast.72, f32[1,768,3072]{2,1,0:T(8,128)} %param.5, f32[768,3072]{1,0:T(8,128)} %fusion.38, f32[768,3072]{1,0:T(8,128)} %fusion.52, bf16[256,3072]{1,0:T(8,128)(2,1)} %collective-permute-done.5, bf16[768,1280]{0,1:T(8,128)(2,1)S(1)} %bitcast.65), kind=kOutput, calls=%fused_computation.34 | convolution fusion | flops 15719989248 | bytes 53870592 | tf_op jit(solution)/shard_map/dot_general | solution.py:48
  609.8 3.6 collective-permute-start.6
  615.0 4.0 fusion.36
  619.0 26.9 %collective-permute-done.6 = bf16[256,3072]{1,0:T(8,128)(2,1)S(1)} collective-permute-done((bf16[256,3072]{1,0:T(8,128)(2,1)S(1)}, bf16[256,3072]{1,0:T(8,128)(2,1)S(1)}, u32[]{:S(2)}, u32[]{:S(2)}) %collective-permute-start.6) | collective-permute-done | bytes 1572896 | tf_op jit(solution)/shard_map/ppermute | solution.py:53
  647.3 33.1 %collective-permute-done.7 = bf16[256,3072]{1,0:T(8,128)(2,1)} collective-permute-done((bf16[256,3072]{1,0:T(8,128)(2,1)S(1)}, bf16[256,3072]{1,0:T(8,128)(2,1)}, u32[]{:S(2)}, u32[]{:S(2)}) %collective-permute-start.7) | collective-permute-done | bytes 1572896 | tf_op jit(solution)/shard_map/ppermute | solution.py:54
  680.4 8.0 fusion.14
  688.5 194.5 %all-reduce.5.cloned.1.call-done = f32[768,3072]{1,0:T(8,128)} async-done(((f32[768,3072]{1,0:T(8,128)}), f32[768,3072]{1,0:T(8,128)}) %all-reduce.5.cloned.1.call-update) | async-done | bytes 9437200 | tf_op jit(solution)/shard_map/psum | solution.py:71
  883.0 13.4 %fusion.15 = (f32[1,768,3072]{2,1,0:T(8,128)}, f32[768,3072]{1,0:T(8,128)}) fusion(bf16[768,3072]{1,0:T(8,128)(2,1)} %get-tuple-element.15, f32[768,3072]{1,0:T(8,128)} %all-reduce.5.cloned.1.call-done, f32[]{:T(128)} %psum.22), kind=kLoop, calls=%fused_computation.20 | loop fusion | flops 7077888 | bytes 33030148 | tf_op jit(solution)/shard_map/broadcast_in_dim | solution.py:73
  (37 shorter events, 24.5 us)
Async XLA Ops:
  7.2 464.1 %all-reduce.3.cloned.1.call-start = ((), (), s32[]{:S(2)}) async-start(), calls=%async_computation | async-start | bytes 18874368 | tf_op jit(solution)/shard_map/psum | solution.py:71
  85.1 2.2 copy-start.3
  85.1 11.7 %copy-start.4 = (s32[24,3]{0,1:T(4,128)S(1)}, s32[24,3]{0,1:T(4,128)}, u32[]{:S(2)}) copy-start(s32[24,3]{0,1:T(4,128)} %param.9) | copy-start | bytes 868
  89.1 38.8 %collective-permute-start = (bf16[256,3072]{0,1:T(8,128)(2,1)}, bf16[256,3072]{0,1:T(8,128)(2,1)}, u32[]{:S(2)}, u32[]{:S(2)}) collective-permute-start(bf16[256,3072]{0,1:T(8,128)(2,1)} %get-tuple-element.11), channel_id=1, source_target_pairs={{0,1},{1,2},{2,3},{4,5},{5,6},{6,7},{8,9},{9,10},{10,11},{12,13},{... | collective-permute-start | bytes 4718600 | tf_op jit(solution)/shard_map/ppermute | solution.py:53
  95.2 68.4 %collective-permute-start.1 = (bf16[256,3072]{0,1:T(8,128)(2,1)}, bf16[256,3072]{0,1:T(8,128)(2,1)}, u32[]{:S(2)}, u32[]{:S(2)}) collective-permute-start(bf16[256,3072]{0,1:T(8,128)(2,1)} %get-tuple-element.10), channel_id=1, source_target_pairs={{1,0},{2,1},{3,2},{5,4},{6,5},{7,6},{9,8},{10,9},{11,10},{13,12},{... | collective-permute-start | bytes 4718600 | tf_op jit(solution)/shard_map/ppermute | solution.py:54
  195.3 8.3 copy-start
  197.5 36.3 %collective-permute-start.2 = (bf16[256,3072]{1,0:T(8,128)(2,1)S(1)}, bf16[256,3072]{1,0:T(8,128)(2,1)S(1)}, u32[]{:S(2)}, u32[]{:S(2)}) collective-permute-start(bf16[256,3072]{1,0:T(8,128)(2,1)S(1)} %get-tuple-element.9), channel_id=1, source_target_pairs={{0,1},{1,2},{2,3},{4,5},{5,6},{6,7},{8,9},{9,10},{10,11},{12,13},{... | collective-permute-start | bytes 4718600 | tf_op jit(solution)/shard_map/ppermute | solution.py:53
  201.2 67.2 %collective-permute-start.3 = (bf16[256,3072]{1,0:T(8,128)(2,1)S(1)}, bf16[256,3072]{1,0:T(8,128)(2,1)}, u32[]{:S(2)}, u32[]{:S(2)}) collective-permute-start(bf16[256,3072]{1,0:T(8,128)(2,1)S(1)} %get-tuple-element.8), channel_id=1, source_target_pairs={{1,0},{2,1},{3,2},{5,4},{6,5},{7,6},{9,8},{10,9},{11,10},{13,12},{... | collective-permute-start | bytes 4718600 | tf_op jit(solution)/shard_map/ppermute | solution.py:54
  276.5 606.5 %all-reduce.5.cloned.1.call-start = ((), (), s32[]{:S(2)}) async-start(), calls=%async_computation.1 | async-start | bytes 18874368 | tf_op jit(solution)/shard_map/psum | solution.py:71
  495.4 7.3 copy-start.2
  497.7 37.0 %collective-permute-start.4 = (bf16[256,3072]{1,0:T(8,128)(2,1)S(1)}, bf16[256,3072]{1,0:T(8,128)(2,1)S(1)}, u32[]{:S(2)}, u32[]{:S(2)}) collective-permute-start(bf16[256,3072]{1,0:T(8,128)(2,1)S(1)} %get-tuple-element.7), channel_id=1, source_target_pairs={{0,1},{1,2},{2,3},{4,5},{5,6},{6,7},{8,9},{9,10},{10,11},{12,13},{... | collective-permute-start | bytes 4718600 | tf_op jit(solution)/shard_map/ppermute | solution.py:53
  501.3 69.1 %collective-permute-start.5 = (bf16[256,3072]{1,0:T(8,128)(2,1)S(1)}, bf16[256,3072]{1,0:T(8,128)(2,1)}, u32[]{:S(2)}, u32[]{:S(2)}) collective-permute-start(bf16[256,3072]{1,0:T(8,128)(2,1)S(1)} %get-tuple-element.6), channel_id=1, source_target_pairs={{1,0},{2,1},{3,2},{5,4},{6,5},{7,6},{9,8},{10,9},{11,10},{13,12},{... | collective-permute-start | bytes 4718600 | tf_op jit(solution)/shard_map/ppermute | solution.py:54
  607.5 7.4 copy-start.1
  609.8 36.1 %collective-permute-start.6 = (bf16[256,3072]{1,0:T(8,128)(2,1)S(1)}, bf16[256,3072]{1,0:T(8,128)(2,1)S(1)}, u32[]{:S(2)}, u32[]{:S(2)}) collective-permute-start(bf16[256,3072]{1,0:T(8,128)(2,1)S(1)} %get-tuple-element.5), channel_id=1, source_target_pairs={{0,1},{1,2},{2,3},{4,5},{5,6},{6,7},{8,9},{9,10},{10,11},{12,13},{... | collective-permute-start | bytes 4718600 | tf_op jit(solution)/shard_map/ppermute | solution.py:53
  613.4 67.0 %collective-permute-start.7 = (bf16[256,3072]{1,0:T(8,128)(2,1)S(1)}, bf16[256,3072]{1,0:T(8,128)(2,1)}, u32[]{:S(2)}, u32[]{:S(2)}) collective-permute-start(bf16[256,3072]{1,0:T(8,128)(2,1)S(1)} %get-tuple-element.4), channel_id=1, source_target_pairs={{1,0},{2,1},{3,2},{5,4},{6,5},{7,6},{9,8},{10,9},{11,10},{13,12},{... | collective-permute-start | bytes 4718600 | tf_op jit(solution)/shard_map/ppermute | solution.py:54
Sparse Core Ops, SparseCore 0:
  276.6 194.6 all-reduce.2
  688.6 194.3 all-reduce.4

commit v2 on v1

v2 whole, which is shorter than its diff:
```python
import jax
import jax.numpy as jnp
from jax import lax
from jax.experimental import pallas as pl
from jax.sharding import PartitionSpec as P

ITERS = 2
HALO = 2
OFFSETS = 2 * HALO + 1


def offset_terms(banded_submatrices, band_starts):
    offsets = jnp.arange(-HALO, HALO + 1, dtype=jnp.int32)
    matches = band_starts[:, None, :] == offsets[None, :, None]
    picked = jnp.where(matches[:, :, :, None, None], banded_submatrices[:, None], jnp.zeros((), jnp.bfloat16))
    return jnp.sum(picked, axis=2)


def column_kernel(x_ref, t_ref, o_ref):
    nblocks = t_ref.shape[0]
    width = t_ref.shape[2]
    x = x_ref[...].astype(jnp.bfloat16)
    for b in range(nblocks):
        acc = None
        for o in range(OFFSETS):
            c = b + o - HALO
            if c < 0 or c >= nblocks:
                continue
            prod = lax.dot_general(
                x[:, c * width : (c + 1) * width],
                t_ref[b, o],
                (((1,), (1,)), ((), ())),
                preferred_element_type=jnp.float32,
            )
            acc = prod if acc is None else acc + prod
        o_ref[:, b * width : (b + 1) * width] = acc.astype(o_ref.dtype)


def column_pass(field, terms, tile_rows=256):
    rows, cols = field.shape
    return pl.pallas_call(
        column_kernel,
        grid=(rows // tile_rows,),
        in_specs=[
            pl.BlockSpec((tile_rows, cols), lambda r: (r, 0)),
            pl.BlockSpec(terms.shape, lambda r: (0, 0, 0, 0)),
        ],
        out_specs=pl.BlockSpec((tile_rows, cols), lambda r: (r, 0)),
        out_shape=jax.ShapeDtypeStruct((rows, cols), jnp.bfloat16),
    )(field, terms)


def row_kernel(prev_ref, mid_ref, next_ref, t_ref, o_ref):
    nlocal = t_ref.shape[0]
    width = t_ref.shape[2]
    for b in range(nlocal):
        acc = None
        for o in range(OFFSETS):
            e = b + o - HALO
            if e < 0:
                src = prev_ref[(e + HALO) * width : (e + HALO + 1) * width, :]
            elif e >= nlocal:
                src = next_ref[(e - nlocal) * width : (e - nlocal + 1) * width, :]
            else:
                src = mid_ref[e * width : (e + 1) * width, :]
            prod = jnp.dot(t_ref[b, o], src, preferred_element_type=jnp.float32)
            acc = prod if acc is None else acc + prod
        o_ref[b * width : (b + 1) * width, :] = acc.astype(o_ref.dtype)


def row_pass(prev, mid, nxt, terms_local, tile_cols=768):
    rows, cols = mid.shape
    halo_rows = prev.shape[0]
    return pl.pallas_call(
        row_kernel,
        grid=(cols // tile_cols,),
        in_specs=[
            pl.BlockSpec((halo_rows, tile_cols), lambda c: (0, c)),
            pl.BlockSpec((rows, tile_cols), lambda c: (0, c)),
            pl.BlockSpec((halo_rows, tile_cols), lambda c: (0, c)),
            pl.BlockSpec(terms_local.shape, lambda c: (0, 0, 0, 0)),
        ],
        out_specs=pl.BlockSpec((rows, tile_cols), lambda c: (0, c)),
        out_shape=jax.ShapeDtypeStruct((rows, cols), jnp.bfloat16),
    )(prev, mid, nxt, terms_local)


def per_device(image_masses, dual_multipliers, fraction_tops, banded_submatrices, band_starts, nslab):
    width = banded_submatrices.shape[2]
    rows = image_masses.shape[1]
    local_blocks = rows // width
    halo = HALO * width
    slab = lax.axis_index("slab")

    terms = offset_terms(banded_submatrices, band_starts)
    terms_local = lax.dynamic_slice_in_dim(terms, slab * local_blocks, local_blocks, axis=0)

    total_weight = lax.psum(jnp.sum(fraction_tops).astype(jnp.float32), "img")
    weight = fraction_tops.astype(jnp.float32)[0]

    up = [(i, i + 1) for i in range(nslab - 1)]
    down = [(i + 1, i) for i in range(nslab - 1)]

    def apply_kernel(field):
        inner = column_pass(field, terms)
        from_prev = lax.ppermute(inner[rows - halo :], "slab", up)
        from_next = lax.ppermute(inner[:halo], "slab", down)
        return row_pass(from_prev, inner, from_next, terms_local)

    masses = image_masses[0]
    scaling = dual_multipliers[0]
    barycenter = None
    for iteration in range(ITERS):
        kernel_v = apply_kernel(scaling.astype(jnp.bfloat16))
        scaled_u = (masses / kernel_v.astype(jnp.float32)).astype(jnp.bfloat16)
        kernel_u = apply_kernel(scaled_u).astype(jnp.float32)
        value_portion = weight * jnp.log(kernel_u)
        barycenter = jnp.exp(lax.psum(value_portion, "img") / total_weight)
        scaling = barycenter / kernel_u
    return (barycenter, scaling[None])


def solution(mesh):
    nslab = mesh.shape["slab"]
    placed = (P("img", "slab", None), P("img", "slab", None), P("img"), P(), P())

    def body(*args):
        return per_device(*args, nslab=nslab)

    return jax.shard_map(
        body,
        mesh=mesh,
        in_specs=placed,
        out_specs=(P("slab", None), P("img", "slab", None)),
        check_vma=False,
    )
```

time: 908 us -> 858 us (0.945)
  matrix products: 172 us -> 0 us
  Pallas kernels: 0 us -> 81.2 us
  starting transfers between devices: 23.3 us -> 83.3 us
  other arithmetic: 45.8 us -> 68.6 us
  waiting for transfers between devices: 591 us -> 572 us
  local copies, waits for them, and re-layouts: 39.6 us -> 21.9 us
    dot_general x14 -> x0, matrix products: 172 us -> none  [the longest x4 118 us: column_pass(): lax.dot_general(field, a_full, (((1,), (1,)), ((), ())), preferred_elemen...]
    ppermute x8, waiting for transfers between devices: 219 us -> 131 us  [the longest x4 130 us: apply_kernel(): from_next = lax.ppermute(inner[:halo], 'slab', down)]
    pallas_call x0 -> x8, Pallas kernels: none -> 81.2 us  [the longest x4 40.9 us: row_pass(): pl.pallas_call(row_kernel, grid=(cols // tile_cols,), in_specs=[pl.BlockS...]
    psum x2, waiting for transfers between devices: 373 us -> 442 us  [per_device(): barycenter = jnp.exp(lax.psum(value_portion, 'img') / total_weight)]
    ppermute x8, starting transfers between devices: 23.2 us -> 83.2 us  [the longest x4 77.9 us: apply_kernel(): from_prev = lax.ppermute(inner[rows - halo:], 'slab', up)]
    convert_element_type x0 -> x4, other arithmetic: none -> 34.6 us  [the longest x2 18.4 us: per_device(): scaled_u = (masses / kernel_v.astype(jnp.float32)).astype(jnp.bfloat16)]
    transpose x2 -> x0, local copies, waits for them, and re-layouts: 25.2 us -> none  [dense_blocks(): return blocks.transpose(0, 2, 1, 3).reshape((rows * width, cols * width))]
    reduce_sum x2 -> x1, other arithmetic: 30.7 us -> 5.69 us  [offset_terms(): return jnp.sum(picked, axis=2)]
  transfers between devices with their start and end apart: 10 -> 10, of which waited for: 10 -> 7; matrix products, arithmetic and copies ran while one was open for 5% -> 0% of each run, Pallas kernels for 0% -> 0%
where the time goes in v2:
time: 858 us; the launch traced here: 857 us
  waiting for transfers between devices  572 us (67%)
  starting transfers between devices  83.3 us (10%)
  Pallas kernels  81.2 us (9%)
  other arithmetic  68.6 us (8%)
  local copies, waits for them, and re-layouts  21.9 us (3%)
  blocking collectives  14.8 us (2%)
  between operations  14.8 us (2%)
    psum x2, waiting for transfers between devices, per_device(): barycenter = jnp.exp(lax.psum(value_portion, 'img') / total_weight)  442 us
    ppermute x4, waiting for transfers between devices, apply_kernel(): from_next = lax.ppermute(inner[:halo], 'slab', down)  130 us
    ppermute x4, starting transfers between devices, apply_kernel(): from_prev = lax.ppermute(inner[rows - halo:], 'slab', up)  77.9 us
    pallas_call x4, Pallas kernels, row_pass(): pl.pallas_call(row_kernel, grid=(cols // tile_cols,), in_specs=[pl.BlockS...  40.9 us
    pallas_call x4, Pallas kernels, column_pass(): pl.pallas_call(column_kernel, grid=(rows // tile_rows,), in_specs=[pl.Blo...  40.3 us
    convert_element_type x2, other arithmetic, per_device(): scaled_u = (masses / kernel_v.astype(jnp.float32)).astype(jnp.bfloat16)  18.4 us
  transfers between devices with their start and end apart: 10, of which 7 were waited for; matrix products, arithmetic and copies ran while one was open for 0% of the time, Pallas kernels for 0%

profile of v2, /device:TPU:0, one launch (start us, length us, event | category | flops | bytes accessed | tf_op | source)
XLA Modules:
  0.0 856.9 jit_solution(16839692114985869694)
XLA Ops:
  8.0 6.7 convert_bitcast_fusion.x_ref
  14.8 5.7 select_reduce_fusion.t_ref
  20.5 10.1 %shard_map.68.mid_ref = bf16[768,3072]{1,0:T(8,128)(2,1)} custom-call(bf16[768,3072]{1,0:T(8,128)(2,1)} %convert_bitcast_fusion.x_ref, bf16[24,5,128,128]{3,2,1,0:T(8,128)(2,1)} %select_reduce_fusion.t_ref), custom_call_target="tpu_custom_call" | custom-call | tf_op jit(solution)/shard_map/pallas_call | solution.py:41
  30.6 3.8 fusion.9
  35.7 5.6 collective-permute-start
  41.2 2.3 constant_dynamic-slice_fusion.t_ref
  43.5 31.1 %collective-permute-done.1.next_ref = bf16[256,3072]{1,0:T(8,128)(2,1)S(1)} collective-permute-done((bf16[256,3072]{1,0:T(8,128)(2,1)}, bf16[256,3072]{1,0:T(8,128)(2,1)S(1)}, u32[]{:S(2)}, u32[]{:S(2)}) %collective-permute-start.1) | collective-permute-done | bytes 1572896 | tf_op jit(solution)/shard_map/ppermute | solution.py:107
  76.9 10.2 %shard_map.69 = bf16[768,3072]{1,0:T(8,128)(2,1)} custom-call(bf16[256,3072]{1,0:T(8,128)(2,1)} %copy-done.2, bf16[768,3072]{1,0:T(8,128)(2,1)} %shard_map.68.mid_ref, bf16[256,3072]{1,0:T(8,128)(2,1)} %copy-done.1, bf16[6,5,128,128]{3,2,1,0:T(8,128)(2,1)} %constant_dynamic-slice_fusion.t_ref), custom_call_target="tpu_custom_call" | custom-call | tf_op jit(solution)/shard_map/pallas_call | solution.py:74
  87.1 9.2 %fusion.4.x_ref = bf16[768,3072]{1,0:T(8,128)(2,1)} fusion(f32[1,768,3072]{2,1,0:T(8,128)} %param.5, bf16[768,3072]{1,0:T(8,128)(2,1)} %shard_map.69), kind=kLoop, calls=%fused_computation.11 | loop fusion | flops 7077888 | bytes 18874368 | tf_op jit(solution)/shard_map/convert_element_type | solution.py:115
  96.3 10.1 %shard_map.70.mid_ref = bf16[768,3072]{1,0:T(8,128)(2,1)} custom-call(bf16[768,3072]{1,0:T(8,128)(2,1)} %fusion.4.x_ref, bf16[24,5,128,128]{3,2,1,0:T(8,128)(2,1)} %select_reduce_fusion.t_ref), custom_call_target="tpu_custom_call" | custom-call | tf_op jit(solution)/shard_map/pallas_call | solution.py:41
  106.4 2.1 fusion.8
  110.0 34.0 %collective-permute-start.2 = (bf16[256,3072]{1,0:T(8,128)(2,1)S(1)}, bf16[256,3072]{1,0:T(8,128)(2,1)S(1)}, u32[]{:S(2)}, u32[]{:S(2)}) collective-permute-start(bf16[256,3072]{1,0:T(8,128)(2,1)S(1)} %get-tuple-element.9), channel_id=1, source_target_pairs={{0,1},{1,2},{2,3},{4,5},{5,6},{6,7},{8,9},{9,10},{10,11},{12,13},{... | collective-permute-start | bytes 4718600 | tf_op jit(solution)/shard_map/ppermute | solution.py:106
  144.7 32.6 %collective-permute-done.3.next_ref = bf16[256,3072]{1,0:T(8,128)(2,1)S(1)} collective-permute-done((bf16[256,3072]{1,0:T(8,128)(2,1)S(1)}, bf16[256,3072]{1,0:T(8,128)(2,1)S(1)}, u32[]{:S(2)}, u32[]{:S(2)}) %collective-permute-start.3) | collective-permute-done | bytes 1572896 | tf_op jit(solution)/shard_map/ppermute | solution.py:107
  179.6 10.3 %shard_map.71 = bf16[768,3072]{1,0:T(8,128)(2,1)} custom-call(bf16[256,3072]{1,0:T(8,128)(2,1)} %copy-done.6, bf16[768,3072]{1,0:T(8,128)(2,1)} %shard_map.70.mid_ref, bf16[256,3072]{1,0:T(8,128)(2,1)} %copy-done.3, bf16[6,5,128,128]{3,2,1,0:T(8,128)(2,1)} %constant_dynamic-slice_fusion.t_ref), custom_call_target="tpu_custom_call" | custom-call | tf_op jit(solution)/shard_map/pallas_call | solution.py:74
  189.9 7.4 fusion
  197.3 14.8 %psum.22 = f32[]{:T(128)} all-reduce(f32[]{:T(128)} %bitcast), channel_id=1, replica_groups=mesh['img'=8,'slab'=4] {'img'}, use_global_device_ids=true, to_apply=%region_2.3 | all-reduce | flops 1 | bytes 8 | tf_op jit(solution)/shard_map/psum | solution.py:98
  212.2 213.9 %all-reduce.3.cloned.1.call-done = f32[768,3072]{1,0:T(8,128)} async-done(((f32[768,3072]{1,0:T(8,128)}), f32[768,3072]{1,0:T(8,128)}) %all-reduce.3.cloned.1.call-update) | async-done | bytes 9437200 | tf_op jit(solution)/shard_map/psum | solution.py:118
  426.0 9.5 %fusion.1.x_ref = bf16[768,3072]{1,0:T(8,128)(2,1)} fusion(bf16[768,3072]{1,0:T(8,128)(2,1)} %shard_map.71, f32[768,3072]{1,0:T(8,128)} %all-reduce.3.cloned.1.call-done, f32[]{:T(128)} %psum.22), kind=kLoop, calls=%fused_computation.6 | loop fusion | flops 9437184 | bytes 18874372 | tf_op jit(solution)/shard_map/convert_element_type | solution.py:114
  435.5 10.1 %shard_map.72.mid_ref = bf16[768,3072]{1,0:T(8,128)(2,1)} custom-call(bf16[768,3072]{1,0:T(8,128)(2,1)} %fusion.1.x_ref, bf16[24,5,128,128]{3,2,1,0:T(8,128)(2,1)} %select_reduce_fusion.t_ref), custom_call_target="tpu_custom_call" | custom-call | tf_op jit(solution)/shard_map/pallas_call | solution.py:41
  445.6 2.1 fusion.7
  449.0 4.6 collective-permute-start.4
  453.6 33.2 %collective-permute-done.5.next_ref = bf16[256,3072]{1,0:T(8,128)(2,1)S(1)} collective-permute-done((bf16[256,3072]{1,0:T(8,128)(2,1)S(1)}, bf16[256,3072]{1,0:T(8,128)(2,1)S(1)}, u32[]{:S(2)}, u32[]{:S(2)}) %collective-permute-start.5) | collective-permute-done | bytes 1572896 | tf_op jit(solution)/shard_map/ppermute | solution.py:107
  489.2 10.2 %shard_map.73 = bf16[768,3072]{1,0:T(8,128)(2,1)} custom-call(bf16[256,3072]{1,0:T(8,128)(2,1)} %copy-done.8, bf16[768,3072]{1,0:T(8,128)(2,1)} %shard_map.72.mid_ref, bf16[256,3072]{1,0:T(8,128)(2,1)} %copy-done.5, bf16[6,5,128,128]{3,2,1,0:T(8,128)(2,1)} %constant_dynamic-slice_fusion.t_ref), custom_call_target="tpu_custom_call" | custom-call | tf_op jit(solution)/shard_map/pallas_call | solution.py:74
  499.4 9.2 %fusion.5.x_ref = bf16[768,3072]{1,0:T(8,128)(2,1)} fusion(f32[1,768,3072]{2,1,0:T(8,128)} %param.5, bf16[768,3072]{1,0:T(8,128)(2,1)} %shard_map.73), kind=kLoop, calls=%fused_computation.12 | loop fusion | flops 7077888 | bytes 18874368 | tf_op jit(solution)/shard_map/convert_element_type | solution.py:115
  508.6 10.1 %shard_map.74.mid_ref = bf16[768,3072]{1,0:T(8,128)(2,1)} custom-call(bf16[768,3072]{1,0:T(8,128)(2,1)} %fusion.5.x_ref, bf16[24,5,128,128]{3,2,1,0:T(8,128)(2,1)} %select_reduce_fusion.t_ref), custom_call_target="tpu_custom_call" | custom-call | tf_op jit(solution)/shard_map/pallas_call | solution.py:41
  518.7 2.1 fusion.6
  522.1 33.6 %collective-permute-start.6 = (bf16[256,3072]{1,0:T(8,128)(2,1)S(1)}, bf16[256,3072]{1,0:T(8,128)(2,1)S(1)}, u32[]{:S(2)}, u32[]{:S(2)}) collective-permute-start(bf16[256,3072]{1,0:T(8,128)(2,1)S(1)} %get-tuple-element.5), channel_id=1, source_target_pairs={{0,1},{1,2},{2,3},{4,5},{5,6},{6,7},{8,9},{9,10},{10,11},{12,13},{... | collective-permute-start | bytes 4718600 | tf_op jit(solution)/shard_map/ppermute | solution.py:106
  555.7 33.1 %collective-permute-done.7.next_ref = bf16[256,3072]{1,0:T(8,128)(2,1)S(1)} collective-permute-done((bf16[256,3072]{1,0:T(8,128)(2,1)S(1)}, bf16[256,3072]{1,0:T(8,128)(2,1)S(1)}, u32[]{:S(2)}, u32[]{:S(2)}) %collective-permute-start.7) | collective-permute-done | bytes 1572896 | tf_op jit(solution)/shard_map/ppermute | solution.py:107
  591.0 10.3 %shard_map.75 = bf16[768,3072]{1,0:T(8,128)(2,1)} custom-call(bf16[256,3072]{1,0:T(8,128)(2,1)} %copy-done.7, bf16[768,3072]{1,0:T(8,128)(2,1)} %shard_map.74.mid_ref, bf16[256,3072]{1,0:T(8,128)(2,1)} %copy-done.4, bf16[6,5,128,128]{3,2,1,0:T(8,128)(2,1)} %constant_dynamic-slice_fusion.t_ref), custom_call_target="tpu_custom_call" | custom-call | tf_op jit(solution)/shard_map/pallas_call | solution.py:74
  601.3 7.4 fusion.2
  608.7 227.9 %all-reduce.5.cloned.1.call-done = f32[768,3072]{1,0:T(8,128)} async-done(((f32[768,3072]{1,0:T(8,128)}), f32[768,3072]{1,0:T(8,128)}) %all-reduce.5.cloned.1.call-update) | async-done | bytes 9437200 | tf_op jit(solution)/shard_map/psum | solution.py:118
  836.6 13.4 %fusion.3 = (f32[1,768,3072]{2,1,0:T(8,128)}, f32[768,3072]{1,0:T(8,128)}) fusion(bf16[768,3072]{1,0:T(8,128)(2,1)} %shard_map.75, f32[768,3072]{1,0:T(8,128)} %all-reduce.5.cloned.1.call-done, f32[]{:T(128)} %psum.22), kind=kLoop, calls=%fused_computation.8 | loop fusion | flops 7077888 | bytes 33030148 | tf_op jit(solution)/shard_map/broadcast_in_dim | solution.py:120
  (33 shorter events, 15.6 us)
Async XLA Ops:
  7.2 418.8 %all-reduce.3.cloned.1.call-start = ((), (), s32[]{:S(2)}) async-start(), calls=%async_computation | async-start | bytes 18874368 | tf_op jit(solution)/shard_map/psum | solution.py:118
  8.0 6.8 copy-start
  34.4 40.3 %collective-permute-start.1 = (bf16[256,3072]{1,0:T(8,128)(2,1)}, bf16[256,3072]{1,0:T(8,128)(2,1)S(1)}, u32[]{:S(2)}, u32[]{:S(2)}) collective-permute-start(bf16[256,3072]{1,0:T(8,128)(2,1)} %get-tuple-element.10), channel_id=1, source_target_pairs={{1,0},{2,1},{3,2},{5,4},{6,5},{7,6},{9,8},{10,9},{11,10},{13,12},{... | collective-permute-start | bytes 4718600 | tf_op jit(solution)/shard_map/ppermute | solution.py:107
  35.7 39.4 %collective-permute-start = (bf16[256,3072]{1,0:T(8,128)(2,1)}, bf16[256,3072]{1,0:T(8,128)(2,1)S(1)}, u32[]{:S(2)}, u32[]{:S(2)}) collective-permute-start(bf16[256,3072]{1,0:T(8,128)(2,1)} %get-tuple-element.11), channel_id=1, source_target_pairs={{0,1},{1,2},{2,3},{4,5},{5,6},{6,7},{8,9},{9,10},{10,11},{12,13},{... | collective-permute-start | bytes 4718600 | tf_op jit(solution)/shard_map/ppermute | solution.py:106
  74.6 1.1 copy-start.1
  75.8 1.2 copy-start.2
  108.5 68.8 %collective-permute-start.3 = (bf16[256,3072]{1,0:T(8,128)(2,1)S(1)}, bf16[256,3072]{1,0:T(8,128)(2,1)S(1)}, u32[]{:S(2)}, u32[]{:S(2)}) collective-permute-start(bf16[256,3072]{1,0:T(8,128)(2,1)S(1)} %get-tuple-element.8), channel_id=1, source_target_pairs={{1,0},{2,1},{3,2},{5,4},{6,5},{7,6},{9,8},{10,9},{11,10},{13,12},{... | collective-permute-start | bytes 4718600 | tf_op jit(solution)/shard_map/ppermute | solution.py:107
  110.0 67.3 %collective-permute-start.2 = (bf16[256,3072]{1,0:T(8,128)(2,1)S(1)}, bf16[256,3072]{1,0:T(8,128)(2,1)S(1)}, u32[]{:S(2)}, u32[]{:S(2)}) collective-permute-start(bf16[256,3072]{1,0:T(8,128)(2,1)S(1)} %get-tuple-element.9), channel_id=1, source_target_pairs={{0,1},{1,2},{2,3},{4,5},{5,6},{6,7},{8,9},{9,10},{10,11},{12,13},{... | collective-permute-start | bytes 4718600 | tf_op jit(solution)/shard_map/ppermute | solution.py:106
  177.3 1.2 copy-start.3
  178.5 1.1 copy-start.6
  197.3 639.3 %all-reduce.5.cloned.1.call-start = ((), (), s32[]{:S(2)}) async-start(), calls=%async_computation.1 | async-start | bytes 18874368 | tf_op jit(solution)/shard_map/psum | solution.py:118
  447.7 39.2 %collective-permute-start.5 = (bf16[256,3072]{1,0:T(8,128)(2,1)S(1)}, bf16[256,3072]{1,0:T(8,128)(2,1)S(1)}, u32[]{:S(2)}, u32[]{:S(2)}) collective-permute-start(bf16[256,3072]{1,0:T(8,128)(2,1)S(1)} %get-tuple-element.6), channel_id=1, source_target_pairs={{1,0},{2,1},{3,2},{5,4},{6,5},{7,6},{9,8},{10,9},{11,10},{13,12},{... | collective-permute-start | bytes 4718600 | tf_op jit(solution)/shard_map/ppermute | solution.py:107
  449.0 37.9 %collective-permute-start.4 = (bf16[256,3072]{1,0:T(8,128)(2,1)S(1)}, bf16[256,3072]{1,0:T(8,128)(2,1)S(1)}, u32[]{:S(2)}, u32[]{:S(2)}) collective-permute-start(bf16[256,3072]{1,0:T(8,128)(2,1)S(1)} %get-tuple-element.7), channel_id=1, source_target_pairs={{0,1},{1,2},{2,3},{4,5},{5,6},{6,7},{8,9},{9,10},{10,11},{12,13},{... | collective-permute-start | bytes 4718600 | tf_op jit(solution)/shard_map/ppermute | solution.py:106
  486.9 1.1 copy-start.5
  488.0 1.2 copy-start.8
  520.8 68.0 %collective-permute-start.7 = (bf16[256,3072]{1,0:T(8,128)(2,1)S(1)}, bf16[256,3072]{1,0:T(8,128)(2,1)S(1)}, u32[]{:S(2)}, u32[]{:S(2)}) collective-permute-start(bf16[256,3072]{1,0:T(8,128)(2,1)S(1)} %get-tuple-element.4), channel_id=1, source_target_pairs={{1,0},{2,1},{3,2},{5,4},{6,5},{7,6},{9,8},{10,9},{11,10},{13,12},{... | collective-permute-start | bytes 4718600 | tf_op jit(solution)/shard_map/ppermute | solution.py:107
  522.1 66.7 %collective-permute-start.6 = (bf16[256,3072]{1,0:T(8,128)(2,1)S(1)}, bf16[256,3072]{1,0:T(8,128)(2,1)S(1)}, u32[]{:S(2)}, u32[]{:S(2)}) collective-permute-start(bf16[256,3072]{1,0:T(8,128)(2,1)S(1)} %get-tuple-element.5), channel_id=1, source_target_pairs={{0,1},{1,2},{2,3},{4,5},{5,6},{6,7},{8,9},{9,10},{10,11},{12,13},{... | collective-permute-start | bytes 4718600 | tf_op jit(solution)/shard_map/ppermute | solution.py:106
  588.7 1.2 copy-start.4
  589.9 1.1 copy-start.7
Sparse Core Ops, SparseCore 0:
  197.4 228.5 all-reduce.2
  608.9 227.7 all-reduce.4

commit v3 on v2

--- a/solution.py
+++ b/solution.py
@@ -115,7 +115,12 @@
         scaled_u = (masses / kernel_v.astype(jnp.float32)).astype(jnp.bfloat16)
         kernel_u = apply_kernel(scaled_u).astype(jnp.float32)
         value_portion = weight * jnp.log(kernel_u)
-        barycenter = jnp.exp(lax.psum(value_portion, "img") / total_weight)
+        if iteration + 1 < ITERS:
+            log_sum = lax.psum_scatter(value_portion, "img", scatter_dimension=0, tiled=True)
+            barycenter = jnp.exp(log_sum / total_weight).astype(jnp.bfloat16)
+            barycenter = lax.all_gather(barycenter, "img", axis=0, tiled=True).astype(jnp.float32)
+        else:
+            barycenter = jnp.exp(lax.psum(value_portion, "img") / total_weight)
         scaling = barycenter / kernel_u
     return (barycenter, scaling[None])
 

time: 858 us -> 813 us (0.948)
  waiting for transfers between devices: 572 us -> 526 us
    psum x2 -> x1, waiting for transfers between devices: 442 us -> 227 us  [per_device(): barycenter = jnp.exp(lax.psum(value_portion, 'img') / total_weight)]
    reduce_scatter x0 -> x1, waiting for transfers between devices: none -> 118 us  [per_device(): lax.psum_scatter(value_portion, 'img', scatter_dimension=0, tiled=True)]
    all_gather x0 -> x1, waiting for transfers between devices: none -> 50.3 us  [per_device(): lax.all_gather(barycenter, 'img', axis=0, tiled=True).astype(jnp.float32)]
  transfers between devices with their start and end apart: 10 -> 11, of which waited for: 7 -> 9; matrix products, arithmetic and copies ran while one was open for 0% -> 0% of each run, Pallas kernels for 0% -> 0%
where the time goes in v3:
time: 813 us; the launch traced here: 812 us
  waiting for transfers between devices  526 us (65%)
  starting transfers between devices  84 us (10%)
  Pallas kernels  81.3 us (10%)
  other arithmetic  70.1 us (9%)
  local copies, waits for them, and re-layouts  21.4 us (3%)
  blocking collectives  14.8 us (2%)
  between operations  14.5 us (2%)
    psum x1, waiting for transfers between devices, per_device(): barycenter = jnp.exp(lax.psum(value_portion, 'img') / total_weight)  227 us
    ppermute x4, waiting for transfers between devices, apply_kernel(): from_next = lax.ppermute(inner[:halo], 'slab', down)  130 us
    reduce_scatter x1, waiting for transfers between devices, per_device(): lax.psum_scatter(value_portion, 'img', scatter_dimension=0, tiled=True)  118 us
    ppermute x4, starting transfers between devices, apply_kernel(): from_prev = lax.ppermute(inner[rows - halo:], 'slab', up)  78.5 us
    all_gather x1, waiting for transfers between devices, per_device(): lax.all_gather(barycenter, 'img', axis=0, tiled=True).astype(jnp.float32)  50.3 us
    pallas_call x4, Pallas kernels, row_pass(): pl.pallas_call(row_kernel, grid=(cols // tile_cols,), in_specs=[pl.BlockS...  40.9 us
    pallas_call x4, Pallas kernels, column_pass(): pl.pallas_call(column_kernel, grid=(rows // tile_rows,), in_specs=[pl.Blo...  40.3 us
    convert_element_type x2, other arithmetic, per_device(): scaled_u = (masses / kernel_v.astype(jnp.float32)).astype(jnp.bfloat16)  18.4 us
  transfers between devices with their start and end apart: 11, of which 9 were waited for; matrix products, arithmetic and copies ran while one was open for 0% of the time, Pallas kernels for 0%

profile of v3, /device:TPU:0, one launch (start us, length us, event | category | flops | bytes accessed | tf_op | source)
XLA Modules:
  0.0 811.7 jit_solution(2977014039814431025)
XLA Ops:
  8.0 6.7 convert_bitcast_fusion.x_ref
  14.8 5.8 select_reduce_fusion.t_ref
  20.6 10.1 %shard_map.68.mid_ref = bf16[768,3072]{1,0:T(8,128)(2,1)} custom-call(bf16[768,3072]{1,0:T(8,128)(2,1)} %convert_bitcast_fusion.x_ref, bf16[24,5,128,128]{3,2,1,0:T(8,128)(2,1)} %select_reduce_fusion.t_ref), custom_call_target="tpu_custom_call" | custom-call | tf_op jit(solution)/shard_map/pallas_call | solution.py:41
  30.7 3.8 fusion.9
  35.8 5.6 collective-permute-start
  41.4 2.3 constant_dynamic-slice_fusion.t_ref
  43.6 31.1 %collective-permute-done.1.next_ref = bf16[256,3072]{1,0:T(8,128)(2,1)S(1)} collective-permute-done((bf16[256,3072]{1,0:T(8,128)(2,1)}, bf16[256,3072]{1,0:T(8,128)(2,1)S(1)}, u32[]{:S(2)}, u32[]{:S(2)}) %collective-permute-start.1) | collective-permute-done | bytes 1572896 | tf_op jit(solution)/shard_map/ppermute | solution.py:107
  77.1 10.2 %shard_map.69 = bf16[768,3072]{1,0:T(8,128)(2,1)} custom-call(bf16[256,3072]{1,0:T(8,128)(2,1)} %copy-done.2, bf16[768,3072]{1,0:T(8,128)(2,1)} %shard_map.68.mid_ref, bf16[256,3072]{1,0:T(8,128)(2,1)} %copy-done.1, bf16[6,5,128,128]{3,2,1,0:T(8,128)(2,1)} %constant_dynamic-slice_fusion.t_ref), custom_call_target="tpu_custom_call" | custom-call | tf_op jit(solution)/shard_map/pallas_call | solution.py:74
  87.2 9.2 %fusion.4.x_ref = bf16[768,3072]{1,0:T(8,128)(2,1)} fusion(f32[1,768,3072]{2,1,0:T(8,128)} %param.5, bf16[768,3072]{1,0:T(8,128)(2,1)} %shard_map.69), kind=kLoop, calls=%fused_computation.11 | loop fusion | flops 7077888 | bytes 18874368 | tf_op jit(solution)/shard_map/convert_element_type | solution.py:115
  96.5 10.1 %shard_map.70.mid_ref = bf16[768,3072]{1,0:T(8,128)(2,1)} custom-call(bf16[768,3072]{1,0:T(8,128)(2,1)} %fusion.4.x_ref, bf16[24,5,128,128]{3,2,1,0:T(8,128)(2,1)} %select_reduce_fusion.t_ref), custom_call_target="tpu_custom_call" | custom-call | tf_op jit(solution)/shard_map/pallas_call | solution.py:41
  110.1 34.0 %collective-permute-start.2 = (bf16[256,3072]{1,0:T(8,128)(2,1)S(1)}, bf16[256,3072]{1,0:T(8,128)(2,1)S(1)}, u32[]{:S(2)}, u32[]{:S(2)}) collective-permute-start(bf16[256,3072]{1,0:T(8,128)(2,1)S(1)} %get-tuple-element.9), channel_id=1, source_target_pairs={{0,1},{1,2},{2,3},{4,5},{5,6},{6,7},{8,9},{9,10},{10,11},{12,13},{... | collective-permute-start | bytes 4718600 | tf_op jit(solution)/shard_map/ppermute | solution.py:106
  144.8 32.6 %collective-permute-done.3.next_ref = bf16[256,3072]{1,0:T(8,128)(2,1)S(1)} collective-permute-done((bf16[256,3072]{1,0:T(8,128)(2,1)S(1)}, bf16[256,3072]{1,0:T(8,128)(2,1)S(1)}, u32[]{:S(2)}, u32[]{:S(2)}) %collective-permute-start.3) | collective-permute-done | bytes 1572896 | tf_op jit(solution)/shard_map/ppermute | solution.py:107
  179.8 10.3 %shard_map.71 = bf16[768,3072]{1,0:T(8,128)(2,1)} custom-call(bf16[256,3072]{1,0:T(8,128)(2,1)} %copy-done.6, bf16[768,3072]{1,0:T(8,128)(2,1)} %shard_map.70.mid_ref, bf16[256,3072]{1,0:T(8,128)(2,1)} %copy-done.3, bf16[6,5,128,128]{3,2,1,0:T(8,128)(2,1)} %constant_dynamic-slice_fusion.t_ref), custom_call_target="tpu_custom_call" | custom-call | tf_op jit(solution)/shard_map/pallas_call | solution.py:74
  190.1 7.4 fusion
  197.5 14.8 %psum.14 = f32[]{:T(128)} all-reduce(f32[]{:T(128)} %bitcast), channel_id=1, replica_groups=mesh['img'=8,'slab'=4] {'img'}, use_global_device_ids=true, to_apply=%region_2.3 | all-reduce | flops 1 | bytes 8 | tf_op jit(solution)/shard_map/psum | solution.py:98
  212.3 117.9 %reduce-scatter.2.cloned.1.call-done = f32[96,3072]{1,0:T(8,128)} async-done(((f32[768,3072]{1,0:T(8,128)}), f32[96,3072]{1,0:T(8,128)}) %reduce-scatter.2.cloned.1.call-update) | async-done | bytes 1179664 | tf_op jit(solution)/shard_map/reduce_scatter | solution.py:119
  330.2 2.9 exponential_convert_fusion
  333.1 50.3 %all-gather.2.cloned.1.call-done = bf16[768,3072]{1,0:T(8,128)(2,1)} async-done(((bf16[96,3072]{1,0:T(8,128)(2,1)}), bf16[768,3072]{1,0:T(8,128)(2,1)}) %all-gather.2.cloned.1.call-update) | async-done | bytes 4718608 | tf_op jit(solution)/shard_map/all_gather | solution.py:121
  383.5 8.0 fusion.1.x_ref
  391.5 10.1 %shard_map.72.mid_ref = bf16[768,3072]{1,0:T(8,128)(2,1)} custom-call(bf16[768,3072]{1,0:T(8,128)(2,1)} %fusion.1.x_ref, bf16[24,5,128,128]{3,2,1,0:T(8,128)(2,1)} %select_reduce_fusion.t_ref), custom_call_target="tpu_custom_call" | custom-call | tf_op jit(solution)/shard_map/pallas_call | solution.py:41
  401.6 2.1 fusion.7
  405.0 4.9 collective-permute-start.4
  409.8 32.9 %collective-permute-done.5.next_ref = bf16[256,3072]{1,0:T(8,128)(2,1)S(1)} collective-permute-done((bf16[256,3072]{1,0:T(8,128)(2,1)S(1)}, bf16[256,3072]{1,0:T(8,128)(2,1)S(1)}, u32[]{:S(2)}, u32[]{:S(2)}) %collective-permute-start.5) | collective-permute-done | bytes 1572896 | tf_op jit(solution)/shard_map/ppermute | solution.py:107
  445.1 10.2 %shard_map.73 = bf16[768,3072]{1,0:T(8,128)(2,1)} custom-call(bf16[256,3072]{1,0:T(8,128)(2,1)} %copy-done.8, bf16[768,3072]{1,0:T(8,128)(2,1)} %shard_map.72.mid_ref, bf16[256,3072]{1,0:T(8,128)(2,1)} %copy-done.5, bf16[6,5,128,128]{3,2,1,0:T(8,128)(2,1)} %constant_dynamic-slice_fusion.t_ref), custom_call_target="tpu_custom_call" | custom-call | tf_op jit(solution)/shard_map/pallas_call | solution.py:74
  455.3 9.2 %fusion.5.x_ref = bf16[768,3072]{1,0:T(8,128)(2,1)} fusion(f32[1,768,3072]{2,1,0:T(8,128)} %param.5, bf16[768,3072]{1,0:T(8,128)(2,1)} %shard_map.73), kind=kLoop, calls=%fused_computation.12 | loop fusion | flops 7077888 | bytes 18874368 | tf_op jit(solution)/shard_map/convert_element_type | solution.py:115
  464.5 10.1 %shard_map.74.mid_ref = bf16[768,3072]{1,0:T(8,128)(2,1)} custom-call(bf16[768,3072]{1,0:T(8,128)(2,1)} %fusion.5.x_ref, bf16[24,5,128,128]{3,2,1,0:T(8,128)(2,1)} %select_reduce_fusion.t_ref), custom_call_target="tpu_custom_call" | custom-call | tf_op jit(solution)/shard_map/pallas_call | solution.py:41
  478.0 34.1 %collective-permute-start.6 = (bf16[256,3072]{1,0:T(8,128)(2,1)S(1)}, bf16[256,3072]{1,0:T(8,128)(2,1)S(1)}, u32[]{:S(2)}, u32[]{:S(2)}) collective-permute-start(bf16[256,3072]{1,0:T(8,128)(2,1)S(1)} %get-tuple-element.5), channel_id=1, source_target_pairs={{0,1},{1,2},{2,3},{4,5},{5,6},{6,7},{8,9},{9,10},{10,11},{12,13},{... | collective-permute-start | bytes 4718600 | tf_op jit(solution)/shard_map/ppermute | solution.py:106
  512.0 33.2 %collective-permute-done.7.next_ref = bf16[256,3072]{1,0:T(8,128)(2,1)S(1)} collective-permute-done((bf16[256,3072]{1,0:T(8,128)(2,1)S(1)}, bf16[256,3072]{1,0:T(8,128)(2,1)S(1)}, u32[]{:S(2)}, u32[]{:S(2)}) %collective-permute-start.7) | collective-permute-done | bytes 1572896 | tf_op jit(solution)/shard_map/ppermute | solution.py:107
  547.6 10.3 %shard_map.75 = bf16[768,3072]{1,0:T(8,128)(2,1)} custom-call(bf16[256,3072]{1,0:T(8,128)(2,1)} %copy-done.7, bf16[768,3072]{1,0:T(8,128)(2,1)} %shard_map.74.mid_ref, bf16[256,3072]{1,0:T(8,128)(2,1)} %copy-done.4, bf16[6,5,128,128]{3,2,1,0:T(8,128)(2,1)} %constant_dynamic-slice_fusion.t_ref), custom_call_target="tpu_custom_call" | custom-call | tf_op jit(solution)/shard_map/pallas_call | solution.py:74
  557.9 7.4 fusion.2
  565.3 226.5 %all-reduce.2.cloned.1.call-done = f32[768,3072]{1,0:T(8,128)} async-done(((f32[768,3072]{1,0:T(8,128)}), f32[768,3072]{1,0:T(8,128)}) %all-reduce.2.cloned.1.call-update) | async-done | bytes 9437200 | tf_op jit(solution)/shard_map/psum | solution.py:123
  791.8 13.3 %fusion.3 = (f32[1,768,3072]{2,1,0:T(8,128)}, f32[768,3072]{1,0:T(8,128)}) fusion(bf16[768,3072]{1,0:T(8,128)(2,1)} %shard_map.75, f32[768,3072]{1,0:T(8,128)} %all-reduce.2.cloned.1.call-done, f32[]{:T(128)} %psum.14), kind=kLoop, calls=%fused_computation.8 | loop fusion | flops 7077888 | bytes 33030148 | tf_op jit(solution)/shard_map/broadcast_in_dim | solution.py:125
  (37 shorter events, 19.8 us)
Async XLA Ops:
  7.2 323.0 %reduce-scatter.2.cloned.1.call-start = ((), (), s32[]{:S(2)}) async-start(), calls=%async_computation.1 | async-start | bytes 10616832 | tf_op jit(solution)/shard_map/reduce_scatter | solution.py:119
  8.0 6.8 copy-start
  34.5 40.3 %collective-permute-start.1 = (bf16[256,3072]{1,0:T(8,128)(2,1)}, bf16[256,3072]{1,0:T(8,128)(2,1)S(1)}, u32[]{:S(2)}, u32[]{:S(2)}) collective-permute-start(bf16[256,3072]{1,0:T(8,128)(2,1)} %get-tuple-element.10), channel_id=1, source_target_pairs={{1,0},{2,1},{3,2},{5,4},{6,5},{7,6},{9,8},{10,9},{11,10},{13,12},{... | collective-permute-start | bytes 4718600 | tf_op jit(solution)/shard_map/ppermute | solution.py:107
  35.8 39.4 %collective-permute-start = (bf16[256,3072]{1,0:T(8,128)(2,1)}, bf16[256,3072]{1,0:T(8,128)(2,1)S(1)}, u32[]{:S(2)}, u32[]{:S(2)}) collective-permute-start(bf16[256,3072]{1,0:T(8,128)(2,1)} %get-tuple-element.11), channel_id=1, source_target_pairs={{0,1},{1,2},{2,3},{4,5},{5,6},{6,7},{8,9},{9,10},{10,11},{12,13},{... | collective-permute-start | bytes 4718600 | tf_op jit(solution)/shard_map/ppermute | solution.py:106
  74.8 1.1 copy-start.1
  75.9 1.2 copy-start.2
  108.6 68.8 %collective-permute-start.3 = (bf16[256,3072]{1,0:T(8,128)(2,1)S(1)}, bf16[256,3072]{1,0:T(8,128)(2,1)S(1)}, u32[]{:S(2)}, u32[]{:S(2)}) collective-permute-start(bf16[256,3072]{1,0:T(8,128)(2,1)S(1)} %get-tuple-element.8), channel_id=1, source_target_pairs={{1,0},{2,1},{3,2},{5,4},{6,5},{7,6},{9,8},{10,9},{11,10},{13,12},{... | collective-permute-start | bytes 4718600 | tf_op jit(solution)/shard_map/ppermute | solution.py:107
  110.1 67.3 %collective-permute-start.2 = (bf16[256,3072]{1,0:T(8,128)(2,1)S(1)}, bf16[256,3072]{1,0:T(8,128)(2,1)S(1)}, u32[]{:S(2)}, u32[]{:S(2)}) collective-permute-start(bf16[256,3072]{1,0:T(8,128)(2,1)S(1)} %get-tuple-element.9), channel_id=1, source_target_pairs={{0,1},{1,2},{2,3},{4,5},{5,6},{6,7},{8,9},{9,10},{10,11},{12,13},{... | collective-permute-start | bytes 4718600 | tf_op jit(solution)/shard_map/ppermute | solution.py:106
  177.4 1.2 copy-start.3
  178.6 1.1 copy-start.6
  197.5 186.0 %all-gather.2.cloned.1.call-start = ((), (), s32[]{:S(2)}) async-start(), calls=%async_computation.2 | async-start | bytes 5308416 | tf_op jit(solution)/shard_map/all_gather | solution.py:121
  333.1 458.7 %all-reduce.2.cloned.1.call-start = ((), (), s32[]{:S(2)}) async-start(), calls=%async_computation.3 | async-start | bytes 18874368 | tf_op jit(solution)/shard_map/psum | solution.py:123
  403.7 39.1 %collective-permute-start.5 = (bf16[256,3072]{1,0:T(8,128)(2,1)S(1)}, bf16[256,3072]{1,0:T(8,128)(2,1)S(1)}, u32[]{:S(2)}, u32[]{:S(2)}) collective-permute-start(bf16[256,3072]{1,0:T(8,128)(2,1)S(1)} %get-tuple-element.6), channel_id=1, source_target_pairs={{1,0},{2,1},{3,2},{5,4},{6,5},{7,6},{9,8},{10,9},{11,10},{13,12},{... | collective-permute-start | bytes 4718600 | tf_op jit(solution)/shard_map/ppermute | solution.py:107
  405.0 38.3 %collective-permute-start.4 = (bf16[256,3072]{1,0:T(8,128)(2,1)S(1)}, bf16[256,3072]{1,0:T(8,128)(2,1)S(1)}, u32[]{:S(2)}, u32[]{:S(2)}) collective-permute-start(bf16[256,3072]{1,0:T(8,128)(2,1)S(1)} %get-tuple-element.7), channel_id=1, source_target_pairs={{0,1},{1,2},{2,3},{4,5},{5,6},{6,7},{8,9},{9,10},{10,11},{12,13},{... | collective-permute-start | bytes 4718600 | tf_op jit(solution)/shard_map/ppermute | solution.py:106
  442.8 1.1 copy-start.5
  443.9 1.2 copy-start.8
  476.7 68.6 %collective-permute-start.7 = (bf16[256,3072]{1,0:T(8,128)(2,1)S(1)}, bf16[256,3072]{1,0:T(8,128)(2,1)S(1)}, u32[]{:S(2)}, u32[]{:S(2)}) collective-permute-start(bf16[256,3072]{1,0:T(8,128)(2,1)S(1)} %get-tuple-element.4), channel_id=1, source_target_pairs={{1,0},{2,1},{3,2},{5,4},{6,5},{7,6},{9,8},{10,9},{11,10},{13,12},{... | collective-permute-start | bytes 4718600 | tf_op jit(solution)/shard_map/ppermute | solution.py:107
  478.0 67.3 %collective-permute-start.6 = (bf16[256,3072]{1,0:T(8,128)(2,1)S(1)}, bf16[256,3072]{1,0:T(8,128)(2,1)S(1)}, u32[]{:S(2)}, u32[]{:S(2)}) collective-permute-start(bf16[256,3072]{1,0:T(8,128)(2,1)S(1)} %get-tuple-element.5), channel_id=1, source_target_pairs={{0,1},{1,2},{2,3},{4,5},{5,6},{6,7},{8,9},{9,10},{10,11},{12,13},{... | collective-permute-start | bytes 4718600 | tf_op jit(solution)/shard_map/ppermute | solution.py:106
  545.3 1.2 copy-start.4
  546.4 1.1 copy-start.7
Sparse Core Ops, SparseCore 0:
  197.6 132.5 reduce-scatter.1
  333.2 50.2 all-gather.1
  565.4 226.3 all-reduce.1

commit v4 on v2

--- a/solution.py
+++ b/solution.py
@@ -101,10 +101,26 @@
     up = [(i, i + 1) for i in range(nslab - 1)]
     down = [(i + 1, i) for i in range(nslab - 1)]
 
+    def exchange(inner):
+        to_up = inner[rows - halo :]
+        to_down = inner[:halo]
+        if nslab != 4:
+            return lax.ppermute(to_up, "slab", up), lax.ppermute(to_down, "slab", down)
+        half = halo // 2
+        direct_prev = lax.ppermute(to_up, "slab", [(0, 1), (2, 3)])
+        direct_next = lax.ppermute(to_down, "slab", [(1, 0), (3, 2)])
+        first = jnp.where(slab == 1, to_up[:half], to_down[:half])
+        second = jnp.where(slab == 1, to_up[half:], to_down[half:])
+        first = lax.ppermute(first, "slab", [(1, 3), (2, 0)])
+        second = lax.ppermute(second, "slab", [(1, 0), (2, 3)])
+        first = lax.ppermute(first, "slab", [(3, 2), (0, 1)])
+        second = lax.ppermute(second, "slab", [(0, 2), (3, 1)])
+        diagonal = jnp.concatenate([first, second], axis=0)
+        return jnp.where(slab == 2, diagonal, direct_prev), jnp.where(slab == 1, diagonal, direct_next)
+
     def apply_kernel(field):
         inner = column_pass(field, terms)
-        from_prev = lax.ppermute(inner[rows - halo :], "slab", up)
-        from_next = lax.ppermute(inner[:halo], "slab", down)
+        from_prev, from_next = exchange(inner)
         return row_pass(from_prev, inner, from_next, terms_local)
 
     masses = image_masses[0]
@@ -115,7 +131,8 @@
         scaled_u = (masses / kernel_v.astype(jnp.float32)).astype(jnp.bfloat16)
         kernel_u = apply_kernel(scaled_u).astype(jnp.float32)
         value_portion = weight * jnp.log(kernel_u)
-        barycenter = jnp.exp(lax.psum(value_portion, "img") / total_weight)
+        log_sum = lax.psum_scatter(value_portion, "img", scatter_dimension=0, tiled=True)
+        barycenter = lax.all_gather(jnp.exp(log_sum / total_weight), "img", axis=0, tiled=True)
         scaling = barycenter / kernel_u
     return (barycenter, scaling[None])
 

time: 858 us -> 812 us (0.946)
  starting transfers between devices: 83.3 us -> 54.3 us
  waiting for transfers between devices: 572 us -> 544 us
  other arithmetic: 68.6 us -> 89.4 us
  local copies, waits for them, and re-layouts: 21.9 us -> 11.4 us
    psum x2 -> x0, waiting for transfers between devices: 442 us -> none  [per_device(): barycenter = jnp.exp(lax.psum(value_portion, 'img') / total_weight)]
    reduce_scatter x0 -> x2, waiting for transfers between devices: none -> 184 us  [per_device(): lax.psum_scatter(value_portion, 'img', scatter_dimension=0, tiled=True)]
    all_gather x0 -> x2, waiting for transfers between devices: none -> 178 us  [per_device(): lax.all_gather(jnp.exp(log_sum / total_weight), 'img', axis=0, tiled=True)]
    ppermute x8 -> x24, waiting for transfers between devices: 131 us -> 182 us  [the longest x4 131 us: exchange(): first = lax.ppermute(first, 'slab', [(3, 2), (0, 1)])]
    ppermute x8 -> x24, starting transfers between devices: 83.2 us -> 53.9 us  [the longest x4 24.6 us: exchange(): direct_prev = lax.ppermute(to_up, 'slab', [(0, 1), (2, 3)])]
    select_n x0 -> x8, other arithmetic: none -> 17.8 us  [the longest x4 9.15 us: exchange(): jnp.where(slab == 1, diagonal, direct_next)]
  transfers between devices with their start and end apart: 10 -> 28, of which waited for: 7 -> 12; matrix products, arithmetic and copies ran while one was open for 0% -> 1% of each run, Pallas kernels for 0% -> 0%
where the time goes in v4:
time: 812 us; the launch traced here: 810 us
  waiting for transfers between devices  544 us (67%)
  other arithmetic  89.4 us (11%)
  Pallas kernels  81.2 us (10%)
  starting transfers between devices  54.3 us (7%)
  blocking collectives  15.7 us (2%)
  between operations  14.9 us (2%)
  local copies, waits for them, and re-layouts  11.4 us (1%)
    reduce_scatter x2, waiting for transfers between devices, per_device(): lax.psum_scatter(value_portion, 'img', scatter_dimension=0, tiled=True)  184 us
    all_gather x2, waiting for transfers between devices, per_device(): lax.all_gather(jnp.exp(log_sum / total_weight), 'img', axis=0, tiled=True)  178 us
    ppermute x4, waiting for transfers between devices, exchange(): first = lax.ppermute(first, 'slab', [(3, 2), (0, 1)])  131 us
    ppermute x4, waiting for transfers between devices, exchange(): first = lax.ppermute(first, 'slab', [(1, 3), (2, 0)])  50.6 us
    pallas_call x4, Pallas kernels, row_pass(): pl.pallas_call(row_kernel, grid=(cols // tile_cols,), in_specs=[pl.BlockS...  40.9 us
    pallas_call x4, Pallas kernels, column_pass(): pl.pallas_call(column_kernel, grid=(rows // tile_rows,), in_specs=[pl.Blo...  40.3 us
    ppermute x4, starting transfers between devices, exchange(): direct_prev = lax.ppermute(to_up, 'slab', [(0, 1), (2, 3)])  24.6 us
    convert_element_type x2, other arithmetic, per_device(): scaled_u = (masses / kernel_v.astype(jnp.float32)).astype(jnp.bfloat16)  18 us
  transfers between devices with their start and end apart: 28, of which 12 were waited for; matrix products, arithmetic and copies ran while one was open for 1% of the time, Pallas kernels for 0%

profile of v4, /device:TPU:0, one launch (start us, length us, event | category | flops | bytes accessed | tf_op | source)
XLA Modules:
  0.0 810.5 jit_solution(8696368082604093172)
XLA Ops:
  8.0 6.7 convert_bitcast_fusion.x_ref
  14.8 5.7 select_reduce_fusion.t_ref
  20.5 10.1 %shard_map.68.mid_ref = bf16[768,3072]{1,0:T(8,128)(2,1)} custom-call(bf16[768,3072]{1,0:T(8,128)(2,1)} %convert_bitcast_fusion.x_ref, bf16[24,5,128,128]{3,2,1,0:T(8,128)(2,1)} %select_reduce_fusion.t_ref), custom_call_target="tpu_custom_call" | custom-call | tf_op jit(solution)/shard_map/pallas_call | solution.py:41
  38.1 9.1 %collective-permute-start.4 = (bf16[256,3072]{1,0:T(8,128)(2,1)S(1)}, bf16[256,3072]{1,0:T(8,128)(2,1)}, u32[]{:S(2)}, u32[]{:S(2)}) collective-permute-start(bf16[256,3072]{1,0:T(8,128)(2,1)S(1)} %get-tuple-element.15), channel_id=1, source_target_pairs={{0,1},{2,3},{4,5},{6,7},{8,9},{10,11},{12,13},{14,15},{16,17},{18,... | collective-permute-start | bytes 4718600 | tf_op jit(solution)/shard_map/ppermute | solution.py:110
  47.2 11.5 %collective-permute-done = bf16[128,3072]{1,0:T(8,128)(2,1)} collective-permute-done((bf16[128,3072]{1,0:T(8,128)(2,1)S(1)}, bf16[128,3072]{1,0:T(8,128)(2,1)}, u32[]{:S(2)}, u32[]{:S(2)}) %collective-permute-start) | collective-permute-done | bytes 786464 | tf_op jit(solution)/shard_map/ppermute | solution.py:114
  65.3 31.0 %collective-permute-done.1 = bf16[128,3072]{1,0:T(8,128)(2,1)} collective-permute-done((bf16[128,3072]{1,0:T(8,128)(2,1)}, bf16[128,3072]{1,0:T(8,128)(2,1)}, u32[]{:S(2)}, u32[]{:S(2)}) %collective-permute-start.1) | collective-permute-done | bytes 786464 | tf_op jit(solution)/shard_map/ppermute | solution.py:116
  102.1 10.2 %shard_map.69 = bf16[768,3072]{1,0:T(8,128)(2,1)} custom-call(bf16[256,3072]{1,0:T(8,128)(2,1)} %get-tuple-element.25.prev_ref, bf16[768,3072]{1,0:T(8,128)(2,1)} %shard_map.68.mid_ref, bf16[256,3072]{1,0:T(8,128)(2,1)} %get-tuple-element.24.next_ref, bf16[6,5,128,128]{3,2,1,0:T(8,128)(2,1)} %constant_dynamic-slice_fusion.t_ref), custom_call_target="tpu_custom_call" | custom-call | tf_op jit(solution)/shard_map/pallas_call | solution.py:74
  112.3 9.0 %fusion.4.x_ref = bf16[768,3072]{1,0:T(8,128)(2,1)} fusion(f32[1,768,3072]{2,1,0:T(8,128)} %param.5, bf16[768,3072]{1,0:T(8,128)(2,1)} %shard_map.69), kind=kLoop, calls=%fused_computation.11 | loop fusion | flops 7077888 | bytes 18874368 | tf_op jit(solution)/shard_map/convert_element_type | solution.py:131
  121.3 10.1 %shard_map.70.mid_ref = bf16[768,3072]{1,0:T(8,128)(2,1)} custom-call(bf16[768,3072]{1,0:T(8,128)(2,1)} %fusion.4.x_ref, bf16[24,5,128,128]{3,2,1,0:T(8,128)(2,1)} %select_reduce_fusion.t_ref), custom_call_target="tpu_custom_call" | custom-call | tf_op jit(solution)/shard_map/pallas_call | solution.py:41
  137.8 4.8 collective-permute-start.10
  142.7 12.3 %collective-permute-done.6 = bf16[128,3072]{1,0:T(8,128)(2,1)S(1)} collective-permute-done((bf16[128,3072]{1,0:T(8,128)(2,1)S(1)}, bf16[128,3072]{1,0:T(8,128)(2,1)S(1)}, u32[]{:S(2)}, u32[]{:S(2)}) %collective-permute-start.6) | collective-permute-done | bytes 786464 | tf_op jit(solution)/shard_map/ppermute | solution.py:114
  158.6 33.1 %collective-permute-done.7 = bf16[128,3072]{1,0:T(8,128)(2,1)S(1)} collective-permute-done((bf16[128,3072]{1,0:T(8,128)(2,1)S(1)}, bf16[128,3072]{1,0:T(8,128)(2,1)S(1)}, u32[]{:S(2)}, u32[]{:S(2)}) %collective-permute-start.7) | collective-permute-done | bytes 786464 | tf_op jit(solution)/shard_map/ppermute | solution.py:116
  193.8 10.3 %shard_map.71 = bf16[768,3072]{1,0:T(8,128)(2,1)} custom-call(bf16[256,3072]{1,0:T(8,128)(2,1)} %get-tuple-element.23.prev_ref, bf16[768,3072]{1,0:T(8,128)(2,1)} %shard_map.70.mid_ref, bf16[256,3072]{1,0:T(8,128)(2,1)} %get-tuple-element.22.next_ref, bf16[6,5,128,128]{3,2,1,0:T(8,128)(2,1)} %constant_dynamic-slice_fusion.t_ref), custom_call_target="tpu_custom_call" | custom-call | tf_op jit(solution)/shard_map/pallas_call | solution.py:74
  204.1 7.4 fusion
  211.5 15.7 %psum.7 = f32[]{:T(128)} all-reduce(f32[]{:T(128)} %bitcast), channel_id=1, replica_groups=mesh['img'=8,'slab'=4] {'img'}, use_global_device_ids=true, to_apply=%region_2.3 | all-reduce | flops 1 | bytes 8 | tf_op jit(solution)/shard_map/psum | solution.py:98
  227.2 85.4 %reduce-scatter.3.cloned.1.call-done = f32[96,3072]{1,0:T(8,128)} async-done(((f32[768,3072]{1,0:T(8,128)}), f32[96,3072]{1,0:T(8,128)}) %reduce-scatter.3.cloned.1.call-update) | async-done | bytes 1179664 | tf_op jit(solution)/shard_map/reduce_scatter | solution.py:134
  316.0 88.9 %all-gather.3.cloned.1.call-done = f32[768,3072]{1,0:T(8,128)} async-done(((f32[96,3072]{1,0:T(8,128)}), f32[768,3072]{1,0:T(8,128)}) %all-gather.3.cloned.1.call-update) | async-done | bytes 9437200 | tf_op jit(solution)/shard_map/all_gather | solution.py:135
  404.8 9.0 %fusion.1.x_ref = bf16[768,3072]{1,0:T(8,128)(2,1)} fusion(f32[768,3072]{1,0:T(8,128)} %all-gather.3.cloned.1.call-done, bf16[768,3072]{1,0:T(8,128)(2,1)} %shard_map.71), kind=kLoop, calls=%fused_computation.6 | loop fusion | flops 7077888 | bytes 18874368 | tf_op jit(solution)/shard_map/convert_element_type | solution.py:130
  413.8 10.1 %shard_map.72.mid_ref = bf16[768,3072]{1,0:T(8,128)(2,1)} custom-call(bf16[768,3072]{1,0:T(8,128)(2,1)} %fusion.1.x_ref, bf16[24,5,128,128]{3,2,1,0:T(8,128)(2,1)} %select_reduce_fusion.t_ref), custom_call_target="tpu_custom_call" | custom-call | tf_op jit(solution)/shard_map/pallas_call | solution.py:41
  430.3 5.7 collective-permute-start.16
  436.0 14.0 %collective-permute-done.12 = bf16[128,3072]{1,0:T(8,128)(2,1)S(1)} collective-permute-done((bf16[128,3072]{1,0:T(8,128)(2,1)S(1)}, bf16[128,3072]{1,0:T(8,128)(2,1)S(1)}, u32[]{:S(2)}, u32[]{:S(2)}) %collective-permute-start.12) | collective-permute-done | bytes 786464 | tf_op jit(solution)/shard_map/ppermute | solution.py:114
  452.9 33.7 %collective-permute-done.13 = bf16[128,3072]{1,0:T(8,128)(2,1)S(1)} collective-permute-done((bf16[128,3072]{1,0:T(8,128)(2,1)S(1)}, bf16[128,3072]{1,0:T(8,128)(2,1)S(1)}, u32[]{:S(2)}, u32[]{:S(2)}) %collective-permute-start.13) | collective-permute-done | bytes 786464 | tf_op jit(solution)/shard_map/ppermute | solution.py:116
  488.6 10.2 %shard_map.73 = bf16[768,3072]{1,0:T(8,128)(2,1)} custom-call(bf16[256,3072]{1,0:T(8,128)(2,1)} %get-tuple-element.21.prev_ref, bf16[768,3072]{1,0:T(8,128)(2,1)} %shard_map.72.mid_ref, bf16[256,3072]{1,0:T(8,128)(2,1)} %get-tuple-element.20.next_ref, bf16[6,5,128,128]{3,2,1,0:T(8,128)(2,1)} %constant_dynamic-slice_fusion.t_ref), custom_call_target="tpu_custom_call" | custom-call | tf_op jit(solution)/shard_map/pallas_call | solution.py:74
  498.8 9.0 %fusion.5.x_ref = bf16[768,3072]{1,0:T(8,128)(2,1)} fusion(f32[1,768,3072]{2,1,0:T(8,128)} %param.5, bf16[768,3072]{1,0:T(8,128)(2,1)} %shard_map.73), kind=kLoop, calls=%fused_computation.12 | loop fusion | flops 7077888 | bytes 18874368 | tf_op jit(solution)/shard_map/convert_element_type | solution.py:131
  507.8 10.1 %shard_map.74.mid_ref = bf16[768,3072]{1,0:T(8,128)(2,1)} custom-call(bf16[768,3072]{1,0:T(8,128)(2,1)} %fusion.5.x_ref, bf16[24,5,128,128]{3,2,1,0:T(8,128)(2,1)} %select_reduce_fusion.t_ref), custom_call_target="tpu_custom_call" | custom-call | tf_op jit(solution)/shard_map/pallas_call | solution.py:41
  529.1 12.8 %collective-permute-done.18 = bf16[128,3072]{1,0:T(8,128)(2,1)S(1)} collective-permute-done((bf16[128,3072]{1,0:T(8,128)(2,1)S(1)}, bf16[128,3072]{1,0:T(8,128)(2,1)S(1)}, u32[]{:S(2)}, u32[]{:S(2)}) %collective-permute-start.18) | collective-permute-done | bytes 786464 | tf_op jit(solution)/shard_map/ppermute | solution.py:114
  545.2 33.4 %collective-permute-done.19 = bf16[128,3072]{1,0:T(8,128)(2,1)S(1)} collective-permute-done((bf16[128,3072]{1,0:T(8,128)(2,1)S(1)}, bf16[128,3072]{1,0:T(8,128)(2,1)S(1)}, u32[]{:S(2)}, u32[]{:S(2)}) %collective-permute-start.19) | collective-permute-done | bytes 786464 | tf_op jit(solution)/shard_map/ppermute | solution.py:116
  580.7 10.3 %shard_map.75 = bf16[768,3072]{1,0:T(8,128)(2,1)} custom-call(bf16[256,3072]{1,0:T(8,128)(2,1)} %get-tuple-element.19.prev_ref, bf16[768,3072]{1,0:T(8,128)(2,1)} %shard_map.74.mid_ref, bf16[256,3072]{1,0:T(8,128)(2,1)} %get-tuple-element.18.next_ref, bf16[6,5,128,128]{3,2,1,0:T(8,128)(2,1)} %constant_dynamic-slice_fusion.t_ref), custom_call_target="tpu_custom_call" | custom-call | tf_op jit(solution)/shard_map/pallas_call | solution.py:74
  591.0 7.4 fusion.2
  598.5 98.2 %reduce-scatter.5.cloned.1.call-done = f32[96,3072]{1,0:T(8,128)} async-done(((f32[768,3072]{1,0:T(8,128)}), f32[96,3072]{1,0:T(8,128)}) %reduce-scatter.5.cloned.1.call-update) | async-done | bytes 1179664 | tf_op jit(solution)/shard_map/reduce_scatter | solution.py:134
  699.7 89.2 %all-gather.5.cloned.1.call-done = f32[768,3072]{1,0:T(8,128)} async-done(((f32[96,3072]{1,0:T(8,128)}), f32[768,3072]{1,0:T(8,128)}) %all-gather.5.cloned.1.call-update) | async-done | bytes 9437200 | tf_op jit(solution)/shard_map/all_gather | solution.py:135
  789.0 11.2 %fusion.3 = f32[1,768,3072]{2,1,0:T(8,128)} fusion(f32[768,3072]{1,0:T(8,128)} %all-gather.5.cloned.1.call-done, bf16[768,3072]{1,0:T(8,128)(2,1)} %shard_map.75), kind=kLoop, calls=%fused_computation.8 | loop fusion | flops 4718592 | bytes 23592960 | tf_op jit(solution)/shard_map/broadcast_in_dim | solution.py:137
  (84 shorter events, 70.1 us)
Async XLA Ops:
  7.2 305.4 %reduce-scatter.3.cloned.1.call-start = ((), (), s32[]{:S(2)}) async-start(), calls=%async_computation.2 | async-start | bytes 10616832 | tf_op jit(solution)/shard_map/reduce_scatter | solution.py:134
  8.0 6.8 copy-start.5
  30.6 4.9 copy-start
  32.7 28.2 %collective-permute-start.2 = (bf16[128,3072]{1,0:T(8,128)(2,1)S(1)}, bf16[128,3072]{1,0:T(8,128)(2,1)}, u32[]{:S(2)}, u32[]{:S(2)}) collective-permute-start(bf16[128,3072]{1,0:T(8,128)(2,1)S(1)} %get-tuple-element.16), channel_id=1, source_target_pairs={{1,0},{2,3},{5,4},{6,7},{9,8},{10,11},{13,12},{14,15},{17,16},{18,... | collective-permute-start | bytes 2359304 | tf_op jit(solution)/shard_map/ppermute | solution.py:115
  34.2 24.6 %collective-permute-start = (bf16[128,3072]{1,0:T(8,128)(2,1)S(1)}, bf16[128,3072]{1,0:T(8,128)(2,1)}, u32[]{:S(2)}, u32[]{:S(2)}) collective-permute-start(bf16[128,3072]{1,0:T(8,128)(2,1)S(1)} %get-tuple-element.17), channel_id=1, source_target_pairs={{1,3},{2,0},{5,7},{6,4},{9,11},{10,8},{13,15},{14,12},{17,19},{18,... | collective-permute-start | bytes 2359304 | tf_op jit(solution)/shard_map/ppermute | solution.py:114
  36.8 62.0 %collective-permute-start.5 = (bf16[256,3072]{1,0:T(8,128)(2,1)}, bf16[256,3072]{1,0:T(8,128)(2,1)S(1)}, u32[]{:S(2)}, u32[]{:S(2)}) collective-permute-start(bf16[256,3072]{1,0:T(8,128)(2,1)} %get-tuple-element.14), channel_id=1, source_target_pairs={{1,0},{3,2},{5,4},{7,6},{9,8},{11,10},{13,12},{15,14},{17,16},{19,... | collective-permute-start | bytes 4718600 | tf_op jit(solution)/shard_map/ppermute | solution.py:111
  38.1 60.7 %collective-permute-start.4 = (bf16[256,3072]{1,0:T(8,128)(2,1)S(1)}, bf16[256,3072]{1,0:T(8,128)(2,1)}, u32[]{:S(2)}, u32[]{:S(2)}) collective-permute-start(bf16[256,3072]{1,0:T(8,128)(2,1)S(1)} %get-tuple-element.15), channel_id=1, source_target_pairs={{0,1},{2,3},{4,5},{6,7},{8,9},{10,11},{12,13},{14,15},{16,17},{18,... | collective-permute-start | bytes 4718600 | tf_op jit(solution)/shard_map/ppermute | solution.py:110
  58.7 37.6 %collective-permute-start.1 = (bf16[128,3072]{1,0:T(8,128)(2,1)}, bf16[128,3072]{1,0:T(8,128)(2,1)}, u32[]{:S(2)}, u32[]{:S(2)}) collective-permute-start(bf16[128,3072]{1,0:T(8,128)(2,1)} %collective-permute-done), channel_id=1, source_target_pairs={{3,2},{0,1},{7,6},{4,5},{11,10},{8,9},{15,14},{12,13},{19,18},{16,... | collective-permute-start | bytes 2359304 | tf_op jit(solution)/shard_map/ppermute | solution.py:116
  60.9 36.7 %collective-permute-start.3 = (bf16[128,3072]{1,0:T(8,128)(2,1)}, bf16[128,3072]{1,0:T(8,128)(2,1)}, u32[]{:S(2)}, u32[]{:S(2)}) collective-permute-start(bf16[128,3072]{1,0:T(8,128)(2,1)} %collective-permute-done.2), channel_id=1, source_target_pairs={{0,2},{3,1},{4,6},{7,5},{8,10},{11,9},{12,14},{15,13},{16,18},{19,... | collective-permute-start | bytes 2359304 | tf_op jit(solution)/shard_map/ppermute | solution.py:117
  131.4 4.9 copy-start.2
  133.6 23.1 %collective-permute-start.8 = (bf16[128,3072]{1,0:T(8,128)(2,1)S(1)}, bf16[128,3072]{1,0:T(8,128)(2,1)S(1)}, u32[]{:S(2)}, u32[]{:S(2)}) collective-permute-start(bf16[128,3072]{1,0:T(8,128)(2,1)S(1)} %get-tuple-element.12), channel_id=1, source_target_pairs={{1,0},{2,3},{5,4},{6,7},{9,8},{10,11},{13,12},{14,15},{17,16},{18,... | collective-permute-start | bytes 2359304 | tf_op jit(solution)/shard_map/ppermute | solution.py:115
  135.0 20.0 %collective-permute-start.6 = (bf16[128,3072]{1,0:T(8,128)(2,1)S(1)}, bf16[128,3072]{1,0:T(8,128)(2,1)S(1)}, u32[]{:S(2)}, u32[]{:S(2)}) collective-permute-start(bf16[128,3072]{1,0:T(8,128)(2,1)S(1)} %get-tuple-element.13), channel_id=1, source_target_pairs={{1,3},{2,0},{5,7},{6,4},{9,11},{10,8},{13,15},{14,12},{17,19},{18,... | collective-permute-start | bytes 2359304 | tf_op jit(solution)/shard_map/ppermute | solution.py:114
  136.5 55.3 %collective-permute-start.11 = (bf16[256,3072]{1,0:T(8,128)(2,1)S(1)}, bf16[256,3072]{1,0:T(8,128)(2,1)S(1)}, u32[]{:S(2)}, u32[]{:S(2)}) collective-permute-start(bf16[256,3072]{1,0:T(8,128)(2,1)S(1)} %get-tuple-element.10), channel_id=1, source_target_pairs={{1,0},{3,2},{5,4},{7,6},{9,8},{11,10},{13,12},{15,14},{17,16},{19,... | collective-permute-start | bytes 4718600 | tf_op jit(solution)/shard_map/ppermute | solution.py:111
  137.8 54.0 %collective-permute-start.10 = (bf16[256,3072]{1,0:T(8,128)(2,1)S(1)}, bf16[256,3072]{1,0:T(8,128)(2,1)S(1)}, u32[]{:S(2)}, u32[]{:S(2)}) collective-permute-start(bf16[256,3072]{1,0:T(8,128)(2,1)S(1)} %get-tuple-element.11), channel_id=1, source_target_pairs={{0,1},{2,3},{4,5},{6,7},{8,9},{10,11},{12,13},{14,15},{16,17},{18,... | collective-permute-start | bytes 4718600 | tf_op jit(solution)/shard_map/ppermute | solution.py:110
  155.0 36.7 %collective-permute-start.7 = (bf16[128,3072]{1,0:T(8,128)(2,1)S(1)}, bf16[128,3072]{1,0:T(8,128)(2,1)S(1)}, u32[]{:S(2)}, u32[]{:S(2)}) collective-permute-start(bf16[128,3072]{1,0:T(8,128)(2,1)S(1)} %collective-permute-done.6), channel_id=1, source_target_pairs={{3,2},{0,1},{7,6},{4,5},{11,10},{8,9},{15,14},{12,13},{19,18},{16,... | collective-permute-start | bytes 2359304 | tf_op jit(solution)/shard_map/ppermute | solution.py:116
  156.6 35.1 %collective-permute-start.9 = (bf16[128,3072]{1,0:T(8,128)(2,1)S(1)}, bf16[128,3072]{1,0:T(8,128)(2,1)S(1)}, u32[]{:S(2)}, u32[]{:S(2)}) collective-permute-start(bf16[128,3072]{1,0:T(8,128)(2,1)S(1)} %collective-permute-done.8), channel_id=1, source_target_pairs={{0,2},{3,1},{4,6},{7,5},{8,10},{11,9},{12,14},{15,13},{16,18},{19,... | collective-permute-start | bytes 2359304 | tf_op jit(solution)/shard_map/ppermute | solution.py:117
  211.5 193.3 %all-gather.3.cloned.1.call-start = ((), (), s32[]{:S(2)}) async-start(), calls=%async_computation.3 | async-start | bytes 10616832 | tf_op jit(solution)/shard_map/all_gather | solution.py:135
  315.7 381.0 %reduce-scatter.5.cloned.1.call-start = ((), (), s32[]{:S(2)}) async-start(), calls=%async_computation.4 | async-start | bytes 10616832 | tf_op jit(solution)/shard_map/reduce_scatter | solution.py:134
  426.0 25.5 %collective-permute-start.14 = (bf16[128,3072]{1,0:T(8,128)(2,1)S(1)}, bf16[128,3072]{1,0:T(8,128)(2,1)S(1)}, u32[]{:S(2)}, u32[]{:S(2)}) collective-permute-start(bf16[128,3072]{1,0:T(8,128)(2,1)S(1)} %get-tuple-element.8), channel_id=1, source_target_pairs={{1,0},{2,3},{5,4},{6,7},{9,8},{10,11},{13,12},{14,15},{17,16},{18,... | collective-permute-start | bytes 2359304 | tf_op jit(solution)/shard_map/ppermute | solution.py:115
  427.5 22.6 %collective-permute-start.12 = (bf16[128,3072]{1,0:T(8,128)(2,1)S(1)}, bf16[128,3072]{1,0:T(8,128)(2,1)S(1)}, u32[]{:S(2)}, u32[]{:S(2)}) collective-permute-start(bf16[128,3072]{1,0:T(8,128)(2,1)S(1)} %get-tuple-element.9), channel_id=1, source_target_pairs={{1,3},{2,0},{5,7},{6,4},{9,11},{10,8},{13,15},{14,12},{17,19},{18,... | collective-permute-start | bytes 2359304 | tf_op jit(solution)/shard_map/ppermute | solution.py:114
  429.0 57.7 %collective-permute-start.17 = (bf16[256,3072]{1,0:T(8,128)(2,1)S(1)}, bf16[256,3072]{1,0:T(8,128)(2,1)S(1)}, u32[]{:S(2)}, u32[]{:S(2)}) collective-permute-start(bf16[256,3072]{1,0:T(8,128)(2,1)S(1)} %get-tuple-element.6), channel_id=1, source_target_pairs={{1,0},{3,2},{5,4},{7,6},{9,8},{11,10},{13,12},{15,14},{17,16},{19,... | collective-permute-start | bytes 4718600 | tf_op jit(solution)/shard_map/ppermute | solution.py:111
  430.3 56.4 %collective-permute-start.16 = (bf16[256,3072]{1,0:T(8,128)(2,1)S(1)}, bf16[256,3072]{1,0:T(8,128)(2,1)S(1)}, u32[]{:S(2)}, u32[]{:S(2)}) collective-permute-start(bf16[256,3072]{1,0:T(8,128)(2,1)S(1)} %get-tuple-element.7), channel_id=1, source_target_pairs={{0,1},{2,3},{4,5},{6,7},{8,9},{10,11},{12,13},{14,15},{16,17},{18,... | collective-permute-start | bytes 4718600 | tf_op jit(solution)/shard_map/ppermute | solution.py:110
  450.1 36.5 %collective-permute-start.13 = (bf16[128,3072]{1,0:T(8,128)(2,1)S(1)}, bf16[128,3072]{1,0:T(8,128)(2,1)S(1)}, u32[]{:S(2)}, u32[]{:S(2)}) collective-permute-start(bf16[128,3072]{1,0:T(8,128)(2,1)S(1)} %collective-permute-done.12), channel_id=1, source_target_pairs={{3,2},{0,1},{7,6},{4,5},{11,10},{8,9},{15,14},{12,13},{19,18},{16,... | collective-permute-start | bytes 2359304 | tf_op jit(solution)/shard_map/ppermute | solution.py:116
  451.5 35.1 %collective-permute-start.15 = (bf16[128,3072]{1,0:T(8,128)(2,1)S(1)}, bf16[128,3072]{1,0:T(8,128)(2,1)S(1)}, u32[]{:S(2)}, u32[]{:S(2)}) collective-permute-start(bf16[128,3072]{1,0:T(8,128)(2,1)S(1)} %collective-permute-done.14), channel_id=1, source_target_pairs={{0,2},{3,1},{4,6},{7,5},{8,10},{11,9},{12,14},{15,13},{16,18},{19,... | collective-permute-start | bytes 2359304 | tf_op jit(solution)/shard_map/ppermute | solution.py:117
  520.0 23.5 %collective-permute-start.20 = (bf16[128,3072]{1,0:T(8,128)(2,1)S(1)}, bf16[128,3072]{1,0:T(8,128)(2,1)S(1)}, u32[]{:S(2)}, u32[]{:S(2)}) collective-permute-start(bf16[128,3072]{1,0:T(8,128)(2,1)S(1)} %get-tuple-element.4), channel_id=1, source_target_pairs={{1,0},{2,3},{5,4},{6,7},{9,8},{10,11},{13,12},{14,15},{17,16},{18,... | collective-permute-start | bytes 2359304 | tf_op jit(solution)/shard_map/ppermute | solution.py:115
  521.5 20.5 %collective-permute-start.18 = (bf16[128,3072]{1,0:T(8,128)(2,1)S(1)}, bf16[128,3072]{1,0:T(8,128)(2,1)S(1)}, u32[]{:S(2)}, u32[]{:S(2)}) collective-permute-start(bf16[128,3072]{1,0:T(8,128)(2,1)S(1)} %get-tuple-element.5), channel_id=1, source_target_pairs={{1,3},{2,0},{5,7},{6,4},{9,11},{10,8},{13,15},{14,12},{17,19},{18,... | collective-permute-start | bytes 2359304 | tf_op jit(solution)/shard_map/ppermute | solution.py:114
  523.0 55.8 %collective-permute-start.23 = (bf16[256,3072]{1,0:T(8,128)(2,1)S(1)}, bf16[256,3072]{1,0:T(8,128)(2,1)S(1)}, u32[]{:S(2)}, u32[]{:S(2)}) collective-permute-start(bf16[256,3072]{1,0:T(8,128)(2,1)S(1)} %get-tuple-element.2), channel_id=1, source_target_pairs={{1,0},{3,2},{5,4},{7,6},{9,8},{11,10},{13,12},{15,14},{17,16},{19,... | collective-permute-start | bytes 4718600 | tf_op jit(solution)/shard_map/ppermute | solution.py:111
  524.3 54.5 %collective-permute-start.22 = (bf16[256,3072]{1,0:T(8,128)(2,1)S(1)}, bf16[256,3072]{1,0:T(8,128)(2,1)S(1)}, u32[]{:S(2)}, u32[]{:S(2)}) collective-permute-start(bf16[256,3072]{1,0:T(8,128)(2,1)S(1)} %get-tuple-element.3), channel_id=1, source_target_pairs={{0,1},{2,3},{4,5},{6,7},{8,9},{10,11},{12,13},{14,15},{16,17},{18,... | collective-permute-start | bytes 4718600 | tf_op jit(solution)/shard_map/ppermute | solution.py:110
  541.9 36.7 %collective-permute-start.19 = (bf16[128,3072]{1,0:T(8,128)(2,1)S(1)}, bf16[128,3072]{1,0:T(8,128)(2,1)S(1)}, u32[]{:S(2)}, u32[]{:S(2)}) collective-permute-start(bf16[128,3072]{1,0:T(8,128)(2,1)S(1)} %collective-permute-done.18), channel_id=1, source_target_pairs={{3,2},{0,1},{7,6},{4,5},{11,10},{8,9},{15,14},{12,13},{19,18},{16,... | collective-permute-start | bytes 2359304 | tf_op jit(solution)/shard_map/ppermute | solution.py:116
  543.6 35.1 %collective-permute-start.21 = (bf16[128,3072]{1,0:T(8,128)(2,1)S(1)}, bf16[128,3072]{1,0:T(8,128)(2,1)S(1)}, u32[]{:S(2)}, u32[]{:S(2)}) collective-permute-start(bf16[128,3072]{1,0:T(8,128)(2,1)S(1)} %collective-permute-done.20), channel_id=1, source_target_pairs={{0,2},{3,1},{4,6},{7,5},{8,10},{11,9},{12,14},{15,13},{16,18},{19,... | collective-permute-start | bytes 2359304 | tf_op jit(solution)/shard_map/ppermute | solution.py:117
  598.4 190.5 %all-gather.5.cloned.1.call-start = ((), (), s32[]{:S(2)}) async-start(), calls=%async_computation.5 | async-start | bytes 10616832 | tf_op jit(solution)/shard_map/all_gather | solution.py:135
  789.0 11.2 %copy-start.4 = (f32[768,3072]{1,0:T(8,128)S(1)}, f32[768,3072]{1,0:T(8,128)}, u32[]{:S(2)}) copy-start(f32[768,3072]{1,0:T(8,128)} %all-gather.5.cloned.1.call-done) | copy-start | bytes 28311556
  (2 other events, 9.8 us)
Sparse Core Ops, SparseCore 0:
  211.6 100.9 reduce-scatter.2
  315.8 88.9 all-gather.2
  598.5 98.0 reduce-scatter.4
  699.8 89.0 all-gather.4

commit v5 on v4

v5 whole, which is shorter than its diff:
```python
import functools

import jax
import jax.numpy as jnp
from jax import lax
from jax.experimental import pallas as pl
import numpy as np
from jax.sharding import PartitionSpec as P

ITERS = 2
HALO = 2
OFFSETS = 2 * HALO + 1


def window_starts(nblocks, group):
    span = group + 2 * HALO
    return [min(max(g * group - HALO, 0), nblocks - span) for g in range(nblocks // group)]


def column_terms(banded_submatrices, band_starts, group):
    nblocks, _, width, _ = banded_submatrices.shape
    span = group + 2 * HALO
    ngroups = nblocks // group
    rows = np.arange(nblocks).reshape(ngroups, group)
    cols = np.array(window_starts(nblocks, group))[:, None] + np.arange(span)[None, :]
    target = rows[:, :, None] + band_starts[rows]
    matches = cols[:, None, :, None] == target[:, :, None, :]
    blocks = banded_submatrices[rows]
    terms = jnp.einsum(
        "gbcj,gbjik->gckbi", matches.astype(jnp.bfloat16), blocks, preferred_element_type=jnp.float32
    ).astype(jnp.bfloat16)
    return terms.reshape((ngroups, span * width, group * width))


def row_terms(banded_submatrices, band_starts, first, local_blocks, group):
    nblocks, _, width, _ = banded_submatrices.shape
    span = group + 2 * HALO
    ngroups = local_blocks // group
    local_rows = np.arange(local_blocks).reshape(ngroups, group)
    block_rows = lax.dynamic_slice_in_dim(banded_submatrices, first, local_blocks, axis=0)[local_rows]
    starts = lax.dynamic_slice_in_dim(band_starts, first, local_blocks, axis=0)[local_rows]
    cols = first + (local_rows[:, :1] - HALO + np.arange(span)[None, :])
    in_range = (cols >= 0) & (cols < nblocks)
    target = first + local_rows[:, :, None] + starts
    matches = (cols[:, None, :, None] == target[:, :, None, :]) & in_range[:, None, :, None]
    terms = jnp.einsum(
        "gbej,gbjik->gbiek", matches.astype(jnp.bfloat16), block_rows, preferred_element_type=jnp.float32
    ).astype(jnp.bfloat16)
    return terms.reshape((ngroups, group * width, span * width))


def column_kernel(x_ref, t_ref, o_ref, *, group, width):
    nblocks = x_ref.shape[1] // width
    span = group + 2 * HALO
    x = x_ref[...].astype(jnp.bfloat16)
    for g, first in enumerate(window_starts(nblocks, group)):
        window = x[:, first * width : (first + span) * width]
        out = jnp.dot(window, t_ref[g], preferred_element_type=jnp.float32)
        o_ref[:, g * group * width : (g + 1) * group * width] = out.astype(o_ref.dtype)


def column_pass(field, terms, group, width, tile_rows=256):
    rows, cols = field.shape
    return pl.pallas_call(
        functools.partial(column_kernel, group=group, width=width),
        grid=(rows // tile_rows,),
        in_specs=[
            pl.BlockSpec((tile_rows, cols), lambda r: (r, 0)),
            pl.BlockSpec(terms.shape, lambda r: (0, 0, 0)),
        ],
        out_specs=pl.BlockSpec((tile_rows, cols), lambda r: (r, 0)),
        out_shape=jax.ShapeDtypeStruct((rows, cols), jnp.bfloat16),
    )(field, terms)


def row_kernel(prev_ref, mid_ref, next_ref, t_ref, o_ref, *, group, width):
    local_blocks = mid_ref.shape[0] // width
    span = group + 2 * HALO
    sources = [(prev_ref, 0, HALO), (mid_ref, HALO, HALO + local_blocks), (next_ref, HALO + local_blocks, 2 * HALO + local_blocks)]
    for g in range(local_blocks // group):
        lo = g * group
        acc = None
        for ref, start, stop in sources:
            a, b = max(lo, start), min(lo + span, stop)
            if a >= b:
                continue
            src = ref[(a - start) * width : (b - start) * width, :]
            prod = jnp.dot(t_ref[g, :, (a - lo) * width : (b - lo) * width], src, preferred_element_type=jnp.float32)
            acc = prod if acc is None else acc + prod
        o_ref[lo * width : (lo + group) * width, :] = acc.astype(o_ref.dtype)


def row_pass(prev, mid, nxt, terms_local, group, width, tile_cols=768):
    rows, cols = mid.shape
    halo_rows = prev.shape[0]
    return pl.pallas_call(
        functools.partial(row_kernel, group=group, width=width),
        grid=(cols // tile_cols,),
        in_specs=[
            pl.BlockSpec((halo_rows, tile_cols), lambda c: (0, c)),
            pl.BlockSpec((rows, tile_cols), lambda c: (0, c)),
            pl.BlockSpec((halo_rows, tile_cols), lambda c: (0, c)),
            pl.BlockSpec(terms_local.shape, lambda c: (0, 0, 0)),
        ],
        out_specs=pl.BlockSpec((rows, tile_cols), lambda c: (0, c)),
        out_shape=jax.ShapeDtypeStruct((rows, cols), jnp.bfloat16),
    )(prev, mid, nxt, terms_local)


def per_device(image_masses, dual_multipliers, fraction_tops, banded_submatrices, band_starts, nslab):
    width = banded_submatrices.shape[2]
    rows = image_masses.shape[1]
    local_blocks = rows // width
    halo = HALO * width
    slab = lax.axis_index("slab")

    nblocks = banded_submatrices.shape[0]
    col_group = 2 if nblocks % 2 == 0 and nblocks >= 2 + 2 * HALO else 1
    row_group = 2 if local_blocks % 2 == 0 else 1
    terms = column_terms(banded_submatrices, band_starts, col_group)
    terms_local = row_terms(banded_submatrices, band_starts, slab * local_blocks, local_blocks, row_group)

    total_weight = lax.psum(jnp.sum(fraction_tops).astype(jnp.float32), "img")
    weight = fraction_tops.astype(jnp.float32)[0]

    up = [(i, i + 1) for i in range(nslab - 1)]
    down = [(i + 1, i) for i in range(nslab - 1)]

    def exchange(inner):
        to_up = inner[rows - halo :]
        to_down = inner[:halo]
        if nslab != 4:
            return lax.ppermute(to_up, "slab", up), lax.ppermute(to_down, "slab", down)
        half = halo // 2
        direct_prev = lax.ppermute(to_up, "slab", [(0, 1), (2, 3)])
        direct_next = lax.ppermute(to_down, "slab", [(1, 0), (3, 2)])
        first = jnp.where(slab == 1, to_up[:half], to_down[:half])
        second = jnp.where(slab == 1, to_up[half:], to_down[half:])
        first = lax.ppermute(first, "slab", [(1, 3), (2, 0)])
        second = lax.ppermute(second, "slab", [(1, 0), (2, 3)])
        first = lax.ppermute(first, "slab", [(3, 2), (0, 1)])
        second = lax.ppermute(second, "slab", [(0, 2), (3, 1)])
        diagonal = jnp.concatenate([first, second], axis=0)
        return jnp.where(slab == 2, diagonal, direct_prev), jnp.where(slab == 1, diagonal, direct_next)

    def apply_kernel(field):
        inner = column_pass(field, terms, col_group, width)
        from_prev, from_next = exchange(inner)
        return row_pass(from_prev, inner, from_next, terms_local, row_group, width)

    masses = image_masses[0]
    scaling = dual_multipliers[0]
    barycenter = None
    for iteration in range(ITERS):
        kernel_v = apply_kernel(scaling.astype(jnp.bfloat16))
        scaled_u = (masses / kernel_v.astype(jnp.float32)).astype(jnp.bfloat16)
        kernel_u = apply_kernel(scaled_u).astype(jnp.float32)
        value_portion = weight * jnp.log(kernel_u)
        log_sum = lax.psum_scatter(value_portion, "img", scatter_dimension=0, tiled=True)
        barycenter = lax.all_gather(jnp.exp(log_sum / total_weight), "img", axis=0, tiled=True)
        scaling = barycenter / kernel_u
    return (barycenter, scaling[None])


def solution(mesh):
    nslab = mesh.shape["slab"]
    placed = (P("img", "slab", None), P("img", "slab", None), P("img"), P(), P())

    def body(*args):
        return per_device(*args, nslab=nslab)

    return jax.shard_map(
        body,
        mesh=mesh,
        in_specs=placed,
        out_specs=(P("slab", None), P("img", "slab", None)),
        check_vma=False,
    )
```

time: 812 us -> 828 us (1.020)
  local copies, waits for them, and re-layouts: 11.4 us -> 37.6 us
  Pallas kernels: 81.2 us -> 69.6 us
    reshape x0 -> x3, local copies, waits for them, and re-layouts: none -> 19.7 us  [the longest x2 17.5 us: column_terms(): return terms.reshape((ngroups, span * width, group * width))]
    pallas_call x8, Pallas kernels: 81.2 us -> 69.6 us  [the longest x4 34.9 us: column_pass(): pl.pallas_call(functools.partial(column_kernel, group=group, width=width)...]
where the time goes in v5:
time: 828 us; the launch traced here: 826 us
  waiting for transfers between devices  541 us (65%)
  other arithmetic  85.2 us (10%)
  Pallas kernels  69.6 us (8%)
  starting transfers between devices  53.7 us (6%)
  local copies, waits for them, and re-layouts  37.6 us (5%)
  blocking collectives  15.5 us (2%)
  between operations  14.9 us (2%)
    reduce_scatter x2, waiting for transfers between devices, per_device(): lax.psum_scatter(value_portion, 'img', scatter_dimension=0, tiled=True)  184 us
    all_gather x2, waiting for transfers between devices, per_device(): lax.all_gather(jnp.exp(log_sum / total_weight), 'img', axis=0, tiled=True)  178 us
    ppermute x4, waiting for transfers between devices, exchange(): first = lax.ppermute(first, 'slab', [(3, 2), (0, 1)])  130 us
    ppermute x4, waiting for transfers between devices, exchange(): first = lax.ppermute(first, 'slab', [(1, 3), (2, 0)])  49.3 us
    pallas_call x4, Pallas kernels, column_pass(): pl.pallas_call(functools.partial(column_kernel, group=group, width=width)...  34.9 us
    pallas_call x4, Pallas kernels, row_pass(): pl.pallas_call(functools.partial(row_kernel, group=group, width=width), g...  34.6 us
    ppermute x4, starting transfers between devices, exchange(): direct_prev = lax.ppermute(to_up, 'slab', [(0, 1), (2, 3)])  25.6 us
    convert_element_type x2, other arithmetic, per_device(): scaled_u = (masses / kernel_v.astype(jnp.float32)).astype(jnp.bfloat16)  18 us
  transfers between devices with their start and end apart: 28, of which 12 were waited for; matrix products, arithmetic and copies ran while one was open for 1% of the time, Pallas kernels for 0%

profile of v5, /device:TPU:0, one launch (start us, length us, event | category | flops | bytes accessed | tf_op | source)
XLA Modules:
  0.0 825.8 jit_solution(12042154313842218260)
XLA Ops:
  17.6 10.8 %reshape.61 = bf16[12,768,256]{1,2,0:T(8,128)(2,1)} reshape(bf16[12,6,128,2,128]{2,1,4,3,0:T(8,128)(2,1)} %convert_bitcast_fusion) | data formatting | bytes 9437184 | tf_op jit(solution)/shard_map/reshape | solution.py:32
  28.4 6.6 copy.36.t_ref
  35.0 6.6 convert_bitcast_fusion.1.x_ref
  41.6 8.7 %shard_map.158.mid_ref = bf16[768,3072]{1,0:T(8,128)(2,1)} custom-call(bf16[768,3072]{1,0:T(8,128)(2,1)} %convert_bitcast_fusion.1.x_ref, bf16[12,768,256]{2,1,0:T(8,128)(2,1)} %copy.36.t_ref), custom_call_target="tpu_custom_call" | custom-call | tf_op jit(solution)/shard_map/pallas_call | solution.py:64
  59.5 10.2 %collective-permute-start.4 = (bf16[256,3072]{1,0:T(8,128)(2,1)}, bf16[256,3072]{1,0:T(8,128)(2,1)}, u32[]{:S(2)}, u32[]{:S(2)}) collective-permute-start(bf16[256,3072]{1,0:T(8,128)(2,1)} %get-tuple-element.15), channel_id=1, source_target_pairs={{0,1},{2,3},{4,5},{6,7},{8,9},{10,11},{12,13},{14,15},{16,17},{18,... | collective-permute-start | bytes 4718600 | tf_op jit(solution)/shard_map/ppermute | solution.py:135
  69.7 10.2 %collective-permute-done = bf16[128,3072]{1,0:T(8,128)(2,1)} collective-permute-done((bf16[128,3072]{1,0:T(8,128)(2,1)}, bf16[128,3072]{1,0:T(8,128)(2,1)}, u32[]{:S(2)}, u32[]{:S(2)}) %collective-permute-start) | collective-permute-done | bytes 786464 | tf_op jit(solution)/shard_map/ppermute | solution.py:139
  89.2 29.9 %collective-permute-done.1 = bf16[128,3072]{1,0:T(8,128)(2,1)S(1)} collective-permute-done((bf16[128,3072]{1,0:T(8,128)(2,1)}, bf16[128,3072]{1,0:T(8,128)(2,1)S(1)}, u32[]{:S(2)}, u32[]{:S(2)}) %collective-permute-start.1) | collective-permute-done | bytes 786464 | tf_op jit(solution)/shard_map/ppermute | solution.py:141
  123.0 8.6 %shard_map.159 = bf16[768,3072]{1,0:T(8,128)(2,1)} custom-call(bf16[256,3072]{1,0:T(8,128)(2,1)} %get-tuple-element.25.prev_ref, bf16[768,3072]{1,0:T(8,128)(2,1)} %shard_map.158.mid_ref, bf16[256,3072]{1,0:T(8,128)(2,1)} %get-tuple-element.24.next_ref, bf16[3,256,768]{2,1,0:T(8,128)(2,1)} %reshape.62.t_ref), custom_call_target="tpu_custom_call" | custom-call | tf_op jit(solution)/shard_map/pallas_call | solution.py:96
  131.6 9.0 %fusion.4.x_ref = bf16[768,3072]{1,0:T(8,128)(2,1)} fusion(f32[1,768,3072]{2,1,0:T(8,128)} %param.15, bf16[768,3072]{1,0:T(8,128)(2,1)} %shard_map.159), kind=kLoop, calls=%fused_computation.14 | loop fusion | flops 7077888 | bytes 18874368 | tf_op jit(solution)/shard_map/convert_element_type | solution.py:156
  140.6 8.7 %shard_map.160.mid_ref = bf16[768,3072]{1,0:T(8,128)(2,1)} custom-call(bf16[768,3072]{1,0:T(8,128)(2,1)} %fusion.4.x_ref, bf16[12,768,256]{2,1,0:T(8,128)(2,1)} %copy.36.t_ref), custom_call_target="tpu_custom_call" | custom-call | tf_op jit(solution)/shard_map/pallas_call | solution.py:64
  160.6 12.3 %collective-permute-done.6 = bf16[128,3072]{1,0:T(8,128)(2,1)S(1)} collective-permute-done((bf16[128,3072]{1,0:T(8,128)(2,1)S(1)}, bf16[128,3072]{1,0:T(8,128)(2,1)S(1)}, u32[]{:S(2)}, u32[]{:S(2)}) %collective-permute-start.6) | collective-permute-done | bytes 786464 | tf_op jit(solution)/shard_map/ppermute | solution.py:139
  176.5 33.1 %collective-permute-done.7 = bf16[128,3072]{1,0:T(8,128)(2,1)S(1)} collective-permute-done((bf16[128,3072]{1,0:T(8,128)(2,1)S(1)}, bf16[128,3072]{1,0:T(8,128)(2,1)S(1)}, u32[]{:S(2)}, u32[]{:S(2)}) %collective-permute-start.7) | collective-permute-done | bytes 786464 | tf_op jit(solution)/shard_map/ppermute | solution.py:141
  211.6 8.7 %shard_map.161 = bf16[768,3072]{1,0:T(8,128)(2,1)} custom-call(bf16[256,3072]{1,0:T(8,128)(2,1)} %get-tuple-element.23.prev_ref, bf16[768,3072]{1,0:T(8,128)(2,1)} %shard_map.160.mid_ref, bf16[256,3072]{1,0:T(8,128)(2,1)} %get-tuple-element.22.next_ref, bf16[3,256,768]{2,1,0:T(8,128)(2,1)} %reshape.62.t_ref), custom_call_target="tpu_custom_call" | custom-call | tf_op jit(solution)/shard_map/pallas_call | solution.py:96
  220.4 7.4 fusion
  227.8 15.5 %psum.7 = f32[]{:T(128)} all-reduce(f32[]{:T(128)} %bitcast), channel_id=1, replica_groups=mesh['img'=8,'slab'=4] {'img'}, use_global_device_ids=true, to_apply=%region_1.0 | all-reduce | flops 1 | bytes 8 | tf_op jit(solution)/shard_map/psum | solution.py:123
  243.4 85.6 %reduce-scatter.3.cloned.1.call-done = f32[96,3072]{1,0:T(8,128)} async-done(((f32[768,3072]{1,0:T(8,128)}), f32[96,3072]{1,0:T(8,128)}) %reduce-scatter.3.cloned.1.call-update) | async-done | bytes 1179664 | tf_op jit(solution)/shard_map/reduce_scatter | solution.py:159
  332.3 88.9 %all-gather.3.cloned.1.call-done = f32[768,3072]{1,0:T(8,128)} async-done(((f32[96,3072]{1,0:T(8,128)}), f32[768,3072]{1,0:T(8,128)}) %all-gather.3.cloned.1.call-update) | async-done | bytes 9437200 | tf_op jit(solution)/shard_map/all_gather | solution.py:160
  421.2 9.0 %fusion.1.x_ref = bf16[768,3072]{1,0:T(8,128)(2,1)} fusion(f32[768,3072]{1,0:T(8,128)} %all-gather.3.cloned.1.call-done, bf16[768,3072]{1,0:T(8,128)(2,1)} %shard_map.161), kind=kLoop, calls=%fused_computation.9 | loop fusion | flops 7077888 | bytes 18874368 | tf_op jit(solution)/shard_map/convert_element_type | solution.py:155
  430.2 8.7 %shard_map.162.mid_ref = bf16[768,3072]{1,0:T(8,128)(2,1)} custom-call(bf16[768,3072]{1,0:T(8,128)(2,1)} %fusion.1.x_ref, bf16[12,768,256]{2,1,0:T(8,128)(2,1)} %copy.36.t_ref), custom_call_target="tpu_custom_call" | custom-call | tf_op jit(solution)/shard_map/pallas_call | solution.py:64
  451.1 14.0 %collective-permute-done.12 = bf16[128,3072]{1,0:T(8,128)(2,1)S(1)} collective-permute-done((bf16[128,3072]{1,0:T(8,128)(2,1)S(1)}, bf16[128,3072]{1,0:T(8,128)(2,1)S(1)}, u32[]{:S(2)}, u32[]{:S(2)}) %collective-permute-start.12) | collective-permute-done | bytes 786464 | tf_op jit(solution)/shard_map/ppermute | solution.py:139
  467.9 33.7 %collective-permute-done.13 = bf16[128,3072]{1,0:T(8,128)(2,1)S(1)} collective-permute-done((bf16[128,3072]{1,0:T(8,128)(2,1)S(1)}, bf16[128,3072]{1,0:T(8,128)(2,1)S(1)}, u32[]{:S(2)}, u32[]{:S(2)}) %collective-permute-start.13) | collective-permute-done | bytes 786464 | tf_op jit(solution)/shard_map/ppermute | solution.py:141
  503.6 8.6 %shard_map.163 = bf16[768,3072]{1,0:T(8,128)(2,1)} custom-call(bf16[256,3072]{1,0:T(8,128)(2,1)} %get-tuple-element.21.prev_ref, bf16[768,3072]{1,0:T(8,128)(2,1)} %shard_map.162.mid_ref, bf16[256,3072]{1,0:T(8,128)(2,1)} %get-tuple-element.20.next_ref, bf16[3,256,768]{2,1,0:T(8,128)(2,1)} %reshape.62.t_ref), custom_call_target="tpu_custom_call" | custom-call | tf_op jit(solution)/shard_map/pallas_call | solution.py:96
  512.2 9.0 %fusion.5.x_ref = bf16[768,3072]{1,0:T(8,128)(2,1)} fusion(f32[1,768,3072]{2,1,0:T(8,128)} %param.15, bf16[768,3072]{1,0:T(8,128)(2,1)} %shard_map.163), kind=kLoop, calls=%fused_computation.15 | loop fusion | flops 7077888 | bytes 18874368 | tf_op jit(solution)/shard_map/convert_element_type | solution.py:156
  521.2 8.7 %shard_map.164.mid_ref = bf16[768,3072]{1,0:T(8,128)(2,1)} custom-call(bf16[768,3072]{1,0:T(8,128)(2,1)} %fusion.5.x_ref, bf16[12,768,256]{2,1,0:T(8,128)(2,1)} %copy.36.t_ref), custom_call_target="tpu_custom_call" | custom-call | tf_op jit(solution)/shard_map/pallas_call | solution.py:64
  541.2 12.8 %collective-permute-done.18 = bf16[128,3072]{1,0:T(8,128)(2,1)S(1)} collective-permute-done((bf16[128,3072]{1,0:T(8,128)(2,1)S(1)}, bf16[128,3072]{1,0:T(8,128)(2,1)S(1)}, u32[]{:S(2)}, u32[]{:S(2)}) %collective-permute-start.18) | collective-permute-done | bytes 786464 | tf_op jit(solution)/shard_map/ppermute | solution.py:139
  557.3 33.4 %collective-permute-done.19 = bf16[128,3072]{1,0:T(8,128)(2,1)S(1)} collective-permute-done((bf16[128,3072]{1,0:T(8,128)(2,1)S(1)}, bf16[128,3072]{1,0:T(8,128)(2,1)S(1)}, u32[]{:S(2)}, u32[]{:S(2)}) %collective-permute-start.19) | collective-permute-done | bytes 786464 | tf_op jit(solution)/shard_map/ppermute | solution.py:141
  592.8 8.7 %shard_map.165 = bf16[768,3072]{1,0:T(8,128)(2,1)} custom-call(bf16[256,3072]{1,0:T(8,128)(2,1)} %get-tuple-element.19.prev_ref, bf16[768,3072]{1,0:T(8,128)(2,1)} %shard_map.164.mid_ref, bf16[256,3072]{1,0:T(8,128)(2,1)} %get-tuple-element.18.next_ref, bf16[3,256,768]{2,1,0:T(8,128)(2,1)} %reshape.62.t_ref), custom_call_target="tpu_custom_call" | custom-call | tf_op jit(solution)/shard_map/pallas_call | solution.py:96
  601.5 7.4 fusion.2
  609.0 98.1 %reduce-scatter.5.cloned.1.call-done = f32[96,3072]{1,0:T(8,128)} async-done(((f32[768,3072]{1,0:T(8,128)}), f32[96,3072]{1,0:T(8,128)}) %reduce-scatter.5.cloned.1.call-update) | async-done | bytes 1179664 | tf_op jit(solution)/shard_map/reduce_scatter | solution.py:159
  710.2 89.2 %all-gather.5.cloned.1.call-done = f32[768,3072]{1,0:T(8,128)} async-done(((f32[96,3072]{1,0:T(8,128)}), f32[768,3072]{1,0:T(8,128)}) %all-gather.5.cloned.1.call-update) | async-done | bytes 9437200 | tf_op jit(solution)/shard_map/all_gather | solution.py:160
  799.5 11.1 %fusion.3 = f32[1,768,3072]{2,1,0:T(8,128)} fusion(f32[768,3072]{1,0:T(8,128)} %all-gather.5.cloned.1.call-done, bf16[768,3072]{1,0:T(8,128)(2,1)} %shard_map.165), kind=kLoop, calls=%fused_computation.11 | loop fusion | flops 4718592 | bytes 23592960 | tf_op jit(solution)/shard_map/broadcast_in_dim | solution.py:162
  810.5 8.8 %copy.48 = f32[768,3072]{1,0:T(8,128)} copy(f32[768,3072]{1,0:T(8,128)} %all-gather.5.cloned.1.call-done) | data formatting | bytes 18874368
  (109 shorter events, 88.7 us)
Async XLA Ops:
  7.2 321.8 %reduce-scatter.3.cloned.1.call-start = ((), (), s32[]{:S(2)}) async-start(), calls=%async_computation.2 | async-start | bytes 10616832 | tf_op jit(solution)/shard_map/reduce_scatter | solution.py:159
  50.4 6.0 copy-start.2
  53.7 29.9 %collective-permute-start.2 = (bf16[128,3072]{1,0:T(8,128)(2,1)}, bf16[128,3072]{1,0:T(8,128)(2,1)}, u32[]{:S(2)}, u32[]{:S(2)}) collective-permute-start(bf16[128,3072]{1,0:T(8,128)(2,1)} %get-tuple-element.16), channel_id=1, source_target_pairs={{1,0},{2,3},{5,4},{6,7},{9,8},{10,11},{13,12},{14,15},{17,16},{18,... | collective-permute-start | bytes 2359304 | tf_op jit(solution)/shard_map/ppermute | solution.py:140
  55.0 14.7 %copy-start.8 = (s32[3,2,1]{0,1,2:T(2,128)S(1)}, s32[3,2,1]{0,1,2:T(2,128)}, u32[]{:S(2)}) copy-start(s32[3,2,1]{0,1,2:T(2,128)} %constant.40.clone) | copy-start | bytes 76
  55.0 14.7 %copy-start.6 = (s32[3,6]{1,0:T(4,128)S(1)}, s32[3,6]{1,0:T(4,128)}, u32[]{:S(2)}) copy-start(s32[3,6]{1,0:T(4,128)} %constant.39.clone) | copy-start | bytes 220
  55.0 24.9 %collective-permute-start = (bf16[128,3072]{1,0:T(8,128)(2,1)}, bf16[128,3072]{1,0:T(8,128)(2,1)}, u32[]{:S(2)}, u32[]{:S(2)}) collective-permute-start(bf16[128,3072]{1,0:T(8,128)(2,1)} %get-tuple-element.17), channel_id=1, source_target_pairs={{1,3},{2,0},{5,7},{6,4},{9,11},{10,8},{13,15},{14,12},{17,19},{18,... | collective-permute-start | bytes 2359304 | tf_op jit(solution)/shard_map/ppermute | solution.py:139
  58.2 61.0 %collective-permute-start.5 = (bf16[256,3072]{1,0:T(8,128)(2,1)}, bf16[256,3072]{1,0:T(8,128)(2,1)}, u32[]{:S(2)}, u32[]{:S(2)}) collective-permute-start(bf16[256,3072]{1,0:T(8,128)(2,1)} %get-tuple-element.14), channel_id=1, source_target_pairs={{1,0},{3,2},{5,4},{7,6},{9,8},{11,10},{13,12},{15,14},{17,16},{19,... | collective-permute-start | bytes 4718600 | tf_op jit(solution)/shard_map/ppermute | solution.py:136
  59.5 59.7 %collective-permute-start.4 = (bf16[256,3072]{1,0:T(8,128)(2,1)}, bf16[256,3072]{1,0:T(8,128)(2,1)}, u32[]{:S(2)}, u32[]{:S(2)}) collective-permute-start(bf16[256,3072]{1,0:T(8,128)(2,1)} %get-tuple-element.15), channel_id=1, source_target_pairs={{0,1},{2,3},{4,5},{6,7},{8,9},{10,11},{12,13},{14,15},{16,17},{18,... | collective-permute-start | bytes 4718600 | tf_op jit(solution)/shard_map/ppermute | solution.py:135
  80.0 39.1 %collective-permute-start.1 = (bf16[128,3072]{1,0:T(8,128)(2,1)}, bf16[128,3072]{1,0:T(8,128)(2,1)S(1)}, u32[]{:S(2)}, u32[]{:S(2)}) collective-permute-start(bf16[128,3072]{1,0:T(8,128)(2,1)} %collective-permute-done), channel_id=1, source_target_pairs={{3,2},{0,1},{7,6},{4,5},{11,10},{8,9},{15,14},{12,13},{19,18},{16,... | collective-permute-start | bytes 2359304 | tf_op jit(solution)/shard_map/ppermute | solution.py:141
  83.6 35.5 %collective-permute-start.3 = (bf16[128,3072]{1,0:T(8,128)(2,1)}, bf16[128,3072]{1,0:T(8,128)(2,1)S(1)}, u32[]{:S(2)}, u32[]{:S(2)}) collective-permute-start(bf16[128,3072]{1,0:T(8,128)(2,1)} %collective-permute-done.2), channel_id=1, source_target_pairs={{0,2},{3,1},{4,6},{7,5},{8,10},{11,9},{12,14},{15,13},{16,18},{19,... | collective-permute-start | bytes 2359304 | tf_op jit(solution)/shard_map/ppermute | solution.py:142
  151.5 23.0 %collective-permute-start.8 = (bf16[128,3072]{1,0:T(8,128)(2,1)S(1)}, bf16[128,3072]{1,0:T(8,128)(2,1)S(1)}, u32[]{:S(2)}, u32[]{:S(2)}) collective-permute-start(bf16[128,3072]{1,0:T(8,128)(2,1)S(1)} %get-tuple-element.12), channel_id=1, source_target_pairs={{1,0},{2,3},{5,4},{6,7},{9,8},{10,11},{13,12},{14,15},{17,16},{18,... | collective-permute-start | bytes 2359304 | tf_op jit(solution)/shard_map/ppermute | solution.py:140
  152.9 20.0 %collective-permute-start.6 = (bf16[128,3072]{1,0:T(8,128)(2,1)S(1)}, bf16[128,3072]{1,0:T(8,128)(2,1)S(1)}, u32[]{:S(2)}, u32[]{:S(2)}) collective-permute-start(bf16[128,3072]{1,0:T(8,128)(2,1)S(1)} %get-tuple-element.13), channel_id=1, source_target_pairs={{1,3},{2,0},{5,7},{6,4},{9,11},{10,8},{13,15},{14,12},{17,19},{18,... | collective-permute-start | bytes 2359304 | tf_op jit(solution)/shard_map/ppermute | solution.py:139
  154.5 55.2 %collective-permute-start.11 = (bf16[256,3072]{1,0:T(8,128)(2,1)S(1)}, bf16[256,3072]{1,0:T(8,128)(2,1)S(1)}, u32[]{:S(2)}, u32[]{:S(2)}) collective-permute-start(bf16[256,3072]{1,0:T(8,128)(2,1)S(1)} %get-tuple-element.10), channel_id=1, source_target_pairs={{1,0},{3,2},{5,4},{7,6},{9,8},{11,10},{13,12},{15,14},{17,16},{19,... | collective-permute-start | bytes 4718600 | tf_op jit(solution)/shard_map/ppermute | solution.py:136
  155.8 53.9 %collective-permute-start.10 = (bf16[256,3072]{1,0:T(8,128)(2,1)S(1)}, bf16[256,3072]{1,0:T(8,128)(2,1)S(1)}, u32[]{:S(2)}, u32[]{:S(2)}) collective-permute-start(bf16[256,3072]{1,0:T(8,128)(2,1)S(1)} %get-tuple-element.11), channel_id=1, source_target_pairs={{0,1},{2,3},{4,5},{6,7},{8,9},{10,11},{12,13},{14,15},{16,17},{18,... | collective-permute-start | bytes 4718600 | tf_op jit(solution)/shard_map/ppermute | solution.py:135
  172.9 36.6 %collective-permute-start.7 = (bf16[128,3072]{1,0:T(8,128)(2,1)S(1)}, bf16[128,3072]{1,0:T(8,128)(2,1)S(1)}, u32[]{:S(2)}, u32[]{:S(2)}) collective-permute-start(bf16[128,3072]{1,0:T(8,128)(2,1)S(1)} %collective-permute-done.6), channel_id=1, source_target_pairs={{3,2},{0,1},{7,6},{4,5},{11,10},{8,9},{15,14},{12,13},{19,18},{16,... | collective-permute-start | bytes 2359304 | tf_op jit(solution)/shard_map/ppermute | solution.py:141
  174.5 35.1 %collective-permute-start.9 = (bf16[128,3072]{1,0:T(8,128)(2,1)S(1)}, bf16[128,3072]{1,0:T(8,128)(2,1)S(1)}, u32[]{:S(2)}, u32[]{:S(2)}) collective-permute-start(bf16[128,3072]{1,0:T(8,128)(2,1)S(1)} %collective-permute-done.8), channel_id=1, source_target_pairs={{0,2},{3,1},{4,6},{7,5},{8,10},{11,9},{12,14},{15,13},{16,18},{19,... | collective-permute-start | bytes 2359304 | tf_op jit(solution)/shard_map/ppermute | solution.py:142
  227.8 193.4 %all-gather.3.cloned.1.call-start = ((), (), s32[]{:S(2)}) async-start(), calls=%async_computation.3 | async-start | bytes 10616832 | tf_op jit(solution)/shard_map/all_gather | solution.py:160
  332.0 375.1 %reduce-scatter.5.cloned.1.call-start = ((), (), s32[]{:S(2)}) async-start(), calls=%async_computation.4 | async-start | bytes 10616832 | tf_op jit(solution)/shard_map/reduce_scatter | solution.py:159
  441.0 25.5 %collective-permute-start.14 = (bf16[128,3072]{1,0:T(8,128)(2,1)S(1)}, bf16[128,3072]{1,0:T(8,128)(2,1)S(1)}, u32[]{:S(2)}, u32[]{:S(2)}) collective-permute-start(bf16[128,3072]{1,0:T(8,128)(2,1)S(1)} %get-tuple-element.8), channel_id=1, source_target_pairs={{1,0},{2,3},{5,4},{6,7},{9,8},{10,11},{13,12},{14,15},{17,16},{18,... | collective-permute-start | bytes 2359304 | tf_op jit(solution)/shard_map/ppermute | solution.py:140
  442.5 22.6 %collective-permute-start.12 = (bf16[128,3072]{1,0:T(8,128)(2,1)S(1)}, bf16[128,3072]{1,0:T(8,128)(2,1)S(1)}, u32[]{:S(2)}, u32[]{:S(2)}) collective-permute-start(bf16[128,3072]{1,0:T(8,128)(2,1)S(1)} %get-tuple-element.9), channel_id=1, source_target_pairs={{1,3},{2,0},{5,7},{6,4},{9,11},{10,8},{13,15},{14,12},{17,19},{18,... | collective-permute-start | bytes 2359304 | tf_op jit(solution)/shard_map/ppermute | solution.py:139
  444.0 57.7 %collective-permute-start.17 = (bf16[256,3072]{1,0:T(8,128)(2,1)S(1)}, bf16[256,3072]{1,0:T(8,128)(2,1)S(1)}, u32[]{:S(2)}, u32[]{:S(2)}) collective-permute-start(bf16[256,3072]{1,0:T(8,128)(2,1)S(1)} %get-tuple-element.6), channel_id=1, source_target_pairs={{1,0},{3,2},{5,4},{7,6},{9,8},{11,10},{13,12},{15,14},{17,16},{19,... | collective-permute-start | bytes 4718600 | tf_op jit(solution)/shard_map/ppermute | solution.py:136
  445.3 56.4 %collective-permute-start.16 = (bf16[256,3072]{1,0:T(8,128)(2,1)S(1)}, bf16[256,3072]{1,0:T(8,128)(2,1)S(1)}, u32[]{:S(2)}, u32[]{:S(2)}) collective-permute-start(bf16[256,3072]{1,0:T(8,128)(2,1)S(1)} %get-tuple-element.7), channel_id=1, source_target_pairs={{0,1},{2,3},{4,5},{6,7},{8,9},{10,11},{12,13},{14,15},{16,17},{18,... | collective-permute-start | bytes 4718600 | tf_op jit(solution)/shard_map/ppermute | solution.py:135
  465.1 36.5 %collective-permute-start.13 = (bf16[128,3072]{1,0:T(8,128)(2,1)S(1)}, bf16[128,3072]{1,0:T(8,128)(2,1)S(1)}, u32[]{:S(2)}, u32[]{:S(2)}) collective-permute-start(bf16[128,3072]{1,0:T(8,128)(2,1)S(1)} %collective-permute-done.12), channel_id=1, source_target_pairs={{3,2},{0,1},{7,6},{4,5},{11,10},{8,9},{15,14},{12,13},{19,18},{16,... | collective-permute-start | bytes 2359304 | tf_op jit(solution)/shard_map/ppermute | solution.py:141
  466.5 35.1 %collective-permute-start.15 = (bf16[128,3072]{1,0:T(8,128)(2,1)S(1)}, bf16[128,3072]{1,0:T(8,128)(2,1)S(1)}, u32[]{:S(2)}, u32[]{:S(2)}) collective-permute-start(bf16[128,3072]{1,0:T(8,128)(2,1)S(1)} %collective-permute-done.14), channel_id=1, source_target_pairs={{0,2},{3,1},{4,6},{7,5},{8,10},{11,9},{12,14},{15,13},{16,18},{19,... | collective-permute-start | bytes 2359304 | tf_op jit(solution)/shard_map/ppermute | solution.py:142
  532.1 23.6 %collective-permute-start.20 = (bf16[128,3072]{1,0:T(8,128)(2,1)S(1)}, bf16[128,3072]{1,0:T(8,128)(2,1)S(1)}, u32[]{:S(2)}, u32[]{:S(2)}) collective-permute-start(bf16[128,3072]{1,0:T(8,128)(2,1)S(1)} %get-tuple-element.4), channel_id=1, source_target_pairs={{1,0},{2,3},{5,4},{6,7},{9,8},{10,11},{13,12},{14,15},{17,16},{18,... | collective-permute-start | bytes 2359304 | tf_op jit(solution)/shard_map/ppermute | solution.py:140
  533.5 20.5 %collective-permute-start.18 = (bf16[128,3072]{1,0:T(8,128)(2,1)S(1)}, bf16[128,3072]{1,0:T(8,128)(2,1)S(1)}, u32[]{:S(2)}, u32[]{:S(2)}) collective-permute-start(bf16[128,3072]{1,0:T(8,128)(2,1)S(1)} %get-tuple-element.5), channel_id=1, source_target_pairs={{1,3},{2,0},{5,7},{6,4},{9,11},{10,8},{13,15},{14,12},{17,19},{18,... | collective-permute-start | bytes 2359304 | tf_op jit(solution)/shard_map/ppermute | solution.py:139
  535.1 55.8 %collective-permute-start.23 = (bf16[256,3072]{1,0:T(8,128)(2,1)S(1)}, bf16[256,3072]{1,0:T(8,128)(2,1)S(1)}, u32[]{:S(2)}, u32[]{:S(2)}) collective-permute-start(bf16[256,3072]{1,0:T(8,128)(2,1)S(1)} %get-tuple-element.2), channel_id=1, source_target_pairs={{1,0},{3,2},{5,4},{7,6},{9,8},{11,10},{13,12},{15,14},{17,16},{19,... | collective-permute-start | bytes 4718600 | tf_op jit(solution)/shard_map/ppermute | solution.py:136
  536.4 54.5 %collective-permute-start.22 = (bf16[256,3072]{1,0:T(8,128)(2,1)S(1)}, bf16[256,3072]{1,0:T(8,128)(2,1)S(1)}, u32[]{:S(2)}, u32[]{:S(2)}) collective-permute-start(bf16[256,3072]{1,0:T(8,128)(2,1)S(1)} %get-tuple-element.3), channel_id=1, source_target_pairs={{0,1},{2,3},{4,5},{6,7},{8,9},{10,11},{12,13},{14,15},{16,17},{18,... | collective-permute-start | bytes 4718600 | tf_op jit(solution)/shard_map/ppermute | solution.py:135
  554.0 36.7 %collective-permute-start.19 = (bf16[128,3072]{1,0:T(8,128)(2,1)S(1)}, bf16[128,3072]{1,0:T(8,128)(2,1)S(1)}, u32[]{:S(2)}, u32[]{:S(2)}) collective-permute-start(bf16[128,3072]{1,0:T(8,128)(2,1)S(1)} %collective-permute-done.18), channel_id=1, source_target_pairs={{3,2},{0,1},{7,6},{4,5},{11,10},{8,9},{15,14},{12,13},{19,18},{16,... | collective-permute-start | bytes 2359304 | tf_op jit(solution)/shard_map/ppermute | solution.py:141
  555.7 35.1 %collective-permute-start.21 = (bf16[128,3072]{1,0:T(8,128)(2,1)S(1)}, bf16[128,3072]{1,0:T(8,128)(2,1)S(1)}, u32[]{:S(2)}, u32[]{:S(2)}) collective-permute-start(bf16[128,3072]{1,0:T(8,128)(2,1)S(1)} %collective-permute-done.20), channel_id=1, source_target_pairs={{0,2},{3,1},{4,6},{7,5},{8,10},{11,9},{12,14},{15,13},{16,18},{19,... | collective-permute-start | bytes 2359304 | tf_op jit(solution)/shard_map/ppermute | solution.py:142
  608.9 190.5 %all-gather.5.cloned.1.call-start = ((), (), s32[]{:S(2)}) async-start(), calls=%async_computation.5 | async-start | bytes 10616832 | tf_op jit(solution)/shard_map/all_gather | solution.py:160
  810.5 8.8 %copy-start.1 = (bf16[24,3,128,128]{3,2,1,0:T(8,128)(2,1)S(1)}, bf16[24,3,128,128]{3,2,1,0:T(8,128)(2,1)}, u32[]{:S(2)}) copy-start(bf16[24,3,128,128]{3,2,1,0:T(8,128)(2,1)} %param.18) | copy-start | bytes 7077892
  (6 other events, 21.1 us)
Sparse Core Ops, SparseCore 0:
  227.9 100.9 reduce-scatter.2
  332.2 88.9 all-gather.2
  609.1 98.0 reduce-scatter.4
  710.3 89.0 all-gather.4

commit v6 on v5

--- a/solution.py
+++ b/solution.py
@@ -59,7 +59,7 @@
         o_ref[:, g * group * width : (g + 1) * group * width] = out.astype(o_ref.dtype)
 
 
-def column_pass(field, terms, group, width, tile_rows=256):
+def column_pass(field, terms, group, width, tile_rows=128):
     rows, cols = field.shape
     return pl.pallas_call(
         functools.partial(column_kernel, group=group, width=width),
@@ -90,7 +90,7 @@
         o_ref[lo * width : (lo + group) * width, :] = acc.astype(o_ref.dtype)
 
 
-def row_pass(prev, mid, nxt, terms_local, group, width, tile_cols=768):
+def row_pass(prev, mid, nxt, terms_local, group, width, tile_cols=384):
     rows, cols = mid.shape
     halo_rows = prev.shape[0]
     return pl.pallas_call(

time: 828 us -> 841 us (1.016)
  Pallas kernels: 69.6 us -> 82.2 us
    pallas_call x4, Pallas kernels: 34.6 us -> 43.7 us  [row_pass(): pl.pallas_call(functools.partial(row_kernel, group=group, width=width), g...]
where the time goes in v6:
time: 841 us; the launch traced here: 839 us
  waiting for transfers between devices  542 us (64%)
  other arithmetic  85.2 us (10%)
  Pallas kernels  82.2 us (10%)
  starting transfers between devices  53.5 us (6%)
  local copies, waits for them, and re-layouts  37.6 us (4%)
  blocking collectives  15.5 us (2%)
  between operations  14.9 us (2%)
    reduce_scatter x2, waiting for transfers between devices, per_device(): lax.psum_scatter(value_portion, 'img', scatter_dimension=0, tiled=True)  184 us
    all_gather x2, waiting for transfers between devices, per_device(): lax.all_gather(jnp.exp(log_sum / total_weight), 'img', axis=0, tiled=True)  178 us
    ppermute x4, waiting for transfers between devices, exchange(): first = lax.ppermute(first, 'slab', [(3, 2), (0, 1)])  130 us
    ppermute x4, waiting for transfers between devices, exchange(): first = lax.ppermute(first, 'slab', [(1, 3), (2, 0)])  49.2 us
    pallas_call x4, Pallas kernels, row_pass(): pl.pallas_call(functools.partial(row_kernel, group=group, width=width), g...  43.7 us
    pallas_call x4, Pallas kernels, column_pass(): pl.pallas_call(functools.partial(column_kernel, group=group, width=width)...  38.5 us
    ppermute x4, starting transfers between devices, exchange(): direct_prev = lax.ppermute(to_up, 'slab', [(0, 1), (2, 3)])  25.6 us
    convert_element_type x2, other arithmetic, per_device(): scaled_u = (masses / kernel_v.astype(jnp.float32)).astype(jnp.bfloat16)  18 us
  transfers between devices with their start and end apart: 28, of which 12 were waited for; matrix products, arithmetic and copies ran while one was open for 1% of the time, Pallas kernels for 0%

profile of v6, /device:TPU:0, one launch (start us, length us, event | category | flops | bytes accessed | tf_op | source)
XLA Modules:
  0.0 838.6 jit_solution(10329229825797186519)
XLA Ops:
  17.6 10.8 %reshape.61 = bf16[12,768,256]{1,2,0:T(8,128)(2,1)} reshape(bf16[12,6,128,2,128]{2,1,4,3,0:T(8,128)(2,1)} %convert_bitcast_fusion) | data formatting | bytes 9437184 | tf_op jit(solution)/shard_map/reshape | solution.py:32
  28.4 6.6 copy.36.t_ref
  35.0 6.6 convert_bitcast_fusion.1.x_ref
  41.6 9.6 %shard_map.158.mid_ref = bf16[768,3072]{1,0:T(8,128)(2,1)} custom-call(bf16[768,3072]{1,0:T(8,128)(2,1)} %convert_bitcast_fusion.1.x_ref, bf16[12,768,256]{2,1,0:T(8,128)(2,1)} %copy.36.t_ref), custom_call_target="tpu_custom_call" | custom-call | tf_op jit(solution)/shard_map/pallas_call | solution.py:64
  60.4 10.2 %collective-permute-start.4 = (bf16[256,3072]{1,0:T(8,128)(2,1)}, bf16[256,3072]{1,0:T(8,128)(2,1)}, u32[]{:S(2)}, u32[]{:S(2)}) collective-permute-start(bf16[256,3072]{1,0:T(8,128)(2,1)} %get-tuple-element.15), channel_id=1, source_target_pairs={{0,1},{2,3},{4,5},{6,7},{8,9},{10,11},{12,13},{14,15},{16,17},{18,... | collective-permute-start | bytes 4718600 | tf_op jit(solution)/shard_map/ppermute | solution.py:135
  70.6 10.2 %collective-permute-done = bf16[128,3072]{1,0:T(8,128)(2,1)} collective-permute-done((bf16[128,3072]{1,0:T(8,128)(2,1)}, bf16[128,3072]{1,0:T(8,128)(2,1)}, u32[]{:S(2)}, u32[]{:S(2)}) %collective-permute-start) | collective-permute-done | bytes 786464 | tf_op jit(solution)/shard_map/ppermute | solution.py:139
  89.9 30.0 %collective-permute-done.1 = bf16[128,3072]{1,0:T(8,128)(2,1)S(1)} collective-permute-done((bf16[128,3072]{1,0:T(8,128)(2,1)}, bf16[128,3072]{1,0:T(8,128)(2,1)S(1)}, u32[]{:S(2)}, u32[]{:S(2)}) %collective-permute-start.1) | collective-permute-done | bytes 786464 | tf_op jit(solution)/shard_map/ppermute | solution.py:141
  123.9 10.9 %shard_map.159 = bf16[768,3072]{1,0:T(8,128)(2,1)} custom-call(bf16[256,3072]{1,0:T(8,128)(2,1)} %get-tuple-element.25.prev_ref, bf16[768,3072]{1,0:T(8,128)(2,1)} %shard_map.158.mid_ref, bf16[256,3072]{1,0:T(8,128)(2,1)} %get-tuple-element.24.next_ref, bf16[3,256,768]{2,1,0:T(8,128)(2,1)} %reshape.62.t_ref), custom_call_target="tpu_custom_call" | custom-call | tf_op jit(solution)/shard_map/pallas_call | solution.py:96
  134.8 9.0 %fusion.4.x_ref = bf16[768,3072]{1,0:T(8,128)(2,1)} fusion(f32[1,768,3072]{2,1,0:T(8,128)} %param.15, bf16[768,3072]{1,0:T(8,128)(2,1)} %shard_map.159), kind=kLoop, calls=%fused_computation.14 | loop fusion | flops 7077888 | bytes 18874368 | tf_op jit(solution)/shard_map/convert_element_type | solution.py:156
  143.8 9.6 %shard_map.160.mid_ref = bf16[768,3072]{1,0:T(8,128)(2,1)} custom-call(bf16[768,3072]{1,0:T(8,128)(2,1)} %fusion.4.x_ref, bf16[12,768,256]{2,1,0:T(8,128)(2,1)} %copy.36.t_ref), custom_call_target="tpu_custom_call" | custom-call | tf_op jit(solution)/shard_map/pallas_call | solution.py:64
  164.8 12.1 %collective-permute-done.6 = bf16[128,3072]{1,0:T(8,128)(2,1)S(1)} collective-permute-done((bf16[128,3072]{1,0:T(8,128)(2,1)S(1)}, bf16[128,3072]{1,0:T(8,128)(2,1)S(1)}, u32[]{:S(2)}, u32[]{:S(2)}) %collective-permute-start.6) | collective-permute-done | bytes 786464 | tf_op jit(solution)/shard_map/ppermute | solution.py:139
  180.5 33.2 %collective-permute-done.7 = bf16[128,3072]{1,0:T(8,128)(2,1)S(1)} collective-permute-done((bf16[128,3072]{1,0:T(8,128)(2,1)S(1)}, bf16[128,3072]{1,0:T(8,128)(2,1)S(1)}, u32[]{:S(2)}, u32[]{:S(2)}) %collective-permute-start.7) | collective-permute-done | bytes 786464 | tf_op jit(solution)/shard_map/ppermute | solution.py:141
  215.9 11.0 %shard_map.161 = bf16[768,3072]{1,0:T(8,128)(2,1)} custom-call(bf16[256,3072]{1,0:T(8,128)(2,1)} %get-tuple-element.23.prev_ref, bf16[768,3072]{1,0:T(8,128)(2,1)} %shard_map.160.mid_ref, bf16[256,3072]{1,0:T(8,128)(2,1)} %get-tuple-element.22.next_ref, bf16[3,256,768]{2,1,0:T(8,128)(2,1)} %reshape.62.t_ref), custom_call_target="tpu_custom_call" | custom-call | tf_op jit(solution)/shard_map/pallas_call | solution.py:96
  226.9 7.4 fusion
  234.3 15.5 %psum.7 = f32[]{:T(128)} all-reduce(f32[]{:T(128)} %bitcast), channel_id=1, replica_groups=mesh['img'=8,'slab'=4] {'img'}, use_global_device_ids=true, to_apply=%region_1.0 | all-reduce | flops 1 | bytes 8 | tf_op jit(solution)/shard_map/psum | solution.py:123
  249.9 85.6 %reduce-scatter.3.cloned.1.call-done = f32[96,3072]{1,0:T(8,128)} async-done(((f32[768,3072]{1,0:T(8,128)}), f32[96,3072]{1,0:T(8,128)}) %reduce-scatter.3.cloned.1.call-update) | async-done | bytes 1179664 | tf_op jit(solution)/shard_map/reduce_scatter | solution.py:159
  338.6 89.1 %all-gather.3.cloned.1.call-done = f32[768,3072]{1,0:T(8,128)} async-done(((f32[96,3072]{1,0:T(8,128)}), f32[768,3072]{1,0:T(8,128)}) %all-gather.3.cloned.1.call-update) | async-done | bytes 9437200 | tf_op jit(solution)/shard_map/all_gather | solution.py:160
  427.7 9.0 %fusion.1.x_ref = bf16[768,3072]{1,0:T(8,128)(2,1)} fusion(f32[768,3072]{1,0:T(8,128)} %all-gather.3.cloned.1.call-done, bf16[768,3072]{1,0:T(8,128)(2,1)} %shard_map.161), kind=kLoop, calls=%fused_computation.9 | loop fusion | flops 7077888 | bytes 18874368 | tf_op jit(solution)/shard_map/convert_element_type | solution.py:155
  436.7 9.6 %shard_map.162.mid_ref = bf16[768,3072]{1,0:T(8,128)(2,1)} custom-call(bf16[768,3072]{1,0:T(8,128)(2,1)} %fusion.1.x_ref, bf16[12,768,256]{2,1,0:T(8,128)(2,1)} %copy.36.t_ref), custom_call_target="tpu_custom_call" | custom-call | tf_op jit(solution)/shard_map/pallas_call | solution.py:64
  458.4 14.0 %collective-permute-done.12 = bf16[128,3072]{1,0:T(8,128)(2,1)S(1)} collective-permute-done((bf16[128,3072]{1,0:T(8,128)(2,1)S(1)}, bf16[128,3072]{1,0:T(8,128)(2,1)S(1)}, u32[]{:S(2)}, u32[]{:S(2)}) %collective-permute-start.12) | collective-permute-done | bytes 786464 | tf_op jit(solution)/shard_map/ppermute | solution.py:139
  475.5 33.5 %collective-permute-done.13 = bf16[128,3072]{1,0:T(8,128)(2,1)S(1)} collective-permute-done((bf16[128,3072]{1,0:T(8,128)(2,1)S(1)}, bf16[128,3072]{1,0:T(8,128)(2,1)S(1)}, u32[]{:S(2)}, u32[]{:S(2)}) %collective-permute-start.13) | collective-permute-done | bytes 786464 | tf_op jit(solution)/shard_map/ppermute | solution.py:141
  511.0 10.9 %shard_map.163 = bf16[768,3072]{1,0:T(8,128)(2,1)} custom-call(bf16[256,3072]{1,0:T(8,128)(2,1)} %get-tuple-element.21.prev_ref, bf16[768,3072]{1,0:T(8,128)(2,1)} %shard_map.162.mid_ref, bf16[256,3072]{1,0:T(8,128)(2,1)} %get-tuple-element.20.next_ref, bf16[3,256,768]{2,1,0:T(8,128)(2,1)} %reshape.62.t_ref), custom_call_target="tpu_custom_call" | custom-call | tf_op jit(solution)/shard_map/pallas_call | solution.py:96
  521.9 9.0 %fusion.5.x_ref = bf16[768,3072]{1,0:T(8,128)(2,1)} fusion(f32[1,768,3072]{2,1,0:T(8,128)} %param.15, bf16[768,3072]{1,0:T(8,128)(2,1)} %shard_map.163), kind=kLoop, calls=%fused_computation.15 | loop fusion | flops 7077888 | bytes 18874368 | tf_op jit(solution)/shard_map/convert_element_type | solution.py:156
  530.9 9.6 %shard_map.164.mid_ref = bf16[768,3072]{1,0:T(8,128)(2,1)} custom-call(bf16[768,3072]{1,0:T(8,128)(2,1)} %fusion.5.x_ref, bf16[12,768,256]{2,1,0:T(8,128)(2,1)} %copy.36.t_ref), custom_call_target="tpu_custom_call" | custom-call | tf_op jit(solution)/shard_map/pallas_call | solution.py:64
  551.7 12.8 %collective-permute-done.18 = bf16[128,3072]{1,0:T(8,128)(2,1)S(1)} collective-permute-done((bf16[128,3072]{1,0:T(8,128)(2,1)S(1)}, bf16[128,3072]{1,0:T(8,128)(2,1)S(1)}, u32[]{:S(2)}, u32[]{:S(2)}) %collective-permute-start.18) | collective-permute-done | bytes 786464 | tf_op jit(solution)/shard_map/ppermute | solution.py:139
  567.5 33.7 %collective-permute-done.19 = bf16[128,3072]{1,0:T(8,128)(2,1)S(1)} collective-permute-done((bf16[128,3072]{1,0:T(8,128)(2,1)S(1)}, bf16[128,3072]{1,0:T(8,128)(2,1)S(1)}, u32[]{:S(2)}, u32[]{:S(2)}) %collective-permute-start.19) | collective-permute-done | bytes 786464 | tf_op jit(solution)/shard_map/ppermute | solution.py:141
  603.4 10.9 %shard_map.165 = bf16[768,3072]{1,0:T(8,128)(2,1)} custom-call(bf16[256,3072]{1,0:T(8,128)(2,1)} %get-tuple-element.19.prev_ref, bf16[768,3072]{1,0:T(8,128)(2,1)} %shard_map.164.mid_ref, bf16[256,3072]{1,0:T(8,128)(2,1)} %get-tuple-element.18.next_ref, bf16[3,256,768]{2,1,0:T(8,128)(2,1)} %reshape.62.t_ref), custom_call_target="tpu_custom_call" | custom-call | tf_op jit(solution)/shard_map/pallas_call | solution.py:96
  614.3 7.4 fusion.2
  621.8 98.2 %reduce-scatter.5.cloned.1.call-done = f32[96,3072]{1,0:T(8,128)} async-done(((f32[768,3072]{1,0:T(8,128)}), f32[96,3072]{1,0:T(8,128)}) %reduce-scatter.5.cloned.1.call-update) | async-done | bytes 1179664 | tf_op jit(solution)/shard_map/reduce_scatter | solution.py:159
  723.0 89.2 %all-gather.5.cloned.1.call-done = f32[768,3072]{1,0:T(8,128)} async-done(((f32[96,3072]{1,0:T(8,128)}), f32[768,3072]{1,0:T(8,128)}) %all-gather.5.cloned.1.call-update) | async-done | bytes 9437200 | tf_op jit(solution)/shard_map/all_gather | solution.py:160
  812.3 11.1 %fusion.3 = f32[1,768,3072]{2,1,0:T(8,128)} fusion(f32[768,3072]{1,0:T(8,128)} %all-gather.5.cloned.1.call-done, bf16[768,3072]{1,0:T(8,128)(2,1)} %shard_map.165), kind=kLoop, calls=%fused_computation.11 | loop fusion | flops 4718592 | bytes 23592960 | tf_op jit(solution)/shard_map/broadcast_in_dim | solution.py:162
  823.3 8.8 %copy.48 = f32[768,3072]{1,0:T(8,128)} copy(f32[768,3072]{1,0:T(8,128)} %all-gather.5.cloned.1.call-done) | data formatting | bytes 18874368
  (109 shorter events, 88.5 us)
Async XLA Ops:
  7.2 328.3 %reduce-scatter.3.cloned.1.call-start = ((), (), s32[]{:S(2)}) async-start(), calls=%async_computation.2 | async-start | bytes 10616832 | tf_op jit(solution)/shard_map/reduce_scatter | solution.py:159
  51.2 6.0 copy-start.2
  54.6 29.9 %collective-permute-start.2 = (bf16[128,3072]{1,0:T(8,128)(2,1)}, bf16[128,3072]{1,0:T(8,128)(2,1)}, u32[]{:S(2)}, u32[]{:S(2)}) collective-permute-start(bf16[128,3072]{1,0:T(8,128)(2,1)} %get-tuple-element.16), channel_id=1, source_target_pairs={{1,0},{2,3},{5,4},{6,7},{9,8},{10,11},{13,12},{14,15},{17,16},{18,... | collective-permute-start | bytes 2359304 | tf_op jit(solution)/shard_map/ppermute | solution.py:140
  55.9 14.7 %copy-start.8 = (s32[3,2,1]{0,1,2:T(2,128)S(1)}, s32[3,2,1]{0,1,2:T(2,128)}, u32[]{:S(2)}) copy-start(s32[3,2,1]{0,1,2:T(2,128)} %constant.40.clone) | copy-start | bytes 76
  55.9 14.7 %copy-start.6 = (s32[3,6]{1,0:T(4,128)S(1)}, s32[3,6]{1,0:T(4,128)}, u32[]{:S(2)}) copy-start(s32[3,6]{1,0:T(4,128)} %constant.39.clone) | copy-start | bytes 220
  55.9 24.9 %collective-permute-start = (bf16[128,3072]{1,0:T(8,128)(2,1)}, bf16[128,3072]{1,0:T(8,128)(2,1)}, u32[]{:S(2)}, u32[]{:S(2)}) collective-permute-start(bf16[128,3072]{1,0:T(8,128)(2,1)} %get-tuple-element.17), channel_id=1, source_target_pairs={{1,3},{2,0},{5,7},{6,4},{9,11},{10,8},{13,15},{14,12},{17,19},{18,... | collective-permute-start | bytes 2359304 | tf_op jit(solution)/shard_map/ppermute | solution.py:139
  59.1 61.0 %collective-permute-start.5 = (bf16[256,3072]{1,0:T(8,128)(2,1)}, bf16[256,3072]{1,0:T(8,128)(2,1)}, u32[]{:S(2)}, u32[]{:S(2)}) collective-permute-start(bf16[256,3072]{1,0:T(8,128)(2,1)} %get-tuple-element.14), channel_id=1, source_target_pairs={{1,0},{3,2},{5,4},{7,6},{9,8},{11,10},{13,12},{15,14},{17,16},{19,... | collective-permute-start | bytes 4718600 | tf_op jit(solution)/shard_map/ppermute | solution.py:136
  60.4 59.7 %collective-permute-start.4 = (bf16[256,3072]{1,0:T(8,128)(2,1)}, bf16[256,3072]{1,0:T(8,128)(2,1)}, u32[]{:S(2)}, u32[]{:S(2)}) collective-permute-start(bf16[256,3072]{1,0:T(8,128)(2,1)} %get-tuple-element.15), channel_id=1, source_target_pairs={{0,1},{2,3},{4,5},{6,7},{8,9},{10,11},{12,13},{14,15},{16,17},{18,... | collective-permute-start | bytes 4718600 | tf_op jit(solution)/shard_map/ppermute | solution.py:135
  80.9 39.1 %collective-permute-start.1 = (bf16[128,3072]{1,0:T(8,128)(2,1)}, bf16[128,3072]{1,0:T(8,128)(2,1)S(1)}, u32[]{:S(2)}, u32[]{:S(2)}) collective-permute-start(bf16[128,3072]{1,0:T(8,128)(2,1)} %collective-permute-done), channel_id=1, source_target_pairs={{3,2},{0,1},{7,6},{4,5},{11,10},{8,9},{15,14},{12,13},{19,18},{16,... | collective-permute-start | bytes 2359304 | tf_op jit(solution)/shard_map/ppermute | solution.py:141
  84.5 35.5 %collective-permute-start.3 = (bf16[128,3072]{1,0:T(8,128)(2,1)}, bf16[128,3072]{1,0:T(8,128)(2,1)S(1)}, u32[]{:S(2)}, u32[]{:S(2)}) collective-permute-start(bf16[128,3072]{1,0:T(8,128)(2,1)} %collective-permute-done.2), channel_id=1, source_target_pairs={{0,2},{3,1},{4,6},{7,5},{8,10},{11,9},{12,14},{15,13},{16,18},{19,... | collective-permute-start | bytes 2359304 | tf_op jit(solution)/shard_map/ppermute | solution.py:142
  155.6 23.0 %collective-permute-start.8 = (bf16[128,3072]{1,0:T(8,128)(2,1)S(1)}, bf16[128,3072]{1,0:T(8,128)(2,1)S(1)}, u32[]{:S(2)}, u32[]{:S(2)}) collective-permute-start(bf16[128,3072]{1,0:T(8,128)(2,1)S(1)} %get-tuple-element.12), channel_id=1, source_target_pairs={{1,0},{2,3},{5,4},{6,7},{9,8},{10,11},{13,12},{14,15},{17,16},{18,... | collective-permute-start | bytes 2359304 | tf_op jit(solution)/shard_map/ppermute | solution.py:140
  157.0 20.0 %collective-permute-start.6 = (bf16[128,3072]{1,0:T(8,128)(2,1)S(1)}, bf16[128,3072]{1,0:T(8,128)(2,1)S(1)}, u32[]{:S(2)}, u32[]{:S(2)}) collective-permute-start(bf16[128,3072]{1,0:T(8,128)(2,1)S(1)} %get-tuple-element.13), channel_id=1, source_target_pairs={{1,3},{2,0},{5,7},{6,4},{9,11},{10,8},{13,15},{14,12},{17,19},{18,... | collective-permute-start | bytes 2359304 | tf_op jit(solution)/shard_map/ppermute | solution.py:139
  158.7 55.2 %collective-permute-start.11 = (bf16[256,3072]{1,0:T(8,128)(2,1)S(1)}, bf16[256,3072]{1,0:T(8,128)(2,1)S(1)}, u32[]{:S(2)}, u32[]{:S(2)}) collective-permute-start(bf16[256,3072]{1,0:T(8,128)(2,1)S(1)} %get-tuple-element.10), channel_id=1, source_target_pairs={{1,0},{3,2},{5,4},{7,6},{9,8},{11,10},{13,12},{15,14},{17,16},{19,... | collective-permute-start | bytes 4718600 | tf_op jit(solution)/shard_map/ppermute | solution.py:136
  160.0 53.9 %collective-permute-start.10 = (bf16[256,3072]{1,0:T(8,128)(2,1)S(1)}, bf16[256,3072]{1,0:T(8,128)(2,1)S(1)}, u32[]{:S(2)}, u32[]{:S(2)}) collective-permute-start(bf16[256,3072]{1,0:T(8,128)(2,1)S(1)} %get-tuple-element.11), channel_id=1, source_target_pairs={{0,1},{2,3},{4,5},{6,7},{8,9},{10,11},{12,13},{14,15},{16,17},{18,... | collective-permute-start | bytes 4718600 | tf_op jit(solution)/shard_map/ppermute | solution.py:135
  177.0 36.8 %collective-permute-start.7 = (bf16[128,3072]{1,0:T(8,128)(2,1)S(1)}, bf16[128,3072]{1,0:T(8,128)(2,1)S(1)}, u32[]{:S(2)}, u32[]{:S(2)}) collective-permute-start(bf16[128,3072]{1,0:T(8,128)(2,1)S(1)} %collective-permute-done.6), channel_id=1, source_target_pairs={{3,2},{0,1},{7,6},{4,5},{11,10},{8,9},{15,14},{12,13},{19,18},{16,... | collective-permute-start | bytes 2359304 | tf_op jit(solution)/shard_map/ppermute | solution.py:141
  178.5 35.3 %collective-permute-start.9 = (bf16[128,3072]{1,0:T(8,128)(2,1)S(1)}, bf16[128,3072]{1,0:T(8,128)(2,1)S(1)}, u32[]{:S(2)}, u32[]{:S(2)}) collective-permute-start(bf16[128,3072]{1,0:T(8,128)(2,1)S(1)} %collective-permute-done.8), channel_id=1, source_target_pairs={{0,2},{3,1},{4,6},{7,5},{8,10},{11,9},{12,14},{15,13},{16,18},{19,... | collective-permute-start | bytes 2359304 | tf_op jit(solution)/shard_map/ppermute | solution.py:142
  234.3 193.4 %all-gather.3.cloned.1.call-start = ((), (), s32[]{:S(2)}) async-start(), calls=%async_computation.3 | async-start | bytes 10616832 | tf_op jit(solution)/shard_map/all_gather | solution.py:160
  338.5 381.4 %reduce-scatter.5.cloned.1.call-start = ((), (), s32[]{:S(2)}) async-start(), calls=%async_computation.4 | async-start | bytes 10616832 | tf_op jit(solution)/shard_map/reduce_scatter | solution.py:159
  448.4 25.5 %collective-permute-start.14 = (bf16[128,3072]{1,0:T(8,128)(2,1)S(1)}, bf16[128,3072]{1,0:T(8,128)(2,1)S(1)}, u32[]{:S(2)}, u32[]{:S(2)}) collective-permute-start(bf16[128,3072]{1,0:T(8,128)(2,1)S(1)} %get-tuple-element.8), channel_id=1, source_target_pairs={{1,0},{2,3},{5,4},{6,7},{9,8},{10,11},{13,12},{14,15},{17,16},{18,... | collective-permute-start | bytes 2359304 | tf_op jit(solution)/shard_map/ppermute | solution.py:140
  449.9 22.6 %collective-permute-start.12 = (bf16[128,3072]{1,0:T(8,128)(2,1)S(1)}, bf16[128,3072]{1,0:T(8,128)(2,1)S(1)}, u32[]{:S(2)}, u32[]{:S(2)}) collective-permute-start(bf16[128,3072]{1,0:T(8,128)(2,1)S(1)} %get-tuple-element.9), channel_id=1, source_target_pairs={{1,3},{2,0},{5,7},{6,4},{9,11},{10,8},{13,15},{14,12},{17,19},{18,... | collective-permute-start | bytes 2359304 | tf_op jit(solution)/shard_map/ppermute | solution.py:139
  451.4 57.7 %collective-permute-start.17 = (bf16[256,3072]{1,0:T(8,128)(2,1)S(1)}, bf16[256,3072]{1,0:T(8,128)(2,1)S(1)}, u32[]{:S(2)}, u32[]{:S(2)}) collective-permute-start(bf16[256,3072]{1,0:T(8,128)(2,1)S(1)} %get-tuple-element.6), channel_id=1, source_target_pairs={{1,0},{3,2},{5,4},{7,6},{9,8},{11,10},{13,12},{15,14},{17,16},{19,... | collective-permute-start | bytes 4718600 | tf_op jit(solution)/shard_map/ppermute | solution.py:136
  452.7 56.4 %collective-permute-start.16 = (bf16[256,3072]{1,0:T(8,128)(2,1)S(1)}, bf16[256,3072]{1,0:T(8,128)(2,1)S(1)}, u32[]{:S(2)}, u32[]{:S(2)}) collective-permute-start(bf16[256,3072]{1,0:T(8,128)(2,1)S(1)} %get-tuple-element.7), channel_id=1, source_target_pairs={{0,1},{2,3},{4,5},{6,7},{8,9},{10,11},{12,13},{14,15},{16,17},{18,... | collective-permute-start | bytes 4718600 | tf_op jit(solution)/shard_map/ppermute | solution.py:135
  472.4 36.5 %collective-permute-start.13 = (bf16[128,3072]{1,0:T(8,128)(2,1)S(1)}, bf16[128,3072]{1,0:T(8,128)(2,1)S(1)}, u32[]{:S(2)}, u32[]{:S(2)}) collective-permute-start(bf16[128,3072]{1,0:T(8,128)(2,1)S(1)} %collective-permute-done.12), channel_id=1, source_target_pairs={{3,2},{0,1},{7,6},{4,5},{11,10},{8,9},{15,14},{12,13},{19,18},{16,... | collective-permute-start | bytes 2359304 | tf_op jit(solution)/shard_map/ppermute | solution.py:141
  473.9 35.1 %collective-permute-start.15 = (bf16[128,3072]{1,0:T(8,128)(2,1)S(1)}, bf16[128,3072]{1,0:T(8,128)(2,1)S(1)}, u32[]{:S(2)}, u32[]{:S(2)}) collective-permute-start(bf16[128,3072]{1,0:T(8,128)(2,1)S(1)} %collective-permute-done.14), channel_id=1, source_target_pairs={{0,2},{3,1},{4,6},{7,5},{8,10},{11,9},{12,14},{15,13},{16,18},{19,... | collective-permute-start | bytes 2359304 | tf_op jit(solution)/shard_map/ppermute | solution.py:142
  542.6 23.5 %collective-permute-start.20 = (bf16[128,3072]{1,0:T(8,128)(2,1)S(1)}, bf16[128,3072]{1,0:T(8,128)(2,1)S(1)}, u32[]{:S(2)}, u32[]{:S(2)}) collective-permute-start(bf16[128,3072]{1,0:T(8,128)(2,1)S(1)} %get-tuple-element.4), channel_id=1, source_target_pairs={{1,0},{2,3},{5,4},{6,7},{9,8},{10,11},{13,12},{14,15},{17,16},{18,... | collective-permute-start | bytes 2359304 | tf_op jit(solution)/shard_map/ppermute | solution.py:140
  544.1 20.4 %collective-permute-start.18 = (bf16[128,3072]{1,0:T(8,128)(2,1)S(1)}, bf16[128,3072]{1,0:T(8,128)(2,1)S(1)}, u32[]{:S(2)}, u32[]{:S(2)}) collective-permute-start(bf16[128,3072]{1,0:T(8,128)(2,1)S(1)} %get-tuple-element.5), channel_id=1, source_target_pairs={{1,3},{2,0},{5,7},{6,4},{9,11},{10,8},{13,15},{14,12},{17,19},{18,... | collective-permute-start | bytes 2359304 | tf_op jit(solution)/shard_map/ppermute | solution.py:139
  545.6 55.8 %collective-permute-start.23 = (bf16[256,3072]{1,0:T(8,128)(2,1)S(1)}, bf16[256,3072]{1,0:T(8,128)(2,1)S(1)}, u32[]{:S(2)}, u32[]{:S(2)}) collective-permute-start(bf16[256,3072]{1,0:T(8,128)(2,1)S(1)} %get-tuple-element.2), channel_id=1, source_target_pairs={{1,0},{3,2},{5,4},{7,6},{9,8},{11,10},{13,12},{15,14},{17,16},{19,... | collective-permute-start | bytes 4718600 | tf_op jit(solution)/shard_map/ppermute | solution.py:136
  546.9 54.5 %collective-permute-start.22 = (bf16[256,3072]{1,0:T(8,128)(2,1)S(1)}, bf16[256,3072]{1,0:T(8,128)(2,1)S(1)}, u32[]{:S(2)}, u32[]{:S(2)}) collective-permute-start(bf16[256,3072]{1,0:T(8,128)(2,1)S(1)} %get-tuple-element.3), channel_id=1, source_target_pairs={{0,1},{2,3},{4,5},{6,7},{8,9},{10,11},{12,13},{14,15},{16,17},{18,... | collective-permute-start | bytes 4718600 | tf_op jit(solution)/shard_map/ppermute | solution.py:135
  564.5 36.7 %collective-permute-start.19 = (bf16[128,3072]{1,0:T(8,128)(2,1)S(1)}, bf16[128,3072]{1,0:T(8,128)(2,1)S(1)}, u32[]{:S(2)}, u32[]{:S(2)}) collective-permute-start(bf16[128,3072]{1,0:T(8,128)(2,1)S(1)} %collective-permute-done.18), channel_id=1, source_target_pairs={{3,2},{0,1},{7,6},{4,5},{11,10},{8,9},{15,14},{12,13},{19,18},{16,... | collective-permute-start | bytes 2359304 | tf_op jit(solution)/shard_map/ppermute | solution.py:141
  566.2 35.1 %collective-permute-start.21 = (bf16[128,3072]{1,0:T(8,128)(2,1)S(1)}, bf16[128,3072]{1,0:T(8,128)(2,1)S(1)}, u32[]{:S(2)}, u32[]{:S(2)}) collective-permute-start(bf16[128,3072]{1,0:T(8,128)(2,1)S(1)} %collective-permute-done.20), channel_id=1, source_target_pairs={{0,2},{3,1},{4,6},{7,5},{8,10},{11,9},{12,14},{15,13},{16,18},{19,... | collective-permute-start | bytes 2359304 | tf_op jit(solution)/shard_map/ppermute | solution.py:142
  621.7 190.5 %all-gather.5.cloned.1.call-start = ((), (), s32[]{:S(2)}) async-start(), calls=%async_computation.5 | async-start | bytes 10616832 | tf_op jit(solution)/shard_map/all_gather | solution.py:160
  823.3 8.8 %copy-start.1 = (bf16[24,3,128,128]{3,2,1,0:T(8,128)(2,1)S(1)}, bf16[24,3,128,128]{3,2,1,0:T(8,128)(2,1)}, u32[]{:S(2)}) copy-start(bf16[24,3,128,128]{3,2,1,0:T(8,128)(2,1)} %param.18) | copy-start | bytes 7077892
  (6 other events, 21.3 us)
Sparse Core Ops, SparseCore 0:
  234.4 100.9 reduce-scatter.2
  338.7 88.9 all-gather.2
  621.8 98.0 reduce-scatter.4
  723.2 89.0 all-gather.4

commit v7 on v4

--- a/solution.py
+++ b/solution.py
@@ -1,3 +1,5 @@
+import functools
+
 import jax
 import jax.numpy as jnp
 from jax import lax
@@ -50,10 +52,14 @@
     )(field, terms)
 
 
-def row_kernel(prev_ref, mid_ref, next_ref, t_ref, o_ref):
+def row_kernel(*refs, blocks, has_halo):
+    if has_halo:
+        prev_ref, mid_ref, next_ref, t_ref, o_ref = refs
+    else:
+        mid_ref, t_ref, o_ref = refs
     nlocal = t_ref.shape[0]
     width = t_ref.shape[2]
-    for b in range(nlocal):
+    for i, b in enumerate(blocks):
         acc = None
         for o in range(OFFSETS):
             e = b + o - HALO
@@ -65,24 +71,26 @@
                 src = mid_ref[e * width : (e + 1) * width, :]
             prod = jnp.dot(t_ref[b, o], src, preferred_element_type=jnp.float32)
             acc = prod if acc is None else acc + prod
-        o_ref[b * width : (b + 1) * width, :] = acc.astype(o_ref.dtype)
+        o_ref[i * width : (i + 1) * width, :] = acc.astype(o_ref.dtype)
 
 
-def row_pass(prev, mid, nxt, terms_local, tile_cols=768):
+def row_pass(mid, terms_local, blocks, halos=None, tile_cols=768):
     rows, cols = mid.shape
-    halo_rows = prev.shape[0]
+    width = terms_local.shape[2]
+    tile = lambda r: pl.BlockSpec((r, tile_cols), lambda c: (0, c))
+    operands = [mid, terms_local]
+    specs = [tile(rows), pl.BlockSpec(terms_local.shape, lambda c: (0, 0, 0, 0))]
+    if halos is not None:
+        prev, nxt = halos
+        operands = [prev, mid, nxt, terms_local]
+        specs = [tile(prev.shape[0]), tile(rows), tile(nxt.shape[0]), specs[1]]
     return pl.pallas_call(
-        row_kernel,
+        functools.partial(row_kernel, blocks=tuple(blocks), has_halo=halos is not None),
         grid=(cols // tile_cols,),
-        in_specs=[
-            pl.BlockSpec((halo_rows, tile_cols), lambda c: (0, c)),
-            pl.BlockSpec((rows, tile_cols), lambda c: (0, c)),
-            pl.BlockSpec((halo_rows, tile_cols), lambda c: (0, c)),
-            pl.BlockSpec(terms_local.shape, lambda c: (0, 0, 0, 0)),
-        ],
-        out_specs=pl.BlockSpec((rows, tile_cols), lambda c: (0, c)),
-        out_shape=jax.ShapeDtypeStruct((rows, cols), jnp.bfloat16),
-    )(prev, mid, nxt, terms_local)
+        in_specs=specs,
+        out_specs=tile(len(blocks) * width),
+        out_shape=jax.ShapeDtypeStruct((len(blocks) * width, cols), jnp.bfloat16),
+    )(*operands)
 
 
 def per_device(image_masses, dual_multipliers, fraction_tops, banded_submatrices, band_starts, nslab):
@@ -118,10 +126,35 @@
         diagonal = jnp.concatenate([first, second], axis=0)
         return jnp.where(slab == 2, diagonal, direct_prev), jnp.where(slab == 1, diagonal, direct_next)
 
+    all_blocks = list(range(local_blocks))
+    interior = all_blocks[HALO : local_blocks - HALO]
+    boundary = all_blocks[:HALO] + all_blocks[local_blocks - HALO :] if interior else all_blocks
+
     def apply_kernel(field):
         inner = column_pass(field, terms)
-        from_prev, from_next = exchange(inner)
-        return row_pass(from_prev, inner, from_next, terms_local)
+        return row_pass(inner, terms_local, all_blocks, exchange(inner))
+
+    def log_barycenter(kernel_u):
+        value_portion = weight * jnp.log(kernel_u)
+        log_sum = lax.psum_scatter(value_portion, "img", scatter_dimension=0, tiled=True)
+        return lax.all_gather(jnp.exp(log_sum / total_weight), "img", axis=0, tiled=True)
+
+    def final_apply(field):
+        inner = column_pass(field, terms)
+        halos = exchange(inner)
+        if not interior:
+            kernel_u = row_pass(inner, terms_local, all_blocks, halos).astype(jnp.float32)
+            return kernel_u, log_barycenter(kernel_u)
+        inside = row_pass(inner, terms_local, interior).astype(jnp.float32)
+        inside_sum = lax.psum_scatter(weight * jnp.log(inside), "img", scatter_dimension=0, tiled=True)
+        halos, inside_sum = lax.optimization_barrier((halos, inside_sum))
+        inside_bary = lax.all_gather(jnp.exp(inside_sum / total_weight), "img", axis=0, tiled=True)
+        edges = row_pass(inner, terms_local, boundary, halos).astype(jnp.float32)
+        edges_bary = log_barycenter(edges)
+        cut = HALO * width
+        kernel_u = jnp.concatenate([edges[:cut], inside, edges[cut:]], axis=0)
+        barycenter = jnp.concatenate([edges_bary[:cut], inside_bary, edges_bary[cut:]], axis=0)
+        return kernel_u, barycenter
 
     masses = image_masses[0]
     scaling = dual_multipliers[0]
@@ -129,10 +162,7 @@
     for iteration in range(ITERS):
         kernel_v = apply_kernel(scaling.astype(jnp.bfloat16))
         scaled_u = (masses / kernel_v.astype(jnp.float32)).astype(jnp.bfloat16)
-        kernel_u = apply_kernel(scaled_u).astype(jnp.float32)
-        value_portion = weight * jnp.log(kernel_u)
-        log_sum = lax.psum_scatter(value_portion, "img", scatter_dimension=0, tiled=True)
-        barycenter = lax.all_gather(jnp.exp(log_sum / total_weight), "img", axis=0, tiled=True)
+        kernel_u, barycenter = final_apply(scaled_u)
         scaling = barycenter / kernel_u
     return (barycenter, scaling[None])
 

time: 812 us -> 803 us (0.989)
  waiting for transfers between devices: 544 us -> 478 us
  local copies, waits for them, and re-layouts: 11.4 us -> 32.9 us
  other arithmetic: 89.4 us -> 110 us
  Pallas kernels: 81.2 us -> 89.5 us
    reduce_scatter x2 -> x4, waiting for transfers between devices: 184 us -> 125 us  [the longest x2 125 us: log_barycenter(): lax.psum_scatter(value_portion, 'img', scatter_dimension=0, tiled=True)]
    div x0 -> x1, other arithmetic: none -> 11.9 us  [per_device(): scaling = barycenter / kernel_u]
    concatenate x0 -> x2, local copies, waits for them, and re-layouts: none -> 11.4 us  [the longest x1 8.34 us: final_apply(): jnp.concatenate([edges_bary[:cut], inside_bary, edges_bary[cut:]], axis=0)]
    broadcast_in_dim x1 -> x0, other arithmetic: 11.2 us -> none  [per_device(): return (barycenter, scaling[None])]
    concatenate x0 -> x2, other arithmetic: none -> 11.1 us  [the longest x1 7.69 us: final_apply(): jnp.concatenate([edges_bary[:cut], inside_bary, edges_bary[cut:]], axis=0)]
    slice x0 -> x2, local copies, waits for them, and re-layouts: none -> 9.91 us  [the longest x1 6.37 us: final_apply(): edges_bary[:cut]]
    pallas_call x4 -> x6, Pallas kernels: 40.9 us -> 49.2 us  [row_pass(): pl.pallas_call(functools.partial(row_kernel, blocks=tuple(blocks), has_ha...]
    all_gather x2 -> x4, waiting for transfers between devices: 178 us -> 171 us  [the longest x2 109 us: log_barycenter(): lax.all_gather(jnp.exp(log_sum / total_weight), 'img', axis=0, tiled=True)]
  transfers between devices with their start and end apart: 28 -> 32, of which waited for: 12 -> 14; matrix products, arithmetic and copies ran while one was open for 1% -> 6% of each run, Pallas kernels for 0% -> 0%
where the time goes in v7:
time: 803 us; the launch traced here: 796 us
  waiting for transfers between devices  478 us (60%)
  other arithmetic  110 us (14%)
  Pallas kernels  89.5 us (11%)
  starting transfers between devices  54.3 us (7%)
  local copies, waits for them, and re-layouts  32.9 us (4%)
  between operations  15.7 us (2%)
  blocking collectives  15.4 us (2%)
    ppermute x4, waiting for transfers between devices, exchange(): first = lax.ppermute(first, 'slab', [(3, 2), (0, 1)])  135 us
    reduce_scatter x2, waiting for transfers between devices, log_barycenter(): lax.psum_scatter(value_portion, 'img', scatter_dimension=0, tiled=True)  125 us
    all_gather x2, waiting for transfers between devices, log_barycenter(): lax.all_gather(jnp.exp(log_sum / total_weight), 'img', axis=0, tiled=True)  109 us
    all_gather x2, waiting for transfers between devices, final_apply(): lax.all_gather(jnp.exp(inside_sum / total_weight), 'img', axis=0, tiled=T...  62.4 us
    pallas_call x6, Pallas kernels, row_pass(): pl.pallas_call(functools.partial(row_kernel, blocks=tuple(blocks), has_ha...  49.2 us
    ppermute x4, waiting for transfers between devices, exchange(): first = lax.ppermute(first, 'slab', [(1, 3), (2, 0)])  46.6 us
    pallas_call x4, Pallas kernels, column_pass(): pl.pallas_call(column_kernel, grid=(rows // tile_rows,), in_specs=[pl.Blo...  40.3 us
    ppermute x4, starting transfers between devices, exchange(): direct_prev = lax.ppermute(to_up, 'slab', [(0, 1), (2, 3)])  24.7 us
  transfers between devices with their start and end apart: 32, of which 14 were waited for; matrix products, arithmetic and copies ran while one was open for 6% of the time, Pallas kernels for 0%

profile of v7, /device:TPU:0, one launch (start us, length us, event | category | flops | bytes accessed | tf_op | source)
XLA Modules:
  0.0 795.9 jit_solution(3339133245137133038)
XLA Ops:
  8.0 6.7 convert_bitcast_fusion.x_ref
  20.6 10.1 %shard_map.68.refs_1_ = bf16[768,3072]{1,0:T(8,128)(2,1)} custom-call(bf16[768,3072]{1,0:T(8,128)(2,1)} %convert_bitcast_fusion.x_ref, bf16[24,5,128,128]{3,2,1,0:T(8,128)(2,1)} %select_reduce_fusion.t_ref), custom_call_target="tpu_custom_call" | custom-call | tf_op jit(solution)/shard_map/pallas_call | solution.py:43
  38.2 9.1 %collective-permute-start.4 = (bf16[256,3072]{1,0:T(8,128)(2,1)S(1)}, bf16[256,3072]{1,0:T(8,128)(2,1)}, u32[]{:S(2)}, u32[]{:S(2)}) collective-permute-start(bf16[256,3072]{1,0:T(8,128)(2,1)S(1)} %get-tuple-element.35), channel_id=1, source_target_pairs={{0,1},{2,3},{4,5},{6,7},{8,9},{10,11},{12,13},{14,15},{16,17},{18,... | collective-permute-start | bytes 4718600 | tf_op jit(solution)/shard_map/ppermute | solution.py:118
  47.3 11.5 %collective-permute-done = bf16[128,3072]{1,0:T(8,128)(2,1)} collective-permute-done((bf16[128,3072]{1,0:T(8,128)(2,1)S(1)}, bf16[128,3072]{1,0:T(8,128)(2,1)}, u32[]{:S(2)}, u32[]{:S(2)}) %collective-permute-start) | collective-permute-done | bytes 786464 | tf_op jit(solution)/shard_map/ppermute | solution.py:122
  66.3 30.2 %collective-permute-done.1 = bf16[128,3072]{1,0:T(8,128)(2,1)} collective-permute-done((bf16[128,3072]{1,0:T(8,128)(2,1)}, bf16[128,3072]{1,0:T(8,128)(2,1)}, u32[]{:S(2)}, u32[]{:S(2)}) %collective-permute-start.1) | collective-permute-done | bytes 786464 | tf_op jit(solution)/shard_map/ppermute | solution.py:124
  102.3 10.2 %shard_map.69 = bf16[768,3072]{1,0:T(8,128)(2,1)} custom-call(bf16[256,3072]{1,0:T(8,128)(2,1)} %get-tuple-element.47.refs_0_, bf16[768,3072]{1,0:T(8,128)(2,1)} %shard_map.68.refs_1_, bf16[256,3072]{1,0:T(8,128)(2,1)} %get-tuple-element.46.refs_2_, bf16[6,5,128,128]{3,2,1,0:T(8,128)(2,1)} %constant_dynamic-slice_fusion.refs_3_.refs_1_), custom_call_target="tpu_custom_call" | custom-call | tf_op jit(solution)/shard_map/pallas_call | solution.py:87
  112.4 9.0 %fusion.1.x_ref = bf16[768,3072]{1,0:T(8,128)(2,1)} fusion(f32[1,768,3072]{2,1,0:T(8,128)} %param.5, bf16[768,3072]{1,0:T(8,128)(2,1)} %shard_map.69), kind=kLoop, calls=%fused_computation.7 | loop fusion | flops 7077888 | bytes 18874368 | tf_op jit(solution)/shard_map/convert_element_type | solution.py:164
  121.4 10.1 %shard_map.70.refs_0_.refs_1_ = bf16[768,3072]{1,0:T(8,128)(2,1)} custom-call(bf16[768,3072]{1,0:T(8,128)(2,1)} %fusion.1.x_ref, bf16[24,5,128,128]{3,2,1,0:T(8,128)(2,1)} %select_reduce_fusion.t_ref), custom_call_target="tpu_custom_call" | custom-call | tf_op jit(solution)/shard_map/pallas_call | solution.py:43
  153.8 10.4 %collective-permute-done.6 = bf16[128,3072]{1,0:T(8,128)(2,1)S(1)} collective-permute-done((bf16[128,3072]{1,0:T(8,128)(2,1)S(1)}, bf16[128,3072]{1,0:T(8,128)(2,1)S(1)}, u32[]{:S(2)}, u32[]{:S(2)}) %collective-permute-start.6) | collective-permute-done | bytes 786464 | tf_op jit(solution)/shard_map/ppermute | solution.py:122
  167.2 35.6 %collective-permute-done.7 = bf16[128,3072]{1,0:T(8,128)(2,1)S(1)} collective-permute-done((bf16[128,3072]{1,0:T(8,128)(2,1)S(1)}, bf16[128,3072]{1,0:T(8,128)(2,1)S(1)}, u32[]{:S(2)}, u32[]{:S(2)}) %collective-permute-start.7) | collective-permute-done | bytes 786464 | tf_op jit(solution)/shard_map/ppermute | solution.py:124
  204.8 8.5 %shard_map.72 = bf16[512,3072]{1,0:T(8,128)(2,1)} custom-call(bf16[256,3072]{1,0:T(8,128)(2,1)} %get-tuple-element.8.refs_0_, bf16[768,3072]{1,0:T(8,128)(2,1)} %shard_map.70.refs_0_.refs_1_, bf16[256,3072]{1,0:T(8,128)(2,1)} %get-tuple-element.9.refs_2_, bf16[6,5,128,128]{3,2,1,0:T(8,128)(2,1)} %constant_dynamic-slice_fusion.refs_3_.refs_1_), custom_call_target="tpu_custom_call" | custom-call | tf_op jit(solution)/shard_map/pallas_call | solution.py:87
  218.9 15.4 %psum.7 = f32[]{:T(128)} all-reduce(f32[]{:T(128)} %bitcast), channel_id=1, replica_groups=mesh['img'=8,'slab'=4] {'img'}, use_global_device_ids=true, to_apply=%region_3.4 | all-reduce | flops 1 | bytes 8 | tf_op jit(solution)/shard_map/psum | solution.py:106
  234.3 56.0 %reduce-scatter.7.cloned.1.call-done = f32[64,3072]{1,0:T(8,128)} async-done(((f32[512,3072]{1,0:T(8,128)}), f32[64,3072]{1,0:T(8,128)}) %reduce-scatter.7.cloned.1.call-update) | async-done | bytes 786448 | tf_op jit(solution)/shard_map/reduce_scatter | solution.py:139
  301.9 54.3 %all-gather.5.cloned.1.call-done = f32[512,3072]{1,0:T(8,128)} async-done(((f32[64,3072]{1,0:T(8,128)}), f32[512,3072]{1,0:T(8,128)}) %all-gather.5.cloned.1.call-update) | async-done | bytes 6291472 | tf_op jit(solution)/shard_map/all_gather | solution.py:140
  356.1 6.4 fusion.4
  362.5 32.1 %all-gather.7.cloned.1.call-done = f32[256,3072]{1,0:T(8,128)} async-done(((f32[32,3072]{1,0:T(8,128)}), f32[256,3072]{1,0:T(8,128)}) %all-gather.7.cloned.1.call-update) | async-done | bytes 3145744 | tf_op jit(solution)/shard_map/all_gather | solution.py:151
  394.6 8.7 %fusion.x_ref = bf16[768,3072]{1,0:T(8,128)(2,1)} fusion(f32[256,3072]{1,0:T(8,128)} %get-tuple-element.21, f32[256,3072]{1,0:T(8,128)} %all-gather.7.cloned.1.call-done, f32[256,3072]{1,0:T(8,128)} %get-tuple-element.20, f32[256,3072]{1,0:T(8,128)} %get-tuple-element.39, f32[256,3072]{1,0:T(8,128)S(1)} %copy-done.5, f32[256,3072]{1,0:T(8,128)} %get-tuple-element.38), kind=kLoop, calls=%fused_computation.2 | loop fusion | flops 14155776 | bytes 23592960 | tf_op jit(solution)/shard_map/convert_element_type | solution.py:163
  403.3 10.1 %shard_map.73.refs_1_ = bf16[768,3072]{1,0:T(8,128)(2,1)} custom-call(bf16[768,3072]{1,0:T(8,128)(2,1)} %fusion.x_ref, bf16[24,5,128,128]{3,2,1,0:T(8,128)(2,1)} %select_reduce_fusion.t_ref), custom_call_target="tpu_custom_call" | custom-call | tf_op jit(solution)/shard_map/pallas_call | solution.py:43
  425.5 14.0 %collective-permute-done.12 = bf16[128,3072]{1,0:T(8,128)(2,1)S(1)} collective-permute-done((bf16[128,3072]{1,0:T(8,128)(2,1)S(1)}, bf16[128,3072]{1,0:T(8,128)(2,1)S(1)}, u32[]{:S(2)}, u32[]{:S(2)}) %collective-permute-start.12) | collective-permute-done | bytes 786464 | tf_op jit(solution)/shard_map/ppermute | solution.py:122
  442.3 33.7 %collective-permute-done.13 = bf16[128,3072]{1,0:T(8,128)(2,1)S(1)} collective-permute-done((bf16[128,3072]{1,0:T(8,128)(2,1)S(1)}, bf16[128,3072]{1,0:T(8,128)(2,1)S(1)}, u32[]{:S(2)}, u32[]{:S(2)}) %collective-permute-start.13) | collective-permute-done | bytes 786464 | tf_op jit(solution)/shard_map/ppermute | solution.py:124
  478.1 10.2 %shard_map.74 = bf16[768,3072]{1,0:T(8,128)(2,1)} custom-call(bf16[256,3072]{1,0:T(8,128)(2,1)} %get-tuple-element.43.refs_0_, bf16[768,3072]{1,0:T(8,128)(2,1)} %shard_map.73.refs_1_, bf16[256,3072]{1,0:T(8,128)(2,1)} %get-tuple-element.42.refs_2_, bf16[6,5,128,128]{3,2,1,0:T(8,128)(2,1)} %constant_dynamic-slice_fusion.refs_3_.refs_1_), custom_call_target="tpu_custom_call" | custom-call | tf_op jit(solution)/shard_map/pallas_call | solution.py:87
  488.3 9.0 %fusion.2.x_ref = bf16[768,3072]{1,0:T(8,128)(2,1)} fusion(f32[1,768,3072]{2,1,0:T(8,128)} %param.5, bf16[768,3072]{1,0:T(8,128)(2,1)} %shard_map.74), kind=kLoop, calls=%fused_computation.8 | loop fusion | flops 7077888 | bytes 18874368 | tf_op jit(solution)/shard_map/convert_element_type | solution.py:164
  497.3 10.1 %shard_map.75.refs_0_.refs_1_ = bf16[768,3072]{1,0:T(8,128)(2,1)} custom-call(bf16[768,3072]{1,0:T(8,128)(2,1)} %fusion.2.x_ref, bf16[24,5,128,128]{3,2,1,0:T(8,128)(2,1)} %select_reduce_fusion.t_ref), custom_call_target="tpu_custom_call" | custom-call | tf_op jit(solution)/shard_map/pallas_call | solution.py:43
  529.9 10.6 %collective-permute-done.18 = bf16[128,3072]{1,0:T(8,128)(2,1)S(1)} collective-permute-done((bf16[128,3072]{1,0:T(8,128)(2,1)S(1)}, bf16[128,3072]{1,0:T(8,128)(2,1)S(1)}, u32[]{:S(2)}, u32[]{:S(2)}) %collective-permute-start.18) | collective-permute-done | bytes 786464 | tf_op jit(solution)/shard_map/ppermute | solution.py:122
  543.5 36.0 %collective-permute-done.19 = bf16[128,3072]{1,0:T(8,128)(2,1)S(1)} collective-permute-done((bf16[128,3072]{1,0:T(8,128)(2,1)S(1)}, bf16[128,3072]{1,0:T(8,128)(2,1)S(1)}, u32[]{:S(2)}, u32[]{:S(2)}) %collective-permute-start.19) | collective-permute-done | bytes 786464 | tf_op jit(solution)/shard_map/ppermute | solution.py:124
  581.6 8.6 %shard_map.77 = bf16[512,3072]{1,0:T(8,128)(2,1)} custom-call(bf16[256,3072]{1,0:T(8,128)(2,1)} %get-tuple-element.11.refs_0_, bf16[768,3072]{1,0:T(8,128)(2,1)} %shard_map.75.refs_0_.refs_1_, bf16[256,3072]{1,0:T(8,128)(2,1)} %get-tuple-element.12.refs_2_, bf16[6,5,128,128]{3,2,1,0:T(8,128)(2,1)} %constant_dynamic-slice_fusion.refs_3_.refs_1_), custom_call_target="tpu_custom_call" | custom-call | tf_op jit(solution)/shard_map/pallas_call | solution.py:87
  595.7 68.7 %reduce-scatter.11.cloned.1.call-done = f32[64,3072]{1,0:T(8,128)} async-done(((f32[512,3072]{1,0:T(8,128)}), f32[64,3072]{1,0:T(8,128)}) %reduce-scatter.11.cloned.1.call-update) | async-done | bytes 786448 | tf_op jit(solution)/shard_map/reduce_scatter | solution.py:139
  676.0 54.4 %all-gather.9.cloned.1.call-done = f32[512,3072]{1,0:T(8,128)} async-done(((f32[64,3072]{1,0:T(8,128)}), f32[512,3072]{1,0:T(8,128)}) %all-gather.9.cloned.1.call-update) | async-done | bytes 6291472 | tf_op jit(solution)/shard_map/all_gather | solution.py:140
  730.4 8.3 %slice_bitcast_fusion.3 = (f32[1,256,3072]{2,1,0:T(8,128)}, f32[1,256,3072]{2,1,0:T(8,128)}, f32[256,3072]{1,0:T(8,128)}, f32[256,3072]{1,0:T(8,128)}) fusion(f32[512,3072]{1,0:T(8,128)} %all-gather.9.cloned.1.call-done), kind=kLoop, calls=%fused_computation.50 | loop fusion | bytes 18874368 | tf_op jit(solution)/shard_map/concatenate | solution.py:156
  738.7 30.3 %all-gather.11.cloned.1.call-done = f32[256,3072]{1,0:T(8,128)} async-done(((f32[32,3072]{1,0:T(8,128)}), f32[256,3072]{1,0:T(8,128)}) %all-gather.11.cloned.1.call-update) | async-done | bytes 3145744 | tf_op jit(solution)/shard_map/all_gather | solution.py:151
  769.0 11.9 %maximum_divide_fusion.1 = f32[1,768,3072]{2,1,0:T(8,128)} fusion(f32[1,256,3072]{2,1,0:T(8,128)} %get-tuple-element.17, f32[1,256,3072]{2,1,0:T(8,128)} %bitcast.21, f32[1,256,3072]{2,1,0:T(8,128)} %get-tuple-element.16, f32[1,256,3072]{2,1,0:T(8,128)} %get-tuple-element.15, f32[1,256,3072]{2,1,0:T(8,128)} %convert_bitcast_fusion.1, ...), kind=kLoop, calls=%fused_computation.4 | loop fusion | flops 11796480 | bytes 28311552 | tf_op jit(solution)/shard_map/div | solution.py:166
  781.0 7.7 pad_maximum_fusion
  (115 shorter events, 132.4 us)
Async XLA Ops:
  7.2 197.7 %reduce-scatter.5.cloned.1.call-start = ((), (), s32[]{:S(2)}) async-start(), calls=%async_computation.4 | async-start | bytes 3538944 | tf_op jit(solution)/shard_map/reduce_scatter | solution.py:149
  32.8 28.2 %collective-permute-start.2 = (bf16[128,3072]{1,0:T(8,128)(2,1)S(1)}, bf16[128,3072]{1,0:T(8,128)(2,1)}, u32[]{:S(2)}, u32[]{:S(2)}) collective-permute-start(bf16[128,3072]{1,0:T(8,128)(2,1)S(1)} %get-tuple-element.36), channel_id=1, source_target_pairs={{1,0},{2,3},{5,4},{6,7},{9,8},{10,11},{13,12},{14,15},{17,16},{18,... | collective-permute-start | bytes 2359304 | tf_op jit(solution)/shard_map/ppermute | solution.py:123
  34.3 24.6 %collective-permute-start = (bf16[128,3072]{1,0:T(8,128)(2,1)S(1)}, bf16[128,3072]{1,0:T(8,128)(2,1)}, u32[]{:S(2)}, u32[]{:S(2)}) collective-permute-start(bf16[128,3072]{1,0:T(8,128)(2,1)S(1)} %get-tuple-element.37), channel_id=1, source_target_pairs={{1,3},{2,0},{5,7},{6,4},{9,11},{10,8},{13,15},{14,12},{17,19},{18,... | collective-permute-start | bytes 2359304 | tf_op jit(solution)/shard_map/ppermute | solution.py:122
  36.9 61.9 %collective-permute-start.5 = (bf16[256,3072]{1,0:T(8,128)(2,1)}, bf16[256,3072]{1,0:T(8,128)(2,1)S(1)}, u32[]{:S(2)}, u32[]{:S(2)}) collective-permute-start(bf16[256,3072]{1,0:T(8,128)(2,1)} %get-tuple-element.34), channel_id=1, source_target_pairs={{1,0},{3,2},{5,4},{7,6},{9,8},{11,10},{13,12},{15,14},{17,16},{19,... | collective-permute-start | bytes 4718600 | tf_op jit(solution)/shard_map/ppermute | solution.py:119
  38.2 60.7 %collective-permute-start.4 = (bf16[256,3072]{1,0:T(8,128)(2,1)S(1)}, bf16[256,3072]{1,0:T(8,128)(2,1)}, u32[]{:S(2)}, u32[]{:S(2)}) collective-permute-start(bf16[256,3072]{1,0:T(8,128)(2,1)S(1)} %get-tuple-element.35), channel_id=1, source_target_pairs={{0,1},{2,3},{4,5},{6,7},{8,9},{10,11},{12,13},{14,15},{16,17},{18,... | collective-permute-start | bytes 4718600 | tf_op jit(solution)/shard_map/ppermute | solution.py:118
  58.9 37.6 %collective-permute-start.1 = (bf16[128,3072]{1,0:T(8,128)(2,1)}, bf16[128,3072]{1,0:T(8,128)(2,1)}, u32[]{:S(2)}, u32[]{:S(2)}) collective-permute-start(bf16[128,3072]{1,0:T(8,128)(2,1)} %collective-permute-done), channel_id=1, source_target_pairs={{3,2},{0,1},{7,6},{4,5},{11,10},{8,9},{15,14},{12,13},{19,18},{16,... | collective-permute-start | bytes 2359304 | tf_op jit(solution)/shard_map/ppermute | solution.py:124
  61.1 36.6 %collective-permute-start.3 = (bf16[128,3072]{1,0:T(8,128)(2,1)}, bf16[128,3072]{1,0:T(8,128)(2,1)}, u32[]{:S(2)}, u32[]{:S(2)}) collective-permute-start(bf16[128,3072]{1,0:T(8,128)(2,1)} %collective-permute-done.2), channel_id=1, source_target_pairs={{0,2},{3,1},{4,6},{7,5},{8,10},{11,9},{12,14},{15,13},{16,18},{19,... | collective-permute-start | bytes 2359304 | tf_op jit(solution)/shard_map/ppermute | solution.py:125
  140.9 149.4 %reduce-scatter.7.cloned.1.call-start = ((), (), s32[]{:S(2)}) async-start(), calls=%async_computation.5 | async-start | bytes 7077888 | tf_op jit(solution)/shard_map/reduce_scatter | solution.py:139
  142.9 23.0 %collective-permute-start.8 = (bf16[128,3072]{1,0:T(8,128)(2,1)S(1)}, bf16[128,3072]{1,0:T(8,128)(2,1)S(1)}, u32[]{:S(2)}, u32[]{:S(2)}) collective-permute-start(bf16[128,3072]{1,0:T(8,128)(2,1)S(1)} %get-tuple-element.32), channel_id=1, source_target_pairs={{1,0},{2,3},{5,4},{6,7},{9,8},{10,11},{13,12},{14,15},{17,16},{18,... | collective-permute-start | bytes 2359304 | tf_op jit(solution)/shard_map/ppermute | solution.py:123
  144.2 20.0 %collective-permute-start.6 = (bf16[128,3072]{1,0:T(8,128)(2,1)S(1)}, bf16[128,3072]{1,0:T(8,128)(2,1)S(1)}, u32[]{:S(2)}, u32[]{:S(2)}) collective-permute-start(bf16[128,3072]{1,0:T(8,128)(2,1)S(1)} %get-tuple-element.33), channel_id=1, source_target_pairs={{1,3},{2,0},{5,7},{6,4},{9,11},{10,8},{13,15},{14,12},{17,19},{18,... | collective-permute-start | bytes 2359304 | tf_op jit(solution)/shard_map/ppermute | solution.py:122
  147.6 55.3 %collective-permute-start.11 = (bf16[256,3072]{1,0:T(8,128)(2,1)S(1)}, bf16[256,3072]{1,0:T(8,128)(2,1)S(1)}, u32[]{:S(2)}, u32[]{:S(2)}) collective-permute-start(bf16[256,3072]{1,0:T(8,128)(2,1)S(1)} %get-tuple-element.30), channel_id=1, source_target_pairs={{1,0},{3,2},{5,4},{7,6},{9,8},{11,10},{13,12},{15,14},{17,16},{19,... | collective-permute-start | bytes 4718600 | tf_op jit(solution)/shard_map/ppermute | solution.py:119
  148.9 54.0 %collective-permute-start.10 = (bf16[256,3072]{1,0:T(8,128)(2,1)S(1)}, bf16[256,3072]{1,0:T(8,128)(2,1)S(1)}, u32[]{:S(2)}, u32[]{:S(2)}) collective-permute-start(bf16[256,3072]{1,0:T(8,128)(2,1)S(1)} %get-tuple-element.31), channel_id=1, source_target_pairs={{0,1},{2,3},{4,5},{6,7},{8,9},{10,11},{12,13},{14,15},{16,17},{18,... | collective-permute-start | bytes 4718600 | tf_op jit(solution)/shard_map/ppermute | solution.py:118
  164.2 38.6 %collective-permute-start.7 = (bf16[128,3072]{1,0:T(8,128)(2,1)S(1)}, bf16[128,3072]{1,0:T(8,128)(2,1)S(1)}, u32[]{:S(2)}, u32[]{:S(2)}) collective-permute-start(bf16[128,3072]{1,0:T(8,128)(2,1)S(1)} %collective-permute-done.6), channel_id=1, source_target_pairs={{3,2},{0,1},{7,6},{4,5},{11,10},{8,9},{15,14},{12,13},{19,18},{16,... | collective-permute-start | bytes 2359304 | tf_op jit(solution)/shard_map/ppermute | solution.py:124
  165.9 37.0 %collective-permute-start.9 = (bf16[128,3072]{1,0:T(8,128)(2,1)S(1)}, bf16[128,3072]{1,0:T(8,128)(2,1)S(1)}, u32[]{:S(2)}, u32[]{:S(2)}) collective-permute-start(bf16[128,3072]{1,0:T(8,128)(2,1)S(1)} %collective-permute-done.8), channel_id=1, source_target_pairs={{0,2},{3,1},{4,6},{7,5},{8,10},{11,9},{12,14},{15,13},{16,18},{19,... | collective-permute-start | bytes 2359304 | tf_op jit(solution)/shard_map/ppermute | solution.py:125
  218.9 137.3 %all-gather.5.cloned.1.call-start = ((), (), s32[]{:S(2)}) async-start(), calls=%async_computation.6 | async-start | bytes 7077888 | tf_op jit(solution)/shard_map/all_gather | solution.py:140
  293.0 101.6 %all-gather.7.cloned.1.call-start = ((), (), s32[]{:S(2)}) async-start(), calls=%async_computation.7 | async-start | bytes 3538944 | tf_op jit(solution)/shard_map/all_gather | solution.py:151
  294.6 286.9 %reduce-scatter.9.cloned.1.call-start = ((), (), s32[]{:S(2)}) async-start(), calls=%async_computation.8 | async-start | bytes 3538944 | tf_op jit(solution)/shard_map/reduce_scatter | solution.py:149
  415.5 25.4 %collective-permute-start.14 = (bf16[128,3072]{1,0:T(8,128)(2,1)S(1)}, bf16[128,3072]{1,0:T(8,128)(2,1)S(1)}, u32[]{:S(2)}, u32[]{:S(2)}) collective-permute-start(bf16[128,3072]{1,0:T(8,128)(2,1)S(1)} %get-tuple-element.28), channel_id=1, source_target_pairs={{1,0},{2,3},{5,4},{6,7},{9,8},{10,11},{13,12},{14,15},{17,16},{18,... | collective-permute-start | bytes 2359304 | tf_op jit(solution)/shard_map/ppermute | solution.py:123
  417.0 22.5 %collective-permute-start.12 = (bf16[128,3072]{1,0:T(8,128)(2,1)S(1)}, bf16[128,3072]{1,0:T(8,128)(2,1)S(1)}, u32[]{:S(2)}, u32[]{:S(2)}) collective-permute-start(bf16[128,3072]{1,0:T(8,128)(2,1)S(1)} %get-tuple-element.29), channel_id=1, source_target_pairs={{1,3},{2,0},{5,7},{6,4},{9,11},{10,8},{13,15},{14,12},{17,19},{18,... | collective-permute-start | bytes 2359304 | tf_op jit(solution)/shard_map/ppermute | solution.py:122
  418.5 57.7 %collective-permute-start.17 = (bf16[256,3072]{1,0:T(8,128)(2,1)S(1)}, bf16[256,3072]{1,0:T(8,128)(2,1)S(1)}, u32[]{:S(2)}, u32[]{:S(2)}) collective-permute-start(bf16[256,3072]{1,0:T(8,128)(2,1)S(1)} %get-tuple-element.26), channel_id=1, source_target_pairs={{1,0},{3,2},{5,4},{7,6},{9,8},{11,10},{13,12},{15,14},{17,16},{19,... | collective-permute-start | bytes 4718600 | tf_op jit(solution)/shard_map/ppermute | solution.py:119
  419.8 56.4 %collective-permute-start.16 = (bf16[256,3072]{1,0:T(8,128)(2,1)S(1)}, bf16[256,3072]{1,0:T(8,128)(2,1)S(1)}, u32[]{:S(2)}, u32[]{:S(2)}) collective-permute-start(bf16[256,3072]{1,0:T(8,128)(2,1)S(1)} %get-tuple-element.27), channel_id=1, source_target_pairs={{0,1},{2,3},{4,5},{6,7},{8,9},{10,11},{12,13},{14,15},{16,17},{18,... | collective-permute-start | bytes 4718600 | tf_op jit(solution)/shard_map/ppermute | solution.py:118
  439.5 36.5 %collective-permute-start.13 = (bf16[128,3072]{1,0:T(8,128)(2,1)S(1)}, bf16[128,3072]{1,0:T(8,128)(2,1)S(1)}, u32[]{:S(2)}, u32[]{:S(2)}) collective-permute-start(bf16[128,3072]{1,0:T(8,128)(2,1)S(1)} %collective-permute-done.12), channel_id=1, source_target_pairs={{3,2},{0,1},{7,6},{4,5},{11,10},{8,9},{15,14},{12,13},{19,18},{16,... | collective-permute-start | bytes 2359304 | tf_op jit(solution)/shard_map/ppermute | solution.py:124
  441.0 35.1 %collective-permute-start.15 = (bf16[128,3072]{1,0:T(8,128)(2,1)S(1)}, bf16[128,3072]{1,0:T(8,128)(2,1)S(1)}, u32[]{:S(2)}, u32[]{:S(2)}) collective-permute-start(bf16[128,3072]{1,0:T(8,128)(2,1)S(1)} %collective-permute-done.14), channel_id=1, source_target_pairs={{0,2},{3,1},{4,6},{7,5},{8,10},{11,9},{12,14},{15,13},{16,18},{19,... | collective-permute-start | bytes 2359304 | tf_op jit(solution)/shard_map/ppermute | solution.py:125
  516.7 147.7 %reduce-scatter.11.cloned.1.call-start = ((), (), s32[]{:S(2)}) async-start(), calls=%async_computation.9 | async-start | bytes 7077888 | tf_op jit(solution)/shard_map/reduce_scatter | solution.py:139
  518.8 23.4 %collective-permute-start.20 = (bf16[128,3072]{1,0:T(8,128)(2,1)S(1)}, bf16[128,3072]{1,0:T(8,128)(2,1)S(1)}, u32[]{:S(2)}, u32[]{:S(2)}) collective-permute-start(bf16[128,3072]{1,0:T(8,128)(2,1)S(1)} %get-tuple-element.24), channel_id=1, source_target_pairs={{1,0},{2,3},{5,4},{6,7},{9,8},{10,11},{13,12},{14,15},{17,16},{18,... | collective-permute-start | bytes 2359304 | tf_op jit(solution)/shard_map/ppermute | solution.py:123
  520.1 20.4 %collective-permute-start.18 = (bf16[128,3072]{1,0:T(8,128)(2,1)S(1)}, bf16[128,3072]{1,0:T(8,128)(2,1)S(1)}, u32[]{:S(2)}, u32[]{:S(2)}) collective-permute-start(bf16[128,3072]{1,0:T(8,128)(2,1)S(1)} %get-tuple-element.25), channel_id=1, source_target_pairs={{1,3},{2,0},{5,7},{6,4},{9,11},{10,8},{13,15},{14,12},{17,19},{18,... | collective-permute-start | bytes 2359304 | tf_op jit(solution)/shard_map/ppermute | solution.py:122
  523.6 56.1 %collective-permute-start.23 = (bf16[256,3072]{1,0:T(8,128)(2,1)S(1)}, bf16[256,3072]{1,0:T(8,128)(2,1)S(1)}, u32[]{:S(2)}, u32[]{:S(2)}) collective-permute-start(bf16[256,3072]{1,0:T(8,128)(2,1)S(1)} %get-tuple-element.22), channel_id=1, source_target_pairs={{1,0},{3,2},{5,4},{7,6},{9,8},{11,10},{13,12},{15,14},{17,16},{19,... | collective-permute-start | bytes 4718600 | tf_op jit(solution)/shard_map/ppermute | solution.py:119
  524.9 54.8 %collective-permute-start.22 = (bf16[256,3072]{1,0:T(8,128)(2,1)S(1)}, bf16[256,3072]{1,0:T(8,128)(2,1)S(1)}, u32[]{:S(2)}, u32[]{:S(2)}) collective-permute-start(bf16[256,3072]{1,0:T(8,128)(2,1)S(1)} %get-tuple-element.23), channel_id=1, source_target_pairs={{0,1},{2,3},{4,5},{6,7},{8,9},{10,11},{12,13},{14,15},{16,17},{18,... | collective-permute-start | bytes 4718600 | tf_op jit(solution)/shard_map/ppermute | solution.py:118
  540.5 39.0 %collective-permute-start.19 = (bf16[128,3072]{1,0:T(8,128)(2,1)S(1)}, bf16[128,3072]{1,0:T(8,128)(2,1)S(1)}, u32[]{:S(2)}, u32[]{:S(2)}) collective-permute-start(bf16[128,3072]{1,0:T(8,128)(2,1)S(1)} %collective-permute-done.18), channel_id=1, source_target_pairs={{3,2},{0,1},{7,6},{4,5},{11,10},{8,9},{15,14},{12,13},{19,18},{16,... | collective-permute-start | bytes 2359304 | tf_op jit(solution)/shard_map/ppermute | solution.py:124
  542.2 37.4 %collective-permute-start.21 = (bf16[128,3072]{1,0:T(8,128)(2,1)S(1)}, bf16[128,3072]{1,0:T(8,128)(2,1)S(1)}, u32[]{:S(2)}, u32[]{:S(2)}) collective-permute-start(bf16[128,3072]{1,0:T(8,128)(2,1)S(1)} %collective-permute-done.20), channel_id=1, source_target_pairs={{0,2},{3,1},{4,6},{7,5},{8,10},{11,9},{12,14},{15,13},{16,18},{19,... | collective-permute-start | bytes 2359304 | tf_op jit(solution)/shard_map/ppermute | solution.py:125
  595.7 134.8 %all-gather.9.cloned.1.call-start = ((), (), s32[]{:S(2)}) async-start(), calls=%async_computation.10 | async-start | bytes 7077888 | tf_op jit(solution)/shard_map/all_gather | solution.py:140
  667.1 101.9 %all-gather.11.cloned.1.call-start = ((), (), s32[]{:S(2)}) async-start(), calls=%async_computation.11 | async-start | bytes 3538944 | tf_op jit(solution)/shard_map/all_gather | solution.py:151
  (9 other events, 277.4 us)
Sparse Core Ops, SparseCore 0:
  141.0 41.6 reduce-scatter.4
  219.0 71.2 reduce-scatter.6
  293.1 62.9 all-gather.4
  357.6 36.9 all-gather.6
  516.8 39.2 reduce-scatter.8
  595.8 68.5 reduce-scatter.10
  667.3 63.1 all-gather.8
  732.0 36.9 all-gather.10

commit v8 on v7

--- a/solution.py
+++ b/solution.py
@@ -109,9 +109,7 @@
     up = [(i, i + 1) for i in range(nslab - 1)]
     down = [(i + 1, i) for i in range(nslab - 1)]
 
-    def exchange(inner):
-        to_up = inner[rows - halo :]
-        to_down = inner[:halo]
+    def exchange(to_up, to_down):
         if nslab != 4:
             return lax.ppermute(to_up, "slab", up), lax.ppermute(to_down, "slab", down)
         half = halo // 2
@@ -132,39 +130,54 @@
 
     def apply_kernel(field):
         inner = column_pass(field, terms)
-        return row_pass(inner, terms_local, all_blocks, exchange(inner))
+        return row_pass(inner, terms_local, all_blocks, exchange(inner[rows - halo :], inner[:halo]))
 
-    def log_barycenter(kernel_u):
-        value_portion = weight * jnp.log(kernel_u)
-        log_sum = lax.psum_scatter(value_portion, "img", scatter_dimension=0, tiled=True)
-        return lax.all_gather(jnp.exp(log_sum / total_weight), "img", axis=0, tiled=True)
+    def apply_split(edges, inside):
+        inner_edges = column_pass(edges, terms)
+        halos = exchange(inner_edges[halo:], inner_edges[:halo])
+        inner = jnp.concatenate([inner_edges[:halo], column_pass(inside, terms), inner_edges[halo:]], axis=0)
+        return row_pass(inner, terms_local, all_blocks, halos)
+
+    def log_sum(kernel_u):
+        return lax.psum_scatter(weight * jnp.log(kernel_u), "img", scatter_dimension=0, tiled=True)
+
+    def gather_barycenter(part_sum):
+        return lax.all_gather(jnp.exp(part_sum / total_weight), "img", axis=0, tiled=True)
 
     def final_apply(field):
         inner = column_pass(field, terms)
-        halos = exchange(inner)
+        halos = exchange(inner[rows - halo :], inner[:halo])
         if not interior:
             kernel_u = row_pass(inner, terms_local, all_blocks, halos).astype(jnp.float32)
-            return kernel_u, log_barycenter(kernel_u)
+            return kernel_u, gather_barycenter(log_sum(kernel_u))
         inside = row_pass(inner, terms_local, interior).astype(jnp.float32)
-        inside_sum = lax.psum_scatter(weight * jnp.log(inside), "img", scatter_dimension=0, tiled=True)
+        inside_sum = log_sum(inside)
         halos, inside_sum = lax.optimization_barrier((halos, inside_sum))
-        inside_bary = lax.all_gather(jnp.exp(inside_sum / total_weight), "img", axis=0, tiled=True)
         edges = row_pass(inner, terms_local, boundary, halos).astype(jnp.float32)
-        edges_bary = log_barycenter(edges)
-        cut = HALO * width
-        kernel_u = jnp.concatenate([edges[:cut], inside, edges[cut:]], axis=0)
-        barycenter = jnp.concatenate([edges_bary[:cut], inside_bary, edges_bary[cut:]], axis=0)
-        return kernel_u, barycenter
+        edges_bary = gather_barycenter(log_sum(edges))
+        edges_bary, inside_sum = lax.optimization_barrier((edges_bary, inside_sum))
+        inside_bary = gather_barycenter(inside_sum)
+        return (edges, inside), (edges_bary, inside_bary)
+
+    def assemble(parts):
+        edges, inside = parts
+        return jnp.concatenate([edges[:halo], inside, edges[halo:]], axis=0)
 
     masses = image_masses[0]
     scaling = dual_multipliers[0]
-    barycenter = None
+    kernel_v = apply_kernel(scaling.astype(jnp.bfloat16))
     for iteration in range(ITERS):
-        kernel_v = apply_kernel(scaling.astype(jnp.bfloat16))
+        if iteration:
+            if interior:
+                side_edges, side_inside = [(b / k).astype(jnp.bfloat16) for b, k in zip(barycenter, kernel_u)]
+                kernel_v = apply_split(side_edges, side_inside)
+            else:
+                kernel_v = apply_kernel((barycenter / kernel_u).astype(jnp.bfloat16))
         scaled_u = (masses / kernel_v.astype(jnp.float32)).astype(jnp.bfloat16)
         kernel_u, barycenter = final_apply(scaled_u)
-        scaling = barycenter / kernel_u
-    return (barycenter, scaling[None])
+    if interior:
+        kernel_u, barycenter = assemble(kernel_u), assemble(barycenter)
+    return (barycenter, (barycenter / kernel_u)[None])
 
 
 def solution(mesh):

time: 803 us -> 774 us (0.964)
  waiting for transfers between devices: 478 us -> 457 us
  local copies, waits for them, and re-layouts: 32.9 us -> 20.9 us
    all_gather x4, waiting for transfers between devices: 171 us -> 150 us  [gather_barycenter(): lax.all_gather(jnp.exp(part_sum / total_weight), 'img', axis=0, tiled=True)]
    slice x6 -> x4, local copies, waits for them, and re-layouts: 15.7 us -> 5.76 us  [the longest x2 4.21 us: final_apply(): halos = exchange(inner[rows - halo:], inner[:halo])]
    convert_element_type x2 -> x1, other arithmetic: 15.4 us -> 6.73 us  [per_device(): kernel_v = apply_kernel(scaling.astype(jnp.bfloat16))]
    pallas_call x4 -> x5, Pallas kernels: 40.3 us -> 44.5 us  [column_pass(): pl.pallas_call(column_kernel, grid=(rows // tile_rows,), in_specs=[pl.Blo...]
  transfers between devices with their start and end apart: 32 -> 32, of which waited for: 14 -> 13; matrix products, arithmetic and copies ran while one was open for 6% -> 5% of each run, Pallas kernels for 0% -> 1%
where the time goes in v8:
time: 774 us; the launch traced here: 767 us
  waiting for transfers between devices  457 us (59%)
  other arithmetic  110 us (14%)
  Pallas kernels  93.6 us (12%)
  starting transfers between devices  54.3 us (7%)
  local copies, waits for them, and re-layouts  20.9 us (3%)
  between operations  15.7 us (2%)
  blocking collectives  15.4 us (2%)
    all_gather x4, waiting for transfers between devices, gather_barycenter(): lax.all_gather(jnp.exp(part_sum / total_weight), 'img', axis=0, tiled=True)  150 us
    ppermute x4, waiting for transfers between devices, exchange(): first = lax.ppermute(first, 'slab', [(3, 2), (0, 1)])  135 us
    reduce_scatter x4, waiting for transfers between devices, log_sum(): lax.psum_scatter(weight * jnp.log(kernel_u), 'img', scatter_dimension=0,...  124 us
    pallas_call x6, Pallas kernels, row_pass(): pl.pallas_call(functools.partial(row_kernel, blocks=tuple(blocks), has_ha...  49.1 us
    ppermute x4, waiting for transfers between devices, exchange(): first = lax.ppermute(first, 'slab', [(1, 3), (2, 0)])  47 us
    pallas_call x5, Pallas kernels, column_pass(): pl.pallas_call(column_kernel, grid=(rows // tile_rows,), in_specs=[pl.Blo...  44.5 us
    ppermute x4, starting transfers between devices, exchange(): direct_prev = lax.ppermute(to_up, 'slab', [(0, 1), (2, 3)])  24.6 us
    convert_element_type x2, other arithmetic, per_device(): scaled_u = (masses / kernel_v.astype(jnp.float32)).astype(jnp.bfloat16)  18 us
  transfers between devices with their start and end apart: 32, of which 13 were waited for; matrix products, arithmetic and copies ran while one was open for 5% of the time, Pallas kernels for 1%

profile of v8, /device:TPU:0, one launch (start us, length us, event | category | flops | bytes accessed | tf_op | source)
XLA Modules:
  0.0 767.0 jit_solution(4940362710713714984)
XLA Ops:
  8.0 6.7 convert_bitcast_fusion.x_ref
  14.8 5.8 select_reduce_fusion.t_ref
  20.6 10.1 %shard_map.68.refs_1_ = bf16[768,3072]{1,0:T(8,128)(2,1)} custom-call(bf16[768,3072]{1,0:T(8,128)(2,1)} %convert_bitcast_fusion.x_ref, bf16[24,5,128,128]{3,2,1,0:T(8,128)(2,1)} %select_reduce_fusion.t_ref), custom_call_target="tpu_custom_call" | custom-call | tf_op jit(solution)/shard_map/pallas_call | solution.py:43
  38.2 9.1 %collective-permute-start.4 = (bf16[256,3072]{1,0:T(8,128)(2,1)S(1)}, bf16[256,3072]{1,0:T(8,128)(2,1)}, u32[]{:S(2)}, u32[]{:S(2)}) collective-permute-start(bf16[256,3072]{1,0:T(8,128)(2,1)S(1)} %get-tuple-element.37), channel_id=1, source_target_pairs={{0,1},{2,3},{4,5},{6,7},{8,9},{10,11},{12,13},{14,15},{16,17},{18,... | collective-permute-start | bytes 4718600 | tf_op jit(solution)/shard_map/ppermute | solution.py:116
  47.4 11.5 %collective-permute-done = bf16[128,3072]{1,0:T(8,128)(2,1)} collective-permute-done((bf16[128,3072]{1,0:T(8,128)(2,1)S(1)}, bf16[128,3072]{1,0:T(8,128)(2,1)}, u32[]{:S(2)}, u32[]{:S(2)}) %collective-permute-start) | collective-permute-done | bytes 786464 | tf_op jit(solution)/shard_map/ppermute | solution.py:120
  66.3 30.2 %collective-permute-done.1 = bf16[128,3072]{1,0:T(8,128)(2,1)} collective-permute-done((bf16[128,3072]{1,0:T(8,128)(2,1)}, bf16[128,3072]{1,0:T(8,128)(2,1)}, u32[]{:S(2)}, u32[]{:S(2)}) %collective-permute-start.1) | collective-permute-done | bytes 786464 | tf_op jit(solution)/shard_map/ppermute | solution.py:122
  102.3 10.2 %shard_map.69 = bf16[768,3072]{1,0:T(8,128)(2,1)} custom-call(bf16[256,3072]{1,0:T(8,128)(2,1)} %get-tuple-element.51.refs_0_, bf16[768,3072]{1,0:T(8,128)(2,1)} %shard_map.68.refs_1_, bf16[256,3072]{1,0:T(8,128)(2,1)} %get-tuple-element.50.refs_2_, bf16[6,5,128,128]{3,2,1,0:T(8,128)(2,1)} %constant_dynamic-slice_fusion.refs_3_.refs_1_), custom_call_target="tpu_custom_call" | custom-call | tf_op jit(solution)/shard_map/pallas_call | solution.py:87
  112.5 9.0 %fusion.x_ref = bf16[768,3072]{1,0:T(8,128)(2,1)} fusion(f32[1,768,3072]{2,1,0:T(8,128)} %param.5, bf16[768,3072]{1,0:T(8,128)(2,1)} %shard_map.69), kind=kLoop, calls=%fused_computation.5 | loop fusion | flops 7077888 | bytes 18874368 | tf_op jit(solution)/shard_map/convert_element_type | solution.py:176
  121.5 10.1 %shard_map.70.refs_0_.refs_1_ = bf16[768,3072]{1,0:T(8,128)(2,1)} custom-call(bf16[768,3072]{1,0:T(8,128)(2,1)} %fusion.x_ref, bf16[24,5,128,128]{3,2,1,0:T(8,128)(2,1)} %select_reduce_fusion.t_ref), custom_call_target="tpu_custom_call" | custom-call | tf_op jit(solution)/shard_map/pallas_call | solution.py:43
  131.6 5.9 shard_map.71
  153.8 10.4 %collective-permute-done.6 = bf16[128,3072]{1,0:T(8,128)(2,1)S(1)} collective-permute-done((bf16[128,3072]{1,0:T(8,128)(2,1)S(1)}, bf16[128,3072]{1,0:T(8,128)(2,1)S(1)}, u32[]{:S(2)}, u32[]{:S(2)}) %collective-permute-start.6) | collective-permute-done | bytes 786464 | tf_op jit(solution)/shard_map/ppermute | solution.py:120
  167.3 35.6 %collective-permute-done.7 = bf16[128,3072]{1,0:T(8,128)(2,1)S(1)} collective-permute-done((bf16[128,3072]{1,0:T(8,128)(2,1)S(1)}, bf16[128,3072]{1,0:T(8,128)(2,1)S(1)}, u32[]{:S(2)}, u32[]{:S(2)}) %collective-permute-start.7) | collective-permute-done | bytes 786464 | tf_op jit(solution)/shard_map/ppermute | solution.py:122
  204.9 8.5 %shard_map.72 = bf16[512,3072]{1,0:T(8,128)(2,1)} custom-call(bf16[256,3072]{1,0:T(8,128)(2,1)} %get-tuple-element.12.refs_0_, bf16[768,3072]{1,0:T(8,128)(2,1)} %shard_map.70.refs_0_.refs_1_, bf16[256,3072]{1,0:T(8,128)(2,1)} %get-tuple-element.13.refs_2_, bf16[6,5,128,128]{3,2,1,0:T(8,128)(2,1)} %constant_dynamic-slice_fusion.refs_3_.refs_1_), custom_call_target="tpu_custom_call" | custom-call | tf_op jit(solution)/shard_map/pallas_call | solution.py:87
  219.0 15.4 %psum.7 = f32[]{:T(128)} all-reduce(f32[]{:T(128)} %bitcast), channel_id=1, replica_groups=mesh['img'=8,'slab'=4] {'img'}, use_global_device_ids=true, to_apply=%region_3.4 | all-reduce | flops 1 | bytes 8 | tf_op jit(solution)/shard_map/psum | solution.py:106
  234.4 55.9 %reduce-scatter.7.cloned.1.call-done = f32[64,3072]{1,0:T(8,128)} async-done(((f32[512,3072]{1,0:T(8,128)}), f32[64,3072]{1,0:T(8,128)}) %reduce-scatter.7.cloned.1.call-update) | async-done | bytes 786448 | tf_op jit(solution)/shard_map/reduce_scatter | solution.py:142
  293.1 63.1 %all-gather.5.cloned.1.call-done = f32[512,3072]{1,0:T(8,128)} async-done(((f32[64,3072]{1,0:T(8,128)}), f32[512,3072]{1,0:T(8,128)}) %all-gather.5.cloned.1.call-update) | async-done | bytes 6291472 | tf_op jit(solution)/shard_map/all_gather | solution.py:145
  363.2 8.3 %shard_map.73 = bf16[512,3072]{1,0:T(8,128)(2,1)} custom-call(bf16[512,3072]{1,0:T(8,128)(2,1)} %fusion.3.x_ref, bf16[24,5,128,128]{3,2,1,0:T(8,128)(2,1)} %select_reduce_fusion.t_ref), custom_call_target="tpu_custom_call" | custom-call | tf_op jit(solution)/shard_map/pallas_call | solution.py:43
  383.5 14.1 %collective-permute-done.12 = bf16[128,3072]{1,0:T(8,128)(2,1)S(1)} collective-permute-done((bf16[128,3072]{1,0:T(8,128)(2,1)S(1)}, bf16[128,3072]{1,0:T(8,128)(2,1)S(1)}, u32[]{:S(2)}, u32[]{:S(2)}) %collective-permute-start.12) | collective-permute-done | bytes 786464 | tf_op jit(solution)/shard_map/ppermute | solution.py:120
  400.6 33.5 %collective-permute-done.13 = bf16[128,3072]{1,0:T(8,128)(2,1)S(1)} collective-permute-done((bf16[128,3072]{1,0:T(8,128)(2,1)S(1)}, bf16[128,3072]{1,0:T(8,128)(2,1)S(1)}, u32[]{:S(2)}, u32[]{:S(2)}) %collective-permute-start.13) | collective-permute-done | bytes 786464 | tf_op jit(solution)/shard_map/ppermute | solution.py:122
  439.8 6.0 shard_map.74
  449.2 10.2 %shard_map.75 = bf16[768,3072]{1,0:T(8,128)(2,1)} custom-call(bf16[256,3072]{1,0:T(8,128)(2,1)} %get-tuple-element.47.refs_0_, bf16[768,3072]{1,0:T(8,128)(2,1)} %pad_maximum_fusion.1.refs_1_, bf16[256,3072]{1,0:T(8,128)(2,1)} %get-tuple-element.46.refs_2_, bf16[6,5,128,128]{3,2,1,0:T(8,128)(2,1)} %constant_dynamic-slice_fusion.refs_3_.refs_1_), custom_call_target="tpu_custom_call" | custom-call | tf_op jit(solution)/shard_map/pallas_call | solution.py:87
  459.4 9.0 %fusion.1.x_ref = bf16[768,3072]{1,0:T(8,128)(2,1)} fusion(f32[1,768,3072]{2,1,0:T(8,128)} %param.5, bf16[768,3072]{1,0:T(8,128)(2,1)} %shard_map.75), kind=kLoop, calls=%fused_computation.6 | loop fusion | flops 7077888 | bytes 18874368 | tf_op jit(solution)/shard_map/convert_element_type | solution.py:176
  468.4 10.1 %shard_map.76.refs_0_.refs_1_ = bf16[768,3072]{1,0:T(8,128)(2,1)} custom-call(bf16[768,3072]{1,0:T(8,128)(2,1)} %fusion.1.x_ref, bf16[24,5,128,128]{3,2,1,0:T(8,128)(2,1)} %select_reduce_fusion.t_ref), custom_call_target="tpu_custom_call" | custom-call | tf_op jit(solution)/shard_map/pallas_call | solution.py:43
  478.5 5.8 shard_map.77
  500.7 11.0 %collective-permute-done.18 = bf16[128,3072]{1,0:T(8,128)(2,1)S(1)} collective-permute-done((bf16[128,3072]{1,0:T(8,128)(2,1)S(1)}, bf16[128,3072]{1,0:T(8,128)(2,1)S(1)}, u32[]{:S(2)}, u32[]{:S(2)}) %collective-permute-start.18) | collective-permute-done | bytes 786464 | tf_op jit(solution)/shard_map/ppermute | solution.py:120
  514.8 35.6 %collective-permute-done.19 = bf16[128,3072]{1,0:T(8,128)(2,1)S(1)} collective-permute-done((bf16[128,3072]{1,0:T(8,128)(2,1)S(1)}, bf16[128,3072]{1,0:T(8,128)(2,1)S(1)}, u32[]{:S(2)}, u32[]{:S(2)}) %collective-permute-start.19) | collective-permute-done | bytes 786464 | tf_op jit(solution)/shard_map/ppermute | solution.py:122
  552.4 8.5 %shard_map.78 = bf16[512,3072]{1,0:T(8,128)(2,1)} custom-call(bf16[256,3072]{1,0:T(8,128)(2,1)} %get-tuple-element.17.refs_0_, bf16[768,3072]{1,0:T(8,128)(2,1)} %shard_map.76.refs_0_.refs_1_, bf16[256,3072]{1,0:T(8,128)(2,1)} %get-tuple-element.18.refs_2_, bf16[6,5,128,128]{3,2,1,0:T(8,128)(2,1)} %constant_dynamic-slice_fusion.refs_3_.refs_1_), custom_call_target="tpu_custom_call" | custom-call | tf_op jit(solution)/shard_map/pallas_call | solution.py:87
  566.7 68.2 %reduce-scatter.11.cloned.1.call-done = f32[64,3072]{1,0:T(8,128)} async-done(((f32[512,3072]{1,0:T(8,128)}), f32[64,3072]{1,0:T(8,128)}) %reduce-scatter.11.cloned.1.call-update) | async-done | bytes 786448 | tf_op jit(solution)/shard_map/reduce_scatter | solution.py:142
  637.6 63.2 %all-gather.9.cloned.1.call-done = f32[512,3072]{1,0:T(8,128)} async-done(((f32[64,3072]{1,0:T(8,128)}), f32[512,3072]{1,0:T(8,128)}) %all-gather.9.cloned.1.call-update) | async-done | bytes 6291472 | tf_op jit(solution)/shard_map/all_gather | solution.py:145
  716.0 24.1 %all-gather.11.cloned.1.call-done = f32[256,3072]{1,0:T(8,128)} async-done(((f32[32,3072]{1,0:T(8,128)}), f32[256,3072]{1,0:T(8,128)}) %all-gather.11.cloned.1.call-update) | async-done | bytes 3145744 | tf_op jit(solution)/shard_map/all_gather | solution.py:145
  740.1 11.9 %maximum_divide_fusion = f32[1,768,3072]{2,1,0:T(8,128)} fusion(f32[1,256,3072]{2,1,0:T(8,128)} %get-tuple-element.25, f32[1,256,3072]{2,1,0:T(8,128)} %bitcast.21, f32[1,256,3072]{2,1,0:T(8,128)} %get-tuple-element.24, f32[1,256,3072]{2,1,0:T(8,128)} %get-tuple-element.23, f32[1,256,3072]{2,1,0:T(8,128)} %convert_bitcast_fusion.1, ...), kind=kLoop, calls=%fused_computation.2 | loop fusion | flops 11796480 | bytes 28311552 | tf_op jit(solution)/shard_map/div | solution.py:180
  752.0 7.7 %pad_maximum_fusion = f32[768,3072]{1,0:T(8,128)} fusion(f32[256,3072]{1,0:T(8,128)} %get-tuple-element.26, f32[256,3072]{1,0:T(8,128)S(1)} %copy-done.5, f32[256,3072]{1,0:T(8,128)} %get-tuple-element.27), kind=kLoop, calls=%fused_computation.1 | loop fusion | flops 4718592 | bytes 18874368 | tf_op jit(solution)/shard_map/concatenate | solution.py:164
  (124 shorter events, 126.6 us)
Async XLA Ops:
  7.2 197.7 %reduce-scatter.5.cloned.1.call-start = ((), (), s32[]{:S(2)}) async-start(), calls=%async_computation.4 | async-start | bytes 3538944 | tf_op jit(solution)/shard_map/reduce_scatter | solution.py:142
  32.8 28.2 %collective-permute-start.2 = (bf16[128,3072]{1,0:T(8,128)(2,1)S(1)}, bf16[128,3072]{1,0:T(8,128)(2,1)}, u32[]{:S(2)}, u32[]{:S(2)}) collective-permute-start(bf16[128,3072]{1,0:T(8,128)(2,1)S(1)} %get-tuple-element.38), channel_id=1, source_target_pairs={{1,0},{2,3},{5,4},{6,7},{9,8},{10,11},{13,12},{14,15},{17,16},{18,... | collective-permute-start | bytes 2359304 | tf_op jit(solution)/shard_map/ppermute | solution.py:121
  34.3 24.6 %collective-permute-start = (bf16[128,3072]{1,0:T(8,128)(2,1)S(1)}, bf16[128,3072]{1,0:T(8,128)(2,1)}, u32[]{:S(2)}, u32[]{:S(2)}) collective-permute-start(bf16[128,3072]{1,0:T(8,128)(2,1)S(1)} %get-tuple-element.39), channel_id=1, source_target_pairs={{1,3},{2,0},{5,7},{6,4},{9,11},{10,8},{13,15},{14,12},{17,19},{18,... | collective-permute-start | bytes 2359304 | tf_op jit(solution)/shard_map/ppermute | solution.py:120
  36.9 62.0 %collective-permute-start.5 = (bf16[256,3072]{1,0:T(8,128)(2,1)}, bf16[256,3072]{1,0:T(8,128)(2,1)S(1)}, u32[]{:S(2)}, u32[]{:S(2)}) collective-permute-start(bf16[256,3072]{1,0:T(8,128)(2,1)} %get-tuple-element.36), channel_id=1, source_target_pairs={{1,0},{3,2},{5,4},{7,6},{9,8},{11,10},{13,12},{15,14},{17,16},{19,... | collective-permute-start | bytes 4718600 | tf_op jit(solution)/shard_map/ppermute | solution.py:117
  38.2 60.7 %collective-permute-start.4 = (bf16[256,3072]{1,0:T(8,128)(2,1)S(1)}, bf16[256,3072]{1,0:T(8,128)(2,1)}, u32[]{:S(2)}, u32[]{:S(2)}) collective-permute-start(bf16[256,3072]{1,0:T(8,128)(2,1)S(1)} %get-tuple-element.37), channel_id=1, source_target_pairs={{0,1},{2,3},{4,5},{6,7},{8,9},{10,11},{12,13},{14,15},{16,17},{18,... | collective-permute-start | bytes 4718600 | tf_op jit(solution)/shard_map/ppermute | solution.py:116
  58.9 37.6 %collective-permute-start.1 = (bf16[128,3072]{1,0:T(8,128)(2,1)}, bf16[128,3072]{1,0:T(8,128)(2,1)}, u32[]{:S(2)}, u32[]{:S(2)}) collective-permute-start(bf16[128,3072]{1,0:T(8,128)(2,1)} %collective-permute-done), channel_id=1, source_target_pairs={{3,2},{0,1},{7,6},{4,5},{11,10},{8,9},{15,14},{12,13},{19,18},{16,... | collective-permute-start | bytes 2359304 | tf_op jit(solution)/shard_map/ppermute | solution.py:122
  61.1 36.6 %collective-permute-start.3 = (bf16[128,3072]{1,0:T(8,128)(2,1)}, bf16[128,3072]{1,0:T(8,128)(2,1)}, u32[]{:S(2)}, u32[]{:S(2)}) collective-permute-start(bf16[128,3072]{1,0:T(8,128)(2,1)} %collective-permute-done.2), channel_id=1, source_target_pairs={{0,2},{3,1},{4,6},{7,5},{8,10},{11,9},{12,14},{15,13},{16,18},{19,... | collective-permute-start | bytes 2359304 | tf_op jit(solution)/shard_map/ppermute | solution.py:123
  140.9 149.4 %reduce-scatter.7.cloned.1.call-start = ((), (), s32[]{:S(2)}) async-start(), calls=%async_computation.5 | async-start | bytes 7077888 | tf_op jit(solution)/shard_map/reduce_scatter | solution.py:142
  143.0 23.0 %collective-permute-start.8 = (bf16[128,3072]{1,0:T(8,128)(2,1)S(1)}, bf16[128,3072]{1,0:T(8,128)(2,1)S(1)}, u32[]{:S(2)}, u32[]{:S(2)}) collective-permute-start(bf16[128,3072]{1,0:T(8,128)(2,1)S(1)} %get-tuple-element.34), channel_id=1, source_target_pairs={{1,0},{2,3},{5,4},{6,7},{9,8},{10,11},{13,12},{14,15},{17,16},{18,... | collective-permute-start | bytes 2359304 | tf_op jit(solution)/shard_map/ppermute | solution.py:121
  144.3 20.0 %collective-permute-start.6 = (bf16[128,3072]{1,0:T(8,128)(2,1)S(1)}, bf16[128,3072]{1,0:T(8,128)(2,1)S(1)}, u32[]{:S(2)}, u32[]{:S(2)}) collective-permute-start(bf16[128,3072]{1,0:T(8,128)(2,1)S(1)} %get-tuple-element.35), channel_id=1, source_target_pairs={{1,3},{2,0},{5,7},{6,4},{9,11},{10,8},{13,15},{14,12},{17,19},{18,... | collective-permute-start | bytes 2359304 | tf_op jit(solution)/shard_map/ppermute | solution.py:120
  147.7 55.3 %collective-permute-start.11 = (bf16[256,3072]{1,0:T(8,128)(2,1)S(1)}, bf16[256,3072]{1,0:T(8,128)(2,1)S(1)}, u32[]{:S(2)}, u32[]{:S(2)}) collective-permute-start(bf16[256,3072]{1,0:T(8,128)(2,1)S(1)} %get-tuple-element.32), channel_id=1, source_target_pairs={{1,0},{3,2},{5,4},{7,6},{9,8},{11,10},{13,12},{15,14},{17,16},{19,... | collective-permute-start | bytes 4718600 | tf_op jit(solution)/shard_map/ppermute | solution.py:117
  149.0 54.0 %collective-permute-start.10 = (bf16[256,3072]{1,0:T(8,128)(2,1)S(1)}, bf16[256,3072]{1,0:T(8,128)(2,1)S(1)}, u32[]{:S(2)}, u32[]{:S(2)}) collective-permute-start(bf16[256,3072]{1,0:T(8,128)(2,1)S(1)} %get-tuple-element.33), channel_id=1, source_target_pairs={{0,1},{2,3},{4,5},{6,7},{8,9},{10,11},{12,13},{14,15},{16,17},{18,... | collective-permute-start | bytes 4718600 | tf_op jit(solution)/shard_map/ppermute | solution.py:116
  164.3 38.6 %collective-permute-start.7 = (bf16[128,3072]{1,0:T(8,128)(2,1)S(1)}, bf16[128,3072]{1,0:T(8,128)(2,1)S(1)}, u32[]{:S(2)}, u32[]{:S(2)}) collective-permute-start(bf16[128,3072]{1,0:T(8,128)(2,1)S(1)} %collective-permute-done.6), channel_id=1, source_target_pairs={{3,2},{0,1},{7,6},{4,5},{11,10},{8,9},{15,14},{12,13},{19,18},{16,... | collective-permute-start | bytes 2359304 | tf_op jit(solution)/shard_map/ppermute | solution.py:122
  166.0 37.0 %collective-permute-start.9 = (bf16[128,3072]{1,0:T(8,128)(2,1)S(1)}, bf16[128,3072]{1,0:T(8,128)(2,1)S(1)}, u32[]{:S(2)}, u32[]{:S(2)}) collective-permute-start(bf16[128,3072]{1,0:T(8,128)(2,1)S(1)} %collective-permute-done.8), channel_id=1, source_target_pairs={{0,2},{3,1},{4,6},{7,5},{8,10},{11,9},{12,14},{15,13},{16,18},{19,... | collective-permute-start | bytes 2359304 | tf_op jit(solution)/shard_map/ppermute | solution.py:123
  218.9 137.3 %all-gather.5.cloned.1.call-start = ((), (), s32[]{:S(2)}) async-start(), calls=%async_computation.6 | async-start | bytes 7077888 | tf_op jit(solution)/shard_map/all_gather | solution.py:145
  293.0 143.2 %all-gather.7.cloned.1.call-start = ((), (), s32[]{:S(2)}) async-start(), calls=%async_computation.7 | async-start | bytes 3538944 | tf_op jit(solution)/shard_map/all_gather | solution.py:145
  357.6 194.8 %reduce-scatter.9.cloned.1.call-start = ((), (), s32[]{:S(2)}) async-start(), calls=%async_computation.8 | async-start | bytes 3538944 | tf_op jit(solution)/shard_map/reduce_scatter | solution.py:142
  373.6 25.4 %collective-permute-start.14 = (bf16[128,3072]{1,0:T(8,128)(2,1)S(1)}, bf16[128,3072]{1,0:T(8,128)(2,1)S(1)}, u32[]{:S(2)}, u32[]{:S(2)}) collective-permute-start(bf16[128,3072]{1,0:T(8,128)(2,1)S(1)} %get-tuple-element.42), channel_id=1, source_target_pairs={{1,0},{2,3},{5,4},{6,7},{9,8},{10,11},{13,12},{14,15},{17,16},{18,... | collective-permute-start | bytes 2359304 | tf_op jit(solution)/shard_map/ppermute | solution.py:121
  374.9 22.7 %collective-permute-start.12 = (bf16[128,3072]{1,0:T(8,128)(2,1)S(1)}, bf16[128,3072]{1,0:T(8,128)(2,1)S(1)}, u32[]{:S(2)}, u32[]{:S(2)}) collective-permute-start(bf16[128,3072]{1,0:T(8,128)(2,1)S(1)} %get-tuple-element.43), channel_id=1, source_target_pairs={{1,3},{2,0},{5,7},{6,4},{9,11},{10,8},{13,15},{14,12},{17,19},{18,... | collective-permute-start | bytes 2359304 | tf_op jit(solution)/shard_map/ppermute | solution.py:120
  376.5 57.8 %collective-permute-start.17 = (bf16[256,3072]{1,0:T(8,128)(2,1)S(1)}, bf16[256,3072]{1,0:T(8,128)(2,1)S(1)}, u32[]{:S(2)}, u32[]{:S(2)}) collective-permute-start(bf16[256,3072]{1,0:T(8,128)(2,1)S(1)} %get-tuple-element.40), channel_id=1, source_target_pairs={{1,0},{3,2},{5,4},{7,6},{9,8},{11,10},{13,12},{15,14},{17,16},{19,... | collective-permute-start | bytes 4718600 | tf_op jit(solution)/shard_map/ppermute | solution.py:117
  377.8 56.5 %collective-permute-start.16 = (bf16[256,3072]{1,0:T(8,128)(2,1)S(1)}, bf16[256,3072]{1,0:T(8,128)(2,1)S(1)}, u32[]{:S(2)}, u32[]{:S(2)}) collective-permute-start(bf16[256,3072]{1,0:T(8,128)(2,1)S(1)} %get-tuple-element.41), channel_id=1, source_target_pairs={{0,1},{2,3},{4,5},{6,7},{8,9},{10,11},{12,13},{14,15},{16,17},{18,... | collective-permute-start | bytes 4718600 | tf_op jit(solution)/shard_map/ppermute | solution.py:116
  397.6 36.5 %collective-permute-start.13 = (bf16[128,3072]{1,0:T(8,128)(2,1)S(1)}, bf16[128,3072]{1,0:T(8,128)(2,1)S(1)}, u32[]{:S(2)}, u32[]{:S(2)}) collective-permute-start(bf16[128,3072]{1,0:T(8,128)(2,1)S(1)} %collective-permute-done.12), channel_id=1, source_target_pairs={{3,2},{0,1},{7,6},{4,5},{11,10},{8,9},{15,14},{12,13},{19,18},{16,... | collective-permute-start | bytes 2359304 | tf_op jit(solution)/shard_map/ppermute | solution.py:122
  399.0 35.1 %collective-permute-start.15 = (bf16[128,3072]{1,0:T(8,128)(2,1)S(1)}, bf16[128,3072]{1,0:T(8,128)(2,1)S(1)}, u32[]{:S(2)}, u32[]{:S(2)}) collective-permute-start(bf16[128,3072]{1,0:T(8,128)(2,1)S(1)} %collective-permute-done.14), channel_id=1, source_target_pairs={{0,2},{3,1},{4,6},{7,5},{8,10},{11,9},{12,14},{15,13},{16,18},{19,... | collective-permute-start | bytes 2359304 | tf_op jit(solution)/shard_map/ppermute | solution.py:123
  487.8 147.0 %reduce-scatter.11.cloned.1.call-start = ((), (), s32[]{:S(2)}) async-start(), calls=%async_computation.9 | async-start | bytes 7077888 | tf_op jit(solution)/shard_map/reduce_scatter | solution.py:142
  489.9 23.5 %collective-permute-start.20 = (bf16[128,3072]{1,0:T(8,128)(2,1)S(1)}, bf16[128,3072]{1,0:T(8,128)(2,1)S(1)}, u32[]{:S(2)}, u32[]{:S(2)}) collective-permute-start(bf16[128,3072]{1,0:T(8,128)(2,1)S(1)} %get-tuple-element.30), channel_id=1, source_target_pairs={{1,0},{2,3},{5,4},{6,7},{9,8},{10,11},{13,12},{14,15},{17,16},{18,... | collective-permute-start | bytes 2359304 | tf_op jit(solution)/shard_map/ppermute | solution.py:121
  491.2 20.5 %collective-permute-start.18 = (bf16[128,3072]{1,0:T(8,128)(2,1)S(1)}, bf16[128,3072]{1,0:T(8,128)(2,1)S(1)}, u32[]{:S(2)}, u32[]{:S(2)}) collective-permute-start(bf16[128,3072]{1,0:T(8,128)(2,1)S(1)} %get-tuple-element.31), channel_id=1, source_target_pairs={{1,3},{2,0},{5,7},{6,4},{9,11},{10,8},{13,15},{14,12},{17,19},{18,... | collective-permute-start | bytes 2359304 | tf_op jit(solution)/shard_map/ppermute | solution.py:120
  494.6 55.9 %collective-permute-start.23 = (bf16[256,3072]{1,0:T(8,128)(2,1)S(1)}, bf16[256,3072]{1,0:T(8,128)(2,1)S(1)}, u32[]{:S(2)}, u32[]{:S(2)}) collective-permute-start(bf16[256,3072]{1,0:T(8,128)(2,1)S(1)} %get-tuple-element.28), channel_id=1, source_target_pairs={{1,0},{3,2},{5,4},{7,6},{9,8},{11,10},{13,12},{15,14},{17,16},{19,... | collective-permute-start | bytes 4718600 | tf_op jit(solution)/shard_map/ppermute | solution.py:117
  495.9 54.6 %collective-permute-start.22 = (bf16[256,3072]{1,0:T(8,128)(2,1)S(1)}, bf16[256,3072]{1,0:T(8,128)(2,1)S(1)}, u32[]{:S(2)}, u32[]{:S(2)}) collective-permute-start(bf16[256,3072]{1,0:T(8,128)(2,1)S(1)} %get-tuple-element.29), channel_id=1, source_target_pairs={{0,1},{2,3},{4,5},{6,7},{8,9},{10,11},{12,13},{14,15},{16,17},{18,... | collective-permute-start | bytes 4718600 | tf_op jit(solution)/shard_map/ppermute | solution.py:116
  511.7 38.7 %collective-permute-start.19 = (bf16[128,3072]{1,0:T(8,128)(2,1)S(1)}, bf16[128,3072]{1,0:T(8,128)(2,1)S(1)}, u32[]{:S(2)}, u32[]{:S(2)}) collective-permute-start(bf16[128,3072]{1,0:T(8,128)(2,1)S(1)} %collective-permute-done.18), channel_id=1, source_target_pairs={{3,2},{0,1},{7,6},{4,5},{11,10},{8,9},{15,14},{12,13},{19,18},{16,... | collective-permute-start | bytes 2359304 | tf_op jit(solution)/shard_map/ppermute | solution.py:122
  513.4 37.0 %collective-permute-start.21 = (bf16[128,3072]{1,0:T(8,128)(2,1)S(1)}, bf16[128,3072]{1,0:T(8,128)(2,1)S(1)}, u32[]{:S(2)}, u32[]{:S(2)}) collective-permute-start(bf16[128,3072]{1,0:T(8,128)(2,1)S(1)} %collective-permute-done.20), channel_id=1, source_target_pairs={{0,2},{3,1},{4,6},{7,5},{8,10},{11,9},{12,14},{15,13},{16,18},{19,... | collective-permute-start | bytes 2359304 | tf_op jit(solution)/shard_map/ppermute | solution.py:123
  566.4 134.5 %all-gather.9.cloned.1.call-start = ((), (), s32[]{:S(2)}) async-start(), calls=%async_computation.10 | async-start | bytes 7077888 | tf_op jit(solution)/shard_map/all_gather | solution.py:145
  637.6 102.5 %all-gather.11.cloned.1.call-start = ((), (), s32[]{:S(2)}) async-start(), calls=%async_computation.11 | async-start | bytes 3538944 | tf_op jit(solution)/shard_map/all_gather | solution.py:145
  (13 other events, 581.3 us)
Sparse Core Ops, SparseCore 0:
  141.0 41.6 reduce-scatter.4
  219.0 71.2 reduce-scatter.6
  293.2 62.9 all-gather.4
  357.7 36.9 all-gather.6
  488.0 38.8 reduce-scatter.8
  566.5 68.3 reduce-scatter.10
  637.7 63.1 all-gather.8
  703.1 36.9 all-gather.10

commit v9 on v8

--- a/solution.py
+++ b/solution.py
@@ -18,10 +18,14 @@
     return jnp.sum(picked, axis=2)
 
 
-def column_kernel(x_ref, t_ref, o_ref):
+def column_kernel(*refs):
+    *in_refs, t_ref, o_ref = refs
     nblocks = t_ref.shape[0]
     width = t_ref.shape[2]
-    x = x_ref[...].astype(jnp.bfloat16)
+    if len(in_refs) == 2:
+        x = (in_refs[0][...] / in_refs[1][...].astype(jnp.float32)).astype(jnp.bfloat16)
+    else:
+        x = in_refs[0][...].astype(jnp.bfloat16)
     for b in range(nblocks):
         acc = None
         for o in range(OFFSETS):
@@ -38,18 +42,17 @@
         o_ref[:, b * width : (b + 1) * width] = acc.astype(o_ref.dtype)
 
 
-def column_pass(field, terms, tile_rows=256):
-    rows, cols = field.shape
+def column_pass(fields, terms, tile_rows=256):
+    fields = fields if isinstance(fields, tuple) else (fields,)
+    rows, cols = fields[0].shape
+    tile = pl.BlockSpec((tile_rows, cols), lambda r: (r, 0))
     return pl.pallas_call(
         column_kernel,
         grid=(rows // tile_rows,),
-        in_specs=[
-            pl.BlockSpec((tile_rows, cols), lambda r: (r, 0)),
-            pl.BlockSpec(terms.shape, lambda r: (0, 0, 0, 0)),
-        ],
-        out_specs=pl.BlockSpec((tile_rows, cols), lambda r: (r, 0)),
+        in_specs=[tile] * len(fields) + [pl.BlockSpec(terms.shape, lambda r: (0, 0, 0, 0))],
+        out_specs=tile,
         out_shape=jax.ShapeDtypeStruct((rows, cols), jnp.bfloat16),
-    )(field, terms)
+    )(*fields, terms)
 
 
 def row_kernel(*refs, blocks, has_halo):
@@ -165,7 +168,7 @@
 
     masses = image_masses[0]
     scaling = dual_multipliers[0]
-    kernel_v = apply_kernel(scaling.astype(jnp.bfloat16))
+    kernel_v = apply_kernel(scaling)
     for iteration in range(ITERS):
         if iteration:
             if interior:
@@ -173,8 +176,7 @@
                 kernel_v = apply_split(side_edges, side_inside)
             else:
                 kernel_v = apply_kernel((barycenter / kernel_u).astype(jnp.bfloat16))
-        scaled_u = (masses / kernel_v.astype(jnp.float32)).astype(jnp.bfloat16)
-        kernel_u, barycenter = final_apply(scaled_u)
+        kernel_u, barycenter = final_apply((masses, kernel_v))
     if interior:
         kernel_u, barycenter = assemble(kernel_u), assemble(barycenter)
     return (barycenter, (barycenter / kernel_u)[None])

time: 774 us -> 752 us (0.972)
  other arithmetic: 110 us -> 88.4 us
    convert_element_type x3 -> x0, other arithmetic: 24.7 us -> none  [the longest x2 18 us: per_device(): scaled_u = (masses / kernel_v.astype(jnp.float32)).astype(jnp.bfloat16)]
  transfers between devices with their start and end apart: 32 -> 32, of which waited for: 13 -> 13; matrix products, arithmetic and copies ran while one was open for 5% -> 6% of each run, Pallas kernels for 1% -> 1%
where the time goes in v9:
time: 752 us; the launch traced here: 751 us
  waiting for transfers between devices  457 us (61%)
  Pallas kernels  99.7 us (13%)
  other arithmetic  88.4 us (12%)
  starting transfers between devices  54.1 us (7%)
  local copies, waits for them, and re-layouts  21 us (3%)
  blocking collectives  15.4 us (2%)
  between operations  15.3 us (2%)
    all_gather x4, waiting for transfers between devices, gather_barycenter(): lax.all_gather(jnp.exp(part_sum / total_weight), 'img', axis=0, tiled=True)  150 us
    ppermute x4, waiting for transfers between devices, exchange(): first = lax.ppermute(first, 'slab', [(3, 2), (0, 1)])  135 us
    reduce_scatter x4, waiting for transfers between devices, log_sum(): lax.psum_scatter(weight * jnp.log(kernel_u), 'img', scatter_dimension=0,...  124 us
    pallas_call x5, Pallas kernels, column_pass(): pl.pallas_call(column_kernel, grid=(rows // tile_rows,), in_specs=[tile]...  50.7 us
    pallas_call x6, Pallas kernels, row_pass(): pl.pallas_call(functools.partial(row_kernel, blocks=tuple(blocks), has_ha...  49 us
    ppermute x4, waiting for transfers between devices, exchange(): first = lax.ppermute(first, 'slab', [(1, 3), (2, 0)])  46.8 us
    ppermute x4, starting transfers between devices, exchange(): direct_prev = lax.ppermute(to_up, 'slab', [(0, 1), (2, 3)])  24.6 us
    mul x4, other arithmetic, log_sum(): weight * jnp.log(kernel_u)  17.9 us
  transfers between devices with their start and end apart: 32, of which 13 were waited for; matrix products, arithmetic and copies ran while one was open for 6% of the time, Pallas kernels for 1%

profile of v9, /device:TPU:0, one launch (start us, length us, event | category | flops | bytes accessed | tf_op | source)
XLA Modules:
  0.0 750.7 jit_solution(6393010875235655893)
XLA Ops:
  8.1 8.3 %select_reduce_fusion.refs_1_.refs_2_ = bf16[24,5,128,128]{3,2,1,0:T(8,128)(2,1)} fusion(pred[24,5,3]{2,1,0:T(8,128)(4,1)S(1)} %broadcast_compare_fusion, bf16[24,3,128,128]{3,2,1,0:T(8,128)(2,1)} %param.8), kind=kLoop, calls=%fused_computation | loop fusion | flops 9830400 | bytes 6291816 | tf_op jit(solution)/shard_map/reduce_sum | solution.py:18
  16.4 10.9 %shard_map.68.refs_1_ = bf16[768,3072]{1,0:T(8,128)(2,1)} custom-call(f32[768,3072]{1,0:T(8,128)} %bitcast.17, bf16[24,5,128,128]{3,2,1,0:T(8,128)(2,1)} %select_reduce_fusion.refs_1_.refs_2_), custom_call_target="tpu_custom_call" | custom-call | tf_op jit(solution)/shard_map/pallas_call | solution.py:49
  34.8 9.1 %collective-permute-start.4 = (bf16[256,3072]{1,0:T(8,128)(2,1)S(1)}, bf16[256,3072]{1,0:T(8,128)(2,1)}, u32[]{:S(2)}, u32[]{:S(2)}) collective-permute-start(bf16[256,3072]{1,0:T(8,128)(2,1)S(1)} %get-tuple-element.37), channel_id=1, source_target_pairs={{0,1},{2,3},{4,5},{6,7},{8,9},{10,11},{12,13},{14,15},{16,17},{18,... | collective-permute-start | bytes 4718600 | tf_op jit(solution)/shard_map/ppermute | solution.py:119
  44.0 11.5 %collective-permute-done = bf16[128,3072]{1,0:T(8,128)(2,1)} collective-permute-done((bf16[128,3072]{1,0:T(8,128)(2,1)S(1)}, bf16[128,3072]{1,0:T(8,128)(2,1)}, u32[]{:S(2)}, u32[]{:S(2)}) %collective-permute-start) | collective-permute-done | bytes 786464 | tf_op jit(solution)/shard_map/ppermute | solution.py:123
  62.8 30.3 %collective-permute-done.1 = bf16[128,3072]{1,0:T(8,128)(2,1)} collective-permute-done((bf16[128,3072]{1,0:T(8,128)(2,1)}, bf16[128,3072]{1,0:T(8,128)(2,1)}, u32[]{:S(2)}, u32[]{:S(2)}) %collective-permute-start.1) | collective-permute-done | bytes 786464 | tf_op jit(solution)/shard_map/ppermute | solution.py:125
  98.9 10.2 %shard_map.69.refs_1_ = bf16[768,3072]{1,0:T(8,128)(2,1)} custom-call(bf16[256,3072]{1,0:T(8,128)(2,1)} %get-tuple-element.51.refs_0_, bf16[768,3072]{1,0:T(8,128)(2,1)} %shard_map.68.refs_1_, bf16[256,3072]{1,0:T(8,128)(2,1)} %get-tuple-element.50.refs_2_, bf16[6,5,128,128]{3,2,1,0:T(8,128)(2,1)} %constant_dynamic-slice_fusion.refs_3_.refs_1_), custom_call_target="tpu_custom_call" | custom-call | tf_op jit(solution)/shard_map/pallas_call | solution.py:90
  109.1 12.7 %shard_map.70.refs_0_.refs_1_ = bf16[768,3072]{1,0:T(8,128)(2,1)} custom-call(f32[768,3072]{1,0:T(8,128)} %bitcast.14, bf16[768,3072]{1,0:T(8,128)(2,1)} %shard_map.69.refs_1_, bf16[24,5,128,128]{3,2,1,0:T(8,128)(2,1)} %select_reduce_fusion.refs_1_.refs_2_), custom_call_target="tpu_custom_call" | custom-call | tf_op jit(solution)/shard_map/pallas_call | solution.py:49
  121.8 5.8 shard_map.71
  144.1 10.4 %collective-permute-done.6 = bf16[128,3072]{1,0:T(8,128)(2,1)S(1)} collective-permute-done((bf16[128,3072]{1,0:T(8,128)(2,1)S(1)}, bf16[128,3072]{1,0:T(8,128)(2,1)S(1)}, u32[]{:S(2)}, u32[]{:S(2)}) %collective-permute-start.6) | collective-permute-done | bytes 786464 | tf_op jit(solution)/shard_map/ppermute | solution.py:123
  157.6 35.6 %collective-permute-done.7 = bf16[128,3072]{1,0:T(8,128)(2,1)S(1)} collective-permute-done((bf16[128,3072]{1,0:T(8,128)(2,1)S(1)}, bf16[128,3072]{1,0:T(8,128)(2,1)S(1)}, u32[]{:S(2)}, u32[]{:S(2)}) %collective-permute-start.7) | collective-permute-done | bytes 786464 | tf_op jit(solution)/shard_map/ppermute | solution.py:125
  195.3 8.5 %shard_map.72 = bf16[512,3072]{1,0:T(8,128)(2,1)} custom-call(bf16[256,3072]{1,0:T(8,128)(2,1)} %get-tuple-element.12.refs_0_, bf16[768,3072]{1,0:T(8,128)(2,1)} %shard_map.70.refs_0_.refs_1_, bf16[256,3072]{1,0:T(8,128)(2,1)} %get-tuple-element.13.refs_2_, bf16[6,5,128,128]{3,2,1,0:T(8,128)(2,1)} %constant_dynamic-slice_fusion.refs_3_.refs_1_), custom_call_target="tpu_custom_call" | custom-call | tf_op jit(solution)/shard_map/pallas_call | solution.py:90
  209.3 15.4 %psum.7 = f32[]{:T(128)} all-reduce(f32[]{:T(128)} %bitcast), channel_id=1, replica_groups=mesh['img'=8,'slab'=4] {'img'}, use_global_device_ids=true, to_apply=%region_3.4 | all-reduce | flops 1 | bytes 8 | tf_op jit(solution)/shard_map/psum | solution.py:109
  224.7 55.9 %reduce-scatter.7.cloned.1.call-done = f32[64,3072]{1,0:T(8,128)} async-done(((f32[512,3072]{1,0:T(8,128)}), f32[64,3072]{1,0:T(8,128)}) %reduce-scatter.7.cloned.1.call-update) | async-done | bytes 786448 | tf_op jit(solution)/shard_map/reduce_scatter | solution.py:145
  283.4 63.1 %all-gather.5.cloned.1.call-done = f32[512,3072]{1,0:T(8,128)} async-done(((f32[64,3072]{1,0:T(8,128)}), f32[512,3072]{1,0:T(8,128)}) %all-gather.5.cloned.1.call-update) | async-done | bytes 6291472 | tf_op jit(solution)/shard_map/all_gather | solution.py:148
  348.0 5.5 fusion.1.refs_0_
  353.5 8.3 %shard_map.73 = bf16[512,3072]{1,0:T(8,128)(2,1)} custom-call(bf16[512,3072]{1,0:T(8,128)(2,1)} %fusion.1.refs_0_, bf16[24,5,128,128]{3,2,1,0:T(8,128)(2,1)} %select_reduce_fusion.refs_1_.refs_2_), custom_call_target="tpu_custom_call" | custom-call | tf_op jit(solution)/shard_map/pallas_call | solution.py:49
  368.3 5.8 collective-permute-start.16
  374.1 13.8 %collective-permute-done.12 = bf16[128,3072]{1,0:T(8,128)(2,1)S(1)} collective-permute-done((bf16[128,3072]{1,0:T(8,128)(2,1)S(1)}, bf16[128,3072]{1,0:T(8,128)(2,1)S(1)}, u32[]{:S(2)}, u32[]{:S(2)}) %collective-permute-start.12) | collective-permute-done | bytes 786464 | tf_op jit(solution)/shard_map/ppermute | solution.py:123
  390.8 33.9 %collective-permute-done.13 = bf16[128,3072]{1,0:T(8,128)(2,1)S(1)} collective-permute-done((bf16[128,3072]{1,0:T(8,128)(2,1)S(1)}, bf16[128,3072]{1,0:T(8,128)(2,1)S(1)}, u32[]{:S(2)}, u32[]{:S(2)}) %collective-permute-start.13) | collective-permute-done | bytes 786464 | tf_op jit(solution)/shard_map/ppermute | solution.py:125
  430.3 6.0 shard_map.74
  439.7 10.2 %shard_map.75.refs_1_ = bf16[768,3072]{1,0:T(8,128)(2,1)} custom-call(bf16[256,3072]{1,0:T(8,128)(2,1)} %get-tuple-element.47.refs_0_, bf16[768,3072]{1,0:T(8,128)(2,1)} %pad_maximum_fusion.1.refs_1_, bf16[256,3072]{1,0:T(8,128)(2,1)} %get-tuple-element.46.refs_2_, bf16[6,5,128,128]{3,2,1,0:T(8,128)(2,1)} %constant_dynamic-slice_fusion.refs_3_.refs_1_), custom_call_target="tpu_custom_call" | custom-call | tf_op jit(solution)/shard_map/pallas_call | solution.py:90
  449.9 12.8 %shard_map.76.refs_0_.refs_1_ = bf16[768,3072]{1,0:T(8,128)(2,1)} custom-call(f32[768,3072]{1,0:T(8,128)} %bitcast.15, bf16[768,3072]{1,0:T(8,128)(2,1)} %shard_map.75.refs_1_, bf16[24,5,128,128]{3,2,1,0:T(8,128)(2,1)} %select_reduce_fusion.refs_1_.refs_2_), custom_call_target="tpu_custom_call" | custom-call | tf_op jit(solution)/shard_map/pallas_call | solution.py:49
  462.7 5.8 shard_map.77
  484.9 11.0 %collective-permute-done.18 = bf16[128,3072]{1,0:T(8,128)(2,1)S(1)} collective-permute-done((bf16[128,3072]{1,0:T(8,128)(2,1)S(1)}, bf16[128,3072]{1,0:T(8,128)(2,1)S(1)}, u32[]{:S(2)}, u32[]{:S(2)}) %collective-permute-start.18) | collective-permute-done | bytes 786464 | tf_op jit(solution)/shard_map/ppermute | solution.py:123
  498.9 35.7 %collective-permute-done.19 = bf16[128,3072]{1,0:T(8,128)(2,1)S(1)} collective-permute-done((bf16[128,3072]{1,0:T(8,128)(2,1)S(1)}, bf16[128,3072]{1,0:T(8,128)(2,1)S(1)}, u32[]{:S(2)}, u32[]{:S(2)}) %collective-permute-start.19) | collective-permute-done | bytes 786464 | tf_op jit(solution)/shard_map/ppermute | solution.py:125
  536.6 8.5 %shard_map.78 = bf16[512,3072]{1,0:T(8,128)(2,1)} custom-call(bf16[256,3072]{1,0:T(8,128)(2,1)} %get-tuple-element.17.refs_0_, bf16[768,3072]{1,0:T(8,128)(2,1)} %shard_map.76.refs_0_.refs_1_, bf16[256,3072]{1,0:T(8,128)(2,1)} %get-tuple-element.18.refs_2_, bf16[6,5,128,128]{3,2,1,0:T(8,128)(2,1)} %constant_dynamic-slice_fusion.refs_3_.refs_1_), custom_call_target="tpu_custom_call" | custom-call | tf_op jit(solution)/shard_map/pallas_call | solution.py:90
  550.6 68.5 %reduce-scatter.11.cloned.1.call-done = f32[64,3072]{1,0:T(8,128)} async-done(((f32[512,3072]{1,0:T(8,128)}), f32[64,3072]{1,0:T(8,128)}) %reduce-scatter.11.cloned.1.call-update) | async-done | bytes 786448 | tf_op jit(solution)/shard_map/reduce_scatter | solution.py:145
  622.1 62.9 %all-gather.9.cloned.1.call-done = f32[512,3072]{1,0:T(8,128)} async-done(((f32[64,3072]{1,0:T(8,128)}), f32[512,3072]{1,0:T(8,128)}) %all-gather.9.cloned.1.call-update) | async-done | bytes 6291472 | tf_op jit(solution)/shard_map/all_gather | solution.py:148
  694.8 5.5 slice_bitcast_fusion.3
  700.2 24.0 %all-gather.11.cloned.1.call-done = f32[256,3072]{1,0:T(8,128)} async-done(((f32[32,3072]{1,0:T(8,128)}), f32[256,3072]{1,0:T(8,128)}) %all-gather.11.cloned.1.call-update) | async-done | bytes 3145744 | tf_op jit(solution)/shard_map/all_gather | solution.py:148
  724.3 11.9 %maximum_divide_fusion = f32[1,768,3072]{2,1,0:T(8,128)} fusion(f32[1,256,3072]{2,1,0:T(8,128)} %get-tuple-element.25, f32[1,256,3072]{2,1,0:T(8,128)} %bitcast.16, f32[1,256,3072]{2,1,0:T(8,128)} %get-tuple-element.24, f32[1,256,3072]{2,1,0:T(8,128)} %get-tuple-element.23, f32[1,256,3072]{2,1,0:T(8,128)} %convert_bitcast_fusion, ...), kind=kLoop, calls=%fused_computation.2 | loop fusion | flops 11796480 | bytes 28311552 | tf_op jit(solution)/shard_map/div | solution.py:182
  736.2 7.7 %pad_maximum_fusion = f32[768,3072]{1,0:T(8,128)} fusion(f32[256,3072]{1,0:T(8,128)} %get-tuple-element.26, f32[256,3072]{1,0:T(8,128)S(1)} %copy-done.5, f32[256,3072]{1,0:T(8,128)} %get-tuple-element.27), kind=kLoop, calls=%fused_computation.1 | loop fusion | flops 4718592 | bytes 18874368 | tf_op jit(solution)/shard_map/concatenate | solution.py:167
  (119 shorter events, 109.8 us)
Async XLA Ops:
  7.2 188.1 %reduce-scatter.5.cloned.1.call-start = ((), (), s32[]{:S(2)}) async-start(), calls=%async_computation.4 | async-start | bytes 3538944 | tf_op jit(solution)/shard_map/reduce_scatter | solution.py:145
  29.4 28.2 %collective-permute-start.2 = (bf16[128,3072]{1,0:T(8,128)(2,1)S(1)}, bf16[128,3072]{1,0:T(8,128)(2,1)}, u32[]{:S(2)}, u32[]{:S(2)}) collective-permute-start(bf16[128,3072]{1,0:T(8,128)(2,1)S(1)} %get-tuple-element.38), channel_id=1, source_target_pairs={{1,0},{2,3},{5,4},{6,7},{9,8},{10,11},{13,12},{14,15},{17,16},{18,... | collective-permute-start | bytes 2359304 | tf_op jit(solution)/shard_map/ppermute | solution.py:124
  30.9 24.6 %collective-permute-start = (bf16[128,3072]{1,0:T(8,128)(2,1)S(1)}, bf16[128,3072]{1,0:T(8,128)(2,1)}, u32[]{:S(2)}, u32[]{:S(2)}) collective-permute-start(bf16[128,3072]{1,0:T(8,128)(2,1)S(1)} %get-tuple-element.39), channel_id=1, source_target_pairs={{1,3},{2,0},{5,7},{6,4},{9,11},{10,8},{13,15},{14,12},{17,19},{18,... | collective-permute-start | bytes 2359304 | tf_op jit(solution)/shard_map/ppermute | solution.py:123
  33.5 62.0 %collective-permute-start.5 = (bf16[256,3072]{1,0:T(8,128)(2,1)}, bf16[256,3072]{1,0:T(8,128)(2,1)S(1)}, u32[]{:S(2)}, u32[]{:S(2)}) collective-permute-start(bf16[256,3072]{1,0:T(8,128)(2,1)} %get-tuple-element.36), channel_id=1, source_target_pairs={{1,0},{3,2},{5,4},{7,6},{9,8},{11,10},{13,12},{15,14},{17,16},{19,... | collective-permute-start | bytes 4718600 | tf_op jit(solution)/shard_map/ppermute | solution.py:120
  34.8 60.7 %collective-permute-start.4 = (bf16[256,3072]{1,0:T(8,128)(2,1)S(1)}, bf16[256,3072]{1,0:T(8,128)(2,1)}, u32[]{:S(2)}, u32[]{:S(2)}) collective-permute-start(bf16[256,3072]{1,0:T(8,128)(2,1)S(1)} %get-tuple-element.37), channel_id=1, source_target_pairs={{0,1},{2,3},{4,5},{6,7},{8,9},{10,11},{12,13},{14,15},{16,17},{18,... | collective-permute-start | bytes 4718600 | tf_op jit(solution)/shard_map/ppermute | solution.py:119
  55.5 37.6 %collective-permute-start.1 = (bf16[128,3072]{1,0:T(8,128)(2,1)}, bf16[128,3072]{1,0:T(8,128)(2,1)}, u32[]{:S(2)}, u32[]{:S(2)}) collective-permute-start(bf16[128,3072]{1,0:T(8,128)(2,1)} %collective-permute-done), channel_id=1, source_target_pairs={{3,2},{0,1},{7,6},{4,5},{11,10},{8,9},{15,14},{12,13},{19,18},{16,... | collective-permute-start | bytes 2359304 | tf_op jit(solution)/shard_map/ppermute | solution.py:125
  57.7 36.6 %collective-permute-start.3 = (bf16[128,3072]{1,0:T(8,128)(2,1)}, bf16[128,3072]{1,0:T(8,128)(2,1)}, u32[]{:S(2)}, u32[]{:S(2)}) collective-permute-start(bf16[128,3072]{1,0:T(8,128)(2,1)} %collective-permute-done.2), channel_id=1, source_target_pairs={{0,2},{3,1},{4,6},{7,5},{8,10},{11,9},{12,14},{15,13},{16,18},{19,... | collective-permute-start | bytes 2359304 | tf_op jit(solution)/shard_map/ppermute | solution.py:126
  131.2 149.5 %reduce-scatter.7.cloned.1.call-start = ((), (), s32[]{:S(2)}) async-start(), calls=%async_computation.5 | async-start | bytes 7077888 | tf_op jit(solution)/shard_map/reduce_scatter | solution.py:145
  133.2 23.0 %collective-permute-start.8 = (bf16[128,3072]{1,0:T(8,128)(2,1)S(1)}, bf16[128,3072]{1,0:T(8,128)(2,1)S(1)}, u32[]{:S(2)}, u32[]{:S(2)}) collective-permute-start(bf16[128,3072]{1,0:T(8,128)(2,1)S(1)} %get-tuple-element.34), channel_id=1, source_target_pairs={{1,0},{2,3},{5,4},{6,7},{9,8},{10,11},{13,12},{14,15},{17,16},{18,... | collective-permute-start | bytes 2359304 | tf_op jit(solution)/shard_map/ppermute | solution.py:124
  134.5 20.0 %collective-permute-start.6 = (bf16[128,3072]{1,0:T(8,128)(2,1)S(1)}, bf16[128,3072]{1,0:T(8,128)(2,1)S(1)}, u32[]{:S(2)}, u32[]{:S(2)}) collective-permute-start(bf16[128,3072]{1,0:T(8,128)(2,1)S(1)} %get-tuple-element.35), channel_id=1, source_target_pairs={{1,3},{2,0},{5,7},{6,4},{9,11},{10,8},{13,15},{14,12},{17,19},{18,... | collective-permute-start | bytes 2359304 | tf_op jit(solution)/shard_map/ppermute | solution.py:123
  137.9 55.3 %collective-permute-start.11 = (bf16[256,3072]{1,0:T(8,128)(2,1)S(1)}, bf16[256,3072]{1,0:T(8,128)(2,1)S(1)}, u32[]{:S(2)}, u32[]{:S(2)}) collective-permute-start(bf16[256,3072]{1,0:T(8,128)(2,1)S(1)} %get-tuple-element.32), channel_id=1, source_target_pairs={{1,0},{3,2},{5,4},{7,6},{9,8},{11,10},{13,12},{15,14},{17,16},{19,... | collective-permute-start | bytes 4718600 | tf_op jit(solution)/shard_map/ppermute | solution.py:120
  139.2 54.0 %collective-permute-start.10 = (bf16[256,3072]{1,0:T(8,128)(2,1)S(1)}, bf16[256,3072]{1,0:T(8,128)(2,1)S(1)}, u32[]{:S(2)}, u32[]{:S(2)}) collective-permute-start(bf16[256,3072]{1,0:T(8,128)(2,1)S(1)} %get-tuple-element.33), channel_id=1, source_target_pairs={{0,1},{2,3},{4,5},{6,7},{8,9},{10,11},{12,13},{14,15},{16,17},{18,... | collective-permute-start | bytes 4718600 | tf_op jit(solution)/shard_map/ppermute | solution.py:119
  154.5 38.6 %collective-permute-start.7 = (bf16[128,3072]{1,0:T(8,128)(2,1)S(1)}, bf16[128,3072]{1,0:T(8,128)(2,1)S(1)}, u32[]{:S(2)}, u32[]{:S(2)}) collective-permute-start(bf16[128,3072]{1,0:T(8,128)(2,1)S(1)} %collective-permute-done.6), channel_id=1, source_target_pairs={{3,2},{0,1},{7,6},{4,5},{11,10},{8,9},{15,14},{12,13},{19,18},{16,... | collective-permute-start | bytes 2359304 | tf_op jit(solution)/shard_map/ppermute | solution.py:125
  156.2 37.0 %collective-permute-start.9 = (bf16[128,3072]{1,0:T(8,128)(2,1)S(1)}, bf16[128,3072]{1,0:T(8,128)(2,1)S(1)}, u32[]{:S(2)}, u32[]{:S(2)}) collective-permute-start(bf16[128,3072]{1,0:T(8,128)(2,1)S(1)} %collective-permute-done.8), channel_id=1, source_target_pairs={{0,2},{3,1},{4,6},{7,5},{8,10},{11,9},{12,14},{15,13},{16,18},{19,... | collective-permute-start | bytes 2359304 | tf_op jit(solution)/shard_map/ppermute | solution.py:126
  209.3 137.3 %all-gather.5.cloned.1.call-start = ((), (), s32[]{:S(2)}) async-start(), calls=%async_computation.6 | async-start | bytes 7077888 | tf_op jit(solution)/shard_map/all_gather | solution.py:148
  283.4 143.4 %all-gather.7.cloned.1.call-start = ((), (), s32[]{:S(2)}) async-start(), calls=%async_computation.7 | async-start | bytes 3538944 | tf_op jit(solution)/shard_map/all_gather | solution.py:148
  348.0 188.6 %reduce-scatter.9.cloned.1.call-start = ((), (), s32[]{:S(2)}) async-start(), calls=%async_computation.8 | async-start | bytes 3538944 | tf_op jit(solution)/shard_map/reduce_scatter | solution.py:145
  364.0 25.4 %collective-permute-start.14 = (bf16[128,3072]{1,0:T(8,128)(2,1)S(1)}, bf16[128,3072]{1,0:T(8,128)(2,1)S(1)}, u32[]{:S(2)}, u32[]{:S(2)}) collective-permute-start(bf16[128,3072]{1,0:T(8,128)(2,1)S(1)} %get-tuple-element.42), channel_id=1, source_target_pairs={{1,0},{2,3},{5,4},{6,7},{9,8},{10,11},{13,12},{14,15},{17,16},{18,... | collective-permute-start | bytes 2359304 | tf_op jit(solution)/shard_map/ppermute | solution.py:124
  365.3 22.7 %collective-permute-start.12 = (bf16[128,3072]{1,0:T(8,128)(2,1)S(1)}, bf16[128,3072]{1,0:T(8,128)(2,1)S(1)}, u32[]{:S(2)}, u32[]{:S(2)}) collective-permute-start(bf16[128,3072]{1,0:T(8,128)(2,1)S(1)} %get-tuple-element.43), channel_id=1, source_target_pairs={{1,3},{2,0},{5,7},{6,4},{9,11},{10,8},{13,15},{14,12},{17,19},{18,... | collective-permute-start | bytes 2359304 | tf_op jit(solution)/shard_map/ppermute | solution.py:123
  366.8 58.0 %collective-permute-start.17 = (bf16[256,3072]{1,0:T(8,128)(2,1)S(1)}, bf16[256,3072]{1,0:T(8,128)(2,1)S(1)}, u32[]{:S(2)}, u32[]{:S(2)}) collective-permute-start(bf16[256,3072]{1,0:T(8,128)(2,1)S(1)} %get-tuple-element.40), channel_id=1, source_target_pairs={{1,0},{3,2},{5,4},{7,6},{9,8},{11,10},{13,12},{15,14},{17,16},{19,... | collective-permute-start | bytes 4718600 | tf_op jit(solution)/shard_map/ppermute | solution.py:120
  368.3 56.5 %collective-permute-start.16 = (bf16[256,3072]{1,0:T(8,128)(2,1)S(1)}, bf16[256,3072]{1,0:T(8,128)(2,1)S(1)}, u32[]{:S(2)}, u32[]{:S(2)}) collective-permute-start(bf16[256,3072]{1,0:T(8,128)(2,1)S(1)} %get-tuple-element.41), channel_id=1, source_target_pairs={{0,1},{2,3},{4,5},{6,7},{8,9},{10,11},{12,13},{14,15},{16,17},{18,... | collective-permute-start | bytes 4718600 | tf_op jit(solution)/shard_map/ppermute | solution.py:119
  387.9 36.7 %collective-permute-start.13 = (bf16[128,3072]{1,0:T(8,128)(2,1)S(1)}, bf16[128,3072]{1,0:T(8,128)(2,1)S(1)}, u32[]{:S(2)}, u32[]{:S(2)}) collective-permute-start(bf16[128,3072]{1,0:T(8,128)(2,1)S(1)} %collective-permute-done.12), channel_id=1, source_target_pairs={{3,2},{0,1},{7,6},{4,5},{11,10},{8,9},{15,14},{12,13},{19,18},{16,... | collective-permute-start | bytes 2359304 | tf_op jit(solution)/shard_map/ppermute | solution.py:125
  389.4 35.3 %collective-permute-start.15 = (bf16[128,3072]{1,0:T(8,128)(2,1)S(1)}, bf16[128,3072]{1,0:T(8,128)(2,1)S(1)}, u32[]{:S(2)}, u32[]{:S(2)}) collective-permute-start(bf16[128,3072]{1,0:T(8,128)(2,1)S(1)} %collective-permute-done.14), channel_id=1, source_target_pairs={{0,2},{3,1},{4,6},{7,5},{8,10},{11,9},{12,14},{15,13},{16,18},{19,... | collective-permute-start | bytes 2359304 | tf_op jit(solution)/shard_map/ppermute | solution.py:126
  472.0 147.1 %reduce-scatter.11.cloned.1.call-start = ((), (), s32[]{:S(2)}) async-start(), calls=%async_computation.9 | async-start | bytes 7077888 | tf_op jit(solution)/shard_map/reduce_scatter | solution.py:145
  474.1 23.5 %collective-permute-start.20 = (bf16[128,3072]{1,0:T(8,128)(2,1)S(1)}, bf16[128,3072]{1,0:T(8,128)(2,1)S(1)}, u32[]{:S(2)}, u32[]{:S(2)}) collective-permute-start(bf16[128,3072]{1,0:T(8,128)(2,1)S(1)} %get-tuple-element.30), channel_id=1, source_target_pairs={{1,0},{2,3},{5,4},{6,7},{9,8},{10,11},{13,12},{14,15},{17,16},{18,... | collective-permute-start | bytes 2359304 | tf_op jit(solution)/shard_map/ppermute | solution.py:124
  475.4 20.5 %collective-permute-start.18 = (bf16[128,3072]{1,0:T(8,128)(2,1)S(1)}, bf16[128,3072]{1,0:T(8,128)(2,1)S(1)}, u32[]{:S(2)}, u32[]{:S(2)}) collective-permute-start(bf16[128,3072]{1,0:T(8,128)(2,1)S(1)} %get-tuple-element.31), channel_id=1, source_target_pairs={{1,3},{2,0},{5,7},{6,4},{9,11},{10,8},{13,15},{14,12},{17,19},{18,... | collective-permute-start | bytes 2359304 | tf_op jit(solution)/shard_map/ppermute | solution.py:123
  478.8 55.9 %collective-permute-start.23 = (bf16[256,3072]{1,0:T(8,128)(2,1)S(1)}, bf16[256,3072]{1,0:T(8,128)(2,1)S(1)}, u32[]{:S(2)}, u32[]{:S(2)}) collective-permute-start(bf16[256,3072]{1,0:T(8,128)(2,1)S(1)} %get-tuple-element.28), channel_id=1, source_target_pairs={{1,0},{3,2},{5,4},{7,6},{9,8},{11,10},{13,12},{15,14},{17,16},{19,... | collective-permute-start | bytes 4718600 | tf_op jit(solution)/shard_map/ppermute | solution.py:120
  480.1 54.6 %collective-permute-start.22 = (bf16[256,3072]{1,0:T(8,128)(2,1)S(1)}, bf16[256,3072]{1,0:T(8,128)(2,1)S(1)}, u32[]{:S(2)}, u32[]{:S(2)}) collective-permute-start(bf16[256,3072]{1,0:T(8,128)(2,1)S(1)} %get-tuple-element.29), channel_id=1, source_target_pairs={{0,1},{2,3},{4,5},{6,7},{8,9},{10,11},{12,13},{14,15},{16,17},{18,... | collective-permute-start | bytes 4718600 | tf_op jit(solution)/shard_map/ppermute | solution.py:119
  495.9 38.6 %collective-permute-start.19 = (bf16[128,3072]{1,0:T(8,128)(2,1)S(1)}, bf16[128,3072]{1,0:T(8,128)(2,1)S(1)}, u32[]{:S(2)}, u32[]{:S(2)}) collective-permute-start(bf16[128,3072]{1,0:T(8,128)(2,1)S(1)} %collective-permute-done.18), channel_id=1, source_target_pairs={{3,2},{0,1},{7,6},{4,5},{11,10},{8,9},{15,14},{12,13},{19,18},{16,... | collective-permute-start | bytes 2359304 | tf_op jit(solution)/shard_map/ppermute | solution.py:125
  497.6 37.1 %collective-permute-start.21 = (bf16[128,3072]{1,0:T(8,128)(2,1)S(1)}, bf16[128,3072]{1,0:T(8,128)(2,1)S(1)}, u32[]{:S(2)}, u32[]{:S(2)}) collective-permute-start(bf16[128,3072]{1,0:T(8,128)(2,1)S(1)} %collective-permute-done.20), channel_id=1, source_target_pairs={{0,2},{3,1},{4,6},{7,5},{8,10},{11,9},{12,14},{15,13},{16,18},{19,... | collective-permute-start | bytes 2359304 | tf_op jit(solution)/shard_map/ppermute | solution.py:126
  550.6 134.5 %all-gather.9.cloned.1.call-start = ((), (), s32[]{:S(2)}) async-start(), calls=%async_computation.10 | async-start | bytes 7077888 | tf_op jit(solution)/shard_map/all_gather | solution.py:148
  621.8 102.4 %all-gather.11.cloned.1.call-start = ((), (), s32[]{:S(2)}) async-start(), calls=%async_computation.11 | async-start | bytes 3538944 | tf_op jit(solution)/shard_map/all_gather | solution.py:148
  (12 other events, 574.7 us)
Sparse Core Ops, SparseCore 0:
  131.3 41.6 reduce-scatter.4
  209.4 71.2 reduce-scatter.6
  283.5 63.0 all-gather.4
  348.1 36.9 all-gather.6
  472.2 38.8 reduce-scatter.8
  550.7 68.3 reduce-scatter.10
  621.9 63.0 all-gather.8
  687.3 36.9 all-gather.10

commit v10 on v9

--- a/solution.py
+++ b/solution.py
@@ -166,9 +166,15 @@
         edges, inside = parts
         return jnp.concatenate([edges[:halo], inside, edges[halo:]], axis=0)
 
+    def first_apply(field):
+        halos = exchange(field[rows - halo :].astype(jnp.bfloat16), field[:halo].astype(jnp.bfloat16))
+        inner = column_pass(field, terms)
+        inner_halos = column_pass(jnp.concatenate(halos, axis=0), terms)
+        return row_pass(inner, terms_local, all_blocks, (inner_halos[:halo], inner_halos[halo:]))
+
     masses = image_masses[0]
     scaling = dual_multipliers[0]
-    kernel_v = apply_kernel(scaling)
+    kernel_v = first_apply(scaling)
     for iteration in range(ITERS):
         if iteration:
             if interior:

time: 752 us -> 764 us (1.016); the launches traced: 751 us -> 752 us
  waiting for transfers between devices: 457 us -> 439 us
  Pallas kernels: 99.7 us -> 108 us
    ppermute x4, waiting for transfers between devices: 135 us -> 118 us  [exchange(): first = lax.ppermute(first, 'slab', [(3, 2), (0, 1)])]
    pallas_call x5 -> x6, Pallas kernels: 50.7 us -> 58.6 us  [column_pass(): pl.pallas_call(column_kernel, grid=(rows // tile_rows,), in_specs=[tile]...]
  transfers between devices with their start and end apart: 32 -> 32, of which waited for: 13 -> 13; matrix products, arithmetic and copies ran while one was open for 6% -> 6% of each run, Pallas kernels for 1% -> 3%
where the time goes in v10:
time: 764 us; the launch traced here: 752 us
  waiting for transfers between devices  439 us (57%)
  Pallas kernels  108 us (14%)
  other arithmetic  94.1 us (12%)
  starting transfers between devices  56.5 us (7%)
  local copies, waits for them, and re-layouts  23.5 us (3%)
  between operations  15.8 us (2%)
  blocking collectives  15.3 us (2%)
    all_gather x4, waiting for transfers between devices, gather_barycenter(): lax.all_gather(jnp.exp(part_sum / total_weight), 'img', axis=0, tiled=True)  150 us
    reduce_scatter x4, waiting for transfers between devices, log_sum(): lax.psum_scatter(weight * jnp.log(kernel_u), 'img', scatter_dimension=0,...  124 us
    ppermute x4, waiting for transfers between devices, exchange(): first = lax.ppermute(first, 'slab', [(3, 2), (0, 1)])  118 us
    pallas_call x6, Pallas kernels, column_pass(): pl.pallas_call(column_kernel, grid=(rows // tile_rows,), in_specs=[tile]...  58.6 us
    pallas_call x6, Pallas kernels, row_pass(): pl.pallas_call(functools.partial(row_kernel, blocks=tuple(blocks), has_ha...  49 us
    ppermute x4, waiting for transfers between devices, exchange(): first = lax.ppermute(first, 'slab', [(1, 3), (2, 0)])  46.5 us
    ppermute x4, starting transfers between devices, exchange(): direct_prev = lax.ppermute(to_up, 'slab', [(0, 1), (2, 3)])  27.9 us
    mul x4, other arithmetic, log_sum(): weight * jnp.log(kernel_u)  17.9 us
  transfers between devices with their start and end apart: 32, of which 13 were waited for; matrix products, arithmetic and copies ran while one was open for 6% of the time, Pallas kernels for 3%

profile of v10, /device:TPU:0, one launch (start us, length us, event | category | flops | bytes accessed | tf_op | source)
XLA Modules:
  0.0 752.3 jit_solution(10855768830101678658)
XLA Ops:
  7.2 6.6 convert.5
  21.5 9.0 %collective-permute-start.4 = (bf16[256,3072]{1,0:T(8,128)(2,1)}, bf16[256,3072]{1,0:T(8,128)(2,1)}, u32[]{:S(2)}, u32[]{:S(2)}) collective-permute-start(bf16[256,3072]{1,0:T(8,128)(2,1)} %get-tuple-element.36), channel_id=1, source_target_pairs={{0,1},{2,3},{4,5},{6,7},{8,9},{10,11},{12,13},{14,15},{16,17},{18,... | collective-permute-start | bytes 4718600 | tf_op jit(solution)/shard_map/ppermute | solution.py:119
  31.9 11.2 %collective-permute-done = bf16[128,3072]{1,0:T(8,128)(2,1)} collective-permute-done((bf16[128,3072]{1,0:T(8,128)(2,1)}, bf16[128,3072]{1,0:T(8,128)(2,1)}, u32[]{:S(2)}, u32[]{:S(2)}) %collective-permute-start) | collective-permute-done | bytes 786464 | tf_op jit(solution)/shard_map/ppermute | solution.py:123
  53.1 10.9 %shard_map.69.refs_1_ = bf16[768,3072]{1,0:T(8,128)(2,1)} custom-call(f32[768,3072]{1,0:T(8,128)} %bitcast.22, bf16[24,5,128,128]{3,2,1,0:T(8,128)(2,1)} %select_reduce_fusion.refs_1_.refs_2_), custom_call_target="tpu_custom_call" | custom-call | tf_op jit(solution)/shard_map/pallas_call | solution.py:49
  66.2 13.6 %collective-permute-done.1 = bf16[128,3072]{1,0:T(8,128)(2,1)} collective-permute-done((bf16[128,3072]{1,0:T(8,128)(2,1)}, bf16[128,3072]{1,0:T(8,128)(2,1)}, u32[]{:S(2)}, u32[]{:S(2)}) %collective-permute-start.1) | collective-permute-done | bytes 786464 | tf_op jit(solution)/shard_map/ppermute | solution.py:125
  85.2 8.0 %shard_map.68 = bf16[512,3072]{1,0:T(8,128)(2,1)} custom-call(bf16[512,3072]{1,0:T(8,128)(2,1)} %pad_maximum_fusion.2.refs_0_, bf16[24,5,128,128]{3,2,1,0:T(8,128)(2,1)} %select_reduce_fusion.refs_1_.refs_2_), custom_call_target="tpu_custom_call" | custom-call | tf_op jit(solution)/shard_map/pallas_call | solution.py:49
  96.9 10.2 %shard_map.70.refs_1_ = bf16[768,3072]{1,0:T(8,128)(2,1)} custom-call(bf16[256,3072]{1,0:T(8,128)(2,1)} %get-tuple-element.45.refs_0_, bf16[768,3072]{1,0:T(8,128)(2,1)} %shard_map.69.refs_1_, bf16[256,3072]{1,0:T(8,128)(2,1)} %get-tuple-element.44.refs_2_, bf16[6,5,128,128]{3,2,1,0:T(8,128)(2,1)} %constant_dynamic-slice_fusion.refs_3_.refs_1_), custom_call_target="tpu_custom_call" | custom-call | tf_op jit(solution)/shard_map/pallas_call | solution.py:90
  107.1 12.8 %shard_map.71.refs_0_.refs_1_ = bf16[768,3072]{1,0:T(8,128)(2,1)} custom-call(f32[768,3072]{1,0:T(8,128)} %bitcast.23, bf16[768,3072]{1,0:T(8,128)(2,1)} %shard_map.70.refs_1_, bf16[24,5,128,128]{3,2,1,0:T(8,128)(2,1)} %select_reduce_fusion.refs_1_.refs_2_), custom_call_target="tpu_custom_call" | custom-call | tf_op jit(solution)/shard_map/pallas_call | solution.py:49
  119.8 5.9 shard_map.72
  137.4 8.3 %collective-permute-start.10 = (bf16[256,3072]{1,0:T(8,128)(2,1)S(1)}, bf16[256,3072]{1,0:T(8,128)(2,1)S(1)}, u32[]{:S(2)}, u32[]{:S(2)}) collective-permute-start(bf16[256,3072]{1,0:T(8,128)(2,1)S(1)} %get-tuple-element.33), channel_id=1, source_target_pairs={{0,1},{2,3},{4,5},{6,7},{8,9},{10,11},{12,13},{14,15},{16,17},{18,... | collective-permute-start | bytes 4718600 | tf_op jit(solution)/shard_map/ppermute | solution.py:119
  145.7 10.3 %collective-permute-done.6 = bf16[128,3072]{1,0:T(8,128)(2,1)S(1)} collective-permute-done((bf16[128,3072]{1,0:T(8,128)(2,1)S(1)}, bf16[128,3072]{1,0:T(8,128)(2,1)S(1)}, u32[]{:S(2)}, u32[]{:S(2)}) %collective-permute-start.6) | collective-permute-done | bytes 786464 | tf_op jit(solution)/shard_map/ppermute | solution.py:123
  158.8 35.6 %collective-permute-done.7 = bf16[128,3072]{1,0:T(8,128)(2,1)S(1)} collective-permute-done((bf16[128,3072]{1,0:T(8,128)(2,1)S(1)}, bf16[128,3072]{1,0:T(8,128)(2,1)S(1)}, u32[]{:S(2)}, u32[]{:S(2)}) %collective-permute-start.7) | collective-permute-done | bytes 786464 | tf_op jit(solution)/shard_map/ppermute | solution.py:125
  196.5 8.5 %shard_map.73 = bf16[512,3072]{1,0:T(8,128)(2,1)} custom-call(bf16[256,3072]{1,0:T(8,128)(2,1)} %get-tuple-element.12.refs_0_, bf16[768,3072]{1,0:T(8,128)(2,1)} %shard_map.71.refs_0_.refs_1_, bf16[256,3072]{1,0:T(8,128)(2,1)} %get-tuple-element.13.refs_2_, bf16[6,5,128,128]{3,2,1,0:T(8,128)(2,1)} %constant_dynamic-slice_fusion.refs_3_.refs_1_), custom_call_target="tpu_custom_call" | custom-call | tf_op jit(solution)/shard_map/pallas_call | solution.py:90
  210.6 15.3 %psum.7 = f32[]{:T(128)} all-reduce(f32[]{:T(128)} %bitcast), channel_id=1, replica_groups=mesh['img'=8,'slab'=4] {'img'}, use_global_device_ids=true, to_apply=%region_3.4 | all-reduce | flops 1 | bytes 8 | tf_op jit(solution)/shard_map/psum | solution.py:109
  225.9 56.0 %reduce-scatter.7.cloned.1.call-done = f32[64,3072]{1,0:T(8,128)} async-done(((f32[512,3072]{1,0:T(8,128)}), f32[64,3072]{1,0:T(8,128)}) %reduce-scatter.7.cloned.1.call-update) | async-done | bytes 786448 | tf_op jit(solution)/shard_map/reduce_scatter | solution.py:145
  284.7 63.1 %all-gather.5.cloned.1.call-done = f32[512,3072]{1,0:T(8,128)} async-done(((f32[64,3072]{1,0:T(8,128)}), f32[512,3072]{1,0:T(8,128)}) %all-gather.5.cloned.1.call-update) | async-done | bytes 6291472 | tf_op jit(solution)/shard_map/all_gather | solution.py:148
  354.9 8.3 %shard_map.74 = bf16[512,3072]{1,0:T(8,128)(2,1)} custom-call(bf16[512,3072]{1,0:T(8,128)(2,1)} %fusion.1.refs_0_, bf16[24,5,128,128]{3,2,1,0:T(8,128)(2,1)} %select_reduce_fusion.refs_1_.refs_2_), custom_call_target="tpu_custom_call" | custom-call | tf_op jit(solution)/shard_map/pallas_call | solution.py:49
  369.5 5.8 collective-permute-start.16
  375.3 14.1 %collective-permute-done.12 = bf16[128,3072]{1,0:T(8,128)(2,1)S(1)} collective-permute-done((bf16[128,3072]{1,0:T(8,128)(2,1)S(1)}, bf16[128,3072]{1,0:T(8,128)(2,1)S(1)}, u32[]{:S(2)}, u32[]{:S(2)}) %collective-permute-start.12) | collective-permute-done | bytes 786464 | tf_op jit(solution)/shard_map/ppermute | solution.py:123
  392.3 33.5 %collective-permute-done.13 = bf16[128,3072]{1,0:T(8,128)(2,1)S(1)} collective-permute-done((bf16[128,3072]{1,0:T(8,128)(2,1)S(1)}, bf16[128,3072]{1,0:T(8,128)(2,1)S(1)}, u32[]{:S(2)}, u32[]{:S(2)}) %collective-permute-start.13) | collective-permute-done | bytes 786464 | tf_op jit(solution)/shard_map/ppermute | solution.py:125
  431.4 6.0 shard_map.75
  440.8 10.2 %shard_map.76.refs_1_ = bf16[768,3072]{1,0:T(8,128)(2,1)} custom-call(bf16[256,3072]{1,0:T(8,128)(2,1)} %get-tuple-element.49.refs_0_, bf16[768,3072]{1,0:T(8,128)(2,1)} %pad_maximum_fusion.1.refs_1_, bf16[256,3072]{1,0:T(8,128)(2,1)} %get-tuple-element.48.refs_2_, bf16[6,5,128,128]{3,2,1,0:T(8,128)(2,1)} %constant_dynamic-slice_fusion.refs_3_.refs_1_), custom_call_target="tpu_custom_call" | custom-call | tf_op jit(solution)/shard_map/pallas_call | solution.py:90
  451.0 12.8 %shard_map.77.refs_0_.refs_1_ = bf16[768,3072]{1,0:T(8,128)(2,1)} custom-call(f32[768,3072]{1,0:T(8,128)} %bitcast.24, bf16[768,3072]{1,0:T(8,128)(2,1)} %shard_map.76.refs_1_, bf16[24,5,128,128]{3,2,1,0:T(8,128)(2,1)} %select_reduce_fusion.refs_1_.refs_2_), custom_call_target="tpu_custom_call" | custom-call | tf_op jit(solution)/shard_map/pallas_call | solution.py:49
  463.8 5.8 shard_map.78
  486.0 11.0 %collective-permute-done.18 = bf16[128,3072]{1,0:T(8,128)(2,1)S(1)} collective-permute-done((bf16[128,3072]{1,0:T(8,128)(2,1)S(1)}, bf16[128,3072]{1,0:T(8,128)(2,1)S(1)}, u32[]{:S(2)}, u32[]{:S(2)}) %collective-permute-start.18) | collective-permute-done | bytes 786464 | tf_op jit(solution)/shard_map/ppermute | solution.py:123
  500.0 35.6 %collective-permute-done.19 = bf16[128,3072]{1,0:T(8,128)(2,1)S(1)} collective-permute-done((bf16[128,3072]{1,0:T(8,128)(2,1)S(1)}, bf16[128,3072]{1,0:T(8,128)(2,1)S(1)}, u32[]{:S(2)}, u32[]{:S(2)}) %collective-permute-start.19) | collective-permute-done | bytes 786464 | tf_op jit(solution)/shard_map/ppermute | solution.py:125
  537.7 8.5 %shard_map.79 = bf16[512,3072]{1,0:T(8,128)(2,1)} custom-call(bf16[256,3072]{1,0:T(8,128)(2,1)} %get-tuple-element.17.refs_0_, bf16[768,3072]{1,0:T(8,128)(2,1)} %shard_map.77.refs_0_.refs_1_, bf16[256,3072]{1,0:T(8,128)(2,1)} %get-tuple-element.18.refs_2_, bf16[6,5,128,128]{3,2,1,0:T(8,128)(2,1)} %constant_dynamic-slice_fusion.refs_3_.refs_1_), custom_call_target="tpu_custom_call" | custom-call | tf_op jit(solution)/shard_map/pallas_call | solution.py:90
  551.7 68.5 %reduce-scatter.11.cloned.1.call-done = f32[64,3072]{1,0:T(8,128)} async-done(((f32[512,3072]{1,0:T(8,128)}), f32[64,3072]{1,0:T(8,128)}) %reduce-scatter.11.cloned.1.call-update) | async-done | bytes 786448 | tf_op jit(solution)/shard_map/reduce_scatter | solution.py:145
  623.3 62.9 %all-gather.9.cloned.1.call-done = f32[512,3072]{1,0:T(8,128)} async-done(((f32[64,3072]{1,0:T(8,128)}), f32[512,3072]{1,0:T(8,128)}) %all-gather.9.cloned.1.call-update) | async-done | bytes 6291472 | tf_op jit(solution)/shard_map/all_gather | solution.py:148
  701.5 24.0 %all-gather.11.cloned.1.call-done = f32[256,3072]{1,0:T(8,128)} async-done(((f32[32,3072]{1,0:T(8,128)}), f32[256,3072]{1,0:T(8,128)}) %all-gather.11.cloned.1.call-update) | async-done | bytes 3145744 | tf_op jit(solution)/shard_map/all_gather | solution.py:148
  725.4 11.9 %maximum_divide_fusion = f32[1,768,3072]{2,1,0:T(8,128)} fusion(f32[1,256,3072]{2,1,0:T(8,128)} %get-tuple-element.25, f32[1,256,3072]{2,1,0:T(8,128)} %bitcast.25, f32[1,256,3072]{2,1,0:T(8,128)} %get-tuple-element.24, f32[1,256,3072]{2,1,0:T(8,128)} %get-tuple-element.23, f32[1,256,3072]{2,1,0:T(8,128)} %convert_bitcast_fusion, ...), kind=kLoop, calls=%fused_computation.2 | loop fusion | flops 11796480 | bytes 28311552 | tf_op jit(solution)/shard_map/div | solution.py:188
  737.4 7.7 %pad_maximum_fusion = f32[768,3072]{1,0:T(8,128)} fusion(f32[256,3072]{1,0:T(8,128)} %get-tuple-element.26, f32[256,3072]{1,0:T(8,128)S(1)} %copy-done.5, f32[256,3072]{1,0:T(8,128)} %get-tuple-element.27), kind=kLoop, calls=%fused_computation.1 | loop fusion | flops 4718592 | bytes 18874368 | tf_op jit(solution)/shard_map/concatenate | solution.py:167
  (127 shorter events, 125.0 us)
Async XLA Ops:
  7.2 189.4 %reduce-scatter.5.cloned.1.call-start = ((), (), s32[]{:S(2)}) async-start(), calls=%async_computation.4 | async-start | bytes 3538944 | tf_op jit(solution)/shard_map/reduce_scatter | solution.py:145
  16.8 28.5 %collective-permute-start.2 = (bf16[128,3072]{1,0:T(8,128)(2,1)S(1)}, bf16[128,3072]{1,0:T(8,128)(2,1)}, u32[]{:S(2)}, u32[]{:S(2)}) collective-permute-start(bf16[128,3072]{1,0:T(8,128)(2,1)S(1)} %get-tuple-element.38), channel_id=1, source_target_pairs={{1,0},{2,3},{5,4},{6,7},{9,8},{10,11},{13,12},{14,15},{17,16},{18,... | collective-permute-start | bytes 2359304 | tf_op jit(solution)/shard_map/ppermute | solution.py:124
  18.1 24.9 %collective-permute-start = (bf16[128,3072]{1,0:T(8,128)(2,1)}, bf16[128,3072]{1,0:T(8,128)(2,1)}, u32[]{:S(2)}, u32[]{:S(2)}) collective-permute-start(bf16[128,3072]{1,0:T(8,128)(2,1)} %get-tuple-element.39), channel_id=1, source_target_pairs={{1,3},{2,0},{5,7},{6,4},{9,11},{10,8},{13,15},{14,12},{17,19},{18,... | collective-permute-start | bytes 2359304 | tf_op jit(solution)/shard_map/ppermute | solution.py:123
  21.5 59.6 %collective-permute-start.4 = (bf16[256,3072]{1,0:T(8,128)(2,1)}, bf16[256,3072]{1,0:T(8,128)(2,1)}, u32[]{:S(2)}, u32[]{:S(2)}) collective-permute-start(bf16[256,3072]{1,0:T(8,128)(2,1)} %get-tuple-element.36), channel_id=1, source_target_pairs={{0,1},{2,3},{4,5},{6,7},{8,9},{10,11},{12,13},{14,15},{16,17},{18,... | collective-permute-start | bytes 4718600 | tf_op jit(solution)/shard_map/ppermute | solution.py:119
  30.5 50.7 %collective-permute-start.5 = (bf16[256,3072]{1,0:T(8,128)(2,1)}, bf16[256,3072]{1,0:T(8,128)(2,1)}, u32[]{:S(2)}, u32[]{:S(2)}) collective-permute-start(bf16[256,3072]{1,0:T(8,128)(2,1)} %get-tuple-element.37), channel_id=1, source_target_pairs={{1,0},{3,2},{5,4},{7,6},{9,8},{11,10},{13,12},{15,14},{17,16},{19,... | collective-permute-start | bytes 4718600 | tf_op jit(solution)/shard_map/ppermute | solution.py:120
  43.0 36.8 %collective-permute-start.1 = (bf16[128,3072]{1,0:T(8,128)(2,1)}, bf16[128,3072]{1,0:T(8,128)(2,1)}, u32[]{:S(2)}, u32[]{:S(2)}) collective-permute-start(bf16[128,3072]{1,0:T(8,128)(2,1)} %collective-permute-done), channel_id=1, source_target_pairs={{3,2},{0,1},{7,6},{4,5},{11,10},{8,9},{15,14},{12,13},{19,18},{16,... | collective-permute-start | bytes 2359304 | tf_op jit(solution)/shard_map/ppermute | solution.py:125
  45.3 35.8 %collective-permute-start.3 = (bf16[128,3072]{1,0:T(8,128)(2,1)}, bf16[128,3072]{1,0:T(8,128)(2,1)S(1)}, u32[]{:S(2)}, u32[]{:S(2)}) collective-permute-start(bf16[128,3072]{1,0:T(8,128)(2,1)} %collective-permute-done.2), channel_id=1, source_target_pairs={{0,2},{3,1},{4,6},{7,5},{8,10},{11,9},{12,14},{15,13},{16,18},{19,... | collective-permute-start | bytes 2359304 | tf_op jit(solution)/shard_map/ppermute | solution.py:126
  129.2 152.7 %reduce-scatter.7.cloned.1.call-start = ((), (), s32[]{:S(2)}) async-start(), calls=%async_computation.5 | async-start | bytes 7077888 | tf_op jit(solution)/shard_map/reduce_scatter | solution.py:145
  131.4 26.1 %collective-permute-start.8 = (bf16[128,3072]{1,0:T(8,128)(2,1)S(1)}, bf16[128,3072]{1,0:T(8,128)(2,1)S(1)}, u32[]{:S(2)}, u32[]{:S(2)}) collective-permute-start(bf16[128,3072]{1,0:T(8,128)(2,1)S(1)} %get-tuple-element.34), channel_id=1, source_target_pairs={{1,0},{2,3},{5,4},{6,7},{9,8},{10,11},{13,12},{14,15},{17,16},{18,... | collective-permute-start | bytes 2359304 | tf_op jit(solution)/shard_map/ppermute | solution.py:124
  132.7 23.3 %collective-permute-start.6 = (bf16[128,3072]{1,0:T(8,128)(2,1)S(1)}, bf16[128,3072]{1,0:T(8,128)(2,1)S(1)}, u32[]{:S(2)}, u32[]{:S(2)}) collective-permute-start(bf16[128,3072]{1,0:T(8,128)(2,1)S(1)} %get-tuple-element.35), channel_id=1, source_target_pairs={{1,3},{2,0},{5,7},{6,4},{9,11},{10,8},{13,15},{14,12},{17,19},{18,... | collective-permute-start | bytes 2359304 | tf_op jit(solution)/shard_map/ppermute | solution.py:123
  136.1 58.4 %collective-permute-start.11 = (bf16[256,3072]{1,0:T(8,128)(2,1)S(1)}, bf16[256,3072]{1,0:T(8,128)(2,1)S(1)}, u32[]{:S(2)}, u32[]{:S(2)}) collective-permute-start(bf16[256,3072]{1,0:T(8,128)(2,1)S(1)} %get-tuple-element.32), channel_id=1, source_target_pairs={{1,0},{3,2},{5,4},{7,6},{9,8},{11,10},{13,12},{15,14},{17,16},{19,... | collective-permute-start | bytes 4718600 | tf_op jit(solution)/shard_map/ppermute | solution.py:120
  137.4 57.1 %collective-permute-start.10 = (bf16[256,3072]{1,0:T(8,128)(2,1)S(1)}, bf16[256,3072]{1,0:T(8,128)(2,1)S(1)}, u32[]{:S(2)}, u32[]{:S(2)}) collective-permute-start(bf16[256,3072]{1,0:T(8,128)(2,1)S(1)} %get-tuple-element.33), channel_id=1, source_target_pairs={{0,1},{2,3},{4,5},{6,7},{8,9},{10,11},{12,13},{14,15},{16,17},{18,... | collective-permute-start | bytes 4718600 | tf_op jit(solution)/shard_map/ppermute | solution.py:119
  156.0 38.4 %collective-permute-start.7 = (bf16[128,3072]{1,0:T(8,128)(2,1)S(1)}, bf16[128,3072]{1,0:T(8,128)(2,1)S(1)}, u32[]{:S(2)}, u32[]{:S(2)}) collective-permute-start(bf16[128,3072]{1,0:T(8,128)(2,1)S(1)} %collective-permute-done.6), channel_id=1, source_target_pairs={{3,2},{0,1},{7,6},{4,5},{11,10},{8,9},{15,14},{12,13},{19,18},{16,... | collective-permute-start | bytes 2359304 | tf_op jit(solution)/shard_map/ppermute | solution.py:125
  157.5 37.0 %collective-permute-start.9 = (bf16[128,3072]{1,0:T(8,128)(2,1)S(1)}, bf16[128,3072]{1,0:T(8,128)(2,1)S(1)}, u32[]{:S(2)}, u32[]{:S(2)}) collective-permute-start(bf16[128,3072]{1,0:T(8,128)(2,1)S(1)} %collective-permute-done.8), channel_id=1, source_target_pairs={{0,2},{3,1},{4,6},{7,5},{8,10},{11,9},{12,14},{15,13},{16,18},{19,... | collective-permute-start | bytes 2359304 | tf_op jit(solution)/shard_map/ppermute | solution.py:126
  210.5 137.3 %all-gather.5.cloned.1.call-start = ((), (), s32[]{:S(2)}) async-start(), calls=%async_computation.6 | async-start | bytes 7077888 | tf_op jit(solution)/shard_map/all_gather | solution.py:148
  284.7 143.2 %all-gather.7.cloned.1.call-start = ((), (), s32[]{:S(2)}) async-start(), calls=%async_computation.7 | async-start | bytes 3538944 | tf_op jit(solution)/shard_map/all_gather | solution.py:148
  349.3 188.4 %reduce-scatter.9.cloned.1.call-start = ((), (), s32[]{:S(2)}) async-start(), calls=%async_computation.8 | async-start | bytes 3538944 | tf_op jit(solution)/shard_map/reduce_scatter | solution.py:145
  365.4 25.4 %collective-permute-start.14 = (bf16[128,3072]{1,0:T(8,128)(2,1)S(1)}, bf16[128,3072]{1,0:T(8,128)(2,1)S(1)}, u32[]{:S(2)}, u32[]{:S(2)}) collective-permute-start(bf16[128,3072]{1,0:T(8,128)(2,1)S(1)} %get-tuple-element.42), channel_id=1, source_target_pairs={{1,0},{2,3},{5,4},{6,7},{9,8},{10,11},{13,12},{14,15},{17,16},{18,... | collective-permute-start | bytes 2359304 | tf_op jit(solution)/shard_map/ppermute | solution.py:124
  366.7 22.7 %collective-permute-start.12 = (bf16[128,3072]{1,0:T(8,128)(2,1)S(1)}, bf16[128,3072]{1,0:T(8,128)(2,1)S(1)}, u32[]{:S(2)}, u32[]{:S(2)}) collective-permute-start(bf16[128,3072]{1,0:T(8,128)(2,1)S(1)} %get-tuple-element.43), channel_id=1, source_target_pairs={{1,3},{2,0},{5,7},{6,4},{9,11},{10,8},{13,15},{14,12},{17,19},{18,... | collective-permute-start | bytes 2359304 | tf_op jit(solution)/shard_map/ppermute | solution.py:123
  368.2 57.8 %collective-permute-start.17 = (bf16[256,3072]{1,0:T(8,128)(2,1)S(1)}, bf16[256,3072]{1,0:T(8,128)(2,1)S(1)}, u32[]{:S(2)}, u32[]{:S(2)}) collective-permute-start(bf16[256,3072]{1,0:T(8,128)(2,1)S(1)} %get-tuple-element.40), channel_id=1, source_target_pairs={{1,0},{3,2},{5,4},{7,6},{9,8},{11,10},{13,12},{15,14},{17,16},{19,... | collective-permute-start | bytes 4718600 | tf_op jit(solution)/shard_map/ppermute | solution.py:120
  369.5 56.5 %collective-permute-start.16 = (bf16[256,3072]{1,0:T(8,128)(2,1)S(1)}, bf16[256,3072]{1,0:T(8,128)(2,1)S(1)}, u32[]{:S(2)}, u32[]{:S(2)}) collective-permute-start(bf16[256,3072]{1,0:T(8,128)(2,1)S(1)} %get-tuple-element.41), channel_id=1, source_target_pairs={{0,1},{2,3},{4,5},{6,7},{8,9},{10,11},{12,13},{14,15},{16,17},{18,... | collective-permute-start | bytes 4718600 | tf_op jit(solution)/shard_map/ppermute | solution.py:119
  389.3 36.5 %collective-permute-start.13 = (bf16[128,3072]{1,0:T(8,128)(2,1)S(1)}, bf16[128,3072]{1,0:T(8,128)(2,1)S(1)}, u32[]{:S(2)}, u32[]{:S(2)}) collective-permute-start(bf16[128,3072]{1,0:T(8,128)(2,1)S(1)} %collective-permute-done.12), channel_id=1, source_target_pairs={{3,2},{0,1},{7,6},{4,5},{11,10},{8,9},{15,14},{12,13},{19,18},{16,... | collective-permute-start | bytes 2359304 | tf_op jit(solution)/shard_map/ppermute | solution.py:125
  390.8 35.1 %collective-permute-start.15 = (bf16[128,3072]{1,0:T(8,128)(2,1)S(1)}, bf16[128,3072]{1,0:T(8,128)(2,1)S(1)}, u32[]{:S(2)}, u32[]{:S(2)}) collective-permute-start(bf16[128,3072]{1,0:T(8,128)(2,1)S(1)} %collective-permute-done.14), channel_id=1, source_target_pairs={{0,2},{3,1},{4,6},{7,5},{8,10},{11,9},{12,14},{15,13},{16,18},{19,... | collective-permute-start | bytes 2359304 | tf_op jit(solution)/shard_map/ppermute | solution.py:126
  473.1 147.1 %reduce-scatter.11.cloned.1.call-start = ((), (), s32[]{:S(2)}) async-start(), calls=%async_computation.9 | async-start | bytes 7077888 | tf_op jit(solution)/shard_map/reduce_scatter | solution.py:145
  475.2 23.5 %collective-permute-start.20 = (bf16[128,3072]{1,0:T(8,128)(2,1)S(1)}, bf16[128,3072]{1,0:T(8,128)(2,1)S(1)}, u32[]{:S(2)}, u32[]{:S(2)}) collective-permute-start(bf16[128,3072]{1,0:T(8,128)(2,1)S(1)} %get-tuple-element.30), channel_id=1, source_target_pairs={{1,0},{2,3},{5,4},{6,7},{9,8},{10,11},{13,12},{14,15},{17,16},{18,... | collective-permute-start | bytes 2359304 | tf_op jit(solution)/shard_map/ppermute | solution.py:124
  476.5 20.5 %collective-permute-start.18 = (bf16[128,3072]{1,0:T(8,128)(2,1)S(1)}, bf16[128,3072]{1,0:T(8,128)(2,1)S(1)}, u32[]{:S(2)}, u32[]{:S(2)}) collective-permute-start(bf16[128,3072]{1,0:T(8,128)(2,1)S(1)} %get-tuple-element.31), channel_id=1, source_target_pairs={{1,3},{2,0},{5,7},{6,4},{9,11},{10,8},{13,15},{14,12},{17,19},{18,... | collective-permute-start | bytes 2359304 | tf_op jit(solution)/shard_map/ppermute | solution.py:123
  479.9 55.9 %collective-permute-start.23 = (bf16[256,3072]{1,0:T(8,128)(2,1)S(1)}, bf16[256,3072]{1,0:T(8,128)(2,1)S(1)}, u32[]{:S(2)}, u32[]{:S(2)}) collective-permute-start(bf16[256,3072]{1,0:T(8,128)(2,1)S(1)} %get-tuple-element.28), channel_id=1, source_target_pairs={{1,0},{3,2},{5,4},{7,6},{9,8},{11,10},{13,12},{15,14},{17,16},{19,... | collective-permute-start | bytes 4718600 | tf_op jit(solution)/shard_map/ppermute | solution.py:120
  481.2 54.6 %collective-permute-start.22 = (bf16[256,3072]{1,0:T(8,128)(2,1)S(1)}, bf16[256,3072]{1,0:T(8,128)(2,1)S(1)}, u32[]{:S(2)}, u32[]{:S(2)}) collective-permute-start(bf16[256,3072]{1,0:T(8,128)(2,1)S(1)} %get-tuple-element.29), channel_id=1, source_target_pairs={{0,1},{2,3},{4,5},{6,7},{8,9},{10,11},{12,13},{14,15},{16,17},{18,... | collective-permute-start | bytes 4718600 | tf_op jit(solution)/shard_map/ppermute | solution.py:119
  497.0 38.7 %collective-permute-start.19 = (bf16[128,3072]{1,0:T(8,128)(2,1)S(1)}, bf16[128,3072]{1,0:T(8,128)(2,1)S(1)}, u32[]{:S(2)}, u32[]{:S(2)}) collective-permute-start(bf16[128,3072]{1,0:T(8,128)(2,1)S(1)} %collective-permute-done.18), channel_id=1, source_target_pairs={{3,2},{0,1},{7,6},{4,5},{11,10},{8,9},{15,14},{12,13},{19,18},{16,... | collective-permute-start | bytes 2359304 | tf_op jit(solution)/shard_map/ppermute | solution.py:125
  498.7 37.0 %collective-permute-start.21 = (bf16[128,3072]{1,0:T(8,128)(2,1)S(1)}, bf16[128,3072]{1,0:T(8,128)(2,1)S(1)}, u32[]{:S(2)}, u32[]{:S(2)}) collective-permute-start(bf16[128,3072]{1,0:T(8,128)(2,1)S(1)} %collective-permute-done.20), channel_id=1, source_target_pairs={{0,2},{3,1},{4,6},{7,5},{8,10},{11,9},{12,14},{15,13},{16,18},{19,... | collective-permute-start | bytes 2359304 | tf_op jit(solution)/shard_map/ppermute | solution.py:126
  551.7 134.6 %all-gather.9.cloned.1.call-start = ((), (), s32[]{:S(2)}) async-start(), calls=%async_computation.10 | async-start | bytes 7077888 | tf_op jit(solution)/shard_map/all_gather | solution.py:148
  623.0 102.4 %all-gather.11.cloned.1.call-start = ((), (), s32[]{:S(2)}) async-start(), calls=%async_computation.11 | async-start | bytes 3538944 | tf_op jit(solution)/shard_map/all_gather | solution.py:148
  (14 other events, 617.8 us)
Sparse Core Ops, SparseCore 0:
  129.3 44.4 reduce-scatter.4
  210.6 71.2 reduce-scatter.6
  284.8 63.0 all-gather.4
  349.5 36.9 all-gather.6
  473.3 38.8 reduce-scatter.8
  551.8 68.3 reduce-scatter.10
  623.1 63.0 all-gather.8
  688.5 36.9 all-gather.10

commit v11 on v9

--- a/solution.py
+++ b/solution.py
@@ -172,8 +172,7 @@
     for iteration in range(ITERS):
         if iteration:
             if interior:
-                side_edges, side_inside = [(b / k).astype(jnp.bfloat16) for b, k in zip(barycenter, kernel_u)]
-                kernel_v = apply_split(side_edges, side_inside)
+                kernel_v = apply_split(*zip(barycenter, kernel_u))
             else:
                 kernel_v = apply_kernel((barycenter / kernel_u).astype(jnp.bfloat16))
         kernel_u, barycenter = final_apply((masses, kernel_v))

time: 752 us -> 749 us (level)
  no operation moved by 1% of the time
where the time goes in v11:
time: 749 us; the launch traced here: 748 us
  waiting for transfers between devices  454 us (61%)
  Pallas kernels  103 us (14%)
  other arithmetic  85.1 us (11%)
  starting transfers between devices  54.1 us (7%)
  local copies, waits for them, and re-layouts  20.9 us (3%)
  blocking collectives  15.5 us (2%)
  between operations  15.3 us (2%)
    all_gather x4, waiting for transfers between devices, gather_barycenter(): lax.all_gather(jnp.exp(part_sum / total_weight), 'img', axis=0, tiled=True)  150 us
    ppermute x4, waiting for transfers between devices, exchange(): first = lax.ppermute(first, 'slab', [(3, 2), (0, 1)])  133 us
    reduce_scatter x4, waiting for transfers between devices, log_sum(): lax.psum_scatter(weight * jnp.log(kernel_u), 'img', scatter_dimension=0,...  124 us
    pallas_call x5, Pallas kernels, column_pass(): pl.pallas_call(column_kernel, grid=(rows // tile_rows,), in_specs=[tile]...  53.5 us
    pallas_call x6, Pallas kernels, row_pass(): pl.pallas_call(functools.partial(row_kernel, blocks=tuple(blocks), has_ha...  49 us
    ppermute x4, waiting for transfers between devices, exchange(): first = lax.ppermute(first, 'slab', [(1, 3), (2, 0)])  46.9 us
    ppermute x4, starting transfers between devices, exchange(): direct_prev = lax.ppermute(to_up, 'slab', [(0, 1), (2, 3)])  24.3 us
    mul x4, other arithmetic, log_sum(): weight * jnp.log(kernel_u)  17.9 us
  transfers between devices with their start and end apart: 32, of which 13 were waited for; matrix products, arithmetic and copies ran while one was open for 6% of the time, Pallas kernels for 1%

profile of v11, /device:TPU:0, one launch (start us, length us, event | category | flops | bytes accessed | tf_op | source)
XLA Modules:
  0.0 747.6 jit_solution(11548422547215091702)
XLA Ops:
  8.1 8.3 %select_reduce_fusion.refs_1_.refs_2_ = bf16[24,5,128,128]{3,2,1,0:T(8,128)(2,1)} fusion(pred[24,5,3]{2,1,0:T(8,128)(4,1)S(1)} %broadcast_compare_fusion, bf16[24,3,128,128]{3,2,1,0:T(8,128)(2,1)} %param.8), kind=kLoop, calls=%fused_computation | loop fusion | flops 9830400 | bytes 6291816 | tf_op jit(solution)/shard_map/reduce_sum | solution.py:18
  16.4 10.9 %shard_map.68.refs_1_ = bf16[768,3072]{1,0:T(8,128)(2,1)} custom-call(f32[768,3072]{1,0:T(8,128)} %bitcast.17, bf16[24,5,128,128]{3,2,1,0:T(8,128)(2,1)} %select_reduce_fusion.refs_1_.refs_2_), custom_call_target="tpu_custom_call" | custom-call | tf_op jit(solution)/shard_map/pallas_call | solution.py:49
  34.8 9.2 %collective-permute-start.4 = (bf16[256,3072]{1,0:T(8,128)(2,1)S(1)}, bf16[256,3072]{1,0:T(8,128)(2,1)}, u32[]{:S(2)}, u32[]{:S(2)}) collective-permute-start(bf16[256,3072]{1,0:T(8,128)(2,1)S(1)} %get-tuple-element.37), channel_id=1, source_target_pairs={{0,1},{2,3},{4,5},{6,7},{8,9},{10,11},{12,13},{14,15},{16,17},{18,... | collective-permute-start | bytes 4718600 | tf_op jit(solution)/shard_map/ppermute | solution.py:119
  44.0 11.5 %collective-permute-done = bf16[128,3072]{1,0:T(8,128)(2,1)} collective-permute-done((bf16[128,3072]{1,0:T(8,128)(2,1)S(1)}, bf16[128,3072]{1,0:T(8,128)(2,1)}, u32[]{:S(2)}, u32[]{:S(2)}) %collective-permute-start) | collective-permute-done | bytes 786464 | tf_op jit(solution)/shard_map/ppermute | solution.py:123
  62.8 30.3 %collective-permute-done.1 = bf16[128,3072]{1,0:T(8,128)(2,1)} collective-permute-done((bf16[128,3072]{1,0:T(8,128)(2,1)}, bf16[128,3072]{1,0:T(8,128)(2,1)}, u32[]{:S(2)}, u32[]{:S(2)}) %collective-permute-start.1) | collective-permute-done | bytes 786464 | tf_op jit(solution)/shard_map/ppermute | solution.py:125
  98.9 10.2 %shard_map.69.refs_1_ = bf16[768,3072]{1,0:T(8,128)(2,1)} custom-call(bf16[256,3072]{1,0:T(8,128)(2,1)} %get-tuple-element.51.refs_0_, bf16[768,3072]{1,0:T(8,128)(2,1)} %shard_map.68.refs_1_, bf16[256,3072]{1,0:T(8,128)(2,1)} %get-tuple-element.50.refs_2_, bf16[6,5,128,128]{3,2,1,0:T(8,128)(2,1)} %constant_dynamic-slice_fusion.refs_3_.refs_1_), custom_call_target="tpu_custom_call" | custom-call | tf_op jit(solution)/shard_map/pallas_call | solution.py:90
  109.1 12.8 %shard_map.70.refs_0_.refs_1_ = bf16[768,3072]{1,0:T(8,128)(2,1)} custom-call(f32[768,3072]{1,0:T(8,128)} %bitcast.14, bf16[768,3072]{1,0:T(8,128)(2,1)} %shard_map.69.refs_1_, bf16[24,5,128,128]{3,2,1,0:T(8,128)(2,1)} %select_reduce_fusion.refs_1_.refs_2_), custom_call_target="tpu_custom_call" | custom-call | tf_op jit(solution)/shard_map/pallas_call | solution.py:49
  121.8 5.8 shard_map.71
  144.1 10.4 %collective-permute-done.6 = bf16[128,3072]{1,0:T(8,128)(2,1)S(1)} collective-permute-done((bf16[128,3072]{1,0:T(8,128)(2,1)S(1)}, bf16[128,3072]{1,0:T(8,128)(2,1)S(1)}, u32[]{:S(2)}, u32[]{:S(2)}) %collective-permute-start.6) | collective-permute-done | bytes 786464 | tf_op jit(solution)/shard_map/ppermute | solution.py:123
  157.5 35.6 %collective-permute-done.7 = bf16[128,3072]{1,0:T(8,128)(2,1)S(1)} collective-permute-done((bf16[128,3072]{1,0:T(8,128)(2,1)S(1)}, bf16[128,3072]{1,0:T(8,128)(2,1)S(1)}, u32[]{:S(2)}, u32[]{:S(2)}) %collective-permute-start.7) | collective-permute-done | bytes 786464 | tf_op jit(solution)/shard_map/ppermute | solution.py:125
  195.2 8.5 %shard_map.72 = bf16[512,3072]{1,0:T(8,128)(2,1)} custom-call(bf16[256,3072]{1,0:T(8,128)(2,1)} %get-tuple-element.12.refs_0_, bf16[768,3072]{1,0:T(8,128)(2,1)} %shard_map.70.refs_0_.refs_1_, bf16[256,3072]{1,0:T(8,128)(2,1)} %get-tuple-element.13.refs_2_, bf16[6,5,128,128]{3,2,1,0:T(8,128)(2,1)} %constant_dynamic-slice_fusion.refs_3_.refs_1_), custom_call_target="tpu_custom_call" | custom-call | tf_op jit(solution)/shard_map/pallas_call | solution.py:90
  209.3 15.5 %psum.7 = f32[]{:T(128)} all-reduce(f32[]{:T(128)} %bitcast), channel_id=1, replica_groups=mesh['img'=8,'slab'=4] {'img'}, use_global_device_ids=true, to_apply=%region_3.4 | all-reduce | flops 1 | bytes 8 | tf_op jit(solution)/shard_map/psum | solution.py:109
  224.8 55.8 %reduce-scatter.7.cloned.1.call-done = f32[64,3072]{1,0:T(8,128)} async-done(((f32[512,3072]{1,0:T(8,128)}), f32[64,3072]{1,0:T(8,128)}) %reduce-scatter.7.cloned.1.call-update) | async-done | bytes 786448 | tf_op jit(solution)/shard_map/reduce_scatter | solution.py:145
  283.4 63.1 %all-gather.5.cloned.1.call-done.refs_0_ = f32[512,3072]{1,0:T(8,128)} async-done(((f32[64,3072]{1,0:T(8,128)}), f32[512,3072]{1,0:T(8,128)}) %all-gather.5.cloned.1.call-update) | async-done | bytes 6291472 | tf_op jit(solution)/shard_map/all_gather | solution.py:148
  351.6 9.9 %shard_map.73 = bf16[512,3072]{1,0:T(8,128)(2,1)} custom-call(f32[512,3072]{1,0:T(8,128)} %all-gather.5.cloned.1.call-done.refs_0_, f32[512,3072]{1,0:T(8,128)} %convert_element_type.21.refs_1_, bf16[24,5,128,128]{3,2,1,0:T(8,128)(2,1)} %select_reduce_fusion.refs_1_.refs_2_), custom_call_target="tpu_custom_call" | custom-call | tf_op jit(solution)/shard_map/pallas_call | solution.py:49
  367.9 5.5 collective-permute-start.16
  373.4 14.0 %collective-permute-done.12 = bf16[128,3072]{1,0:T(8,128)(2,1)S(1)} collective-permute-done((bf16[128,3072]{1,0:T(8,128)(2,1)S(1)}, bf16[128,3072]{1,0:T(8,128)(2,1)S(1)}, u32[]{:S(2)}, u32[]{:S(2)}) %collective-permute-start.12) | collective-permute-done | bytes 786464 | tf_op jit(solution)/shard_map/ppermute | solution.py:123
  392.5 31.4 %collective-permute-done.13 = bf16[128,3072]{1,0:T(8,128)(2,1)S(1)} collective-permute-done((bf16[128,3072]{1,0:T(8,128)(2,1)S(1)}, bf16[128,3072]{1,0:T(8,128)(2,1)S(1)}, u32[]{:S(2)}, u32[]{:S(2)}) %collective-permute-start.13) | collective-permute-done | bytes 786464 | tf_op jit(solution)/shard_map/ppermute | solution.py:125
  426.0 7.2 shard_map.74
  436.7 10.2 %shard_map.75.refs_1_ = bf16[768,3072]{1,0:T(8,128)(2,1)} custom-call(bf16[256,3072]{1,0:T(8,128)(2,1)} %get-tuple-element.47.refs_0_, bf16[768,3072]{1,0:T(8,128)(2,1)} %pad_maximum_fusion.1.refs_1_, bf16[256,3072]{1,0:T(8,128)(2,1)} %get-tuple-element.46.refs_2_, bf16[6,5,128,128]{3,2,1,0:T(8,128)(2,1)} %constant_dynamic-slice_fusion.refs_3_.refs_1_), custom_call_target="tpu_custom_call" | custom-call | tf_op jit(solution)/shard_map/pallas_call | solution.py:90
  446.9 12.8 %shard_map.76.refs_0_.refs_1_ = bf16[768,3072]{1,0:T(8,128)(2,1)} custom-call(f32[768,3072]{1,0:T(8,128)} %bitcast.15, bf16[768,3072]{1,0:T(8,128)(2,1)} %shard_map.75.refs_1_, bf16[24,5,128,128]{3,2,1,0:T(8,128)(2,1)} %select_reduce_fusion.refs_1_.refs_2_), custom_call_target="tpu_custom_call" | custom-call | tf_op jit(solution)/shard_map/pallas_call | solution.py:49
  459.7 5.8 shard_map.77
  481.9 11.0 %collective-permute-done.18 = bf16[128,3072]{1,0:T(8,128)(2,1)S(1)} collective-permute-done((bf16[128,3072]{1,0:T(8,128)(2,1)S(1)}, bf16[128,3072]{1,0:T(8,128)(2,1)S(1)}, u32[]{:S(2)}, u32[]{:S(2)}) %collective-permute-start.18) | collective-permute-done | bytes 786464 | tf_op jit(solution)/shard_map/ppermute | solution.py:123
  495.9 35.6 %collective-permute-done.19 = bf16[128,3072]{1,0:T(8,128)(2,1)S(1)} collective-permute-done((bf16[128,3072]{1,0:T(8,128)(2,1)S(1)}, bf16[128,3072]{1,0:T(8,128)(2,1)S(1)}, u32[]{:S(2)}, u32[]{:S(2)}) %collective-permute-start.19) | collective-permute-done | bytes 786464 | tf_op jit(solution)/shard_map/ppermute | solution.py:125
  533.6 8.5 %shard_map.78 = bf16[512,3072]{1,0:T(8,128)(2,1)} custom-call(bf16[256,3072]{1,0:T(8,128)(2,1)} %get-tuple-element.17.refs_0_, bf16[768,3072]{1,0:T(8,128)(2,1)} %shard_map.76.refs_0_.refs_1_, bf16[256,3072]{1,0:T(8,128)(2,1)} %get-tuple-element.18.refs_2_, bf16[6,5,128,128]{3,2,1,0:T(8,128)(2,1)} %constant_dynamic-slice_fusion.refs_3_.refs_1_), custom_call_target="tpu_custom_call" | custom-call | tf_op jit(solution)/shard_map/pallas_call | solution.py:90
  542.1 5.5 log_multiply_fusion
  547.6 68.3 %reduce-scatter.11.cloned.1.call-done = f32[64,3072]{1,0:T(8,128)} async-done(((f32[512,3072]{1,0:T(8,128)}), f32[64,3072]{1,0:T(8,128)}) %reduce-scatter.11.cloned.1.call-update) | async-done | bytes 786448 | tf_op jit(solution)/shard_map/reduce_scatter | solution.py:145
  619.0 62.9 %all-gather.9.cloned.1.call-done = f32[512,3072]{1,0:T(8,128)} async-done(((f32[64,3072]{1,0:T(8,128)}), f32[512,3072]{1,0:T(8,128)}) %all-gather.9.cloned.1.call-update) | async-done | bytes 6291472 | tf_op jit(solution)/shard_map/all_gather | solution.py:148
  691.7 5.5 slice_bitcast_fusion.3
  697.2 24.0 %all-gather.11.cloned.1.call-done = f32[256,3072]{1,0:T(8,128)} async-done(((f32[32,3072]{1,0:T(8,128)}), f32[256,3072]{1,0:T(8,128)}) %all-gather.11.cloned.1.call-update) | async-done | bytes 3145744 | tf_op jit(solution)/shard_map/all_gather | solution.py:148
  721.1 11.9 %maximum_divide_fusion = f32[1,768,3072]{2,1,0:T(8,128)} fusion(f32[1,256,3072]{2,1,0:T(8,128)} %get-tuple-element.25, f32[1,256,3072]{2,1,0:T(8,128)} %bitcast.16, f32[1,256,3072]{2,1,0:T(8,128)} %get-tuple-element.24, f32[1,256,3072]{2,1,0:T(8,128)} %get-tuple-element.23, f32[1,256,3072]{2,1,0:T(8,128)} %convert_bitcast_fusion, ...), kind=kLoop, calls=%fused_computation.2 | loop fusion | flops 11796480 | bytes 28311552 | tf_op jit(solution)/shard_map/div | solution.py:181
  733.1 7.7 %pad_maximum_fusion = f32[768,3072]{1,0:T(8,128)} fusion(f32[256,3072]{1,0:T(8,128)} %get-tuple-element.26, f32[256,3072]{1,0:T(8,128)S(1)} %copy-done.5, f32[256,3072]{1,0:T(8,128)} %get-tuple-element.27), kind=kLoop, calls=%fused_computation.1 | loop fusion | flops 4718592 | bytes 18874368 | tf_op jit(solution)/shard_map/concatenate | solution.py:167
  (115 shorter events, 106.7 us)
Async XLA Ops:
  7.2 188.1 %reduce-scatter.5.cloned.1.call-start = ((), (), s32[]{:S(2)}) async-start(), calls=%async_computation.4 | async-start | bytes 3538944 | tf_op jit(solution)/shard_map/reduce_scatter | solution.py:145
  29.4 28.2 %collective-permute-start.2 = (bf16[128,3072]{1,0:T(8,128)(2,1)S(1)}, bf16[128,3072]{1,0:T(8,128)(2,1)}, u32[]{:S(2)}, u32[]{:S(2)}) collective-permute-start(bf16[128,3072]{1,0:T(8,128)(2,1)S(1)} %get-tuple-element.38), channel_id=1, source_target_pairs={{1,0},{2,3},{5,4},{6,7},{9,8},{10,11},{13,12},{14,15},{17,16},{18,... | collective-permute-start | bytes 2359304 | tf_op jit(solution)/shard_map/ppermute | solution.py:124
  30.9 24.6 %collective-permute-start = (bf16[128,3072]{1,0:T(8,128)(2,1)S(1)}, bf16[128,3072]{1,0:T(8,128)(2,1)}, u32[]{:S(2)}, u32[]{:S(2)}) collective-permute-start(bf16[128,3072]{1,0:T(8,128)(2,1)S(1)} %get-tuple-element.39), channel_id=1, source_target_pairs={{1,3},{2,0},{5,7},{6,4},{9,11},{10,8},{13,15},{14,12},{17,19},{18,... | collective-permute-start | bytes 2359304 | tf_op jit(solution)/shard_map/ppermute | solution.py:123
  33.5 62.0 %collective-permute-start.5 = (bf16[256,3072]{1,0:T(8,128)(2,1)}, bf16[256,3072]{1,0:T(8,128)(2,1)S(1)}, u32[]{:S(2)}, u32[]{:S(2)}) collective-permute-start(bf16[256,3072]{1,0:T(8,128)(2,1)} %get-tuple-element.36), channel_id=1, source_target_pairs={{1,0},{3,2},{5,4},{7,6},{9,8},{11,10},{13,12},{15,14},{17,16},{19,... | collective-permute-start | bytes 4718600 | tf_op jit(solution)/shard_map/ppermute | solution.py:120
  34.8 60.7 %collective-permute-start.4 = (bf16[256,3072]{1,0:T(8,128)(2,1)S(1)}, bf16[256,3072]{1,0:T(8,128)(2,1)}, u32[]{:S(2)}, u32[]{:S(2)}) collective-permute-start(bf16[256,3072]{1,0:T(8,128)(2,1)S(1)} %get-tuple-element.37), channel_id=1, source_target_pairs={{0,1},{2,3},{4,5},{6,7},{8,9},{10,11},{12,13},{14,15},{16,17},{18,... | collective-permute-start | bytes 4718600 | tf_op jit(solution)/shard_map/ppermute | solution.py:119
  55.4 37.6 %collective-permute-start.1 = (bf16[128,3072]{1,0:T(8,128)(2,1)}, bf16[128,3072]{1,0:T(8,128)(2,1)}, u32[]{:S(2)}, u32[]{:S(2)}) collective-permute-start(bf16[128,3072]{1,0:T(8,128)(2,1)} %collective-permute-done), channel_id=1, source_target_pairs={{3,2},{0,1},{7,6},{4,5},{11,10},{8,9},{15,14},{12,13},{19,18},{16,... | collective-permute-start | bytes 2359304 | tf_op jit(solution)/shard_map/ppermute | solution.py:125
  57.7 36.6 %collective-permute-start.3 = (bf16[128,3072]{1,0:T(8,128)(2,1)}, bf16[128,3072]{1,0:T(8,128)(2,1)}, u32[]{:S(2)}, u32[]{:S(2)}) collective-permute-start(bf16[128,3072]{1,0:T(8,128)(2,1)} %collective-permute-done.2), channel_id=1, source_target_pairs={{0,2},{3,1},{4,6},{7,5},{8,10},{11,9},{12,14},{15,13},{16,18},{19,... | collective-permute-start | bytes 2359304 | tf_op jit(solution)/shard_map/ppermute | solution.py:126
  131.2 149.4 %reduce-scatter.7.cloned.1.call-start = ((), (), s32[]{:S(2)}) async-start(), calls=%async_computation.5 | async-start | bytes 7077888 | tf_op jit(solution)/shard_map/reduce_scatter | solution.py:145
  133.2 22.9 %collective-permute-start.8 = (bf16[128,3072]{1,0:T(8,128)(2,1)S(1)}, bf16[128,3072]{1,0:T(8,128)(2,1)S(1)}, u32[]{:S(2)}, u32[]{:S(2)}) collective-permute-start(bf16[128,3072]{1,0:T(8,128)(2,1)S(1)} %get-tuple-element.34), channel_id=1, source_target_pairs={{1,0},{2,3},{5,4},{6,7},{9,8},{10,11},{13,12},{14,15},{17,16},{18,... | collective-permute-start | bytes 2359304 | tf_op jit(solution)/shard_map/ppermute | solution.py:124
  134.5 20.0 %collective-permute-start.6 = (bf16[128,3072]{1,0:T(8,128)(2,1)S(1)}, bf16[128,3072]{1,0:T(8,128)(2,1)S(1)}, u32[]{:S(2)}, u32[]{:S(2)}) collective-permute-start(bf16[128,3072]{1,0:T(8,128)(2,1)S(1)} %get-tuple-element.35), channel_id=1, source_target_pairs={{1,3},{2,0},{5,7},{6,4},{9,11},{10,8},{13,15},{14,12},{17,19},{18,... | collective-permute-start | bytes 2359304 | tf_op jit(solution)/shard_map/ppermute | solution.py:123
  137.9 55.3 %collective-permute-start.11 = (bf16[256,3072]{1,0:T(8,128)(2,1)S(1)}, bf16[256,3072]{1,0:T(8,128)(2,1)S(1)}, u32[]{:S(2)}, u32[]{:S(2)}) collective-permute-start(bf16[256,3072]{1,0:T(8,128)(2,1)S(1)} %get-tuple-element.32), channel_id=1, source_target_pairs={{1,0},{3,2},{5,4},{7,6},{9,8},{11,10},{13,12},{15,14},{17,16},{19,... | collective-permute-start | bytes 4718600 | tf_op jit(solution)/shard_map/ppermute | solution.py:120
  139.2 54.0 %collective-permute-start.10 = (bf16[256,3072]{1,0:T(8,128)(2,1)S(1)}, bf16[256,3072]{1,0:T(8,128)(2,1)S(1)}, u32[]{:S(2)}, u32[]{:S(2)}) collective-permute-start(bf16[256,3072]{1,0:T(8,128)(2,1)S(1)} %get-tuple-element.33), channel_id=1, source_target_pairs={{0,1},{2,3},{4,5},{6,7},{8,9},{10,11},{12,13},{14,15},{16,17},{18,... | collective-permute-start | bytes 4718600 | tf_op jit(solution)/shard_map/ppermute | solution.py:119
  154.5 38.6 %collective-permute-start.7 = (bf16[128,3072]{1,0:T(8,128)(2,1)S(1)}, bf16[128,3072]{1,0:T(8,128)(2,1)S(1)}, u32[]{:S(2)}, u32[]{:S(2)}) collective-permute-start(bf16[128,3072]{1,0:T(8,128)(2,1)S(1)} %collective-permute-done.6), channel_id=1, source_target_pairs={{3,2},{0,1},{7,6},{4,5},{11,10},{8,9},{15,14},{12,13},{19,18},{16,... | collective-permute-start | bytes 2359304 | tf_op jit(solution)/shard_map/ppermute | solution.py:125
  156.2 37.0 %collective-permute-start.9 = (bf16[128,3072]{1,0:T(8,128)(2,1)S(1)}, bf16[128,3072]{1,0:T(8,128)(2,1)S(1)}, u32[]{:S(2)}, u32[]{:S(2)}) collective-permute-start(bf16[128,3072]{1,0:T(8,128)(2,1)S(1)} %collective-permute-done.8), channel_id=1, source_target_pairs={{0,2},{3,1},{4,6},{7,5},{8,10},{11,9},{12,14},{15,13},{16,18},{19,... | collective-permute-start | bytes 2359304 | tf_op jit(solution)/shard_map/ppermute | solution.py:126
  209.2 137.3 %all-gather.5.cloned.1.call-start = ((), (), s32[]{:S(2)}) async-start(), calls=%async_computation.6 | async-start | bytes 7077888 | tf_op jit(solution)/shard_map/all_gather | solution.py:148
  283.4 142.6 %all-gather.7.cloned.1.call-start = ((), (), s32[]{:S(2)}) async-start(), calls=%async_computation.7 | async-start | bytes 3538944 | tf_op jit(solution)/shard_map/all_gather | solution.py:148
  348.0 185.6 %reduce-scatter.9.cloned.1.call-start = ((), (), s32[]{:S(2)}) async-start(), calls=%async_computation.8 | async-start | bytes 3538944 | tf_op jit(solution)/shard_map/reduce_scatter | solution.py:145
  363.6 25.5 %collective-permute-start.14 = (bf16[128,3072]{1,0:T(8,128)(2,1)S(1)}, bf16[128,3072]{1,0:T(8,128)(2,1)S(1)}, u32[]{:S(2)}, u32[]{:S(2)}) collective-permute-start(bf16[128,3072]{1,0:T(8,128)(2,1)S(1)} %get-tuple-element.42), channel_id=1, source_target_pairs={{1,0},{2,3},{5,4},{6,7},{9,8},{10,11},{13,12},{14,15},{17,16},{18,... | collective-permute-start | bytes 2359304 | tf_op jit(solution)/shard_map/ppermute | solution.py:124
  365.0 22.5 %collective-permute-start.12 = (bf16[128,3072]{1,0:T(8,128)(2,1)S(1)}, bf16[128,3072]{1,0:T(8,128)(2,1)S(1)}, u32[]{:S(2)}, u32[]{:S(2)}) collective-permute-start(bf16[128,3072]{1,0:T(8,128)(2,1)S(1)} %get-tuple-element.43), channel_id=1, source_target_pairs={{1,3},{2,0},{5,7},{6,4},{9,11},{10,8},{13,15},{14,12},{17,19},{18,... | collective-permute-start | bytes 2359304 | tf_op jit(solution)/shard_map/ppermute | solution.py:123
  366.6 57.5 %collective-permute-start.17 = (bf16[256,3072]{1,0:T(8,128)(2,1)S(1)}, bf16[256,3072]{1,0:T(8,128)(2,1)S(1)}, u32[]{:S(2)}, u32[]{:S(2)}) collective-permute-start(bf16[256,3072]{1,0:T(8,128)(2,1)S(1)} %get-tuple-element.40), channel_id=1, source_target_pairs={{1,0},{3,2},{5,4},{7,6},{9,8},{11,10},{13,12},{15,14},{17,16},{19,... | collective-permute-start | bytes 4718600 | tf_op jit(solution)/shard_map/ppermute | solution.py:120
  367.9 56.2 %collective-permute-start.16 = (bf16[256,3072]{1,0:T(8,128)(2,1)S(1)}, bf16[256,3072]{1,0:T(8,128)(2,1)S(1)}, u32[]{:S(2)}, u32[]{:S(2)}) collective-permute-start(bf16[256,3072]{1,0:T(8,128)(2,1)S(1)} %get-tuple-element.41), channel_id=1, source_target_pairs={{0,1},{2,3},{4,5},{6,7},{8,9},{10,11},{12,13},{14,15},{16,17},{18,... | collective-permute-start | bytes 4718600 | tf_op jit(solution)/shard_map/ppermute | solution.py:119
  387.5 36.5 %collective-permute-start.13 = (bf16[128,3072]{1,0:T(8,128)(2,1)S(1)}, bf16[128,3072]{1,0:T(8,128)(2,1)S(1)}, u32[]{:S(2)}, u32[]{:S(2)}) collective-permute-start(bf16[128,3072]{1,0:T(8,128)(2,1)S(1)} %collective-permute-done.12), channel_id=1, source_target_pairs={{3,2},{0,1},{7,6},{4,5},{11,10},{8,9},{15,14},{12,13},{19,18},{16,... | collective-permute-start | bytes 2359304 | tf_op jit(solution)/shard_map/ppermute | solution.py:125
  389.1 34.9 %collective-permute-start.15 = (bf16[128,3072]{1,0:T(8,128)(2,1)S(1)}, bf16[128,3072]{1,0:T(8,128)(2,1)S(1)}, u32[]{:S(2)}, u32[]{:S(2)}) collective-permute-start(bf16[128,3072]{1,0:T(8,128)(2,1)S(1)} %collective-permute-done.14), channel_id=1, source_target_pairs={{0,2},{3,1},{4,6},{7,5},{8,10},{11,9},{12,14},{15,13},{16,18},{19,... | collective-permute-start | bytes 2359304 | tf_op jit(solution)/shard_map/ppermute | solution.py:126
  469.0 146.9 %reduce-scatter.11.cloned.1.call-start = ((), (), s32[]{:S(2)}) async-start(), calls=%async_computation.9 | async-start | bytes 7077888 | tf_op jit(solution)/shard_map/reduce_scatter | solution.py:145
  471.1 23.5 %collective-permute-start.20 = (bf16[128,3072]{1,0:T(8,128)(2,1)S(1)}, bf16[128,3072]{1,0:T(8,128)(2,1)S(1)}, u32[]{:S(2)}, u32[]{:S(2)}) collective-permute-start(bf16[128,3072]{1,0:T(8,128)(2,1)S(1)} %get-tuple-element.30), channel_id=1, source_target_pairs={{1,0},{2,3},{5,4},{6,7},{9,8},{10,11},{13,12},{14,15},{17,16},{18,... | collective-permute-start | bytes 2359304 | tf_op jit(solution)/shard_map/ppermute | solution.py:124
  472.4 20.5 %collective-permute-start.18 = (bf16[128,3072]{1,0:T(8,128)(2,1)S(1)}, bf16[128,3072]{1,0:T(8,128)(2,1)S(1)}, u32[]{:S(2)}, u32[]{:S(2)}) collective-permute-start(bf16[128,3072]{1,0:T(8,128)(2,1)S(1)} %get-tuple-element.31), channel_id=1, source_target_pairs={{1,3},{2,0},{5,7},{6,4},{9,11},{10,8},{13,15},{14,12},{17,19},{18,... | collective-permute-start | bytes 2359304 | tf_op jit(solution)/shard_map/ppermute | solution.py:123
  475.8 55.8 %collective-permute-start.23 = (bf16[256,3072]{1,0:T(8,128)(2,1)S(1)}, bf16[256,3072]{1,0:T(8,128)(2,1)S(1)}, u32[]{:S(2)}, u32[]{:S(2)}) collective-permute-start(bf16[256,3072]{1,0:T(8,128)(2,1)S(1)} %get-tuple-element.28), channel_id=1, source_target_pairs={{1,0},{3,2},{5,4},{7,6},{9,8},{11,10},{13,12},{15,14},{17,16},{19,... | collective-permute-start | bytes 4718600 | tf_op jit(solution)/shard_map/ppermute | solution.py:120
  477.1 54.6 %collective-permute-start.22 = (bf16[256,3072]{1,0:T(8,128)(2,1)S(1)}, bf16[256,3072]{1,0:T(8,128)(2,1)S(1)}, u32[]{:S(2)}, u32[]{:S(2)}) collective-permute-start(bf16[256,3072]{1,0:T(8,128)(2,1)S(1)} %get-tuple-element.29), channel_id=1, source_target_pairs={{0,1},{2,3},{4,5},{6,7},{8,9},{10,11},{12,13},{14,15},{16,17},{18,... | collective-permute-start | bytes 4718600 | tf_op jit(solution)/shard_map/ppermute | solution.py:119
  492.9 38.7 %collective-permute-start.19 = (bf16[128,3072]{1,0:T(8,128)(2,1)S(1)}, bf16[128,3072]{1,0:T(8,128)(2,1)S(1)}, u32[]{:S(2)}, u32[]{:S(2)}) collective-permute-start(bf16[128,3072]{1,0:T(8,128)(2,1)S(1)} %collective-permute-done.18), channel_id=1, source_target_pairs={{3,2},{0,1},{7,6},{4,5},{11,10},{8,9},{15,14},{12,13},{19,18},{16,... | collective-permute-start | bytes 2359304 | tf_op jit(solution)/shard_map/ppermute | solution.py:125
  494.5 37.0 %collective-permute-start.21 = (bf16[128,3072]{1,0:T(8,128)(2,1)S(1)}, bf16[128,3072]{1,0:T(8,128)(2,1)S(1)}, u32[]{:S(2)}, u32[]{:S(2)}) collective-permute-start(bf16[128,3072]{1,0:T(8,128)(2,1)S(1)} %collective-permute-done.20), channel_id=1, source_target_pairs={{0,2},{3,1},{4,6},{7,5},{8,10},{11,9},{12,14},{15,13},{16,18},{19,... | collective-permute-start | bytes 2359304 | tf_op jit(solution)/shard_map/ppermute | solution.py:126
  547.5 134.4 %all-gather.9.cloned.1.call-start = ((), (), s32[]{:S(2)}) async-start(), calls=%async_computation.10 | async-start | bytes 7077888 | tf_op jit(solution)/shard_map/all_gather | solution.py:148
  618.7 102.4 %all-gather.11.cloned.1.call-start = ((), (), s32[]{:S(2)}) async-start(), calls=%async_computation.11 | async-start | bytes 3538944 | tf_op jit(solution)/shard_map/all_gather | solution.py:148
  (10 other events, 534.5 us)
Sparse Core Ops, SparseCore 0:
  131.3 41.6 reduce-scatter.4
  209.3 71.2 reduce-scatter.6
  283.5 63.0 all-gather.4
  348.1 36.9 all-gather.6
  469.2 38.8 reduce-scatter.8
  547.7 68.2 reduce-scatter.10
  618.8 63.0 all-gather.8
  684.2 36.9 all-gather.10

commit v12 on v11

--- a/solution.py
+++ b/solution.py
@@ -4,6 +4,7 @@
 import jax.numpy as jnp
 from jax import lax
 from jax.experimental import pallas as pl
+from jax.experimental.pallas import tpu as pltpu
 from jax.sharding import PartitionSpec as P
 
 ITERS = 2
@@ -55,11 +56,15 @@
     )(*fields, terms)
 
 
-def row_kernel(*refs, blocks, has_halo):
+def row_kernel(*refs, blocks, has_halo, with_log):
+    if with_log:
+        *refs, w_ref, o_ref, log_ref = refs
+    else:
+        *refs, o_ref = refs
     if has_halo:
-        prev_ref, mid_ref, next_ref, t_ref, o_ref = refs
+        prev_ref, mid_ref, next_ref, t_ref = refs
     else:
-        mid_ref, t_ref, o_ref = refs
+        mid_ref, t_ref = refs
     nlocal = t_ref.shape[0]
     width = t_ref.shape[2]
     for i, b in enumerate(blocks):
@@ -74,10 +79,13 @@
                 src = mid_ref[e * width : (e + 1) * width, :]
             prod = jnp.dot(t_ref[b, o], src, preferred_element_type=jnp.float32)
             acc = prod if acc is None else acc + prod
-        o_ref[i * width : (i + 1) * width, :] = acc.astype(o_ref.dtype)
-
-
-def row_pass(mid, terms_local, blocks, halos=None, tile_cols=768):
+        rounded = acc.astype(o_ref.dtype)
+        o_ref[i * width : (i + 1) * width, :] = rounded
+        if with_log:
+            log_ref[i * width : (i + 1) * width, :] = w_ref[0] * jnp.log(rounded.astype(jnp.float32))
+
+
+def row_pass(mid, terms_local, blocks, halos=None, weight=None, tile_cols=768):
     rows, cols = mid.shape
     width = terms_local.shape[2]
     tile = lambda r: pl.BlockSpec((r, tile_cols), lambda c: (0, c))
@@ -87,12 +95,20 @@
         prev, nxt = halos
         operands = [prev, mid, nxt, terms_local]
         specs = [tile(prev.shape[0]), tile(rows), tile(nxt.shape[0]), specs[1]]
+    out_rows = len(blocks) * width
+    out_specs = tile(out_rows)
+    out_shape = jax.ShapeDtypeStruct((out_rows, cols), jnp.bfloat16)
+    if weight is not None:
+        operands.append(weight.reshape((1,)))
+        specs.append(pl.BlockSpec(memory_space=pltpu.SMEM))
+        out_specs = [out_specs, tile(out_rows)]
+        out_shape = [out_shape, jax.ShapeDtypeStruct((out_rows, cols), jnp.float32)]
     return pl.pallas_call(
-        functools.partial(row_kernel, blocks=tuple(blocks), has_halo=halos is not None),
+        functools.partial(row_kernel, blocks=tuple(blocks), has_halo=halos is not None, with_log=weight is not None),
         grid=(cols // tile_cols,),
         in_specs=specs,
-        out_specs=tile(len(blocks) * width),
-        out_shape=jax.ShapeDtypeStruct((len(blocks) * width, cols), jnp.bfloat16),
+        out_specs=out_specs,
+        out_shape=out_shape,
     )(*operands)
 
 
@@ -141,8 +157,8 @@
         inner = jnp.concatenate([inner_edges[:halo], column_pass(inside, terms), inner_edges[halo:]], axis=0)
         return row_pass(inner, terms_local, all_blocks, halos)
 
-    def log_sum(kernel_u):
-        return lax.psum_scatter(weight * jnp.log(kernel_u), "img", scatter_dimension=0, tiled=True)
+    def log_sum(value_portion):
+        return lax.psum_scatter(value_portion, "img", scatter_dimension=0, tiled=True)
 
     def gather_barycenter(part_sum):
         return lax.all_gather(jnp.exp(part_sum / total_weight), "img", axis=0, tiled=True)
@@ -151,13 +167,15 @@
         inner = column_pass(field, terms)
         halos = exchange(inner[rows - halo :], inner[:halo])
         if not interior:
-            kernel_u = row_pass(inner, terms_local, all_blocks, halos).astype(jnp.float32)
-            return kernel_u, gather_barycenter(log_sum(kernel_u))
-        inside = row_pass(inner, terms_local, interior).astype(jnp.float32)
-        inside_sum = log_sum(inside)
+            kernel_u, portion = row_pass(inner, terms_local, all_blocks, halos, weight)
+            return kernel_u.astype(jnp.float32), gather_barycenter(log_sum(portion))
+        inside, portion = row_pass(inner, terms_local, interior, weight=weight)
+        inside = inside.astype(jnp.float32)
+        inside_sum = log_sum(portion)
         halos, inside_sum = lax.optimization_barrier((halos, inside_sum))
-        edges = row_pass(inner, terms_local, boundary, halos).astype(jnp.float32)
-        edges_bary = gather_barycenter(log_sum(edges))
+        edges, portion = row_pass(inner, terms_local, boundary, halos, weight)
+        edges = edges.astype(jnp.float32)
+        edges_bary = gather_barycenter(log_sum(portion))
         edges_bary, inside_sum = lax.optimization_barrier((edges_bary, inside_sum))
         inside_bary = gather_barycenter(inside_sum)
         return (edges, inside), (edges_bary, inside_bary)

time: 749 us -> 733 us (0.979)
  other arithmetic: 85.1 us -> 67.7 us
    mul x4 -> x0, other arithmetic: 17.9 us -> none  [log_sum(): weight * jnp.log(kernel_u)]
  transfers between devices with their start and end apart: 32 -> 32, of which waited for: 13 -> 13; matrix products, arithmetic and copies ran while one was open for 6% -> 5% of each run, Pallas kernels for 1% -> 1%
where the time goes in v12:
time: 733 us; the launch traced here: 732 us
  waiting for transfers between devices  454 us (62%)
  Pallas kernels  107 us (15%)
  other arithmetic  67.7 us (9%)
  starting transfers between devices  54.5 us (7%)
  local copies, waits for them, and re-layouts  17.1 us (2%)
  blocking collectives  15.7 us (2%)
  between operations  15.3 us (2%)
    all_gather x4, waiting for transfers between devices, gather_barycenter(): lax.all_gather(jnp.exp(part_sum / total_weight), 'img', axis=0, tiled=True)  150 us
    ppermute x4, waiting for transfers between devices, exchange(): first = lax.ppermute(first, 'slab', [(3, 2), (0, 1)])  129 us
    reduce_scatter x4, waiting for transfers between devices, log_sum(): lax.psum_scatter(value_portion, 'img', scatter_dimension=0, tiled=True)  124 us
    pallas_call x6, Pallas kernels, row_pass(): pl.pallas_call(functools.partial(row_kernel, blocks=tuple(blocks), has_ha...  53.7 us
    pallas_call x5, Pallas kernels, column_pass(): pl.pallas_call(column_kernel, grid=(rows // tile_rows,), in_specs=[tile]...  53.6 us
    ppermute x4, waiting for transfers between devices, exchange(): first = lax.ppermute(first, 'slab', [(1, 3), (2, 0)])  50.6 us
    ppermute x4, starting transfers between devices, exchange(): direct_prev = lax.ppermute(to_up, 'slab', [(0, 1), (2, 3)])  24.3 us
    psum x1, blocking collectives, per_device(): total_weight = lax.psum(jnp.sum(fraction_tops).astype(jnp.float32), 'img')  15.7 us
  transfers between devices with their start and end apart: 32, of which 13 were waited for; matrix products, arithmetic and copies ran while one was open for 5% of the time, Pallas kernels for 1%

profile of v12, /device:TPU:0, one launch (start us, length us, event | category | flops | bytes accessed | tf_op | source)
XLA Modules:
  0.0 731.7 jit_solution(6605649139796695776)
XLA Ops:
  8.1 8.3 %select_reduce_fusion.refs_1_.refs_2_ = bf16[24,5,128,128]{3,2,1,0:T(8,128)(2,1)} fusion(pred[24,5,3]{2,1,0:T(8,128)(4,1)S(1)} %broadcast_compare_fusion, bf16[24,3,128,128]{3,2,1,0:T(8,128)(2,1)} %param.8), kind=kLoop, calls=%fused_computation | loop fusion | flops 9830400 | bytes 6291816 | tf_op jit(solution)/shard_map/reduce_sum | solution.py:19
  16.4 10.9 %shard_map.68.refs_1_ = bf16[768,3072]{1,0:T(8,128)(2,1)} custom-call(f32[768,3072]{1,0:T(8,128)} %bitcast.18, bf16[24,5,128,128]{3,2,1,0:T(8,128)(2,1)} %select_reduce_fusion.refs_1_.refs_2_), custom_call_target="tpu_custom_call" | custom-call | tf_op jit(solution)/shard_map/pallas_call | solution.py:50
  34.8 9.2 %collective-permute-start.4 = (bf16[256,3072]{1,0:T(8,128)(2,1)S(1)}, bf16[256,3072]{1,0:T(8,128)(2,1)}, u32[]{:S(2)}, u32[]{:S(2)}) collective-permute-start(bf16[256,3072]{1,0:T(8,128)(2,1)S(1)} %get-tuple-element.53), channel_id=1, source_target_pairs={{0,1},{2,3},{4,5},{6,7},{8,9},{10,11},{12,13},{14,15},{16,17},{18,... | collective-permute-start | bytes 4718600 | tf_op jit(solution)/shard_map/ppermute | solution.py:135
  44.0 11.5 %collective-permute-done = bf16[128,3072]{1,0:T(8,128)(2,1)} collective-permute-done((bf16[128,3072]{1,0:T(8,128)(2,1)S(1)}, bf16[128,3072]{1,0:T(8,128)(2,1)}, u32[]{:S(2)}, u32[]{:S(2)}) %collective-permute-start) | collective-permute-done | bytes 786464 | tf_op jit(solution)/shard_map/ppermute | solution.py:139
  62.7 30.4 %collective-permute-done.1 = bf16[128,3072]{1,0:T(8,128)(2,1)} collective-permute-done((bf16[128,3072]{1,0:T(8,128)(2,1)}, bf16[128,3072]{1,0:T(8,128)(2,1)}, u32[]{:S(2)}, u32[]{:S(2)}) %collective-permute-start.1) | collective-permute-done | bytes 786464 | tf_op jit(solution)/shard_map/ppermute | solution.py:141
  98.9 10.2 %shard_map.69.refs_1_ = bf16[768,3072]{1,0:T(8,128)(2,1)} custom-call(bf16[256,3072]{1,0:T(8,128)(2,1)} %get-tuple-element.67.refs_0_, bf16[768,3072]{1,0:T(8,128)(2,1)} %shard_map.68.refs_1_, bf16[256,3072]{1,0:T(8,128)(2,1)} %get-tuple-element.66.refs_2_, bf16[6,5,128,128]{3,2,1,0:T(8,128)(2,1)} %constant_dynamic-slice_fusion.refs_3_.refs_1_), custom_call_target="tpu_custom_call" | custom-call | tf_op jit(solution)/shard_map/pallas_call | solution.py:106
  109.0 12.8 %shard_map.70.refs_0_.refs_1_ = bf16[768,3072]{1,0:T(8,128)(2,1)} custom-call(f32[768,3072]{1,0:T(8,128)} %bitcast.15, bf16[768,3072]{1,0:T(8,128)(2,1)} %shard_map.69.refs_1_, bf16[24,5,128,128]{3,2,1,0:T(8,128)(2,1)} %select_reduce_fusion.refs_1_.refs_2_), custom_call_target="tpu_custom_call" | custom-call | tf_op jit(solution)/shard_map/pallas_call | solution.py:50
  121.8 6.6 shard_map.71
  139.9 12.3 %collective-permute-done.6 = bf16[128,3072]{1,0:T(8,128)(2,1)S(1)} collective-permute-done((bf16[128,3072]{1,0:T(8,128)(2,1)S(1)}, bf16[128,3072]{1,0:T(8,128)(2,1)S(1)}, u32[]{:S(2)}, u32[]{:S(2)}) %collective-permute-start.6) | collective-permute-done | bytes 786464 | tf_op jit(solution)/shard_map/ppermute | solution.py:139
  155.2 33.7 %collective-permute-done.7 = bf16[128,3072]{1,0:T(8,128)(2,1)S(1)} collective-permute-done((bf16[128,3072]{1,0:T(8,128)(2,1)S(1)}, bf16[128,3072]{1,0:T(8,128)(2,1)S(1)}, u32[]{:S(2)}, u32[]{:S(2)}) %collective-permute-start.7) | collective-permute-done | bytes 786464 | tf_op jit(solution)/shard_map/ppermute | solution.py:141
  191.1 10.1 %shard_map.72 = (bf16[512,3072]{1,0:T(8,128)(2,1)}, f32[512,3072]{1,0:T(8,128)}) custom-call(bf16[256,3072]{1,0:T(8,128)(2,1)} %get-tuple-element.21.refs_0_, bf16[768,3072]{1,0:T(8,128)(2,1)} %shard_map.70.refs_0_.refs_1_, bf16[256,3072]{1,0:T(8,128)(2,1)} %get-tuple-element.22.refs_2_, bf16[6,5,128,128]{3,2,1,0:T(8,128)(2,1)} %constant_dynamic-slice_fusion.refs_3_.refs_1_, ...), custom_call_target="tpu_custom_call" | custom-call | tf_op jit(solution)/shard_map/pallas_call | solution.py:106
  201.3 15.7 %psum.7 = f32[]{:T(128)} all-reduce(f32[]{:T(128)} %bitcast.2), channel_id=1, replica_groups=mesh['img'=8,'slab'=4] {'img'}, use_global_device_ids=true, to_apply=%region_3.4 | all-reduce | flops 1 | bytes 8 | tf_op jit(solution)/shard_map/psum | solution.py:125
  217.0 55.6 %reduce-scatter.7.cloned.1.call-done = f32[64,3072]{1,0:T(8,128)} async-done(((f32[512,3072]{1,0:T(8,128)}), f32[64,3072]{1,0:T(8,128)}) %reduce-scatter.7.cloned.1.call-update) | async-done | bytes 786448 | tf_op jit(solution)/shard_map/reduce_scatter | solution.py:161
  275.5 63.1 %all-gather.5.cloned.1.call-done.refs_0_ = f32[512,3072]{1,0:T(8,128)} async-done(((f32[64,3072]{1,0:T(8,128)}), f32[512,3072]{1,0:T(8,128)}) %all-gather.5.cloned.1.call-update) | async-done | bytes 6291472 | tf_op jit(solution)/shard_map/all_gather | solution.py:164
  343.7 9.9 %shard_map.73 = bf16[512,3072]{1,0:T(8,128)(2,1)} custom-call(f32[512,3072]{1,0:T(8,128)} %all-gather.5.cloned.1.call-done.refs_0_, f32[512,3072]{1,0:T(8,128)} %convert_element_type.21.refs_1_, bf16[24,5,128,128]{3,2,1,0:T(8,128)(2,1)} %select_reduce_fusion.refs_1_.refs_2_), custom_call_target="tpu_custom_call" | custom-call | tf_op jit(solution)/shard_map/pallas_call | solution.py:50
  360.0 5.5 collective-permute-start.16
  365.5 14.0 %collective-permute-done.12 = bf16[128,3072]{1,0:T(8,128)(2,1)S(1)} collective-permute-done((bf16[128,3072]{1,0:T(8,128)(2,1)S(1)}, bf16[128,3072]{1,0:T(8,128)(2,1)S(1)}, u32[]{:S(2)}, u32[]{:S(2)}) %collective-permute-start.12) | collective-permute-done | bytes 786464 | tf_op jit(solution)/shard_map/ppermute | solution.py:139
  384.6 31.4 %collective-permute-done.13 = bf16[128,3072]{1,0:T(8,128)(2,1)S(1)} collective-permute-done((bf16[128,3072]{1,0:T(8,128)(2,1)S(1)}, bf16[128,3072]{1,0:T(8,128)(2,1)S(1)}, u32[]{:S(2)}, u32[]{:S(2)}) %collective-permute-start.13) | collective-permute-done | bytes 786464 | tf_op jit(solution)/shard_map/ppermute | solution.py:141
  418.1 7.2 shard_map.74
  428.8 10.2 %shard_map.75.refs_1_ = bf16[768,3072]{1,0:T(8,128)(2,1)} custom-call(bf16[256,3072]{1,0:T(8,128)(2,1)} %get-tuple-element.63.refs_0_, bf16[768,3072]{1,0:T(8,128)(2,1)} %pad_maximum_fusion.1.refs_1_, bf16[256,3072]{1,0:T(8,128)(2,1)} %get-tuple-element.62.refs_2_, bf16[6,5,128,128]{3,2,1,0:T(8,128)(2,1)} %constant_dynamic-slice_fusion.refs_3_.refs_1_), custom_call_target="tpu_custom_call" | custom-call | tf_op jit(solution)/shard_map/pallas_call | solution.py:106
  439.0 12.8 %shard_map.76.refs_0_.refs_1_ = bf16[768,3072]{1,0:T(8,128)(2,1)} custom-call(f32[768,3072]{1,0:T(8,128)} %bitcast.16, bf16[768,3072]{1,0:T(8,128)(2,1)} %shard_map.75.refs_1_, bf16[24,5,128,128]{3,2,1,0:T(8,128)(2,1)} %select_reduce_fusion.refs_1_.refs_2_), custom_call_target="tpu_custom_call" | custom-call | tf_op jit(solution)/shard_map/pallas_call | solution.py:50
  451.8 6.6 shard_map.77
  464.8 4.8 collective-permute-start.22
  469.7 12.8 %collective-permute-done.18 = bf16[128,3072]{1,0:T(8,128)(2,1)S(1)} collective-permute-done((bf16[128,3072]{1,0:T(8,128)(2,1)S(1)}, bf16[128,3072]{1,0:T(8,128)(2,1)S(1)}, u32[]{:S(2)}, u32[]{:S(2)}) %collective-permute-start.18) | collective-permute-done | bytes 786464 | tf_op jit(solution)/shard_map/ppermute | solution.py:139
  485.5 33.7 %collective-permute-done.19 = bf16[128,3072]{1,0:T(8,128)(2,1)S(1)} collective-permute-done((bf16[128,3072]{1,0:T(8,128)(2,1)S(1)}, bf16[128,3072]{1,0:T(8,128)(2,1)S(1)}, u32[]{:S(2)}, u32[]{:S(2)}) %collective-permute-start.19) | collective-permute-done | bytes 786464 | tf_op jit(solution)/shard_map/ppermute | solution.py:141
  521.3 10.1 %shard_map.78 = (bf16[512,3072]{1,0:T(8,128)(2,1)}, f32[512,3072]{1,0:T(8,128)}) custom-call(bf16[256,3072]{1,0:T(8,128)(2,1)} %get-tuple-element.30.refs_0_, bf16[768,3072]{1,0:T(8,128)(2,1)} %shard_map.76.refs_0_.refs_1_, bf16[256,3072]{1,0:T(8,128)(2,1)} %get-tuple-element.31.refs_2_, bf16[6,5,128,128]{3,2,1,0:T(8,128)(2,1)} %constant_dynamic-slice_fusion.refs_3_.refs_1_, ...), custom_call_target="tpu_custom_call" | custom-call | tf_op jit(solution)/shard_map/pallas_call | solution.py:106
  531.5 68.4 %reduce-scatter.11.cloned.1.call-done = f32[64,3072]{1,0:T(8,128)} async-done(((f32[512,3072]{1,0:T(8,128)}), f32[64,3072]{1,0:T(8,128)}) %reduce-scatter.11.cloned.1.call-update) | async-done | bytes 786448 | tf_op jit(solution)/shard_map/reduce_scatter | solution.py:161
  603.1 62.9 %all-gather.9.cloned.1.call-done = f32[512,3072]{1,0:T(8,128)} async-done(((f32[64,3072]{1,0:T(8,128)}), f32[512,3072]{1,0:T(8,128)}) %all-gather.9.cloned.1.call-update) | async-done | bytes 6291472 | tf_op jit(solution)/shard_map/all_gather | solution.py:164
  675.8 5.5 slice_bitcast_fusion.3
  681.3 23.9 %all-gather.11.cloned.1.call-done = f32[256,3072]{1,0:T(8,128)} async-done(((f32[32,3072]{1,0:T(8,128)}), f32[256,3072]{1,0:T(8,128)}) %all-gather.11.cloned.1.call-update) | async-done | bytes 3145744 | tf_op jit(solution)/shard_map/all_gather | solution.py:164
  705.2 11.9 %maximum_divide_fusion = f32[1,768,3072]{2,1,0:T(8,128)} fusion(f32[1,256,3072]{2,1,0:T(8,128)} %get-tuple-element.41, f32[1,256,3072]{2,1,0:T(8,128)} %bitcast.17, f32[1,256,3072]{2,1,0:T(8,128)} %get-tuple-element.40, f32[1,256,3072]{2,1,0:T(8,128)} %get-tuple-element.39, f32[1,256,3072]{2,1,0:T(8,128)} %bitcast_convert_fusion, ...), kind=kLoop, calls=%fused_computation.2 | loop fusion | flops 11796480 | bytes 28311552 | tf_op jit(solution)/shard_map/div | solution.py:199
  717.1 7.7 %pad_maximum_fusion = f32[768,3072]{1,0:T(8,128)} fusion(f32[256,3072]{1,0:T(8,128)} %get-tuple-element.42, f32[256,3072]{1,0:T(8,128)S(1)} %copy-done.4, f32[256,3072]{1,0:T(8,128)} %get-tuple-element.43), kind=kLoop, calls=%fused_computation.1 | loop fusion | flops 4718592 | bytes 18874368 | tf_op jit(solution)/shard_map/concatenate | solution.py:185
  (115 shorter events, 86.6 us)
Async XLA Ops:
  7.2 183.9 %reduce-scatter.5.cloned.1.call-start = ((), (), s32[]{:S(2)}) async-start(), calls=%async_computation.4 | async-start | bytes 3538944 | tf_op jit(solution)/shard_map/reduce_scatter | solution.py:161
  29.4 28.2 %collective-permute-start.2 = (bf16[128,3072]{1,0:T(8,128)(2,1)S(1)}, bf16[128,3072]{1,0:T(8,128)(2,1)}, u32[]{:S(2)}, u32[]{:S(2)}) collective-permute-start(bf16[128,3072]{1,0:T(8,128)(2,1)S(1)} %get-tuple-element.54), channel_id=1, source_target_pairs={{1,0},{2,3},{5,4},{6,7},{9,8},{10,11},{13,12},{14,15},{17,16},{18,... | collective-permute-start | bytes 2359304 | tf_op jit(solution)/shard_map/ppermute | solution.py:140
  30.8 24.6 %collective-permute-start = (bf16[128,3072]{1,0:T(8,128)(2,1)S(1)}, bf16[128,3072]{1,0:T(8,128)(2,1)}, u32[]{:S(2)}, u32[]{:S(2)}) collective-permute-start(bf16[128,3072]{1,0:T(8,128)(2,1)S(1)} %get-tuple-element.55), channel_id=1, source_target_pairs={{1,3},{2,0},{5,7},{6,4},{9,11},{10,8},{13,15},{14,12},{17,19},{18,... | collective-permute-start | bytes 2359304 | tf_op jit(solution)/shard_map/ppermute | solution.py:139
  33.5 62.0 %collective-permute-start.5 = (bf16[256,3072]{1,0:T(8,128)(2,1)}, bf16[256,3072]{1,0:T(8,128)(2,1)S(1)}, u32[]{:S(2)}, u32[]{:S(2)}) collective-permute-start(bf16[256,3072]{1,0:T(8,128)(2,1)} %get-tuple-element.52), channel_id=1, source_target_pairs={{1,0},{3,2},{5,4},{7,6},{9,8},{11,10},{13,12},{15,14},{17,16},{19,... | collective-permute-start | bytes 4718600 | tf_op jit(solution)/shard_map/ppermute | solution.py:136
  34.8 60.7 %collective-permute-start.4 = (bf16[256,3072]{1,0:T(8,128)(2,1)S(1)}, bf16[256,3072]{1,0:T(8,128)(2,1)}, u32[]{:S(2)}, u32[]{:S(2)}) collective-permute-start(bf16[256,3072]{1,0:T(8,128)(2,1)S(1)} %get-tuple-element.53), channel_id=1, source_target_pairs={{0,1},{2,3},{4,5},{6,7},{8,9},{10,11},{12,13},{14,15},{16,17},{18,... | collective-permute-start | bytes 4718600 | tf_op jit(solution)/shard_map/ppermute | solution.py:135
  55.4 37.6 %collective-permute-start.1 = (bf16[128,3072]{1,0:T(8,128)(2,1)}, bf16[128,3072]{1,0:T(8,128)(2,1)}, u32[]{:S(2)}, u32[]{:S(2)}) collective-permute-start(bf16[128,3072]{1,0:T(8,128)(2,1)} %collective-permute-done), channel_id=1, source_target_pairs={{3,2},{0,1},{7,6},{4,5},{11,10},{8,9},{15,14},{12,13},{19,18},{16,... | collective-permute-start | bytes 2359304 | tf_op jit(solution)/shard_map/ppermute | solution.py:141
  57.6 36.6 %collective-permute-start.3 = (bf16[128,3072]{1,0:T(8,128)(2,1)}, bf16[128,3072]{1,0:T(8,128)(2,1)}, u32[]{:S(2)}, u32[]{:S(2)}) collective-permute-start(bf16[128,3072]{1,0:T(8,128)(2,1)} %collective-permute-done.2), channel_id=1, source_target_pairs={{0,2},{3,1},{4,6},{7,5},{8,10},{11,9},{12,14},{15,13},{16,18},{19,... | collective-permute-start | bytes 2359304 | tf_op jit(solution)/shard_map/ppermute | solution.py:142
  128.4 144.2 %reduce-scatter.7.cloned.1.call-start = ((), (), s32[]{:S(2)}) async-start(), calls=%async_computation.5 | async-start | bytes 7077888 | tf_op jit(solution)/shard_map/reduce_scatter | solution.py:161
  130.6 23.3 %collective-permute-start.8 = (bf16[128,3072]{1,0:T(8,128)(2,1)S(1)}, bf16[128,3072]{1,0:T(8,128)(2,1)S(1)}, u32[]{:S(2)}, u32[]{:S(2)}) collective-permute-start(bf16[128,3072]{1,0:T(8,128)(2,1)S(1)} %get-tuple-element.50), channel_id=1, source_target_pairs={{1,0},{2,3},{5,4},{6,7},{9,8},{10,11},{13,12},{14,15},{17,16},{18,... | collective-permute-start | bytes 2359304 | tf_op jit(solution)/shard_map/ppermute | solution.py:140
  132.2 20.0 %collective-permute-start.6 = (bf16[128,3072]{1,0:T(8,128)(2,1)S(1)}, bf16[128,3072]{1,0:T(8,128)(2,1)S(1)}, u32[]{:S(2)}, u32[]{:S(2)}) collective-permute-start(bf16[128,3072]{1,0:T(8,128)(2,1)S(1)} %get-tuple-element.51), channel_id=1, source_target_pairs={{1,3},{2,0},{5,7},{6,4},{9,11},{10,8},{13,15},{14,12},{17,19},{18,... | collective-permute-start | bytes 2359304 | tf_op jit(solution)/shard_map/ppermute | solution.py:139
  133.7 55.3 %collective-permute-start.11 = (bf16[256,3072]{1,0:T(8,128)(2,1)S(1)}, bf16[256,3072]{1,0:T(8,128)(2,1)S(1)}, u32[]{:S(2)}, u32[]{:S(2)}) collective-permute-start(bf16[256,3072]{1,0:T(8,128)(2,1)S(1)} %get-tuple-element.48), channel_id=1, source_target_pairs={{1,0},{3,2},{5,4},{7,6},{9,8},{11,10},{13,12},{15,14},{17,16},{19,... | collective-permute-start | bytes 4718600 | tf_op jit(solution)/shard_map/ppermute | solution.py:136
  135.0 54.0 %collective-permute-start.10 = (bf16[256,3072]{1,0:T(8,128)(2,1)S(1)}, bf16[256,3072]{1,0:T(8,128)(2,1)S(1)}, u32[]{:S(2)}, u32[]{:S(2)}) collective-permute-start(bf16[256,3072]{1,0:T(8,128)(2,1)S(1)} %get-tuple-element.49), channel_id=1, source_target_pairs={{0,1},{2,3},{4,5},{6,7},{8,9},{10,11},{12,13},{14,15},{16,17},{18,... | collective-permute-start | bytes 4718600 | tf_op jit(solution)/shard_map/ppermute | solution.py:135
  152.2 36.7 %collective-permute-start.7 = (bf16[128,3072]{1,0:T(8,128)(2,1)S(1)}, bf16[128,3072]{1,0:T(8,128)(2,1)S(1)}, u32[]{:S(2)}, u32[]{:S(2)}) collective-permute-start(bf16[128,3072]{1,0:T(8,128)(2,1)S(1)} %collective-permute-done.6), channel_id=1, source_target_pairs={{3,2},{0,1},{7,6},{4,5},{11,10},{8,9},{15,14},{12,13},{19,18},{16,... | collective-permute-start | bytes 2359304 | tf_op jit(solution)/shard_map/ppermute | solution.py:141
  153.9 35.1 %collective-permute-start.9 = (bf16[128,3072]{1,0:T(8,128)(2,1)S(1)}, bf16[128,3072]{1,0:T(8,128)(2,1)S(1)}, u32[]{:S(2)}, u32[]{:S(2)}) collective-permute-start(bf16[128,3072]{1,0:T(8,128)(2,1)S(1)} %collective-permute-done.8), channel_id=1, source_target_pairs={{0,2},{3,1},{4,6},{7,5},{8,10},{11,9},{12,14},{15,13},{16,18},{19,... | collective-permute-start | bytes 2359304 | tf_op jit(solution)/shard_map/ppermute | solution.py:142
  201.2 137.4 %all-gather.5.cloned.1.call-start = ((), (), s32[]{:S(2)}) async-start(), calls=%async_computation.6 | async-start | bytes 7077888 | tf_op jit(solution)/shard_map/all_gather | solution.py:164
  275.4 142.7 %all-gather.7.cloned.1.call-start = ((), (), s32[]{:S(2)}) async-start(), calls=%async_computation.7 | async-start | bytes 3538944 | tf_op jit(solution)/shard_map/all_gather | solution.py:164
  340.1 181.2 %reduce-scatter.9.cloned.1.call-start = ((), (), s32[]{:S(2)}) async-start(), calls=%async_computation.8 | async-start | bytes 3538944 | tf_op jit(solution)/shard_map/reduce_scatter | solution.py:161
  355.8 25.3 %collective-permute-start.14 = (bf16[128,3072]{1,0:T(8,128)(2,1)S(1)}, bf16[128,3072]{1,0:T(8,128)(2,1)S(1)}, u32[]{:S(2)}, u32[]{:S(2)}) collective-permute-start(bf16[128,3072]{1,0:T(8,128)(2,1)S(1)} %get-tuple-element.58), channel_id=1, source_target_pairs={{1,0},{2,3},{5,4},{6,7},{9,8},{10,11},{13,12},{14,15},{17,16},{18,... | collective-permute-start | bytes 2359304 | tf_op jit(solution)/shard_map/ppermute | solution.py:140
  357.1 22.5 %collective-permute-start.12 = (bf16[128,3072]{1,0:T(8,128)(2,1)S(1)}, bf16[128,3072]{1,0:T(8,128)(2,1)S(1)}, u32[]{:S(2)}, u32[]{:S(2)}) collective-permute-start(bf16[128,3072]{1,0:T(8,128)(2,1)S(1)} %get-tuple-element.59), channel_id=1, source_target_pairs={{1,3},{2,0},{5,7},{6,4},{9,11},{10,8},{13,15},{14,12},{17,19},{18,... | collective-permute-start | bytes 2359304 | tf_op jit(solution)/shard_map/ppermute | solution.py:139
  358.7 57.5 %collective-permute-start.17 = (bf16[256,3072]{1,0:T(8,128)(2,1)S(1)}, bf16[256,3072]{1,0:T(8,128)(2,1)S(1)}, u32[]{:S(2)}, u32[]{:S(2)}) collective-permute-start(bf16[256,3072]{1,0:T(8,128)(2,1)S(1)} %get-tuple-element.56), channel_id=1, source_target_pairs={{1,0},{3,2},{5,4},{7,6},{9,8},{11,10},{13,12},{15,14},{17,16},{19,... | collective-permute-start | bytes 4718600 | tf_op jit(solution)/shard_map/ppermute | solution.py:136
  360.0 56.2 %collective-permute-start.16 = (bf16[256,3072]{1,0:T(8,128)(2,1)S(1)}, bf16[256,3072]{1,0:T(8,128)(2,1)S(1)}, u32[]{:S(2)}, u32[]{:S(2)}) collective-permute-start(bf16[256,3072]{1,0:T(8,128)(2,1)S(1)} %get-tuple-element.57), channel_id=1, source_target_pairs={{0,1},{2,3},{4,5},{6,7},{8,9},{10,11},{12,13},{14,15},{16,17},{18,... | collective-permute-start | bytes 4718600 | tf_op jit(solution)/shard_map/ppermute | solution.py:135
  379.6 36.5 %collective-permute-start.13 = (bf16[128,3072]{1,0:T(8,128)(2,1)S(1)}, bf16[128,3072]{1,0:T(8,128)(2,1)S(1)}, u32[]{:S(2)}, u32[]{:S(2)}) collective-permute-start(bf16[128,3072]{1,0:T(8,128)(2,1)S(1)} %collective-permute-done.12), channel_id=1, source_target_pairs={{3,2},{0,1},{7,6},{4,5},{11,10},{8,9},{15,14},{12,13},{19,18},{16,... | collective-permute-start | bytes 2359304 | tf_op jit(solution)/shard_map/ppermute | solution.py:141
  381.0 35.1 %collective-permute-start.15 = (bf16[128,3072]{1,0:T(8,128)(2,1)S(1)}, bf16[128,3072]{1,0:T(8,128)(2,1)S(1)}, u32[]{:S(2)}, u32[]{:S(2)}) collective-permute-start(bf16[128,3072]{1,0:T(8,128)(2,1)S(1)} %collective-permute-done.14), channel_id=1, source_target_pairs={{0,2},{3,1},{4,6},{7,5},{8,10},{11,9},{12,14},{15,13},{16,18},{19,... | collective-permute-start | bytes 2359304 | tf_op jit(solution)/shard_map/ppermute | solution.py:142
  458.4 141.6 %reduce-scatter.11.cloned.1.call-start = ((), (), s32[]{:S(2)}) async-start(), calls=%async_computation.9 | async-start | bytes 7077888 | tf_op jit(solution)/shard_map/reduce_scatter | solution.py:161
  460.6 23.6 %collective-permute-start.20 = (bf16[128,3072]{1,0:T(8,128)(2,1)S(1)}, bf16[128,3072]{1,0:T(8,128)(2,1)S(1)}, u32[]{:S(2)}, u32[]{:S(2)}) collective-permute-start(bf16[128,3072]{1,0:T(8,128)(2,1)S(1)} %get-tuple-element.46), channel_id=1, source_target_pairs={{1,0},{2,3},{5,4},{6,7},{9,8},{10,11},{13,12},{14,15},{17,16},{18,... | collective-permute-start | bytes 2359304 | tf_op jit(solution)/shard_map/ppermute | solution.py:140
  462.0 20.5 %collective-permute-start.18 = (bf16[128,3072]{1,0:T(8,128)(2,1)S(1)}, bf16[128,3072]{1,0:T(8,128)(2,1)S(1)}, u32[]{:S(2)}, u32[]{:S(2)}) collective-permute-start(bf16[128,3072]{1,0:T(8,128)(2,1)S(1)} %get-tuple-element.47), channel_id=1, source_target_pairs={{1,3},{2,0},{5,7},{6,4},{9,11},{10,8},{13,15},{14,12},{17,19},{18,... | collective-permute-start | bytes 2359304 | tf_op jit(solution)/shard_map/ppermute | solution.py:139
  463.5 55.8 %collective-permute-start.23 = (bf16[256,3072]{1,0:T(8,128)(2,1)S(1)}, bf16[256,3072]{1,0:T(8,128)(2,1)S(1)}, u32[]{:S(2)}, u32[]{:S(2)}) collective-permute-start(bf16[256,3072]{1,0:T(8,128)(2,1)S(1)} %get-tuple-element.44), channel_id=1, source_target_pairs={{1,0},{3,2},{5,4},{7,6},{9,8},{11,10},{13,12},{15,14},{17,16},{19,... | collective-permute-start | bytes 4718600 | tf_op jit(solution)/shard_map/ppermute | solution.py:136
  464.8 54.5 %collective-permute-start.22 = (bf16[256,3072]{1,0:T(8,128)(2,1)S(1)}, bf16[256,3072]{1,0:T(8,128)(2,1)S(1)}, u32[]{:S(2)}, u32[]{:S(2)}) collective-permute-start(bf16[256,3072]{1,0:T(8,128)(2,1)S(1)} %get-tuple-element.45), channel_id=1, source_target_pairs={{0,1},{2,3},{4,5},{6,7},{8,9},{10,11},{12,13},{14,15},{16,17},{18,... | collective-permute-start | bytes 4718600 | tf_op jit(solution)/shard_map/ppermute | solution.py:135
  482.5 36.7 %collective-permute-start.19 = (bf16[128,3072]{1,0:T(8,128)(2,1)S(1)}, bf16[128,3072]{1,0:T(8,128)(2,1)S(1)}, u32[]{:S(2)}, u32[]{:S(2)}) collective-permute-start(bf16[128,3072]{1,0:T(8,128)(2,1)S(1)} %collective-permute-done.18), channel_id=1, source_target_pairs={{3,2},{0,1},{7,6},{4,5},{11,10},{8,9},{15,14},{12,13},{19,18},{16,... | collective-permute-start | bytes 2359304 | tf_op jit(solution)/shard_map/ppermute | solution.py:141
  484.2 35.1 %collective-permute-start.21 = (bf16[128,3072]{1,0:T(8,128)(2,1)S(1)}, bf16[128,3072]{1,0:T(8,128)(2,1)S(1)}, u32[]{:S(2)}, u32[]{:S(2)}) collective-permute-start(bf16[128,3072]{1,0:T(8,128)(2,1)S(1)} %collective-permute-done.20), channel_id=1, source_target_pairs={{0,2},{3,1},{4,6},{7,5},{8,10},{11,9},{12,14},{15,13},{16,18},{19,... | collective-permute-start | bytes 2359304 | tf_op jit(solution)/shard_map/ppermute | solution.py:142
  531.4 134.6 %all-gather.9.cloned.1.call-start = ((), (), s32[]{:S(2)}) async-start(), calls=%async_computation.10 | async-start | bytes 7077888 | tf_op jit(solution)/shard_map/all_gather | solution.py:164
  602.8 102.4 %all-gather.11.cloned.1.call-start = ((), (), s32[]{:S(2)}) async-start(), calls=%async_computation.11 | async-start | bytes 3538944 | tf_op jit(solution)/shard_map/all_gather | solution.py:164
  (12 other events, 544.9 us)
Sparse Core Ops, SparseCore 0:
  128.5 41.6 reduce-scatter.4
  201.3 71.2 reduce-scatter.6
  275.5 63.0 all-gather.4
  340.2 36.9 all-gather.6
  458.5 38.8 reduce-scatter.8
  531.6 68.3 reduce-scatter.10
  602.9 63.0 all-gather.8
  668.2 36.9 all-gather.10

commit v13 on v12

--- a/solution.py
+++ b/solution.py
@@ -61,10 +61,20 @@
         *refs, w_ref, o_ref, log_ref = refs
     else:
         *refs, o_ref = refs
-    if has_halo:
+    diag_ref = slab_ref = None
+    if has_halo == 2:
+        prev_ref, mid_ref, next_ref, t_ref, diag_ref, slab_ref = refs
+    elif has_halo:
         prev_ref, mid_ref, next_ref, t_ref = refs
     else:
         mid_ref, t_ref = refs
+
+    def halo_block(ref, start, owner):
+        block = ref[start : start + width, :]
+        if diag_ref is None:
+            return block
+        return jnp.where(slab_ref[0] == owner, diag_ref[start : start + width, :], block)
+
     nlocal = t_ref.shape[0]
     width = t_ref.shape[2]
     for i, b in enumerate(blocks):
@@ -72,9 +82,9 @@
         for o in range(OFFSETS):
             e = b + o - HALO
             if e < 0:
-                src = prev_ref[(e + HALO) * width : (e + HALO + 1) * width, :]
+                src = halo_block(prev_ref, (e + HALO) * width, 2)
             elif e >= nlocal:
-                src = next_ref[(e - nlocal) * width : (e - nlocal + 1) * width, :]
+                src = halo_block(next_ref, (e - nlocal) * width, 1)
             else:
                 src = mid_ref[e * width : (e + 1) * width, :]
             prod = jnp.dot(t_ref[b, o], src, preferred_element_type=jnp.float32)
@@ -91,10 +101,16 @@
     tile = lambda r: pl.BlockSpec((r, tile_cols), lambda c: (0, c))
     operands = [mid, terms_local]
     specs = [tile(rows), pl.BlockSpec(terms_local.shape, lambda c: (0, 0, 0, 0))]
+    has_halo = 0
     if halos is not None:
-        prev, nxt = halos
+        prev, nxt, diagonal, slab_index = halos
         operands = [prev, mid, nxt, terms_local]
         specs = [tile(prev.shape[0]), tile(rows), tile(nxt.shape[0]), specs[1]]
+        has_halo = 1
+        if diagonal is not None:
+            operands += [diagonal, slab_index]
+            specs += [tile(diagonal.shape[0]), pl.BlockSpec(memory_space=pltpu.SMEM)]
+            has_halo = 2
     out_rows = len(blocks) * width
     out_specs = tile(out_rows)
     out_shape = jax.ShapeDtypeStruct((out_rows, cols), jnp.bfloat16)
@@ -104,7 +120,7 @@
         out_specs = [out_specs, tile(out_rows)]
         out_shape = [out_shape, jax.ShapeDtypeStruct((out_rows, cols), jnp.float32)]
     return pl.pallas_call(
-        functools.partial(row_kernel, blocks=tuple(blocks), has_halo=halos is not None, with_log=weight is not None),
+        functools.partial(row_kernel, blocks=tuple(blocks), has_halo=has_halo, with_log=weight is not None),
         grid=(cols // tile_cols,),
         in_specs=specs,
         out_specs=out_specs,
@@ -130,7 +146,7 @@
 
     def exchange(to_up, to_down):
         if nslab != 4:
-            return lax.ppermute(to_up, "slab", up), lax.ppermute(to_down, "slab", down)
+            return lax.ppermute(to_up, "slab", up), lax.ppermute(to_down, "slab", down), None, None
         half = halo // 2
         direct_prev = lax.ppermute(to_up, "slab", [(0, 1), (2, 3)])
         direct_next = lax.ppermute(to_down, "slab", [(1, 0), (3, 2)])
@@ -141,7 +157,7 @@
         first = lax.ppermute(first, "slab", [(3, 2), (0, 1)])
         second = lax.ppermute(second, "slab", [(0, 2), (3, 1)])
         diagonal = jnp.concatenate([first, second], axis=0)
-        return jnp.where(slab == 2, diagonal, direct_prev), jnp.where(slab == 1, diagonal, direct_next)
+        return direct_prev, direct_next, diagonal, slab.astype(jnp.int32).reshape((1,))
 
     all_blocks = list(range(local_blocks))
     interior = all_blocks[HALO : local_blocks - HALO]

time: 733 us -> 737 us (level)
    ppermute x4, waiting for transfers between devices: 129 us -> 105 us  [exchange(): first = lax.ppermute(first, 'slab', [(3, 2), (0, 1)])]
    ppermute x4, waiting for transfers between devices: 0.01 us -> 10.8 us  [exchange(): direct_prev = lax.ppermute(to_up, 'slab', [(0, 1), (2, 3)])]
    ppermute x4, waiting for transfers between devices: 0.01 us -> 9.35 us  [exchange(): direct_next = lax.ppermute(to_down, 'slab', [(1, 0), (3, 2)])]
    select_n x8 -> x4, other arithmetic: 17.8 us -> 8.62 us  [exchange(): first = jnp.where(slab == 1, to_up[:half], to_down[:half])]
  transfers between devices with their start and end apart: 32 -> 32, of which waited for: 13 -> 18; matrix products, arithmetic and copies ran while one was open for 5% -> 5% of each run, Pallas kernels for 1% -> 2%
where the time goes in v13:
time: 737 us; the launch traced here: 736 us
  waiting for transfers between devices  453 us (61%)
  Pallas kernels  109 us (15%)
  other arithmetic  65 us (9%)
  starting transfers between devices  58.1 us (8%)
  local copies, waits for them, and re-layouts  20 us (3%)
  blocking collectives  15.7 us (2%)
  between operations  15.2 us (2%)
    all_gather x4, waiting for transfers between devices, gather_barycenter(): lax.all_gather(jnp.exp(part_sum / total_weight), 'img', axis=0, tiled=True)  150 us
    reduce_scatter x4, waiting for transfers between devices, log_sum(): lax.psum_scatter(value_portion, 'img', scatter_dimension=0, tiled=True)  124 us
    ppermute x4, waiting for transfers between devices, exchange(): first = lax.ppermute(first, 'slab', [(3, 2), (0, 1)])  105 us
    pallas_call x6, Pallas kernels, row_pass(): pl.pallas_call(functools.partial(row_kernel, blocks=tuple(blocks), has_ha...  55.3 us
    pallas_call x5, Pallas kernels, column_pass(): pl.pallas_call(column_kernel, grid=(rows // tile_rows,), in_specs=[tile]...  53.6 us
    ppermute x4, waiting for transfers between devices, exchange(): first = lax.ppermute(first, 'slab', [(1, 3), (2, 0)])  48.5 us
    ppermute x4, starting transfers between devices, exchange(): direct_prev = lax.ppermute(to_up, 'slab', [(0, 1), (2, 3)])  25.6 us
    psum x1, blocking collectives, per_device(): total_weight = lax.psum(jnp.sum(fraction_tops).astype(jnp.float32), 'img')  15.7 us
  transfers between devices with their start and end apart: 32, of which 18 were waited for; matrix products, arithmetic and copies ran while one was open for 5% of the time, Pallas kernels for 2%

profile of v13, /device:TPU:0, one launch (start us, length us, event | category | flops | bytes accessed | tf_op | source)
XLA Modules:
  0.0 735.7 jit_solution(12158720346020063960)
XLA Ops:
  8.1 8.3 %select_reduce_fusion.refs_1_.refs_2_ = bf16[24,5,128,128]{3,2,1,0:T(8,128)(2,1)} fusion(pred[24,5,3]{2,1,0:T(8,128)(4,1)S(1)} %broadcast_compare_fusion, bf16[24,3,128,128]{3,2,1,0:T(8,128)(2,1)} %param.8), kind=kLoop, calls=%fused_computation | loop fusion | flops 9830400 | bytes 6291816 | tf_op jit(solution)/shard_map/reduce_sum | solution.py:19
  16.4 10.9 %shard_map.68.refs_1_ = bf16[768,3072]{1,0:T(8,128)(2,1)} custom-call(f32[768,3072]{1,0:T(8,128)} %bitcast.19, bf16[24,5,128,128]{3,2,1,0:T(8,128)(2,1)} %select_reduce_fusion.refs_1_.refs_2_), custom_call_target="tpu_custom_call" | custom-call | tf_op jit(solution)/shard_map/pallas_call | solution.py:50
  35.4 8.9 %collective-permute-start = (bf16[256,3072]{1,0:T(8,128)(2,1)}, bf16[256,3072]{1,0:T(8,128)(2,1)S(1)}, u32[]{:S(2)}, u32[]{:S(2)}) collective-permute-start(bf16[256,3072]{1,0:T(8,128)(2,1)} %get-tuple-element.63), channel_id=1, source_target_pairs={{0,1},{2,3},{4,5},{6,7},{8,9},{10,11},{12,13},{14,15},{16,17},{18,... | collective-permute-start | bytes 4718600 | tf_op jit(solution)/shard_map/ppermute | solution.py:151
  44.3 7.1 collective-permute-done.2
  61.7 33.0 %collective-permute-done.3 = bf16[128,3072]{1,0:T(8,128)(2,1)} collective-permute-done((bf16[128,3072]{1,0:T(8,128)(2,1)}, bf16[128,3072]{1,0:T(8,128)(2,1)}, u32[]{:S(2)}, u32[]{:S(2)}) %collective-permute-start.3) | collective-permute-done | bytes 786464 | tf_op jit(solution)/shard_map/ppermute | solution.py:157
  99.0 10.5 %shard_map.69.refs_1_ = bf16[768,3072]{1,0:T(8,128)(2,1)} custom-call(bf16[256,3072]{1,0:T(8,128)(2,1)} %copy-done.8, bf16[768,3072]{1,0:T(8,128)(2,1)} %shard_map.68.refs_1_, bf16[256,3072]{1,0:T(8,128)(2,1)} %copy-done.7, bf16[6,5,128,128]{3,2,1,0:T(8,128)(2,1)} %constant_dynamic-slice_fusion.refs_3_.refs_1_, bf16[256,3072]{1,0:T(8,128)(2,1)} %pad_maximum_fusion.2.refs_4_, ...), custom_call_target="tpu_custom_call" | custom-call | tf_op jit(solution)/shard_map/pallas_call | solution.py:122
  109.5 12.8 %shard_map.70.refs_0_.refs_1_ = bf16[768,3072]{1,0:T(8,128)(2,1)} custom-call(f32[768,3072]{1,0:T(8,128)} %bitcast.16, bf16[768,3072]{1,0:T(8,128)(2,1)} %shard_map.69.refs_1_, bf16[24,5,128,128]{3,2,1,0:T(8,128)(2,1)} %select_reduce_fusion.refs_1_.refs_2_), custom_call_target="tpu_custom_call" | custom-call | tf_op jit(solution)/shard_map/pallas_call | solution.py:50
  122.3 6.6 shard_map.71
  140.3 11.1 %collective-permute-done.8 = bf16[128,3072]{1,0:T(8,128)(2,1)S(1)} collective-permute-done((bf16[128,3072]{1,0:T(8,128)(2,1)S(1)}, bf16[128,3072]{1,0:T(8,128)(2,1)S(1)}, u32[]{:S(2)}, u32[]{:S(2)}) %collective-permute-start.8) | collective-permute-done | bytes 786464 | tf_op jit(solution)/shard_map/ppermute | solution.py:155
  156.6 32.8 %collective-permute-done.9 = bf16[128,3072]{1,0:T(8,128)(2,1)S(1)} collective-permute-done((bf16[128,3072]{1,0:T(8,128)(2,1)S(1)}, bf16[128,3072]{1,0:T(8,128)(2,1)S(1)}, u32[]{:S(2)}, u32[]{:S(2)}) %collective-permute-start.9) | collective-permute-done | bytes 786464 | tf_op jit(solution)/shard_map/ppermute | solution.py:157
  192.4 10.6 %shard_map.72 = (bf16[512,3072]{1,0:T(8,128)(2,1)}, f32[512,3072]{1,0:T(8,128)}) custom-call(bf16[256,3072]{1,0:T(8,128)(2,1)} %copy-done.13, bf16[768,3072]{1,0:T(8,128)(2,1)} %shard_map.70.refs_0_.refs_1_, bf16[256,3072]{1,0:T(8,128)(2,1)} %copy-done.11, bf16[6,5,128,128]{3,2,1,0:T(8,128)(2,1)} %constant_dynamic-slice_fusion.refs_3_.refs_1_, ...), custom_call_target="tpu_custom_call" | custom-call | tf_op jit(solution)/shard_map/pallas_call | solution.py:122
  203.1 15.7 %psum.7 = f32[]{:T(128)} all-reduce(f32[]{:T(128)} %bitcast.3), channel_id=1, replica_groups=mesh['img'=8,'slab'=4] {'img'}, use_global_device_ids=true, to_apply=%region_3.4 | all-reduce | flops 1 | bytes 8 | tf_op jit(solution)/shard_map/psum | solution.py:141
  218.9 55.6 %reduce-scatter.7.cloned.1.call-done = f32[64,3072]{1,0:T(8,128)} async-done(((f32[512,3072]{1,0:T(8,128)}), f32[64,3072]{1,0:T(8,128)}) %reduce-scatter.7.cloned.1.call-update) | async-done | bytes 786448 | tf_op jit(solution)/shard_map/reduce_scatter | solution.py:177
  277.4 63.1 %all-gather.5.cloned.1.call-done.refs_0_ = f32[512,3072]{1,0:T(8,128)} async-done(((f32[64,3072]{1,0:T(8,128)}), f32[512,3072]{1,0:T(8,128)}) %all-gather.5.cloned.1.call-update) | async-done | bytes 6291472 | tf_op jit(solution)/shard_map/all_gather | solution.py:180
  345.6 9.9 %shard_map.73 = bf16[512,3072]{1,0:T(8,128)(2,1)} custom-call(f32[512,3072]{1,0:T(8,128)} %all-gather.5.cloned.1.call-done.refs_0_, f32[512,3072]{1,0:T(8,128)} %convert_element_type.21.refs_1_, bf16[24,5,128,128]{3,2,1,0:T(8,128)(2,1)} %select_reduce_fusion.refs_1_.refs_2_), custom_call_target="tpu_custom_call" | custom-call | tf_op jit(solution)/shard_map/pallas_call | solution.py:50
  360.4 18.9 %collective-permute-done.14 = bf16[128,3072]{1,0:T(8,128)(2,1)S(1)} collective-permute-done((bf16[128,3072]{1,0:T(8,128)(2,1)S(1)}, bf16[128,3072]{1,0:T(8,128)(2,1)S(1)}, u32[]{:S(2)}, u32[]{:S(2)}) %collective-permute-start.14) | collective-permute-done | bytes 786464 | tf_op jit(solution)/shard_map/ppermute | solution.py:155
  384.4 6.9 collective-permute-start.12
  393.3 6.1 collective-permute-done.15
  400.7 7.2 shard_map.74
  411.4 9.3 %collective-permute-done.13.refs_2_ = bf16[256,3072]{1,0:T(8,128)(2,1)} collective-permute-done((bf16[256,3072]{1,0:T(8,128)(2,1)S(1)}, bf16[256,3072]{1,0:T(8,128)(2,1)}, u32[]{:S(2)}, u32[]{:S(2)}) %collective-permute-start.13) | collective-permute-done | bytes 1572896 | tf_op jit(solution)/shard_map/ppermute | solution.py:152
  420.7 10.8 %collective-permute-done.12.refs_0_ = bf16[256,3072]{1,0:T(8,128)(2,1)} collective-permute-done((bf16[256,3072]{1,0:T(8,128)(2,1)S(1)}, bf16[256,3072]{1,0:T(8,128)(2,1)}, u32[]{:S(2)}, u32[]{:S(2)}) %collective-permute-start.12) | collective-permute-done | bytes 1572896 | tf_op jit(solution)/shard_map/ppermute | solution.py:151
  431.5 10.5 %shard_map.75.refs_1_ = bf16[768,3072]{1,0:T(8,128)(2,1)} custom-call(bf16[256,3072]{1,0:T(8,128)(2,1)} %collective-permute-done.12.refs_0_, bf16[768,3072]{1,0:T(8,128)(2,1)} %pad_maximum_fusion.1.refs_1_, bf16[256,3072]{1,0:T(8,128)(2,1)} %collective-permute-done.13.refs_2_, bf16[6,5,128,128]{3,2,1,0:T(8,128)(2,1)} %constant_dynamic-slice_fusion.refs_3_.refs_1_, ...), custom_call_target="tpu_custom_call" | custom-call | tf_op jit(solution)/shard_map/pallas_call | solution.py:122
  442.0 12.8 %shard_map.76.refs_0_.refs_1_ = bf16[768,3072]{1,0:T(8,128)(2,1)} custom-call(f32[768,3072]{1,0:T(8,128)} %bitcast.17, bf16[768,3072]{1,0:T(8,128)(2,1)} %shard_map.75.refs_1_, bf16[24,5,128,128]{3,2,1,0:T(8,128)(2,1)} %select_reduce_fusion.refs_1_.refs_2_), custom_call_target="tpu_custom_call" | custom-call | tf_op jit(solution)/shard_map/pallas_call | solution.py:50
  454.8 6.6 shard_map.77
  472.8 11.4 %collective-permute-done.20 = bf16[128,3072]{1,0:T(8,128)(2,1)S(1)} collective-permute-done((bf16[128,3072]{1,0:T(8,128)(2,1)S(1)}, bf16[128,3072]{1,0:T(8,128)(2,1)S(1)}, u32[]{:S(2)}, u32[]{:S(2)}) %collective-permute-start.20) | collective-permute-done | bytes 786464 | tf_op jit(solution)/shard_map/ppermute | solution.py:155
  489.0 32.9 %collective-permute-done.21 = bf16[128,3072]{1,0:T(8,128)(2,1)S(1)} collective-permute-done((bf16[128,3072]{1,0:T(8,128)(2,1)S(1)}, bf16[128,3072]{1,0:T(8,128)(2,1)S(1)}, u32[]{:S(2)}, u32[]{:S(2)}) %collective-permute-start.21) | collective-permute-done | bytes 786464 | tf_op jit(solution)/shard_map/ppermute | solution.py:157
  524.9 10.6 %shard_map.78 = (bf16[512,3072]{1,0:T(8,128)(2,1)}, f32[512,3072]{1,0:T(8,128)}) custom-call(bf16[256,3072]{1,0:T(8,128)(2,1)} %copy-done.12, bf16[768,3072]{1,0:T(8,128)(2,1)} %shard_map.76.refs_0_.refs_1_, bf16[256,3072]{1,0:T(8,128)(2,1)} %copy-done.10, bf16[6,5,128,128]{3,2,1,0:T(8,128)(2,1)} %constant_dynamic-slice_fusion.refs_3_.refs_1_, ...), custom_call_target="tpu_custom_call" | custom-call | tf_op jit(solution)/shard_map/pallas_call | solution.py:122
  535.6 68.3 %reduce-scatter.11.cloned.1.call-done = f32[64,3072]{1,0:T(8,128)} async-done(((f32[512,3072]{1,0:T(8,128)}), f32[64,3072]{1,0:T(8,128)}) %reduce-scatter.11.cloned.1.call-update) | async-done | bytes 786448 | tf_op jit(solution)/shard_map/reduce_scatter | solution.py:177
  607.0 62.9 %all-gather.9.cloned.1.call-done = f32[512,3072]{1,0:T(8,128)} async-done(((f32[64,3072]{1,0:T(8,128)}), f32[512,3072]{1,0:T(8,128)}) %all-gather.9.cloned.1.call-update) | async-done | bytes 6291472 | tf_op jit(solution)/shard_map/all_gather | solution.py:180
  685.3 23.9 %all-gather.11.cloned.1.call-done = f32[256,3072]{1,0:T(8,128)} async-done(((f32[32,3072]{1,0:T(8,128)}), f32[256,3072]{1,0:T(8,128)}) %all-gather.11.cloned.1.call-update) | async-done | bytes 3145744 | tf_op jit(solution)/shard_map/all_gather | solution.py:180
  709.2 11.9 %maximum_divide_fusion = f32[1,768,3072]{2,1,0:T(8,128)} fusion(f32[1,256,3072]{2,1,0:T(8,128)} %get-tuple-element.49, f32[1,256,3072]{2,1,0:T(8,128)} %bitcast.18, f32[1,256,3072]{2,1,0:T(8,128)} %get-tuple-element.48, f32[1,256,3072]{2,1,0:T(8,128)} %get-tuple-element.47, f32[1,256,3072]{2,1,0:T(8,128)} %bitcast_convert_fusion, ...), kind=kLoop, calls=%fused_computation.2 | loop fusion | flops 11796480 | bytes 28311552 | tf_op jit(solution)/shard_map/div | solution.py:215
  721.1 7.7 %pad_maximum_fusion = f32[768,3072]{1,0:T(8,128)} fusion(f32[256,3072]{1,0:T(8,128)} %get-tuple-element.50, f32[256,3072]{1,0:T(8,128)S(1)} %copy-done.4, f32[256,3072]{1,0:T(8,128)} %get-tuple-element.51), kind=kLoop, calls=%fused_computation.1 | loop fusion | flops 4718592 | bytes 18874368 | tf_op jit(solution)/shard_map/concatenate | solution.py:201
  (119 shorter events, 104.8 us)
Async XLA Ops:
  7.2 183.6 %reduce-scatter.5.cloned.1.call-start = ((), (), s32[]{:S(2)}) async-start(), calls=%async_computation.4 | async-start | bytes 3538944 | tf_op jit(solution)/shard_map/reduce_scatter | solution.py:177
  29.4 22.0 %collective-permute-start.2 = (bf16[128,3072]{1,0:T(8,128)(2,1)S(1)}, bf16[128,3072]{1,0:T(8,128)(2,1)}, u32[]{:S(2)}, u32[]{:S(2)}) collective-permute-start(bf16[128,3072]{1,0:T(8,128)(2,1)S(1)} %get-tuple-element.60), channel_id=1, source_target_pairs={{1,3},{2,0},{5,7},{6,4},{9,11},{10,8},{13,15},{14,12},{17,19},{18,... | collective-permute-start | bytes 2359304 | tf_op jit(solution)/shard_map/ppermute | solution.py:155
  30.8 25.8 %collective-permute-start.4 = (bf16[128,3072]{1,0:T(8,128)(2,1)S(1)}, bf16[128,3072]{1,0:T(8,128)(2,1)}, u32[]{:S(2)}, u32[]{:S(2)}) collective-permute-start(bf16[128,3072]{1,0:T(8,128)(2,1)S(1)} %get-tuple-element.61), channel_id=1, source_target_pairs={{1,0},{2,3},{5,4},{6,7},{9,8},{10,11},{13,12},{14,15},{17,16},{18,... | collective-permute-start | bytes 2359304 | tf_op jit(solution)/shard_map/ppermute | solution.py:156
  34.1 63.3 %collective-permute-start.1 = (bf16[256,3072]{1,0:T(8,128)(2,1)}, bf16[256,3072]{1,0:T(8,128)(2,1)S(1)}, u32[]{:S(2)}, u32[]{:S(2)}) collective-permute-start(bf16[256,3072]{1,0:T(8,128)(2,1)} %get-tuple-element.62), channel_id=1, source_target_pairs={{1,0},{3,2},{5,4},{7,6},{9,8},{11,10},{13,12},{15,14},{17,16},{19,... | collective-permute-start | bytes 4718600 | tf_op jit(solution)/shard_map/ppermute | solution.py:152
  35.4 62.0 %collective-permute-start = (bf16[256,3072]{1,0:T(8,128)(2,1)}, bf16[256,3072]{1,0:T(8,128)(2,1)S(1)}, u32[]{:S(2)}, u32[]{:S(2)}) collective-permute-start(bf16[256,3072]{1,0:T(8,128)(2,1)} %get-tuple-element.63), channel_id=1, source_target_pairs={{0,1},{2,3},{4,5},{6,7},{8,9},{10,11},{12,13},{14,15},{16,17},{18,... | collective-permute-start | bytes 4718600 | tf_op jit(solution)/shard_map/ppermute | solution.py:151
  51.4 43.3 %collective-permute-start.3 = (bf16[128,3072]{1,0:T(8,128)(2,1)}, bf16[128,3072]{1,0:T(8,128)(2,1)}, u32[]{:S(2)}, u32[]{:S(2)}) collective-permute-start(bf16[128,3072]{1,0:T(8,128)(2,1)} %collective-permute-done.2), channel_id=1, source_target_pairs={{3,2},{0,1},{7,6},{4,5},{11,10},{8,9},{15,14},{12,13},{19,18},{16,... | collective-permute-start | bytes 2359304 | tf_op jit(solution)/shard_map/ppermute | solution.py:157
  56.6 38.1 %collective-permute-start.5 = (bf16[128,3072]{1,0:T(8,128)(2,1)}, bf16[128,3072]{1,0:T(8,128)(2,1)}, u32[]{:S(2)}, u32[]{:S(2)}) collective-permute-start(bf16[128,3072]{1,0:T(8,128)(2,1)} %collective-permute-done.4), channel_id=1, source_target_pairs={{0,2},{3,1},{4,6},{7,5},{8,10},{11,9},{12,14},{15,13},{16,18},{19,... | collective-permute-start | bytes 2359304 | tf_op jit(solution)/shard_map/ppermute | solution.py:158
  128.9 145.6 %reduce-scatter.7.cloned.1.call-start = ((), (), s32[]{:S(2)}) async-start(), calls=%async_computation.5 | async-start | bytes 7077888 | tf_op jit(solution)/shard_map/reduce_scatter | solution.py:177
  131.3 20.1 %collective-permute-start.8 = (bf16[128,3072]{1,0:T(8,128)(2,1)S(1)}, bf16[128,3072]{1,0:T(8,128)(2,1)S(1)}, u32[]{:S(2)}, u32[]{:S(2)}) collective-permute-start(bf16[128,3072]{1,0:T(8,128)(2,1)S(1)} %get-tuple-element.56), channel_id=1, source_target_pairs={{1,3},{2,0},{5,7},{6,4},{9,11},{10,8},{13,15},{14,12},{17,19},{18,... | collective-permute-start | bytes 2359304 | tf_op jit(solution)/shard_map/ppermute | solution.py:155
  132.7 22.4 %collective-permute-start.10 = (bf16[128,3072]{1,0:T(8,128)(2,1)S(1)}, bf16[128,3072]{1,0:T(8,128)(2,1)S(1)}, u32[]{:S(2)}, u32[]{:S(2)}) collective-permute-start(bf16[128,3072]{1,0:T(8,128)(2,1)S(1)} %get-tuple-element.57), channel_id=1, source_target_pairs={{1,0},{2,3},{5,4},{6,7},{9,8},{10,11},{13,12},{14,15},{17,16},{18,... | collective-permute-start | bytes 2359304 | tf_op jit(solution)/shard_map/ppermute | solution.py:156
  134.2 56.5 %collective-permute-start.7 = (bf16[256,3072]{1,0:T(8,128)(2,1)S(1)}, bf16[256,3072]{1,0:T(8,128)(2,1)S(1)}, u32[]{:S(2)}, u32[]{:S(2)}) collective-permute-start(bf16[256,3072]{1,0:T(8,128)(2,1)S(1)} %get-tuple-element.58), channel_id=1, source_target_pairs={{1,0},{3,2},{5,4},{7,6},{9,8},{11,10},{13,12},{15,14},{17,16},{19,... | collective-permute-start | bytes 4718600 | tf_op jit(solution)/shard_map/ppermute | solution.py:152
  135.5 55.2 %collective-permute-start.6 = (bf16[256,3072]{1,0:T(8,128)(2,1)S(1)}, bf16[256,3072]{1,0:T(8,128)(2,1)S(1)}, u32[]{:S(2)}, u32[]{:S(2)}) collective-permute-start(bf16[256,3072]{1,0:T(8,128)(2,1)S(1)} %get-tuple-element.59), channel_id=1, source_target_pairs={{0,1},{2,3},{4,5},{6,7},{8,9},{10,11},{12,13},{14,15},{16,17},{18,... | collective-permute-start | bytes 4718600 | tf_op jit(solution)/shard_map/ppermute | solution.py:151
  151.4 38.0 %collective-permute-start.9 = (bf16[128,3072]{1,0:T(8,128)(2,1)S(1)}, bf16[128,3072]{1,0:T(8,128)(2,1)S(1)}, u32[]{:S(2)}, u32[]{:S(2)}) collective-permute-start(bf16[128,3072]{1,0:T(8,128)(2,1)S(1)} %collective-permute-done.8), channel_id=1, source_target_pairs={{3,2},{0,1},{7,6},{4,5},{11,10},{8,9},{15,14},{12,13},{19,18},{16,... | collective-permute-start | bytes 2359304 | tf_op jit(solution)/shard_map/ppermute | solution.py:157
  155.1 34.3 %collective-permute-start.11 = (bf16[128,3072]{1,0:T(8,128)(2,1)S(1)}, bf16[128,3072]{1,0:T(8,128)(2,1)S(1)}, u32[]{:S(2)}, u32[]{:S(2)}) collective-permute-start(bf16[128,3072]{1,0:T(8,128)(2,1)S(1)} %collective-permute-done.10), channel_id=1, source_target_pairs={{0,2},{3,1},{4,6},{7,5},{8,10},{11,9},{12,14},{15,13},{16,18},{19,... | collective-permute-start | bytes 2359304 | tf_op jit(solution)/shard_map/ppermute | solution.py:158
  203.1 137.4 %all-gather.5.cloned.1.call-start = ((), (), s32[]{:S(2)}) async-start(), calls=%async_computation.6 | async-start | bytes 7077888 | tf_op jit(solution)/shard_map/all_gather | solution.py:180
  277.3 123.4 %all-gather.7.cloned.1.call-start = ((), (), s32[]{:S(2)}) async-start(), calls=%async_computation.7 | async-start | bytes 3538944 | tf_op jit(solution)/shard_map/all_gather | solution.py:180
  342.0 181.2 %reduce-scatter.9.cloned.1.call-start = ((), (), s32[]{:S(2)}) async-start(), calls=%async_computation.8 | async-start | bytes 3538944 | tf_op jit(solution)/shard_map/reduce_scatter | solution.py:177
  357.6 21.6 %collective-permute-start.14 = (bf16[128,3072]{1,0:T(8,128)(2,1)S(1)}, bf16[128,3072]{1,0:T(8,128)(2,1)S(1)}, u32[]{:S(2)}, u32[]{:S(2)}) collective-permute-start(bf16[128,3072]{1,0:T(8,128)(2,1)S(1)} %get-tuple-element.64), channel_id=1, source_target_pairs={{1,3},{2,0},{5,7},{6,4},{9,11},{10,8},{13,15},{14,12},{17,19},{18,... | collective-permute-start | bytes 2359304 | tf_op jit(solution)/shard_map/ppermute | solution.py:155
  359.0 22.5 %collective-permute-start.16 = (bf16[128,3072]{1,0:T(8,128)(2,1)S(1)}, bf16[128,3072]{1,0:T(8,128)(2,1)S(1)}, u32[]{:S(2)}, u32[]{:S(2)}) collective-permute-start(bf16[128,3072]{1,0:T(8,128)(2,1)S(1)} %get-tuple-element.65), channel_id=1, source_target_pairs={{1,0},{2,3},{5,4},{6,7},{9,8},{10,11},{13,12},{14,15},{17,16},{18,... | collective-permute-start | bytes 2359304 | tf_op jit(solution)/shard_map/ppermute | solution.py:156
  379.3 20.1 %collective-permute-start.15 = (bf16[128,3072]{1,0:T(8,128)(2,1)S(1)}, bf16[128,3072]{1,0:T(8,128)(2,1)S(1)}, u32[]{:S(2)}, u32[]{:S(2)}) collective-permute-start(bf16[128,3072]{1,0:T(8,128)(2,1)S(1)} %collective-permute-done.14), channel_id=1, source_target_pairs={{3,2},{0,1},{7,6},{4,5},{11,10},{8,9},{15,14},{12,13},{19,18},{16,... | collective-permute-start | bytes 2359304 | tf_op jit(solution)/shard_map/ppermute | solution.py:157
  381.5 17.9 %collective-permute-start.17 = (bf16[128,3072]{1,0:T(8,128)(2,1)S(1)}, bf16[128,3072]{1,0:T(8,128)(2,1)S(1)}, u32[]{:S(2)}, u32[]{:S(2)}) collective-permute-start(bf16[128,3072]{1,0:T(8,128)(2,1)S(1)} %collective-permute-done.16), channel_id=1, source_target_pairs={{0,2},{3,1},{4,6},{7,5},{8,10},{11,9},{12,14},{15,13},{16,18},{19,... | collective-permute-start | bytes 2359304 | tf_op jit(solution)/shard_map/ppermute | solution.py:158
  383.1 37.6 %collective-permute-start.13 = (bf16[256,3072]{1,0:T(8,128)(2,1)S(1)}, bf16[256,3072]{1,0:T(8,128)(2,1)}, u32[]{:S(2)}, u32[]{:S(2)}) collective-permute-start(bf16[256,3072]{1,0:T(8,128)(2,1)S(1)} %get-tuple-element.66), channel_id=1, source_target_pairs={{1,0},{3,2},{5,4},{7,6},{9,8},{11,10},{13,12},{15,14},{17,16},{19,... | collective-permute-start | bytes 4718600 | tf_op jit(solution)/shard_map/ppermute | solution.py:152
  384.4 47.1 %collective-permute-start.12 = (bf16[256,3072]{1,0:T(8,128)(2,1)S(1)}, bf16[256,3072]{1,0:T(8,128)(2,1)}, u32[]{:S(2)}, u32[]{:S(2)}) collective-permute-start(bf16[256,3072]{1,0:T(8,128)(2,1)S(1)} %get-tuple-element.67), channel_id=1, source_target_pairs={{0,1},{2,3},{4,5},{6,7},{8,9},{10,11},{12,13},{14,15},{16,17},{18,... | collective-permute-start | bytes 4718600 | tf_op jit(solution)/shard_map/ppermute | solution.py:151
  461.3 142.6 %reduce-scatter.11.cloned.1.call-start = ((), (), s32[]{:S(2)}) async-start(), calls=%async_computation.9 | async-start | bytes 7077888 | tf_op jit(solution)/shard_map/reduce_scatter | solution.py:177
  463.6 20.7 %collective-permute-start.20 = (bf16[128,3072]{1,0:T(8,128)(2,1)S(1)}, bf16[128,3072]{1,0:T(8,128)(2,1)S(1)}, u32[]{:S(2)}, u32[]{:S(2)}) collective-permute-start(bf16[128,3072]{1,0:T(8,128)(2,1)S(1)} %get-tuple-element.52), channel_id=1, source_target_pairs={{1,3},{2,0},{5,7},{6,4},{9,11},{10,8},{13,15},{14,12},{17,19},{18,... | collective-permute-start | bytes 2359304 | tf_op jit(solution)/shard_map/ppermute | solution.py:155
  465.0 22.6 %collective-permute-start.22 = (bf16[128,3072]{1,0:T(8,128)(2,1)S(1)}, bf16[128,3072]{1,0:T(8,128)(2,1)S(1)}, u32[]{:S(2)}, u32[]{:S(2)}) collective-permute-start(bf16[128,3072]{1,0:T(8,128)(2,1)S(1)} %get-tuple-element.53), channel_id=1, source_target_pairs={{1,0},{2,3},{5,4},{6,7},{9,8},{10,11},{13,12},{14,15},{17,16},{18,... | collective-permute-start | bytes 2359304 | tf_op jit(solution)/shard_map/ppermute | solution.py:156
  466.5 56.7 %collective-permute-start.19 = (bf16[256,3072]{1,0:T(8,128)(2,1)S(1)}, bf16[256,3072]{1,0:T(8,128)(2,1)S(1)}, u32[]{:S(2)}, u32[]{:S(2)}) collective-permute-start(bf16[256,3072]{1,0:T(8,128)(2,1)S(1)} %get-tuple-element.54), channel_id=1, source_target_pairs={{1,0},{3,2},{5,4},{7,6},{9,8},{11,10},{13,12},{15,14},{17,16},{19,... | collective-permute-start | bytes 4718600 | tf_op jit(solution)/shard_map/ppermute | solution.py:152
  467.8 55.4 %collective-permute-start.18 = (bf16[256,3072]{1,0:T(8,128)(2,1)S(1)}, bf16[256,3072]{1,0:T(8,128)(2,1)S(1)}, u32[]{:S(2)}, u32[]{:S(2)}) collective-permute-start(bf16[256,3072]{1,0:T(8,128)(2,1)S(1)} %get-tuple-element.55), channel_id=1, source_target_pairs={{0,1},{2,3},{4,5},{6,7},{8,9},{10,11},{12,13},{14,15},{16,17},{18,... | collective-permute-start | bytes 4718600 | tf_op jit(solution)/shard_map/ppermute | solution.py:151
  484.2 37.7 %collective-permute-start.21 = (bf16[128,3072]{1,0:T(8,128)(2,1)S(1)}, bf16[128,3072]{1,0:T(8,128)(2,1)S(1)}, u32[]{:S(2)}, u32[]{:S(2)}) collective-permute-start(bf16[128,3072]{1,0:T(8,128)(2,1)S(1)} %collective-permute-done.20), channel_id=1, source_target_pairs={{3,2},{0,1},{7,6},{4,5},{11,10},{8,9},{15,14},{12,13},{19,18},{16,... | collective-permute-start | bytes 2359304 | tf_op jit(solution)/shard_map/ppermute | solution.py:157
  487.5 34.4 %collective-permute-start.23 = (bf16[128,3072]{1,0:T(8,128)(2,1)S(1)}, bf16[128,3072]{1,0:T(8,128)(2,1)S(1)}, u32[]{:S(2)}, u32[]{:S(2)}) collective-permute-start(bf16[128,3072]{1,0:T(8,128)(2,1)S(1)} %collective-permute-done.22), channel_id=1, source_target_pairs={{0,2},{3,1},{4,6},{7,5},{8,10},{11,9},{12,14},{15,13},{16,18},{19,... | collective-permute-start | bytes 2359304 | tf_op jit(solution)/shard_map/ppermute | solution.py:158
  535.5 134.5 %all-gather.9.cloned.1.call-start = ((), (), s32[]{:S(2)}) async-start(), calls=%async_computation.10 | async-start | bytes 7077888 | tf_op jit(solution)/shard_map/all_gather | solution.py:180
  606.7 102.4 %all-gather.11.cloned.1.call-start = ((), (), s32[]{:S(2)}) async-start(), calls=%async_computation.11 | async-start | bytes 3538944 | tf_op jit(solution)/shard_map/all_gather | solution.py:180
  (18 other events, 582.5 us)
Sparse Core Ops, SparseCore 0:
  129.0 41.6 reduce-scatter.4
  203.2 71.2 reduce-scatter.6
  277.4 62.9 all-gather.4
  342.1 36.9 all-gather.6
  461.5 39.0 reduce-scatter.8
  535.7 68.1 reduce-scatter.10
  606.8 63.1 all-gather.8
  672.2 36.9 all-gather.10

commit v14 on v12

--- a/solution.py
+++ b/solution.py
@@ -85,7 +85,7 @@
             log_ref[i * width : (i + 1) * width, :] = w_ref[0] * jnp.log(rounded.astype(jnp.float32))
 
 
-def row_pass(mid, terms_local, blocks, halos=None, weight=None, tile_cols=768):
+def row_pass(mid, terms_local, blocks, halos=None, weight=None, tile_cols=1536):
     rows, cols = mid.shape
     width = terms_local.shape[2]
     tile = lambda r: pl.BlockSpec((r, tile_cols), lambda c: (0, c))

time: 733 us -> 732 us (level)
  no operation moved by 1% of the time
where the time goes in v14:
time: 732 us; the launch traced here: 731 us
  waiting for transfers between devices  454 us (62%)
  Pallas kernels  106 us (14%)
  other arithmetic  67.7 us (9%)
  starting transfers between devices  54.3 us (7%)
  local copies, waits for them, and re-layouts  17.1 us (2%)
  blocking collectives  15.7 us (2%)
  between operations  15.3 us (2%)
    all_gather x4, waiting for transfers between devices, gather_barycenter(): lax.all_gather(jnp.exp(part_sum / total_weight), 'img', axis=0, tiled=True)  150 us
    ppermute x4, waiting for transfers between devices, exchange(): first = lax.ppermute(first, 'slab', [(3, 2), (0, 1)])  129 us
    reduce_scatter x4, waiting for transfers between devices, log_sum(): lax.psum_scatter(value_portion, 'img', scatter_dimension=0, tiled=True)  124 us
    pallas_call x5, Pallas kernels, column_pass(): pl.pallas_call(column_kernel, grid=(rows // tile_rows,), in_specs=[tile]...  53.6 us
    pallas_call x6, Pallas kernels, row_pass(): pl.pallas_call(functools.partial(row_kernel, blocks=tuple(blocks), has_ha...  52.6 us
    ppermute x4, waiting for transfers between devices, exchange(): first = lax.ppermute(first, 'slab', [(1, 3), (2, 0)])  50.4 us
    ppermute x4, starting transfers between devices, exchange(): direct_prev = lax.ppermute(to_up, 'slab', [(0, 1), (2, 3)])  24.3 us
    psum x1, blocking collectives, per_device(): total_weight = lax.psum(jnp.sum(fraction_tops).astype(jnp.float32), 'img')  15.7 us
  transfers between devices with their start and end apart: 32, of which 13 were waited for; matrix products, arithmetic and copies ran while one was open for 5% of the time, Pallas kernels for 1%

profile of v14, /device:TPU:0, one launch (start us, length us, event | category | flops | bytes accessed | tf_op | source)
XLA Modules:
  0.0 730.6 jit_solution(15433404618129548859)
XLA Ops:
  8.1 8.3 %select_reduce_fusion.refs_1_.refs_2_ = bf16[24,5,128,128]{3,2,1,0:T(8,128)(2,1)} fusion(pred[24,5,3]{2,1,0:T(8,128)(4,1)S(1)} %broadcast_compare_fusion, bf16[24,3,128,128]{3,2,1,0:T(8,128)(2,1)} %param.8), kind=kLoop, calls=%fused_computation | loop fusion | flops 9830400 | bytes 6291816 | tf_op jit(solution)/shard_map/reduce_sum | solution.py:19
  16.4 10.9 %shard_map.68.refs_1_ = bf16[768,3072]{1,0:T(8,128)(2,1)} custom-call(f32[768,3072]{1,0:T(8,128)} %bitcast.18, bf16[24,5,128,128]{3,2,1,0:T(8,128)(2,1)} %select_reduce_fusion.refs_1_.refs_2_), custom_call_target="tpu_custom_call" | custom-call | tf_op jit(solution)/shard_map/pallas_call | solution.py:50
  34.8 9.2 %collective-permute-start.4 = (bf16[256,3072]{1,0:T(8,128)(2,1)S(1)}, bf16[256,3072]{1,0:T(8,128)(2,1)}, u32[]{:S(2)}, u32[]{:S(2)}) collective-permute-start(bf16[256,3072]{1,0:T(8,128)(2,1)S(1)} %get-tuple-element.53), channel_id=1, source_target_pairs={{0,1},{2,3},{4,5},{6,7},{8,9},{10,11},{12,13},{14,15},{16,17},{18,... | collective-permute-start | bytes 4718600 | tf_op jit(solution)/shard_map/ppermute | solution.py:135
  44.0 11.5 %collective-permute-done = bf16[128,3072]{1,0:T(8,128)(2,1)} collective-permute-done((bf16[128,3072]{1,0:T(8,128)(2,1)S(1)}, bf16[128,3072]{1,0:T(8,128)(2,1)}, u32[]{:S(2)}, u32[]{:S(2)}) %collective-permute-start) | collective-permute-done | bytes 786464 | tf_op jit(solution)/shard_map/ppermute | solution.py:139
  62.7 30.4 %collective-permute-done.1 = bf16[128,3072]{1,0:T(8,128)(2,1)} collective-permute-done((bf16[128,3072]{1,0:T(8,128)(2,1)}, bf16[128,3072]{1,0:T(8,128)(2,1)}, u32[]{:S(2)}, u32[]{:S(2)}) %collective-permute-start.1) | collective-permute-done | bytes 786464 | tf_op jit(solution)/shard_map/ppermute | solution.py:141
  98.9 10.9 %shard_map.69.refs_1_ = bf16[768,3072]{1,0:T(8,128)(2,1)} custom-call(bf16[256,3072]{1,0:T(8,128)(2,1)} %get-tuple-element.67.refs_0_, bf16[768,3072]{1,0:T(8,128)(2,1)} %shard_map.68.refs_1_, bf16[256,3072]{1,0:T(8,128)(2,1)} %get-tuple-element.66.refs_2_, bf16[6,5,128,128]{3,2,1,0:T(8,128)(2,1)} %constant_dynamic-slice_fusion.refs_3_.refs_1_), custom_call_target="tpu_custom_call" | custom-call | tf_op jit(solution)/shard_map/pallas_call | solution.py:106
  109.7 12.8 %shard_map.70.refs_0_.refs_1_ = bf16[768,3072]{1,0:T(8,128)(2,1)} custom-call(f32[768,3072]{1,0:T(8,128)} %bitcast.15, bf16[768,3072]{1,0:T(8,128)(2,1)} %shard_map.69.refs_1_, bf16[24,5,128,128]{3,2,1,0:T(8,128)(2,1)} %select_reduce_fusion.refs_1_.refs_2_), custom_call_target="tpu_custom_call" | custom-call | tf_op jit(solution)/shard_map/pallas_call | solution.py:50
  122.5 5.7 shard_map.71
  134.7 4.8 collective-permute-start.10
  139.6 12.3 %collective-permute-done.6 = bf16[128,3072]{1,0:T(8,128)(2,1)S(1)} collective-permute-done((bf16[128,3072]{1,0:T(8,128)(2,1)S(1)}, bf16[128,3072]{1,0:T(8,128)(2,1)S(1)}, u32[]{:S(2)}, u32[]{:S(2)}) %collective-permute-start.6) | collective-permute-done | bytes 786464 | tf_op jit(solution)/shard_map/ppermute | solution.py:139
  154.9 33.7 %collective-permute-done.7 = bf16[128,3072]{1,0:T(8,128)(2,1)S(1)} collective-permute-done((bf16[128,3072]{1,0:T(8,128)(2,1)S(1)}, bf16[128,3072]{1,0:T(8,128)(2,1)S(1)}, u32[]{:S(2)}, u32[]{:S(2)}) %collective-permute-start.7) | collective-permute-done | bytes 786464 | tf_op jit(solution)/shard_map/ppermute | solution.py:141
  190.8 9.7 %shard_map.72 = (bf16[512,3072]{1,0:T(8,128)(2,1)}, f32[512,3072]{1,0:T(8,128)}) custom-call(bf16[256,3072]{1,0:T(8,128)(2,1)} %get-tuple-element.21.refs_0_, bf16[768,3072]{1,0:T(8,128)(2,1)} %shard_map.70.refs_0_.refs_1_, bf16[256,3072]{1,0:T(8,128)(2,1)} %get-tuple-element.22.refs_2_, bf16[6,5,128,128]{3,2,1,0:T(8,128)(2,1)} %constant_dynamic-slice_fusion.refs_3_.refs_1_, ...), custom_call_target="tpu_custom_call" | custom-call | tf_op jit(solution)/shard_map/pallas_call | solution.py:106
  200.6 15.7 %psum.7 = f32[]{:T(128)} all-reduce(f32[]{:T(128)} %bitcast.2), channel_id=1, replica_groups=mesh['img'=8,'slab'=4] {'img'}, use_global_device_ids=true, to_apply=%region_3.4 | all-reduce | flops 1 | bytes 8 | tf_op jit(solution)/shard_map/psum | solution.py:125
  216.3 55.6 %reduce-scatter.7.cloned.1.call-done = f32[64,3072]{1,0:T(8,128)} async-done(((f32[512,3072]{1,0:T(8,128)}), f32[64,3072]{1,0:T(8,128)}) %reduce-scatter.7.cloned.1.call-update) | async-done | bytes 786448 | tf_op jit(solution)/shard_map/reduce_scatter | solution.py:161
  274.8 63.1 %all-gather.5.cloned.1.call-done.refs_0_ = f32[512,3072]{1,0:T(8,128)} async-done(((f32[64,3072]{1,0:T(8,128)}), f32[512,3072]{1,0:T(8,128)}) %all-gather.5.cloned.1.call-update) | async-done | bytes 6291472 | tf_op jit(solution)/shard_map/all_gather | solution.py:164
  342.9 9.9 %shard_map.73 = bf16[512,3072]{1,0:T(8,128)(2,1)} custom-call(f32[512,3072]{1,0:T(8,128)} %all-gather.5.cloned.1.call-done.refs_0_, f32[512,3072]{1,0:T(8,128)} %convert_element_type.21.refs_1_, bf16[24,5,128,128]{3,2,1,0:T(8,128)(2,1)} %select_reduce_fusion.refs_1_.refs_2_), custom_call_target="tpu_custom_call" | custom-call | tf_op jit(solution)/shard_map/pallas_call | solution.py:50
  359.5 5.5 collective-permute-start.16
  365.0 13.8 %collective-permute-done.12 = bf16[128,3072]{1,0:T(8,128)(2,1)S(1)} collective-permute-done((bf16[128,3072]{1,0:T(8,128)(2,1)S(1)}, bf16[128,3072]{1,0:T(8,128)(2,1)S(1)}, u32[]{:S(2)}, u32[]{:S(2)}) %collective-permute-start.12) | collective-permute-done | bytes 786464 | tf_op jit(solution)/shard_map/ppermute | solution.py:139
  383.7 31.9 %collective-permute-done.13 = bf16[128,3072]{1,0:T(8,128)(2,1)S(1)} collective-permute-done((bf16[128,3072]{1,0:T(8,128)(2,1)S(1)}, bf16[128,3072]{1,0:T(8,128)(2,1)S(1)}, u32[]{:S(2)}, u32[]{:S(2)}) %collective-permute-start.13) | collective-permute-done | bytes 786464 | tf_op jit(solution)/shard_map/ppermute | solution.py:141
  417.6 7.2 shard_map.74
  428.3 10.9 %shard_map.75.refs_1_ = bf16[768,3072]{1,0:T(8,128)(2,1)} custom-call(bf16[256,3072]{1,0:T(8,128)(2,1)} %get-tuple-element.63.refs_0_, bf16[768,3072]{1,0:T(8,128)(2,1)} %pad_maximum_fusion.1.refs_1_, bf16[256,3072]{1,0:T(8,128)(2,1)} %get-tuple-element.62.refs_2_, bf16[6,5,128,128]{3,2,1,0:T(8,128)(2,1)} %constant_dynamic-slice_fusion.refs_3_.refs_1_), custom_call_target="tpu_custom_call" | custom-call | tf_op jit(solution)/shard_map/pallas_call | solution.py:106
  439.2 12.8 %shard_map.76.refs_0_.refs_1_ = bf16[768,3072]{1,0:T(8,128)(2,1)} custom-call(f32[768,3072]{1,0:T(8,128)} %bitcast.16, bf16[768,3072]{1,0:T(8,128)(2,1)} %shard_map.75.refs_1_, bf16[24,5,128,128]{3,2,1,0:T(8,128)(2,1)} %select_reduce_fusion.refs_1_.refs_2_), custom_call_target="tpu_custom_call" | custom-call | tf_op jit(solution)/shard_map/pallas_call | solution.py:50
  452.0 5.7 shard_map.77
  469.1 12.8 %collective-permute-done.18 = bf16[128,3072]{1,0:T(8,128)(2,1)S(1)} collective-permute-done((bf16[128,3072]{1,0:T(8,128)(2,1)S(1)}, bf16[128,3072]{1,0:T(8,128)(2,1)S(1)}, u32[]{:S(2)}, u32[]{:S(2)}) %collective-permute-start.18) | collective-permute-done | bytes 786464 | tf_op jit(solution)/shard_map/ppermute | solution.py:139
  485.2 33.4 %collective-permute-done.19 = bf16[128,3072]{1,0:T(8,128)(2,1)S(1)} collective-permute-done((bf16[128,3072]{1,0:T(8,128)(2,1)S(1)}, bf16[128,3072]{1,0:T(8,128)(2,1)S(1)}, u32[]{:S(2)}, u32[]{:S(2)}) %collective-permute-start.19) | collective-permute-done | bytes 786464 | tf_op jit(solution)/shard_map/ppermute | solution.py:141
  520.7 9.7 %shard_map.78 = (bf16[512,3072]{1,0:T(8,128)(2,1)}, f32[512,3072]{1,0:T(8,128)}) custom-call(bf16[256,3072]{1,0:T(8,128)(2,1)} %get-tuple-element.30.refs_0_, bf16[768,3072]{1,0:T(8,128)(2,1)} %shard_map.76.refs_0_.refs_1_, bf16[256,3072]{1,0:T(8,128)(2,1)} %get-tuple-element.31.refs_2_, bf16[6,5,128,128]{3,2,1,0:T(8,128)(2,1)} %constant_dynamic-slice_fusion.refs_3_.refs_1_, ...), custom_call_target="tpu_custom_call" | custom-call | tf_op jit(solution)/shard_map/pallas_call | solution.py:106
  530.5 68.4 %reduce-scatter.11.cloned.1.call-done = f32[64,3072]{1,0:T(8,128)} async-done(((f32[512,3072]{1,0:T(8,128)}), f32[64,3072]{1,0:T(8,128)}) %reduce-scatter.11.cloned.1.call-update) | async-done | bytes 786448 | tf_op jit(solution)/shard_map/reduce_scatter | solution.py:161
  601.8 63.2 %all-gather.9.cloned.1.call-done = f32[512,3072]{1,0:T(8,128)} async-done(((f32[64,3072]{1,0:T(8,128)}), f32[512,3072]{1,0:T(8,128)}) %all-gather.9.cloned.1.call-update) | async-done | bytes 6291472 | tf_op jit(solution)/shard_map/all_gather | solution.py:164
  674.7 5.5 slice_bitcast_fusion.3
  680.2 23.9 %all-gather.11.cloned.1.call-done = f32[256,3072]{1,0:T(8,128)} async-done(((f32[32,3072]{1,0:T(8,128)}), f32[256,3072]{1,0:T(8,128)}) %all-gather.11.cloned.1.call-update) | async-done | bytes 3145744 | tf_op jit(solution)/shard_map/all_gather | solution.py:164
  704.1 11.9 %maximum_divide_fusion = f32[1,768,3072]{2,1,0:T(8,128)} fusion(f32[1,256,3072]{2,1,0:T(8,128)} %get-tuple-element.41, f32[1,256,3072]{2,1,0:T(8,128)} %bitcast.17, f32[1,256,3072]{2,1,0:T(8,128)} %get-tuple-element.40, f32[1,256,3072]{2,1,0:T(8,128)} %get-tuple-element.39, f32[1,256,3072]{2,1,0:T(8,128)} %bitcast_convert_fusion, ...), kind=kLoop, calls=%fused_computation.2 | loop fusion | flops 11796480 | bytes 28311552 | tf_op jit(solution)/shard_map/div | solution.py:199
  716.1 7.7 %pad_maximum_fusion = f32[768,3072]{1,0:T(8,128)} fusion(f32[256,3072]{1,0:T(8,128)} %get-tuple-element.42, f32[256,3072]{1,0:T(8,128)S(1)} %copy-done.4, f32[256,3072]{1,0:T(8,128)} %get-tuple-element.43), kind=kLoop, calls=%fused_computation.1 | loop fusion | flops 4718592 | bytes 18874368 | tf_op jit(solution)/shard_map/concatenate | solution.py:185
  (115 shorter events, 86.4 us)
Async XLA Ops:
  7.2 183.6 %reduce-scatter.5.cloned.1.call-start = ((), (), s32[]{:S(2)}) async-start(), calls=%async_computation.4 | async-start | bytes 3538944 | tf_op jit(solution)/shard_map/reduce_scatter | solution.py:161
  29.4 28.2 %collective-permute-start.2 = (bf16[128,3072]{1,0:T(8,128)(2,1)S(1)}, bf16[128,3072]{1,0:T(8,128)(2,1)}, u32[]{:S(2)}, u32[]{:S(2)}) collective-permute-start(bf16[128,3072]{1,0:T(8,128)(2,1)S(1)} %get-tuple-element.54), channel_id=1, source_target_pairs={{1,0},{2,3},{5,4},{6,7},{9,8},{10,11},{13,12},{14,15},{17,16},{18,... | collective-permute-start | bytes 2359304 | tf_op jit(solution)/shard_map/ppermute | solution.py:140
  30.8 24.6 %collective-permute-start = (bf16[128,3072]{1,0:T(8,128)(2,1)S(1)}, bf16[128,3072]{1,0:T(8,128)(2,1)}, u32[]{:S(2)}, u32[]{:S(2)}) collective-permute-start(bf16[128,3072]{1,0:T(8,128)(2,1)S(1)} %get-tuple-element.55), channel_id=1, source_target_pairs={{1,3},{2,0},{5,7},{6,4},{9,11},{10,8},{13,15},{14,12},{17,19},{18,... | collective-permute-start | bytes 2359304 | tf_op jit(solution)/shard_map/ppermute | solution.py:139
  33.5 62.0 %collective-permute-start.5 = (bf16[256,3072]{1,0:T(8,128)(2,1)}, bf16[256,3072]{1,0:T(8,128)(2,1)S(1)}, u32[]{:S(2)}, u32[]{:S(2)}) collective-permute-start(bf16[256,3072]{1,0:T(8,128)(2,1)} %get-tuple-element.52), channel_id=1, source_target_pairs={{1,0},{3,2},{5,4},{7,6},{9,8},{11,10},{13,12},{15,14},{17,16},{19,... | collective-permute-start | bytes 4718600 | tf_op jit(solution)/shard_map/ppermute | solution.py:136
  34.8 60.7 %collective-permute-start.4 = (bf16[256,3072]{1,0:T(8,128)(2,1)S(1)}, bf16[256,3072]{1,0:T(8,128)(2,1)}, u32[]{:S(2)}, u32[]{:S(2)}) collective-permute-start(bf16[256,3072]{1,0:T(8,128)(2,1)S(1)} %get-tuple-element.53), channel_id=1, source_target_pairs={{0,1},{2,3},{4,5},{6,7},{8,9},{10,11},{12,13},{14,15},{16,17},{18,... | collective-permute-start | bytes 4718600 | tf_op jit(solution)/shard_map/ppermute | solution.py:135
  55.4 37.6 %collective-permute-start.1 = (bf16[128,3072]{1,0:T(8,128)(2,1)}, bf16[128,3072]{1,0:T(8,128)(2,1)}, u32[]{:S(2)}, u32[]{:S(2)}) collective-permute-start(bf16[128,3072]{1,0:T(8,128)(2,1)} %collective-permute-done), channel_id=1, source_target_pairs={{3,2},{0,1},{7,6},{4,5},{11,10},{8,9},{15,14},{12,13},{19,18},{16,... | collective-permute-start | bytes 2359304 | tf_op jit(solution)/shard_map/ppermute | solution.py:141
  57.6 36.6 %collective-permute-start.3 = (bf16[128,3072]{1,0:T(8,128)(2,1)}, bf16[128,3072]{1,0:T(8,128)(2,1)}, u32[]{:S(2)}, u32[]{:S(2)}) collective-permute-start(bf16[128,3072]{1,0:T(8,128)(2,1)} %collective-permute-done.2), channel_id=1, source_target_pairs={{0,2},{3,1},{4,6},{7,5},{8,10},{11,9},{12,14},{15,13},{16,18},{19,... | collective-permute-start | bytes 2359304 | tf_op jit(solution)/shard_map/ppermute | solution.py:142
  128.3 143.6 %reduce-scatter.7.cloned.1.call-start = ((), (), s32[]{:S(2)}) async-start(), calls=%async_computation.5 | async-start | bytes 7077888 | tf_op jit(solution)/shard_map/reduce_scatter | solution.py:161
  130.5 23.1 %collective-permute-start.8 = (bf16[128,3072]{1,0:T(8,128)(2,1)S(1)}, bf16[128,3072]{1,0:T(8,128)(2,1)S(1)}, u32[]{:S(2)}, u32[]{:S(2)}) collective-permute-start(bf16[128,3072]{1,0:T(8,128)(2,1)S(1)} %get-tuple-element.50), channel_id=1, source_target_pairs={{1,0},{2,3},{5,4},{6,7},{9,8},{10,11},{13,12},{14,15},{17,16},{18,... | collective-permute-start | bytes 2359304 | tf_op jit(solution)/shard_map/ppermute | solution.py:140
  131.9 20.0 %collective-permute-start.6 = (bf16[128,3072]{1,0:T(8,128)(2,1)S(1)}, bf16[128,3072]{1,0:T(8,128)(2,1)S(1)}, u32[]{:S(2)}, u32[]{:S(2)}) collective-permute-start(bf16[128,3072]{1,0:T(8,128)(2,1)S(1)} %get-tuple-element.51), channel_id=1, source_target_pairs={{1,3},{2,0},{5,7},{6,4},{9,11},{10,8},{13,15},{14,12},{17,19},{18,... | collective-permute-start | bytes 2359304 | tf_op jit(solution)/shard_map/ppermute | solution.py:139
  133.4 55.3 %collective-permute-start.11 = (bf16[256,3072]{1,0:T(8,128)(2,1)S(1)}, bf16[256,3072]{1,0:T(8,128)(2,1)S(1)}, u32[]{:S(2)}, u32[]{:S(2)}) collective-permute-start(bf16[256,3072]{1,0:T(8,128)(2,1)S(1)} %get-tuple-element.48), channel_id=1, source_target_pairs={{1,0},{3,2},{5,4},{7,6},{9,8},{11,10},{13,12},{15,14},{17,16},{19,... | collective-permute-start | bytes 4718600 | tf_op jit(solution)/shard_map/ppermute | solution.py:136
  134.7 54.0 %collective-permute-start.10 = (bf16[256,3072]{1,0:T(8,128)(2,1)S(1)}, bf16[256,3072]{1,0:T(8,128)(2,1)S(1)}, u32[]{:S(2)}, u32[]{:S(2)}) collective-permute-start(bf16[256,3072]{1,0:T(8,128)(2,1)S(1)} %get-tuple-element.49), channel_id=1, source_target_pairs={{0,1},{2,3},{4,5},{6,7},{8,9},{10,11},{12,13},{14,15},{16,17},{18,... | collective-permute-start | bytes 4718600 | tf_op jit(solution)/shard_map/ppermute | solution.py:135
  151.9 36.7 %collective-permute-start.7 = (bf16[128,3072]{1,0:T(8,128)(2,1)S(1)}, bf16[128,3072]{1,0:T(8,128)(2,1)S(1)}, u32[]{:S(2)}, u32[]{:S(2)}) collective-permute-start(bf16[128,3072]{1,0:T(8,128)(2,1)S(1)} %collective-permute-done.6), channel_id=1, source_target_pairs={{3,2},{0,1},{7,6},{4,5},{11,10},{8,9},{15,14},{12,13},{19,18},{16,... | collective-permute-start | bytes 2359304 | tf_op jit(solution)/shard_map/ppermute | solution.py:141
  153.6 35.1 %collective-permute-start.9 = (bf16[128,3072]{1,0:T(8,128)(2,1)S(1)}, bf16[128,3072]{1,0:T(8,128)(2,1)S(1)}, u32[]{:S(2)}, u32[]{:S(2)}) collective-permute-start(bf16[128,3072]{1,0:T(8,128)(2,1)S(1)} %collective-permute-done.8), channel_id=1, source_target_pairs={{0,2},{3,1},{4,6},{7,5},{8,10},{11,9},{12,14},{15,13},{16,18},{19,... | collective-permute-start | bytes 2359304 | tf_op jit(solution)/shard_map/ppermute | solution.py:142
  200.5 137.4 %all-gather.5.cloned.1.call-start = ((), (), s32[]{:S(2)}) async-start(), calls=%async_computation.6 | async-start | bytes 7077888 | tf_op jit(solution)/shard_map/all_gather | solution.py:164
  274.7 142.9 %all-gather.7.cloned.1.call-start = ((), (), s32[]{:S(2)}) async-start(), calls=%async_computation.7 | async-start | bytes 3538944 | tf_op jit(solution)/shard_map/all_gather | solution.py:164
  339.4 181.3 %reduce-scatter.9.cloned.1.call-start = ((), (), s32[]{:S(2)}) async-start(), calls=%async_computation.8 | async-start | bytes 3538944 | tf_op jit(solution)/shard_map/reduce_scatter | solution.py:161
  355.1 25.3 %collective-permute-start.14 = (bf16[128,3072]{1,0:T(8,128)(2,1)S(1)}, bf16[128,3072]{1,0:T(8,128)(2,1)S(1)}, u32[]{:S(2)}, u32[]{:S(2)}) collective-permute-start(bf16[128,3072]{1,0:T(8,128)(2,1)S(1)} %get-tuple-element.58), channel_id=1, source_target_pairs={{1,0},{2,3},{5,4},{6,7},{9,8},{10,11},{13,12},{14,15},{17,16},{18,... | collective-permute-start | bytes 2359304 | tf_op jit(solution)/shard_map/ppermute | solution.py:140
  356.4 22.5 %collective-permute-start.12 = (bf16[128,3072]{1,0:T(8,128)(2,1)S(1)}, bf16[128,3072]{1,0:T(8,128)(2,1)S(1)}, u32[]{:S(2)}, u32[]{:S(2)}) collective-permute-start(bf16[128,3072]{1,0:T(8,128)(2,1)S(1)} %get-tuple-element.59), channel_id=1, source_target_pairs={{1,3},{2,0},{5,7},{6,4},{9,11},{10,8},{13,15},{14,12},{17,19},{18,... | collective-permute-start | bytes 2359304 | tf_op jit(solution)/shard_map/ppermute | solution.py:139
  358.2 57.5 %collective-permute-start.17 = (bf16[256,3072]{1,0:T(8,128)(2,1)S(1)}, bf16[256,3072]{1,0:T(8,128)(2,1)S(1)}, u32[]{:S(2)}, u32[]{:S(2)}) collective-permute-start(bf16[256,3072]{1,0:T(8,128)(2,1)S(1)} %get-tuple-element.56), channel_id=1, source_target_pairs={{1,0},{3,2},{5,4},{7,6},{9,8},{11,10},{13,12},{15,14},{17,16},{19,... | collective-permute-start | bytes 4718600 | tf_op jit(solution)/shard_map/ppermute | solution.py:136
  359.5 56.2 %collective-permute-start.16 = (bf16[256,3072]{1,0:T(8,128)(2,1)S(1)}, bf16[256,3072]{1,0:T(8,128)(2,1)S(1)}, u32[]{:S(2)}, u32[]{:S(2)}) collective-permute-start(bf16[256,3072]{1,0:T(8,128)(2,1)S(1)} %get-tuple-element.57), channel_id=1, source_target_pairs={{0,1},{2,3},{4,5},{6,7},{8,9},{10,11},{12,13},{14,15},{16,17},{18,... | collective-permute-start | bytes 4718600 | tf_op jit(solution)/shard_map/ppermute | solution.py:135
  378.9 36.7 %collective-permute-start.13 = (bf16[128,3072]{1,0:T(8,128)(2,1)S(1)}, bf16[128,3072]{1,0:T(8,128)(2,1)S(1)}, u32[]{:S(2)}, u32[]{:S(2)}) collective-permute-start(bf16[128,3072]{1,0:T(8,128)(2,1)S(1)} %collective-permute-done.12), channel_id=1, source_target_pairs={{3,2},{0,1},{7,6},{4,5},{11,10},{8,9},{15,14},{12,13},{19,18},{16,... | collective-permute-start | bytes 2359304 | tf_op jit(solution)/shard_map/ppermute | solution.py:141
  380.3 35.3 %collective-permute-start.15 = (bf16[128,3072]{1,0:T(8,128)(2,1)S(1)}, bf16[128,3072]{1,0:T(8,128)(2,1)S(1)}, u32[]{:S(2)}, u32[]{:S(2)}) collective-permute-start(bf16[128,3072]{1,0:T(8,128)(2,1)S(1)} %collective-permute-done.14), channel_id=1, source_target_pairs={{0,2},{3,1},{4,6},{7,5},{8,10},{11,9},{12,14},{15,13},{16,18},{19,... | collective-permute-start | bytes 2359304 | tf_op jit(solution)/shard_map/ppermute | solution.py:142
  457.8 141.1 %reduce-scatter.11.cloned.1.call-start = ((), (), s32[]{:S(2)}) async-start(), calls=%async_computation.9 | async-start | bytes 7077888 | tf_op jit(solution)/shard_map/reduce_scatter | solution.py:161
  460.0 23.6 %collective-permute-start.20 = (bf16[128,3072]{1,0:T(8,128)(2,1)S(1)}, bf16[128,3072]{1,0:T(8,128)(2,1)S(1)}, u32[]{:S(2)}, u32[]{:S(2)}) collective-permute-start(bf16[128,3072]{1,0:T(8,128)(2,1)S(1)} %get-tuple-element.46), channel_id=1, source_target_pairs={{1,0},{2,3},{5,4},{6,7},{9,8},{10,11},{13,12},{14,15},{17,16},{18,... | collective-permute-start | bytes 2359304 | tf_op jit(solution)/shard_map/ppermute | solution.py:140
  461.4 20.5 %collective-permute-start.18 = (bf16[128,3072]{1,0:T(8,128)(2,1)S(1)}, bf16[128,3072]{1,0:T(8,128)(2,1)S(1)}, u32[]{:S(2)}, u32[]{:S(2)}) collective-permute-start(bf16[128,3072]{1,0:T(8,128)(2,1)S(1)} %get-tuple-element.47), channel_id=1, source_target_pairs={{1,3},{2,0},{5,7},{6,4},{9,11},{10,8},{13,15},{14,12},{17,19},{18,... | collective-permute-start | bytes 2359304 | tf_op jit(solution)/shard_map/ppermute | solution.py:139
  462.9 55.8 %collective-permute-start.23 = (bf16[256,3072]{1,0:T(8,128)(2,1)S(1)}, bf16[256,3072]{1,0:T(8,128)(2,1)S(1)}, u32[]{:S(2)}, u32[]{:S(2)}) collective-permute-start(bf16[256,3072]{1,0:T(8,128)(2,1)S(1)} %get-tuple-element.44), channel_id=1, source_target_pairs={{1,0},{3,2},{5,4},{7,6},{9,8},{11,10},{13,12},{15,14},{17,16},{19,... | collective-permute-start | bytes 4718600 | tf_op jit(solution)/shard_map/ppermute | solution.py:136
  464.2 54.5 %collective-permute-start.22 = (bf16[256,3072]{1,0:T(8,128)(2,1)S(1)}, bf16[256,3072]{1,0:T(8,128)(2,1)S(1)}, u32[]{:S(2)}, u32[]{:S(2)}) collective-permute-start(bf16[256,3072]{1,0:T(8,128)(2,1)S(1)} %get-tuple-element.45), channel_id=1, source_target_pairs={{0,1},{2,3},{4,5},{6,7},{8,9},{10,11},{12,13},{14,15},{16,17},{18,... | collective-permute-start | bytes 4718600 | tf_op jit(solution)/shard_map/ppermute | solution.py:135
  481.9 36.7 %collective-permute-start.19 = (bf16[128,3072]{1,0:T(8,128)(2,1)S(1)}, bf16[128,3072]{1,0:T(8,128)(2,1)S(1)}, u32[]{:S(2)}, u32[]{:S(2)}) collective-permute-start(bf16[128,3072]{1,0:T(8,128)(2,1)S(1)} %collective-permute-done.18), channel_id=1, source_target_pairs={{3,2},{0,1},{7,6},{4,5},{11,10},{8,9},{15,14},{12,13},{19,18},{16,... | collective-permute-start | bytes 2359304 | tf_op jit(solution)/shard_map/ppermute | solution.py:141
  483.5 35.1 %collective-permute-start.21 = (bf16[128,3072]{1,0:T(8,128)(2,1)S(1)}, bf16[128,3072]{1,0:T(8,128)(2,1)S(1)}, u32[]{:S(2)}, u32[]{:S(2)}) collective-permute-start(bf16[128,3072]{1,0:T(8,128)(2,1)S(1)} %collective-permute-done.20), channel_id=1, source_target_pairs={{0,2},{3,1},{4,6},{7,5},{8,10},{11,9},{12,14},{15,13},{16,18},{19,... | collective-permute-start | bytes 2359304 | tf_op jit(solution)/shard_map/ppermute | solution.py:142
  530.5 134.5 %all-gather.9.cloned.1.call-start = ((), (), s32[]{:S(2)}) async-start(), calls=%async_computation.10 | async-start | bytes 7077888 | tf_op jit(solution)/shard_map/all_gather | solution.py:164
  601.7 102.4 %all-gather.11.cloned.1.call-start = ((), (), s32[]{:S(2)}) async-start(), calls=%async_computation.11 | async-start | bytes 3538944 | tf_op jit(solution)/shard_map/all_gather | solution.py:164
  (12 other events, 544.5 us)
Sparse Core Ops, SparseCore 0:
  128.4 41.6 reduce-scatter.4
  200.6 71.2 reduce-scatter.6
  274.8 62.9 all-gather.4
  339.5 36.9 all-gather.6
  457.9 38.8 reduce-scatter.8
  530.6 68.2 reduce-scatter.10
  601.8 63.0 all-gather.8
  667.2 36.9 all-gather.10

commit v15 on v14

--- a/solution.py
+++ b/solution.py
@@ -43,9 +43,11 @@
         o_ref[:, b * width : (b + 1) * width] = acc.astype(o_ref.dtype)
 
 
-def column_pass(fields, terms, tile_rows=256):
+def column_pass(fields, terms, tile_rows=384):
     fields = fields if isinstance(fields, tuple) else (fields,)
     rows, cols = fields[0].shape
+    if rows % tile_rows:
+        tile_rows = 256
     tile = pl.BlockSpec((tile_rows, cols), lambda r: (r, 0))
     return pl.pallas_call(
         column_kernel,

time: 732 us -> 736 us (level)
  no operation moved by 1% of the time
where the time goes in v15:
time: 736 us; the launch traced here: 729 us
  waiting for transfers between devices  454 us (62%)
  Pallas kernels  105 us (14%)
  other arithmetic  67.7 us (9%)
  starting transfers between devices  54.4 us (7%)
  local copies, waits for them, and re-layouts  17.1 us (2%)
  blocking collectives  15.7 us (2%)
  between operations  15.7 us (2%)
    all_gather x4, waiting for transfers between devices, gather_barycenter(): lax.all_gather(jnp.exp(part_sum / total_weight), 'img', axis=0, tiled=True)  150 us
    ppermute x4, waiting for transfers between devices, exchange(): first = lax.ppermute(first, 'slab', [(3, 2), (0, 1)])  129 us
    reduce_scatter x4, waiting for transfers between devices, log_sum(): lax.psum_scatter(value_portion, 'img', scatter_dimension=0, tiled=True)  124 us
    pallas_call x6, Pallas kernels, row_pass(): pl.pallas_call(functools.partial(row_kernel, blocks=tuple(blocks), has_ha...  52.6 us
    pallas_call x5, Pallas kernels, column_pass(): pl.pallas_call(column_kernel, grid=(rows // tile_rows,), in_specs=[tile]...  52 us
    ppermute x4, waiting for transfers between devices, exchange(): first = lax.ppermute(first, 'slab', [(1, 3), (2, 0)])  50.6 us
    ppermute x4, starting transfers between devices, exchange(): direct_prev = lax.ppermute(to_up, 'slab', [(0, 1), (2, 3)])  24.3 us
    psum x1, blocking collectives, per_device(): total_weight = lax.psum(jnp.sum(fraction_tops).astype(jnp.float32), 'img')  15.7 us
  transfers between devices with their start and end apart: 32, of which 13 were waited for; matrix products, arithmetic and copies ran while one was open for 5% of the time, Pallas kernels for 1%

profile of v15, /device:TPU:0, one launch (start us, length us, event | category | flops | bytes accessed | tf_op | source)
XLA Modules:
  0.0 729.2 jit_solution(8401578463168904054)
XLA Ops:
  8.1 8.3 %select_reduce_fusion.refs_1_.refs_2_ = bf16[24,5,128,128]{3,2,1,0:T(8,128)(2,1)} fusion(pred[24,5,3]{2,1,0:T(8,128)(4,1)S(1)} %broadcast_compare_fusion, bf16[24,3,128,128]{3,2,1,0:T(8,128)(2,1)} %param.8), kind=kLoop, calls=%fused_computation | loop fusion | flops 9830400 | bytes 6291816 | tf_op jit(solution)/shard_map/reduce_sum | solution.py:19
  16.4 11.1 %shard_map.68.refs_1_ = bf16[768,3072]{1,0:T(8,128)(2,1)} custom-call(f32[768,3072]{1,0:T(8,128)} %bitcast.18, bf16[24,5,128,128]{3,2,1,0:T(8,128)(2,1)} %select_reduce_fusion.refs_1_.refs_2_), custom_call_target="tpu_custom_call" | custom-call | tf_op jit(solution)/shard_map/pallas_call | solution.py:52
  35.0 9.2 %collective-permute-start.4 = (bf16[256,3072]{1,0:T(8,128)(2,1)S(1)}, bf16[256,3072]{1,0:T(8,128)(2,1)}, u32[]{:S(2)}, u32[]{:S(2)}) collective-permute-start(bf16[256,3072]{1,0:T(8,128)(2,1)S(1)} %get-tuple-element.53), channel_id=1, source_target_pairs={{0,1},{2,3},{4,5},{6,7},{8,9},{10,11},{12,13},{14,15},{16,17},{18,... | collective-permute-start | bytes 4718600 | tf_op jit(solution)/shard_map/ppermute | solution.py:137
  44.2 11.5 %collective-permute-done = bf16[128,3072]{1,0:T(8,128)(2,1)} collective-permute-done((bf16[128,3072]{1,0:T(8,128)(2,1)S(1)}, bf16[128,3072]{1,0:T(8,128)(2,1)}, u32[]{:S(2)}, u32[]{:S(2)}) %collective-permute-start) | collective-permute-done | bytes 786464 | tf_op jit(solution)/shard_map/ppermute | solution.py:141
  63.1 30.2 %collective-permute-done.1 = bf16[128,3072]{1,0:T(8,128)(2,1)} collective-permute-done((bf16[128,3072]{1,0:T(8,128)(2,1)}, bf16[128,3072]{1,0:T(8,128)(2,1)}, u32[]{:S(2)}, u32[]{:S(2)}) %collective-permute-start.1) | collective-permute-done | bytes 786464 | tf_op jit(solution)/shard_map/ppermute | solution.py:143
  99.1 10.9 %shard_map.69.refs_1_ = bf16[768,3072]{1,0:T(8,128)(2,1)} custom-call(bf16[256,3072]{1,0:T(8,128)(2,1)} %get-tuple-element.67.refs_0_, bf16[768,3072]{1,0:T(8,128)(2,1)} %shard_map.68.refs_1_, bf16[256,3072]{1,0:T(8,128)(2,1)} %get-tuple-element.66.refs_2_, bf16[6,5,128,128]{3,2,1,0:T(8,128)(2,1)} %constant_dynamic-slice_fusion.refs_3_.refs_1_), custom_call_target="tpu_custom_call" | custom-call | tf_op jit(solution)/shard_map/pallas_call | solution.py:108
  110.0 11.9 %shard_map.70.refs_0_.refs_1_ = bf16[768,3072]{1,0:T(8,128)(2,1)} custom-call(f32[768,3072]{1,0:T(8,128)} %bitcast.15, bf16[768,3072]{1,0:T(8,128)(2,1)} %shard_map.69.refs_1_, bf16[24,5,128,128]{3,2,1,0:T(8,128)(2,1)} %select_reduce_fusion.refs_1_.refs_2_), custom_call_target="tpu_custom_call" | custom-call | tf_op jit(solution)/shard_map/pallas_call | solution.py:52
  121.8 5.7 shard_map.71
  134.0 4.8 collective-permute-start.10
  138.9 12.3 %collective-permute-done.6 = bf16[128,3072]{1,0:T(8,128)(2,1)S(1)} collective-permute-done((bf16[128,3072]{1,0:T(8,128)(2,1)S(1)}, bf16[128,3072]{1,0:T(8,128)(2,1)S(1)}, u32[]{:S(2)}, u32[]{:S(2)}) %collective-permute-start.6) | collective-permute-done | bytes 786464 | tf_op jit(solution)/shard_map/ppermute | solution.py:141
  154.2 33.7 %collective-permute-done.7 = bf16[128,3072]{1,0:T(8,128)(2,1)S(1)} collective-permute-done((bf16[128,3072]{1,0:T(8,128)(2,1)S(1)}, bf16[128,3072]{1,0:T(8,128)(2,1)S(1)}, u32[]{:S(2)}, u32[]{:S(2)}) %collective-permute-start.7) | collective-permute-done | bytes 786464 | tf_op jit(solution)/shard_map/ppermute | solution.py:143
  190.1 9.7 %shard_map.72 = (bf16[512,3072]{1,0:T(8,128)(2,1)}, f32[512,3072]{1,0:T(8,128)}) custom-call(bf16[256,3072]{1,0:T(8,128)(2,1)} %get-tuple-element.21.refs_0_, bf16[768,3072]{1,0:T(8,128)(2,1)} %shard_map.70.refs_0_.refs_1_, bf16[256,3072]{1,0:T(8,128)(2,1)} %get-tuple-element.22.refs_2_, bf16[6,5,128,128]{3,2,1,0:T(8,128)(2,1)} %constant_dynamic-slice_fusion.refs_3_.refs_1_, ...), custom_call_target="tpu_custom_call" | custom-call | tf_op jit(solution)/shard_map/pallas_call | solution.py:108
  199.9 15.7 %psum.7 = f32[]{:T(128)} all-reduce(f32[]{:T(128)} %bitcast.2), channel_id=1, replica_groups=mesh['img'=8,'slab'=4] {'img'}, use_global_device_ids=true, to_apply=%region_3.4 | all-reduce | flops 1 | bytes 8 | tf_op jit(solution)/shard_map/psum | solution.py:127
  215.6 55.6 %reduce-scatter.7.cloned.1.call-done = f32[64,3072]{1,0:T(8,128)} async-done(((f32[512,3072]{1,0:T(8,128)}), f32[64,3072]{1,0:T(8,128)}) %reduce-scatter.7.cloned.1.call-update) | async-done | bytes 786448 | tf_op jit(solution)/shard_map/reduce_scatter | solution.py:163
  274.1 63.1 %all-gather.5.cloned.1.call-done.refs_0_ = f32[512,3072]{1,0:T(8,128)} async-done(((f32[64,3072]{1,0:T(8,128)}), f32[512,3072]{1,0:T(8,128)}) %all-gather.5.cloned.1.call-update) | async-done | bytes 6291472 | tf_op jit(solution)/shard_map/all_gather | solution.py:166
  342.3 9.9 %shard_map.73 = bf16[512,3072]{1,0:T(8,128)(2,1)} custom-call(f32[512,3072]{1,0:T(8,128)} %all-gather.5.cloned.1.call-done.refs_0_, f32[512,3072]{1,0:T(8,128)} %convert_element_type.21.refs_1_, bf16[24,5,128,128]{3,2,1,0:T(8,128)(2,1)} %select_reduce_fusion.refs_1_.refs_2_), custom_call_target="tpu_custom_call" | custom-call | tf_op jit(solution)/shard_map/pallas_call | solution.py:52
  358.6 5.5 collective-permute-start.16
  364.1 14.0 %collective-permute-done.12 = bf16[128,3072]{1,0:T(8,128)(2,1)S(1)} collective-permute-done((bf16[128,3072]{1,0:T(8,128)(2,1)S(1)}, bf16[128,3072]{1,0:T(8,128)(2,1)S(1)}, u32[]{:S(2)}, u32[]{:S(2)}) %collective-permute-start.12) | collective-permute-done | bytes 786464 | tf_op jit(solution)/shard_map/ppermute | solution.py:141
  383.2 31.4 %collective-permute-done.13 = bf16[128,3072]{1,0:T(8,128)(2,1)S(1)} collective-permute-done((bf16[128,3072]{1,0:T(8,128)(2,1)S(1)}, bf16[128,3072]{1,0:T(8,128)(2,1)S(1)}, u32[]{:S(2)}, u32[]{:S(2)}) %collective-permute-start.13) | collective-permute-done | bytes 786464 | tf_op jit(solution)/shard_map/ppermute | solution.py:143
  416.7 7.2 shard_map.74
  427.4 10.9 %shard_map.75.refs_1_ = bf16[768,3072]{1,0:T(8,128)(2,1)} custom-call(bf16[256,3072]{1,0:T(8,128)(2,1)} %get-tuple-element.63.refs_0_, bf16[768,3072]{1,0:T(8,128)(2,1)} %pad_maximum_fusion.1.refs_1_, bf16[256,3072]{1,0:T(8,128)(2,1)} %get-tuple-element.62.refs_2_, bf16[6,5,128,128]{3,2,1,0:T(8,128)(2,1)} %constant_dynamic-slice_fusion.refs_3_.refs_1_), custom_call_target="tpu_custom_call" | custom-call | tf_op jit(solution)/shard_map/pallas_call | solution.py:108
  438.3 11.8 %shard_map.76.refs_0_.refs_1_ = bf16[768,3072]{1,0:T(8,128)(2,1)} custom-call(f32[768,3072]{1,0:T(8,128)} %bitcast.16, bf16[768,3072]{1,0:T(8,128)(2,1)} %shard_map.75.refs_1_, bf16[24,5,128,128]{3,2,1,0:T(8,128)(2,1)} %select_reduce_fusion.refs_1_.refs_2_), custom_call_target="tpu_custom_call" | custom-call | tf_op jit(solution)/shard_map/pallas_call | solution.py:52
  450.1 5.7 shard_map.77
  467.2 12.8 %collective-permute-done.18 = bf16[128,3072]{1,0:T(8,128)(2,1)S(1)} collective-permute-done((bf16[128,3072]{1,0:T(8,128)(2,1)S(1)}, bf16[128,3072]{1,0:T(8,128)(2,1)S(1)}, u32[]{:S(2)}, u32[]{:S(2)}) %collective-permute-start.18) | collective-permute-done | bytes 786464 | tf_op jit(solution)/shard_map/ppermute | solution.py:141
  483.0 33.7 %collective-permute-done.19 = bf16[128,3072]{1,0:T(8,128)(2,1)S(1)} collective-permute-done((bf16[128,3072]{1,0:T(8,128)(2,1)S(1)}, bf16[128,3072]{1,0:T(8,128)(2,1)S(1)}, u32[]{:S(2)}, u32[]{:S(2)}) %collective-permute-start.19) | collective-permute-done | bytes 786464 | tf_op jit(solution)/shard_map/ppermute | solution.py:143
  518.8 9.7 %shard_map.78 = (bf16[512,3072]{1,0:T(8,128)(2,1)}, f32[512,3072]{1,0:T(8,128)}) custom-call(bf16[256,3072]{1,0:T(8,128)(2,1)} %get-tuple-element.30.refs_0_, bf16[768,3072]{1,0:T(8,128)(2,1)} %shard_map.76.refs_0_.refs_1_, bf16[256,3072]{1,0:T(8,128)(2,1)} %get-tuple-element.31.refs_2_, bf16[6,5,128,128]{3,2,1,0:T(8,128)(2,1)} %constant_dynamic-slice_fusion.refs_3_.refs_1_, ...), custom_call_target="tpu_custom_call" | custom-call | tf_op jit(solution)/shard_map/pallas_call | solution.py:108
  528.9 68.2 %reduce-scatter.11.cloned.1.call-done = f32[64,3072]{1,0:T(8,128)} async-done(((f32[512,3072]{1,0:T(8,128)}), f32[64,3072]{1,0:T(8,128)}) %reduce-scatter.11.cloned.1.call-update) | async-done | bytes 786448 | tf_op jit(solution)/shard_map/reduce_scatter | solution.py:163
  599.9 63.2 %all-gather.9.cloned.1.call-done = f32[512,3072]{1,0:T(8,128)} async-done(((f32[64,3072]{1,0:T(8,128)}), f32[512,3072]{1,0:T(8,128)}) %all-gather.9.cloned.1.call-update) | async-done | bytes 6291472 | tf_op jit(solution)/shard_map/all_gather | solution.py:166
  672.9 5.5 slice_bitcast_fusion.3
  678.4 23.9 %all-gather.11.cloned.1.call-done = f32[256,3072]{1,0:T(8,128)} async-done(((f32[32,3072]{1,0:T(8,128)}), f32[256,3072]{1,0:T(8,128)}) %all-gather.11.cloned.1.call-update) | async-done | bytes 3145744 | tf_op jit(solution)/shard_map/all_gather | solution.py:166
  702.3 11.9 %maximum_divide_fusion = f32[1,768,3072]{2,1,0:T(8,128)} fusion(f32[1,256,3072]{2,1,0:T(8,128)} %get-tuple-element.41, f32[1,256,3072]{2,1,0:T(8,128)} %bitcast.17, f32[1,256,3072]{2,1,0:T(8,128)} %get-tuple-element.40, f32[1,256,3072]{2,1,0:T(8,128)} %get-tuple-element.39, f32[1,256,3072]{2,1,0:T(8,128)} %bitcast_convert_fusion, ...), kind=kLoop, calls=%fused_computation.2 | loop fusion | flops 11796480 | bytes 28311552 | tf_op jit(solution)/shard_map/div | solution.py:201
  714.3 7.7 %pad_maximum_fusion = f32[768,3072]{1,0:T(8,128)} fusion(f32[256,3072]{1,0:T(8,128)} %get-tuple-element.42, f32[256,3072]{1,0:T(8,128)S(1)} %copy-done.4, f32[256,3072]{1,0:T(8,128)} %get-tuple-element.43), kind=kLoop, calls=%fused_computation.1 | loop fusion | flops 4718592 | bytes 18874368 | tf_op jit(solution)/shard_map/concatenate | solution.py:187
  (115 shorter events, 86.5 us)
Async XLA Ops:
  7.2 182.9 %reduce-scatter.5.cloned.1.call-start = ((), (), s32[]{:S(2)}) async-start(), calls=%async_computation.4 | async-start | bytes 3538944 | tf_op jit(solution)/shard_map/reduce_scatter | solution.py:163
  29.6 28.2 %collective-permute-start.2 = (bf16[128,3072]{1,0:T(8,128)(2,1)S(1)}, bf16[128,3072]{1,0:T(8,128)(2,1)}, u32[]{:S(2)}, u32[]{:S(2)}) collective-permute-start(bf16[128,3072]{1,0:T(8,128)(2,1)S(1)} %get-tuple-element.54), channel_id=1, source_target_pairs={{1,0},{2,3},{5,4},{6,7},{9,8},{10,11},{13,12},{14,15},{17,16},{18,... | collective-permute-start | bytes 2359304 | tf_op jit(solution)/shard_map/ppermute | solution.py:142
  31.1 24.6 %collective-permute-start = (bf16[128,3072]{1,0:T(8,128)(2,1)S(1)}, bf16[128,3072]{1,0:T(8,128)(2,1)}, u32[]{:S(2)}, u32[]{:S(2)}) collective-permute-start(bf16[128,3072]{1,0:T(8,128)(2,1)S(1)} %get-tuple-element.55), channel_id=1, source_target_pairs={{1,3},{2,0},{5,7},{6,4},{9,11},{10,8},{13,15},{14,12},{17,19},{18,... | collective-permute-start | bytes 2359304 | tf_op jit(solution)/shard_map/ppermute | solution.py:141
  33.7 62.0 %collective-permute-start.5 = (bf16[256,3072]{1,0:T(8,128)(2,1)}, bf16[256,3072]{1,0:T(8,128)(2,1)S(1)}, u32[]{:S(2)}, u32[]{:S(2)}) collective-permute-start(bf16[256,3072]{1,0:T(8,128)(2,1)} %get-tuple-element.52), channel_id=1, source_target_pairs={{1,0},{3,2},{5,4},{7,6},{9,8},{11,10},{13,12},{15,14},{17,16},{19,... | collective-permute-start | bytes 4718600 | tf_op jit(solution)/shard_map/ppermute | solution.py:138
  35.0 60.7 %collective-permute-start.4 = (bf16[256,3072]{1,0:T(8,128)(2,1)S(1)}, bf16[256,3072]{1,0:T(8,128)(2,1)}, u32[]{:S(2)}, u32[]{:S(2)}) collective-permute-start(bf16[256,3072]{1,0:T(8,128)(2,1)S(1)} %get-tuple-element.53), channel_id=1, source_target_pairs={{0,1},{2,3},{4,5},{6,7},{8,9},{10,11},{12,13},{14,15},{16,17},{18,... | collective-permute-start | bytes 4718600 | tf_op jit(solution)/shard_map/ppermute | solution.py:137
  55.7 37.6 %collective-permute-start.1 = (bf16[128,3072]{1,0:T(8,128)(2,1)}, bf16[128,3072]{1,0:T(8,128)(2,1)}, u32[]{:S(2)}, u32[]{:S(2)}) collective-permute-start(bf16[128,3072]{1,0:T(8,128)(2,1)} %collective-permute-done), channel_id=1, source_target_pairs={{3,2},{0,1},{7,6},{4,5},{11,10},{8,9},{15,14},{12,13},{19,18},{16,... | collective-permute-start | bytes 2359304 | tf_op jit(solution)/shard_map/ppermute | solution.py:143
  57.9 36.6 %collective-permute-start.3 = (bf16[128,3072]{1,0:T(8,128)(2,1)}, bf16[128,3072]{1,0:T(8,128)(2,1)}, u32[]{:S(2)}, u32[]{:S(2)}) collective-permute-start(bf16[128,3072]{1,0:T(8,128)(2,1)} %collective-permute-done.2), channel_id=1, source_target_pairs={{0,2},{3,1},{4,6},{7,5},{8,10},{11,9},{12,14},{15,13},{16,18},{19,... | collective-permute-start | bytes 2359304 | tf_op jit(solution)/shard_map/ppermute | solution.py:144
  127.6 143.6 %reduce-scatter.7.cloned.1.call-start = ((), (), s32[]{:S(2)}) async-start(), calls=%async_computation.5 | async-start | bytes 7077888 | tf_op jit(solution)/shard_map/reduce_scatter | solution.py:163
  129.8 23.1 %collective-permute-start.8 = (bf16[128,3072]{1,0:T(8,128)(2,1)S(1)}, bf16[128,3072]{1,0:T(8,128)(2,1)S(1)}, u32[]{:S(2)}, u32[]{:S(2)}) collective-permute-start(bf16[128,3072]{1,0:T(8,128)(2,1)S(1)} %get-tuple-element.50), channel_id=1, source_target_pairs={{1,0},{2,3},{5,4},{6,7},{9,8},{10,11},{13,12},{14,15},{17,16},{18,... | collective-permute-start | bytes 2359304 | tf_op jit(solution)/shard_map/ppermute | solution.py:142
  131.2 20.0 %collective-permute-start.6 = (bf16[128,3072]{1,0:T(8,128)(2,1)S(1)}, bf16[128,3072]{1,0:T(8,128)(2,1)S(1)}, u32[]{:S(2)}, u32[]{:S(2)}) collective-permute-start(bf16[128,3072]{1,0:T(8,128)(2,1)S(1)} %get-tuple-element.51), channel_id=1, source_target_pairs={{1,3},{2,0},{5,7},{6,4},{9,11},{10,8},{13,15},{14,12},{17,19},{18,... | collective-permute-start | bytes 2359304 | tf_op jit(solution)/shard_map/ppermute | solution.py:141
  132.7 55.3 %collective-permute-start.11 = (bf16[256,3072]{1,0:T(8,128)(2,1)S(1)}, bf16[256,3072]{1,0:T(8,128)(2,1)S(1)}, u32[]{:S(2)}, u32[]{:S(2)}) collective-permute-start(bf16[256,3072]{1,0:T(8,128)(2,1)S(1)} %get-tuple-element.48), channel_id=1, source_target_pairs={{1,0},{3,2},{5,4},{7,6},{9,8},{11,10},{13,12},{15,14},{17,16},{19,... | collective-permute-start | bytes 4718600 | tf_op jit(solution)/shard_map/ppermute | solution.py:138
  134.0 54.0 %collective-permute-start.10 = (bf16[256,3072]{1,0:T(8,128)(2,1)S(1)}, bf16[256,3072]{1,0:T(8,128)(2,1)S(1)}, u32[]{:S(2)}, u32[]{:S(2)}) collective-permute-start(bf16[256,3072]{1,0:T(8,128)(2,1)S(1)} %get-tuple-element.49), channel_id=1, source_target_pairs={{0,1},{2,3},{4,5},{6,7},{8,9},{10,11},{12,13},{14,15},{16,17},{18,... | collective-permute-start | bytes 4718600 | tf_op jit(solution)/shard_map/ppermute | solution.py:137
  151.2 36.7 %collective-permute-start.7 = (bf16[128,3072]{1,0:T(8,128)(2,1)S(1)}, bf16[128,3072]{1,0:T(8,128)(2,1)S(1)}, u32[]{:S(2)}, u32[]{:S(2)}) collective-permute-start(bf16[128,3072]{1,0:T(8,128)(2,1)S(1)} %collective-permute-done.6), channel_id=1, source_target_pairs={{3,2},{0,1},{7,6},{4,5},{11,10},{8,9},{15,14},{12,13},{19,18},{16,... | collective-permute-start | bytes 2359304 | tf_op jit(solution)/shard_map/ppermute | solution.py:143
  152.9 35.1 %collective-permute-start.9 = (bf16[128,3072]{1,0:T(8,128)(2,1)S(1)}, bf16[128,3072]{1,0:T(8,128)(2,1)S(1)}, u32[]{:S(2)}, u32[]{:S(2)}) collective-permute-start(bf16[128,3072]{1,0:T(8,128)(2,1)S(1)} %collective-permute-done.8), channel_id=1, source_target_pairs={{0,2},{3,1},{4,6},{7,5},{8,10},{11,9},{12,14},{15,13},{16,18},{19,... | collective-permute-start | bytes 2359304 | tf_op jit(solution)/shard_map/ppermute | solution.py:144
  199.8 137.4 %all-gather.5.cloned.1.call-start = ((), (), s32[]{:S(2)}) async-start(), calls=%async_computation.6 | async-start | bytes 7077888 | tf_op jit(solution)/shard_map/all_gather | solution.py:166
  274.0 142.7 %all-gather.7.cloned.1.call-start = ((), (), s32[]{:S(2)}) async-start(), calls=%async_computation.7 | async-start | bytes 3538944 | tf_op jit(solution)/shard_map/all_gather | solution.py:166
  338.7 180.1 %reduce-scatter.9.cloned.1.call-start = ((), (), s32[]{:S(2)}) async-start(), calls=%async_computation.8 | async-start | bytes 3538944 | tf_op jit(solution)/shard_map/reduce_scatter | solution.py:163
  354.4 25.2 %collective-permute-start.14 = (bf16[128,3072]{1,0:T(8,128)(2,1)S(1)}, bf16[128,3072]{1,0:T(8,128)(2,1)S(1)}, u32[]{:S(2)}, u32[]{:S(2)}) collective-permute-start(bf16[128,3072]{1,0:T(8,128)(2,1)S(1)} %get-tuple-element.58), channel_id=1, source_target_pairs={{1,0},{2,3},{5,4},{6,7},{9,8},{10,11},{13,12},{14,15},{17,16},{18,... | collective-permute-start | bytes 2359304 | tf_op jit(solution)/shard_map/ppermute | solution.py:142
  355.7 22.5 %collective-permute-start.12 = (bf16[128,3072]{1,0:T(8,128)(2,1)S(1)}, bf16[128,3072]{1,0:T(8,128)(2,1)S(1)}, u32[]{:S(2)}, u32[]{:S(2)}) collective-permute-start(bf16[128,3072]{1,0:T(8,128)(2,1)S(1)} %get-tuple-element.59), channel_id=1, source_target_pairs={{1,3},{2,0},{5,7},{6,4},{9,11},{10,8},{13,15},{14,12},{17,19},{18,... | collective-permute-start | bytes 2359304 | tf_op jit(solution)/shard_map/ppermute | solution.py:141
  357.3 57.5 %collective-permute-start.17 = (bf16[256,3072]{1,0:T(8,128)(2,1)S(1)}, bf16[256,3072]{1,0:T(8,128)(2,1)S(1)}, u32[]{:S(2)}, u32[]{:S(2)}) collective-permute-start(bf16[256,3072]{1,0:T(8,128)(2,1)S(1)} %get-tuple-element.56), channel_id=1, source_target_pairs={{1,0},{3,2},{5,4},{7,6},{9,8},{11,10},{13,12},{15,14},{17,16},{19,... | collective-permute-start | bytes 4718600 | tf_op jit(solution)/shard_map/ppermute | solution.py:138
  358.6 56.2 %collective-permute-start.16 = (bf16[256,3072]{1,0:T(8,128)(2,1)S(1)}, bf16[256,3072]{1,0:T(8,128)(2,1)S(1)}, u32[]{:S(2)}, u32[]{:S(2)}) collective-permute-start(bf16[256,3072]{1,0:T(8,128)(2,1)S(1)} %get-tuple-element.57), channel_id=1, source_target_pairs={{0,1},{2,3},{4,5},{6,7},{8,9},{10,11},{12,13},{14,15},{16,17},{18,... | collective-permute-start | bytes 4718600 | tf_op jit(solution)/shard_map/ppermute | solution.py:137
  378.2 36.5 %collective-permute-start.13 = (bf16[128,3072]{1,0:T(8,128)(2,1)S(1)}, bf16[128,3072]{1,0:T(8,128)(2,1)S(1)}, u32[]{:S(2)}, u32[]{:S(2)}) collective-permute-start(bf16[128,3072]{1,0:T(8,128)(2,1)S(1)} %collective-permute-done.12), channel_id=1, source_target_pairs={{3,2},{0,1},{7,6},{4,5},{11,10},{8,9},{15,14},{12,13},{19,18},{16,... | collective-permute-start | bytes 2359304 | tf_op jit(solution)/shard_map/ppermute | solution.py:143
  379.6 35.1 %collective-permute-start.15 = (bf16[128,3072]{1,0:T(8,128)(2,1)S(1)}, bf16[128,3072]{1,0:T(8,128)(2,1)S(1)}, u32[]{:S(2)}, u32[]{:S(2)}) collective-permute-start(bf16[128,3072]{1,0:T(8,128)(2,1)S(1)} %collective-permute-done.14), channel_id=1, source_target_pairs={{0,2},{3,1},{4,6},{7,5},{8,10},{11,9},{12,14},{15,13},{16,18},{19,... | collective-permute-start | bytes 2359304 | tf_op jit(solution)/shard_map/ppermute | solution.py:144
  455.9 141.2 %reduce-scatter.11.cloned.1.call-start = ((), (), s32[]{:S(2)}) async-start(), calls=%async_computation.9 | async-start | bytes 7077888 | tf_op jit(solution)/shard_map/reduce_scatter | solution.py:163
  458.1 23.5 %collective-permute-start.20 = (bf16[128,3072]{1,0:T(8,128)(2,1)S(1)}, bf16[128,3072]{1,0:T(8,128)(2,1)S(1)}, u32[]{:S(2)}, u32[]{:S(2)}) collective-permute-start(bf16[128,3072]{1,0:T(8,128)(2,1)S(1)} %get-tuple-element.46), channel_id=1, source_target_pairs={{1,0},{2,3},{5,4},{6,7},{9,8},{10,11},{13,12},{14,15},{17,16},{18,... | collective-permute-start | bytes 2359304 | tf_op jit(solution)/shard_map/ppermute | solution.py:142
  459.5 20.4 %collective-permute-start.18 = (bf16[128,3072]{1,0:T(8,128)(2,1)S(1)}, bf16[128,3072]{1,0:T(8,128)(2,1)S(1)}, u32[]{:S(2)}, u32[]{:S(2)}) collective-permute-start(bf16[128,3072]{1,0:T(8,128)(2,1)S(1)} %get-tuple-element.47), channel_id=1, source_target_pairs={{1,3},{2,0},{5,7},{6,4},{9,11},{10,8},{13,15},{14,12},{17,19},{18,... | collective-permute-start | bytes 2359304 | tf_op jit(solution)/shard_map/ppermute | solution.py:141
  461.1 55.8 %collective-permute-start.23 = (bf16[256,3072]{1,0:T(8,128)(2,1)S(1)}, bf16[256,3072]{1,0:T(8,128)(2,1)S(1)}, u32[]{:S(2)}, u32[]{:S(2)}) collective-permute-start(bf16[256,3072]{1,0:T(8,128)(2,1)S(1)} %get-tuple-element.44), channel_id=1, source_target_pairs={{1,0},{3,2},{5,4},{7,6},{9,8},{11,10},{13,12},{15,14},{17,16},{19,... | collective-permute-start | bytes 4718600 | tf_op jit(solution)/shard_map/ppermute | solution.py:138
  462.4 54.5 %collective-permute-start.22 = (bf16[256,3072]{1,0:T(8,128)(2,1)S(1)}, bf16[256,3072]{1,0:T(8,128)(2,1)S(1)}, u32[]{:S(2)}, u32[]{:S(2)}) collective-permute-start(bf16[256,3072]{1,0:T(8,128)(2,1)S(1)} %get-tuple-element.45), channel_id=1, source_target_pairs={{0,1},{2,3},{4,5},{6,7},{8,9},{10,11},{12,13},{14,15},{16,17},{18,... | collective-permute-start | bytes 4718600 | tf_op jit(solution)/shard_map/ppermute | solution.py:137
  480.0 36.7 %collective-permute-start.19 = (bf16[128,3072]{1,0:T(8,128)(2,1)S(1)}, bf16[128,3072]{1,0:T(8,128)(2,1)S(1)}, u32[]{:S(2)}, u32[]{:S(2)}) collective-permute-start(bf16[128,3072]{1,0:T(8,128)(2,1)S(1)} %collective-permute-done.18), channel_id=1, source_target_pairs={{3,2},{0,1},{7,6},{4,5},{11,10},{8,9},{15,14},{12,13},{19,18},{16,... | collective-permute-start | bytes 2359304 | tf_op jit(solution)/shard_map/ppermute | solution.py:143
  481.7 35.1 %collective-permute-start.21 = (bf16[128,3072]{1,0:T(8,128)(2,1)S(1)}, bf16[128,3072]{1,0:T(8,128)(2,1)S(1)}, u32[]{:S(2)}, u32[]{:S(2)}) collective-permute-start(bf16[128,3072]{1,0:T(8,128)(2,1)S(1)} %collective-permute-done.20), channel_id=1, source_target_pairs={{0,2},{3,1},{4,6},{7,5},{8,10},{11,9},{12,14},{15,13},{16,18},{19,... | collective-permute-start | bytes 2359304 | tf_op jit(solution)/shard_map/ppermute | solution.py:144
  528.6 134.6 %all-gather.9.cloned.1.call-start = ((), (), s32[]{:S(2)}) async-start(), calls=%async_computation.10 | async-start | bytes 7077888 | tf_op jit(solution)/shard_map/all_gather | solution.py:166
  599.9 102.4 %all-gather.11.cloned.1.call-start = ((), (), s32[]{:S(2)}) async-start(), calls=%async_computation.11 | async-start | bytes 3538944 | tf_op jit(solution)/shard_map/all_gather | solution.py:166
  (12 other events, 544.6 us)
Sparse Core Ops, SparseCore 0:
  127.7 41.6 reduce-scatter.4
  199.9 71.2 reduce-scatter.6
  274.1 63.0 all-gather.4
  338.8 36.9 all-gather.6
  456.0 38.8 reduce-scatter.8
  528.7 68.3 reduce-scatter.10
  600.0 63.0 all-gather.8
  665.3 36.9 all-gather.10
